TPU v7x, 32 devices: a whole 2x2x4 slice. The times are simulated.
32 devices in a mesh: grp: 2 (over y), seq: 4 (over z), head: 4 (over x, core).
Axes of the slice: x: 2, y: 2, z: 4, core: 2. Of those that a mesh axis runs over, the one named last changes fastest.
Arguments:
- lin_query: bfloat16 [2560, 8192], P(('grp', 'seq'), 'head'), parts along dimension 0, may hold values from -6 to 6
- lin_key: bfloat16 [2560, 8192], P(('grp', 'seq'), 'head'), parts along dimension 0, may hold values from -6 to 6
- lin_value: bfloat16 [2560, 8192], P(('grp', 'seq'), 'head'), parts along dimension 0, may hold values from -6 to 6
- norm_gain: bfloat16 [8192], P('head'), may hold values from 0.25 to 1.75
- out_gate: bfloat16 [2560, 8192], P(('grp', 'seq'), 'head'), parts along dimension 0, may hold values from -6 to 6
- soft_query: bfloat16 [2560, 8192], P(('grp', 'seq'), 'head'), parts along dimension 0, may hold values from -24 to 24
- soft_key: bfloat16 [2560, 8192], P(('grp', 'seq'), 'head'), parts along dimension 0, may hold values from -24 to 24
- doc_id: int32 [2560], P(('grp', 'seq')), parts along dimension 0, may hold values from 0 to 7, never falling along the last dimension, each value on 1 to 640 neighbouring positions
Outputs:
- lin_out: bfloat16 [2560, 8192], P(('grp', 'seq'), 'head'), parts along dimension 0
- soft_out: bfloat16 [2560, 8192], P(('grp', 'seq'), 'head'), parts along dimension 0
There are 2 independent parts, one for each index of `grp`. A program takes and returns all parts, laid end to end along the dimension named above; an argument that names none is the same for every part. Nothing has to cross between parts.
Inputs may be any that keep to these rules, and one draw needn't show every extreme that they name: `doc_id`: never falls along the sequence; every document holds 1 to half of 1280 tokens, and one holds exactly half of 1280.
All inputs are finite; a program needn't handle non-finite values.
Results may differ from a plain program's by a relative error of at most 0.0095.
Values may be sent and summed in bfloat16 or wider, within the bound.
No kernel may reach another device: no remote copies, remote signals or barrier semaphores. Data moves between devices by JAX's collectives and lax.ppermute only.
A program may use at most 192 MiB of HBM per device.

v0:
```python
import math

import jax
import jax.numpy as jnp
from jax import lax
from jax.sharding import PartitionSpec as P

HD = 128


norm_eps = 1e-06


def per_device(lin_query, lin_key, lin_value, norm_gain, out_gate, soft_query, soft_key, doc_id):
    row_count = lin_query.shape[0]
    head_count = lin_query.shape[1] // HD
    my_index = lax.axis_index("seq")
    queries = lin_query.reshape(row_count, head_count, HD)
    key_rows = lin_key.reshape(row_count, head_count, HD)
    value_rows = lin_value.reshape(row_count, head_count, HD)
    first_doc = doc_id[0]
    last_doc = doc_id[-1]
    tail_keys = jnp.where((doc_id == last_doc)[:, None, None], key_rows, jnp.zeros_like(key_rows))
    local_state = jnp.einsum(
        "thd,the->hde", tail_keys, value_rows, preferred_element_type=jnp.float32
    )
    empty_state = jnp.zeros_like(local_state)
    states = lax.all_gather(
        local_state[None].astype(jnp.bfloat16), "seq", axis=0, tiled=True
    ).astype(jnp.float32)
    tags = lax.all_gather(last_doc[None], "seq", axis=0, tiled=True)
    sources = jnp.arange(tags.shape[0], dtype=jnp.int32)
    wanted = (tags == first_doc) & (sources < my_index)
    carried = empty_state + jnp.sum(
        jnp.where(wanted[:, None, None, None], states, jnp.zeros_like(states)), axis=0
    )
    positions = jnp.arange(row_count, dtype=jnp.int32)
    causal = positions[:, None] >= positions[None, :]
    keep_local = causal & (doc_id[:, None] == doc_id[None, :])
    scores = jnp.einsum("qhd,khd->hqk", queries, key_rows, preferred_element_type=jnp.float32)
    rounded = jnp.where(keep_local[None], scores, jnp.zeros_like(scores)).astype(jnp.bfloat16)
    block_term = jnp.einsum("hqk,khd->qhd", rounded, value_rows, preferred_element_type=jnp.float32)
    carried_term = jnp.einsum(
        "qhd,hde->qhe", queries.astype(jnp.float32), carried, precision=lax.Precision.HIGHEST
    )
    carried_term = jnp.where(
        (doc_id == first_doc)[:, None, None], carried_term, jnp.zeros_like(carried_term)
    )
    lin_raw = block_term + carried_term
    mean_square = jnp.mean(lin_raw * lin_raw, axis=-1, keepdims=True)
    gain_rows = norm_gain.astype(jnp.float32).reshape(head_count, HD)
    gate_rows = jax.nn.sigmoid(out_gate.astype(jnp.float32).reshape(row_count, head_count, HD))
    normed = lin_raw * lax.rsqrt(mean_square + norm_eps) * gain_rows * gate_rows
    lin_out = normed.astype(jnp.bfloat16).reshape(row_count, head_count * HD)
    query_soft = soft_query.reshape(row_count, head_count, HD)
    query_pos = my_index * row_count + positions
    score_scale = 1.0 / math.sqrt(HD)
    key_flat = lax.all_gather(soft_key, "seq", axis=0, tiled=True)
    row_max = jnp.full((head_count, row_count), -1e30, jnp.float32)
    piece_rows = key_flat.shape[0]
    key_part = key_flat.reshape(piece_rows, head_count, HD)
    value_part = lax.all_gather(lin_out, "seq", axis=0, tiled=True).reshape(
        piece_rows, head_count, HD
    )
    key_pos = jnp.arange(piece_rows, dtype=jnp.int32)
    logits = (
        jnp.einsum("qhd,khd->hqk", query_soft, key_part, preferred_element_type=jnp.float32)
        * score_scale
    )
    keep_mask = (
        (query_pos[:, None] >= key_pos[None, :])
        & (doc_id[:, None] == lax.all_gather(doc_id, "seq", axis=0, tiled=True)[None, :])
        & True
    )
    logits = jnp.where(keep_mask[None], logits, -1e30)
    new_max = jnp.maximum(row_max, jnp.max(logits, axis=-1))
    probs = jnp.where(keep_mask[None], jnp.exp(logits - new_max[..., None]), 0.0)
    denom_sum = jnp.sum(probs, axis=-1)
    update = jnp.einsum(
        "hqk,khd->qhd", probs.astype(jnp.bfloat16), value_part, preferred_element_type=jnp.float32
    )
    soft_out = update / jnp.transpose(denom_sum)[:, :, None]
    return (lin_out, soft_out.astype(jnp.bfloat16).reshape(row_count, head_count * HD))


def solution(mesh):
    return jax.shard_map(
        per_device,
        mesh=mesh,
        in_specs=(
            P(("grp", "seq"), "head"),
            P(("grp", "seq"), "head"),
            P(("grp", "seq"), "head"),
            P("head"),
            P(("grp", "seq"), "head"),
            P(("grp", "seq"), "head"),
            P(("grp", "seq"), "head"),
            P(("grp", "seq")),
        ),
        out_specs=(P(("grp", "seq"), "head"), P(("grp", "seq"), "head")),
        check_vma=False,
    )
```

profile of v0, /device:TPU:0, one launch (start us, length us, event | category | flops | bytes accessed | tf_op | source)
XLA Modules:
  0.0 291.2 jit_solution(3869232572104715279)
XLA Ops:
  7.2 0.0 copy-start
  7.2 0.0 all-gather.9.cloned.1.call-start
  7.2 1.3 dynamic-slice
  8.6 2.0 fusion.52
  10.6 2.0 broadcast_compare_fusion.1
  12.5 3.4 %fusion.34 = bf16[16,128,128]{2,1,0:T(8,128)(2,1)} fusion(pred[320]{0:T(512)(128)(4,1)S(1)} %get-tuple-element.5, bf16[320,2048]{1,0:T(8,128)(2,1)} %param.10, bf16[320,2048]{1,0:T(8,128)(2,1)} %param.9), kind=kOutput, calls=%fused_computation.39 | convolution fusion | flops 168689664 | bytes 3146048 | tf_op jit(solution)/shard_map/thd,the->hde/dot_general | solution.py:24
  15.9 0.0 all-gather.9.cloned.1.call-update
  16.0 0.0 all-gather.7.cloned.1.call-start
  16.0 0.7 all-gather.7.cloned.1.call-update
  16.7 0.0 all-gather.5.cloned.1.call-start
  17.4 0.0 copy-done.4
  17.4 0.3 dynamic-update-slice.1
  17.7 10.1 %all-reduce.2 = (s32[4]{0:T(128)S(1)}, s32[1280]{0:T(1024)S(1)}) all-reduce(s32[4]{0:T(128)S(1)} %get-tuple-element.7, s32[1280]{0:T(1024)S(1)} %dynamic-update-slice.1), channel_id=1, replica_groups=mesh['grp'=2,'seq'=4,'head'=4] {'seq'}, use_global_device_ids=true, to_apply=%add | all-reduce | flops 1284 | bytes 10272
  27.8 0.6 compare_and_fusion
  28.5 0.0 copy-done.5
  28.5 0.1 fusion.46
  28.6 36.1 %all-gather.9.cloned.1.call-done = bf16[64,128,128]{2,1,0:T(8,128)(2,1)} async-done(((bf16[16,128,128]{2,1,0:T(8,128)(2,1)}), bf16[64,128,128]{2,1,0:T(8,128)(2,1)}) %all-gather.9.cloned.1.call-update) | async-done | bytes 2097168 | tf_op jit(solution)/shard_map/all_gather | solution.py:28
  64.8 2.2 fusion.6
  67.0 0.0 copy-done.3
  67.0 2.7 fusion.29
  69.7 7.2 %multiply_reduce_fusion = (f32[320,16]{0,1:T(8,128)S(1)}, f32[320,16,128]{2,0,1:T(8,128)}) fusion(f32[16,128,320]{1,2,0:T(8,128)} %fusion.29, pred[320]{0:T(512)(128)(4,1)S(1)} %get-tuple-element.4, pred[320,320]{1,0:T(8,128)(4,1)S(1)} %fusion.46, bf16[320,2048]{1,0:T(8,128)(2,1)} %param.10, bf16[320,2048]{1,0:T(8,128)(2,1)} %param.9, ...), kind=kOutput, calls=%fused_computation.20 | convolution fusion | flops 844753920 | bytes 9298240 | tf_op jit(solution)/shard_map/hqk,khd->qhd/dot_general | solution.py:42
  76.9 3.2 %copy_bitcast_fusion.1 = bf16[320,2048]{1,0:T(8,128)(2,1)} fusion(f32[320,16,128]{2,0,1:T(8,128)} %get-tuple-element.10, f32[16,128]{1,0:T(8,128)S(1)} %bitcast_convert_fusion, f32[320,16]{0,1:T(8,128)S(1)} %add_rsqrt_fusion, bf16[320,2048]{1,0:T(8,128)(2,1)S(1)} %copy-done.2), kind=kLoop, calls=%fused_computation.26 | loop fusion | flops 5242880 | bytes 5271552 | tf_op jit(solution)/shard_map/reshape | solution.py:54
  80.1 0.0 all-gather.5.cloned.1.call-update
  80.2 0.4 fusion.16
  80.6 82.6 %all-gather.7.cloned.1.call-done = bf16[1280,2048]{1,0:T(8,128)(2,1)} async-done(((bf16[320,2048]{1,0:T(8,128)(2,1)}), bf16[1280,2048]{1,0:T(8,128)(2,1)}) %all-gather.7.cloned.1.call-update) | async-done | bytes 5242896 | tf_op jit(solution)/shard_map/all_gather | solution.py:58
  163.1 7.9 %copy.36 = bf16[1280,2048]{0,1:T(8,128)(2,1)} copy(bf16[1280,2048]{1,0:T(8,128)(2,1)} %all-gather.7.cloned.1.call-done) | data formatting | bytes 10485760 | tf_op jit(solution)/shard_map/all_gather | solution.py:58
  171.1 13.3 %fusion = (f32[16,320]{1,0:T(8,128)S(1)}, f32[16,320,1280]{2,1,0:T(8,128)}) fusion(pred[320,1280]{1,0:T(8,128)(4,1)S(1)} %fusion.16, bf16[1280,16,128]{0,2,1:T(8,128)(2,1)} %bitcast.105, bf16[320,2048]{1,0:T(8,128)(2,1)S(1)} %copy-done), kind=kOutput, calls=%fused_computation.2 | convolution fusion | flops 1697377280 | bytes 33198080 | tf_op jit(solution)/shard_map/qhd,khd->hqk/dot_general | solution.py:67
  184.4 13.9 %fusion.1 = f32[16,320]{1,0:T(8,128)S(1)} fusion(f32[16,320,1280]{2,1,0:T(8,128)} %get-tuple-element.12, f32[16,320]{1,0:T(8,128)S(1)} %broadcast_maximum_fusion, pred[320,1280]{1,0:T(8,128)(4,1)S(1)} %fusion.16), kind=kLoop, calls=%fused_computation.3 | loop fusion | flops 32762880 | bytes 26664960 | tf_op jit(solution)/shard_map/reduce_sum | solution.py:78
  198.3 63.4 %all-gather.5.cloned.1.call-done = bf16[1280,2048]{1,0:T(8,128)(2,1)} async-done(((bf16[320,2048]{1,0:T(8,128)(2,1)}), bf16[1280,2048]{1,0:T(8,128)(2,1)}) %all-gather.5.cloned.1.call-update) | async-done | bytes 5242896 | tf_op jit(solution)/shard_map/all_gather | solution.py:62
  261.8 7.9 %copy.35 = bf16[1280,2048]{0,1:T(8,128)(2,1)} copy(bf16[1280,2048]{1,0:T(8,128)(2,1)} %all-gather.5.cloned.1.call-done) | data formatting | bytes 10485760 | tf_op jit(solution)/shard_map/all_gather | solution.py:62
  269.7 13.5 %fusion.17 = bf16[16,40,8,128]{3,2,1,0:T(8,128)(2,1)S(1)} fusion(bf16[1280,16,128]{0,2,1:T(8,128)(2,1)} %bitcast.106, f32[16,320,1280]{2,1,0:T(8,128)} %get-tuple-element.12, f32[16,320]{1,0:T(8,128)S(1)} %broadcast_maximum_fusion, pred[320,1280]{1,0:T(8,128)(4,1)S(1)} %fusion.16, f32[320,16]{0,1:T(8,128)S(1)} %bitcast.109), kind=kOutput, calls=%fused_computation.23 | convolution fusion | flops 1711800320 | bytes 33218560 | tf_op jit(solution)/shard_map/hqk,khd->qhd/dot_general | solution.py:79
  283.2 1.4 copy.94
  (14 shorter events, 0.0 us)
Async XLA Ops:
  7.2 163.9 %copy-start = (bf16[320,2048]{1,0:T(8,128)(2,1)S(1)}, bf16[320,2048]{1,0:T(8,128)(2,1)}, u32[]{:S(2)}) copy-start(bf16[320,2048]{1,0:T(8,128)(2,1)} %param.13) | copy-start | bytes 3932164
  7.2 57.6 %all-gather.9.cloned.1.call-start = ((), (), s32[]{:S(2)}) async-start(), calls=%async_computation.2 | async-start | bytes 2621440 | tf_op jit(solution)/shard_map/all_gather | solution.py:28
  12.5 4.9 %copy-start.4 = (s32[320]{0:T(512)S(1)}, s32[320]{0:T(512)}, u32[]{:S(2)}) copy-start(s32[320]{0:T(512)} %param.15) | copy-start | bytes 3844
  12.5 15.9 %copy-start.5 = (bf16[2048]{0:T(1024)(128)(2,1)S(1)}, bf16[2048]{0:T(1024)(128)(2,1)}, u32[]{:S(2)}) copy-start(bf16[2048]{0:T(1024)(128)(2,1)} %param.11) | copy-start | bytes 12292
  15.9 51.1 %copy-start.3 = (bf16[320,2048]{1,0:T(8,128)(2,1)S(1)}, bf16[320,2048]{1,0:T(8,128)(2,1)}, u32[]{:S(2)}) copy-start(bf16[320,2048]{1,0:T(8,128)(2,1)} %param.8) | copy-start | bytes 3932164
  16.0 147.2 %all-gather.7.cloned.1.call-start = ((), (), s32[]{:S(2)}) async-start(), calls=%async_computation.1 | async-start | bytes 6553600 | tf_op jit(solution)/shard_map/all_gather | solution.py:58
  16.7 245.0 %all-gather.5.cloned.1.call-start = ((), (), s32[]{:S(2)}) async-start(), calls=%async_computation | async-start | bytes 6553600 | tf_op jit(solution)/shard_map/all_gather | solution.py:62
  69.7 7.2 %copy-start.2 = (bf16[320,2048]{1,0:T(8,128)(2,1)S(1)}, bf16[320,2048]{1,0:T(8,128)(2,1)}, u32[]{:S(2)}) copy-start(bf16[320,2048]{1,0:T(8,128)(2,1)} %param.12) | copy-start | bytes 3932164
  269.7 15.0 %copy-start.1 = (bf16[320,2048]{1,0:T(8,128)(2,1)S(1)}, bf16[320,2048]{1,0:T(8,128)(2,1)}, u32[]{:S(2)}) copy-start(bf16[320,2048]{1,0:T(8,128)(2,1)} %param.13) | copy-start | bytes 3932164
Sparse Core Ops, SparseCore 0:
  16.1 48.6 all-gather.8
  66.3 96.7 all-gather.6
  165.3 96.4 all-gather.4
where the time goes:
time: 292 us; the launch traced here: 291 us
  waiting for transfers between devices  183 us (63%)
  matrix products  40.1 us (14%)
  other arithmetic  22.5 us (8%)
  local copies, waits for them, and re-layouts  20.9 us (7%)
  between operations  14.5 us (5%)
  blocking collectives  10.1 us (3%)
    all_gather x1, waiting for transfers between devices, per_device(): key_flat = lax.all_gather(soft_key, 'seq', axis=0, tiled=True)  82.6 us
    all_gather x1, waiting for transfers between devices, per_device(): lax.all_gather(lin_out, 'seq', axis=0, tiled=True)  63.4 us
    all_gather x1, waiting for transfers between devices, per_device(): lax.all_gather(local_state[None].astype(jnp.bfloat16), 'seq', axis=0, til...  36.1 us
    reduce_sum x1, other arithmetic, per_device(): denom_sum = jnp.sum(probs, axis=-1)  13.9 us
    dot_general x1, matrix products, per_device(): jnp.einsum('hqk,khd->qhd', probs.astype(jnp.bfloat16), value_part, prefer...  13.5 us
    dot_general x1, matrix products, per_device(): jnp.einsum('qhd,khd->hqk', query_soft, key_part, preferred_element_type=j...  13.3 us
    unnamed x1, blocking collectives  10.1 us
    all_gather x1, local copies, waits for them, and re-layouts, per_device(): key_flat = lax.all_gather(soft_key, 'seq', axis=0, tiled=True)  7.92 us
  transfers between devices with their start and end apart: 3, of which 3 were waited for; matrix products, arithmetic and copies ran while one was open for 18% of the time, Pallas kernels for 0%

commit v1 on v0

--- a/solution.py
+++ b/solution.py
@@ -11,29 +11,40 @@
 norm_eps = 1e-06
 
 
+def shift_from_below(x, dist, n_seq):
+    return lax.ppermute(x, "seq", [(s, s + dist) for s in range(n_seq - dist)])
+
+
 def per_device(lin_query, lin_key, lin_value, norm_gain, out_gate, soft_query, soft_key, doc_id):
     row_count = lin_query.shape[0]
     head_count = lin_query.shape[1] // HD
+    n_seq = lax.axis_size("seq")
     my_index = lax.axis_index("seq")
+    max_doc = n_seq * row_count // 2
+    reach = min(n_seq - 1, (max_doc + row_count - 2) // row_count)
+    dists = list(range(1, reach + 1))
+
     queries = lin_query.reshape(row_count, head_count, HD)
     key_rows = lin_key.reshape(row_count, head_count, HD)
     value_rows = lin_value.reshape(row_count, head_count, HD)
     first_doc = doc_id[0]
     last_doc = doc_id[-1]
+
+    soft_key_rows = soft_key.reshape(row_count, head_count, HD)
+    key_blocks = [soft_key_rows] + [shift_from_below(soft_key_rows, d, n_seq) for d in dists]
+    doc_blocks = [doc_id] + [shift_from_below(doc_id, d, n_seq) for d in dists]
+
     tail_keys = jnp.where((doc_id == last_doc)[:, None, None], key_rows, jnp.zeros_like(key_rows))
     local_state = jnp.einsum(
         "thd,the->hde", tail_keys, value_rows, preferred_element_type=jnp.float32
     )
-    empty_state = jnp.zeros_like(local_state)
-    states = lax.all_gather(
-        local_state[None].astype(jnp.bfloat16), "seq", axis=0, tiled=True
-    ).astype(jnp.float32)
-    tags = lax.all_gather(last_doc[None], "seq", axis=0, tiled=True)
-    sources = jnp.arange(tags.shape[0], dtype=jnp.int32)
-    wanted = (tags == first_doc) & (sources < my_index)
-    carried = empty_state + jnp.sum(
-        jnp.where(wanted[:, None, None, None], states, jnp.zeros_like(states)), axis=0
-    )
+    state_bf = local_state.astype(jnp.bfloat16)
+    carried = jnp.zeros_like(local_state)
+    for d in dists:
+        state_in = shift_from_below(state_bf, d, n_seq).astype(jnp.float32)
+        wanted = (my_index >= d) & (doc_blocks[d][-1] == first_doc)
+        carried = carried + jnp.where(wanted, state_in, jnp.zeros_like(state_in))
+
     positions = jnp.arange(row_count, dtype=jnp.int32)
     causal = positions[:, None] >= positions[None, :]
     keep_local = causal & (doc_id[:, None] == doc_id[None, :])
@@ -52,29 +63,31 @@
     gate_rows = jax.nn.sigmoid(out_gate.astype(jnp.float32).reshape(row_count, head_count, HD))
     normed = lin_raw * lax.rsqrt(mean_square + norm_eps) * gain_rows * gate_rows
     lin_out = normed.astype(jnp.bfloat16).reshape(row_count, head_count * HD)
+
+    value_own = lin_out.reshape(row_count, head_count, HD)
+    value_blocks = [value_own] + [shift_from_below(value_own, d, n_seq) for d in dists]
+
     query_soft = soft_query.reshape(row_count, head_count, HD)
-    query_pos = my_index * row_count + positions
     score_scale = 1.0 / math.sqrt(HD)
-    key_flat = lax.all_gather(soft_key, "seq", axis=0, tiled=True)
-    row_max = jnp.full((head_count, row_count), -1e30, jnp.float32)
-    piece_rows = key_flat.shape[0]
-    key_part = key_flat.reshape(piece_rows, head_count, HD)
-    value_part = lax.all_gather(lin_out, "seq", axis=0, tiled=True).reshape(
-        piece_rows, head_count, HD
+    key_part = jnp.concatenate(key_blocks, axis=0)
+    value_part = jnp.concatenate(value_blocks, axis=0)
+    key_docs = jnp.concatenate(doc_blocks, axis=0)
+    valid = jnp.concatenate(
+        [jnp.full((row_count,), my_index >= d, jnp.bool_) for d in [0] + dists]
     )
-    key_pos = jnp.arange(piece_rows, dtype=jnp.int32)
+    key_off = jnp.concatenate([positions - d * row_count for d in [0] + dists])
+    keep_mask = (
+        (positions[:, None] >= key_off[None, :])
+        & (doc_id[:, None] == key_docs[None, :])
+        & valid[None, :]
+    )
     logits = (
         jnp.einsum("qhd,khd->hqk", query_soft, key_part, preferred_element_type=jnp.float32)
         * score_scale
     )
-    keep_mask = (
-        (query_pos[:, None] >= key_pos[None, :])
-        & (doc_id[:, None] == lax.all_gather(doc_id, "seq", axis=0, tiled=True)[None, :])
-        & True
-    )
     logits = jnp.where(keep_mask[None], logits, -1e30)
-    new_max = jnp.maximum(row_max, jnp.max(logits, axis=-1))
-    probs = jnp.where(keep_mask[None], jnp.exp(logits - new_max[..., None]), 0.0)
+    row_max = jnp.max(logits, axis=-1)
+    probs = jnp.where(keep_mask[None], jnp.exp(logits - row_max[..., None]), 0.0)
     denom_sum = jnp.sum(probs, axis=-1)
     update = jnp.einsum(
         "hqk,khd->qhd", probs.astype(jnp.bfloat16), value_part, preferred_element_type=jnp.float32

time: 292 us -> 226 us (0.77)
  the two profiles are of different devices: /device:TPU:0 before, /device:TPU:26 now
where the time goes in v1:
time: 226 us
  waiting for transfers between devices  148 us (65%)
  matrix products  31.2 us (14%)
  other arithmetic  26.6 us (12%)
  starting transfers between devices  10.8 us (5%)
  local copies, waits for them, and re-layouts  5.66 us (3%)
  between operations  3.41 us (2%)
    ppermute x8, waiting for transfers between devices, shift_from_below(): return lax.ppermute(x, 'seq', [(s, s + dist) for s in range(n_seq - dist)])  148 us
    sub x1, other arithmetic, per_device(): logits - row_max[..., None]  23 us
    dot_general x1, matrix products, per_device(): jnp.einsum('qhd,khd->hqk', query_soft, key_part, preferred_element_type=j...  11.6 us
    ppermute x8, starting transfers between devices, shift_from_below(): return lax.ppermute(x, 'seq', [(s, s + dist) for s in range(n_seq - dist)])  10.8 us
    dot_general x1, matrix products, per_device(): jnp.einsum('hqk,khd->qhd', rounded, value_rows, preferred_element_type=jn...  5.82 us
    dot_general x1, matrix products, per_device(): jnp.einsum('hqk,khd->qhd', probs.astype(jnp.bfloat16), value_part, prefer...  5.64 us
    dot_general x1, matrix products, per_device(): jnp.einsum('qhd,hde->qhe', queries.astype(jnp.float32), carried, precisio...  4.63 us
  transfers between devices with their start and end apart: 8, of which 5 were waited for; matrix products, arithmetic and copies ran while one was open for 25% of the time, Pallas kernels for 0%

profile of v1, /device:TPU:26, one launch (start us, length us, event | category | flops | bytes accessed | tf_op | source)
XLA Modules:
  0.0 226.0 jit_solution(13275523689679989657)
XLA Ops:
  0.6 1.4 collective-permute-start
  2.1 1.3 collective-permute-start.2
  3.4 1.3 fusion.75
  4.7 2.0 broadcast_compare_fusion
  6.7 3.5 %fusion.47 = bf16[16,128,128]{2,1,0:T(8,128)(2,1)} fusion(pred[320]{0:T(512)(128)(4,1)S(1)} %get-tuple-element.2, bf16[320,2048]{1,0:T(8,128)(2,1)} %param.10, bf16[320,2048]{1,0:T(8,128)(2,1)} %param.9), kind=kOutput, calls=%fused_computation.49 | convolution fusion | flops 168689664 | bytes 3146048 | tf_op jit(solution)/shard_map/thd,the->hde/dot_general | solution.py:38
  10.2 1.4 collective-permute-start.1
  11.6 1.3 collective-permute-start.3
  12.9 0.3 copy_bitcast_fusion.2
  13.3 1.3 collective-permute-start.6
  14.6 0.1 fusion.67
  14.7 5.8 %fusion.7 = f32[16,320,128]{2,1,0:T(8,128)} fusion(pred[320,320]{1,0:T(8,128)(4,1)S(1)} %fusion.67, bf16[320,2048]{1,0:T(8,128)(2,1)} %param.10, bf16[320,2048]{1,0:T(8,128)(2,1)} %param.9, bf16[320,2048]{1,0:T(8,128)(2,1)} %param.8), kind=kOutput, calls=%fused_computation.10 | convolution fusion | flops 842137600 | bytes 6656000 | tf_op jit(solution)/shard_map/hqk,khd->qhd/dot_general | solution.py:53
  20.6 0.1 pad_add_fusion
  20.7 0.1 pad_add_fusion.2
  20.8 1.3 collective-permute-start.7
  22.0 0.6 slice.13
  24.0 0.6 slice.15
  25.9 0.1 pad_add_fusion.1
  26.0 0.4 fusion.46
  26.4 2.3 %collective-permute-done.1 = bf16[16,128,128]{2,1,0:T(8,128)(2,1)S(1)} collective-permute-done((bf16[16,128,128]{2,1,0:T(8,128)(2,1)}, bf16[16,128,128]{2,1,0:T(8,128)(2,1)S(1)}, u32[]{:S(2)}, u32[]{:S(2)}) %collective-permute-start.1) | collective-permute-done | bytes 524320 | tf_op jit(solution)/shard_map/ppermute | solution.py:15
  28.6 23.3 %collective-permute-done.3 = bf16[16,128,128]{2,1,0:T(8,128)(2,1)} collective-permute-done((bf16[16,128,128]{2,1,0:T(8,128)(2,1)}, bf16[16,128,128]{2,1,0:T(8,128)(2,1)}, u32[]{:S(2)}, u32[]{:S(2)}) %collective-permute-start.3) | collective-permute-done | bytes 524320 | tf_op jit(solution)/shard_map/ppermute | solution.py:15
  52.0 4.6 %multiply_reduce_fusion = (f32[320,16]{0,1:T(8,128)S(1)}, f32[320,16,128]{2,0,1:T(8,128)S(1)}) fusion(bf16[16,128,128]{2,1,0:T(8,128)(2,1)} %collective-permute-done.3, bf16[16,128,128]{2,1,0:T(8,128)(2,1)S(1)} %collective-permute-done.1, pred[]{:T(512)S(6)} %and.35, pred[]{:T(512)S(6)} %and.34, pred[320]{0:T(512)(128)(4,1)S(1)} %get-tuple-element.3, ...), kind=kOutput, calls=%fused_computation.31 | convolution fusion | flops 1010560000 | bytes 7622978 | tf_op jit(solution)/shard_map/qhd,hde->qhe/dot_general | solution.py:54
  56.6 0.9 fusion.23
  57.6 1.3 collective-permute-start.4
  58.9 1.5 collective-permute-start.5
  60.4 1.3 copy_bitcast_fusion.1
  61.6 5.7 %collective-permute-done.6 = bf16[320,16,128]{2,0,1:T(8,128)(2,1)} collective-permute-done((bf16[320,16,128]{2,0,1:T(8,128)(2,1)S(1)}, bf16[320,16,128]{2,0,1:T(8,128)(2,1)}, u32[]{:S(2)}, u32[]{:S(2)}) %collective-permute-start.6) | collective-permute-done | bytes 1310752 | tf_op jit(solution)/shard_map/ppermute | solution.py:15
  67.3 97.0 %collective-permute-done.7 = bf16[320,16,128]{2,0,1:T(8,128)(2,1)} collective-permute-done((bf16[320,16,128]{2,0,1:T(8,128)(2,1)S(1)}, bf16[320,16,128]{2,0,1:T(8,128)(2,1)}, u32[]{:S(2)}, u32[]{:S(2)}) %collective-permute-start.7) | collective-permute-done | bytes 1310752 | tf_op jit(solution)/shard_map/ppermute | solution.py:15
  164.3 11.6 %fusion.8 = f32[16,960,320]{1,2,0:T(8,128)} fusion(bf16[320,16,128]{2,0,1:T(8,128)(2,1)} %collective-permute-done.7, bf16[320,16,128]{2,0,1:T(8,128)(2,1)} %collective-permute-done.6, bf16[320,16,128]{2,0,1:T(8,128)(2,1)S(1)} %copy_bitcast_fusion.2, bf16[320,2048]{1,0:T(8,128)(2,1)S(1)} %copy-done), kind=kOutput, calls=%fused_computation.11 | convolution fusion | flops 1270087680 | bytes 24903680 | tf_op jit(solution)/shard_map/qhd,khd->hqk/dot_general | solution.py:85
  175.9 23.0 %fusion.76 = (f32[16,320]{1,0:T(8,128)S(1)}, bf16[16,320,960]{2,1,0:T(8,128)(2,1)}) fusion(f32[16,960,320]{1,2,0:T(8,128)} %fusion.8, pred[320,960]{1,0:T(8,128)(4,1)S(1)} %fusion.46), kind=kOutput, calls=%fused_computation.84 | output fusion | flops 39322560 | bytes 29818880 | tf_op jit(solution)/shard_map/sub | solution.py:90
  198.9 20.0 %collective-permute-done.5 = bf16[320,16,128]{2,0,1:T(8,128)(2,1)S(1)} collective-permute-done((bf16[320,16,128]{2,0,1:T(8,128)(2,1)S(1)}, bf16[320,16,128]{2,0,1:T(8,128)(2,1)S(1)}, u32[]{:S(2)}, u32[]{:S(2)}) %collective-permute-start.5) | collective-permute-done | bytes 1310752 | tf_op jit(solution)/shard_map/ppermute | solution.py:15
  218.9 5.6 %fusion.29 = bf16[16,40,8,128]{3,2,1,0:T(8,128)(2,1)S(1)} fusion(bf16[320,16,128]{2,0,1:T(8,128)(2,1)S(1)} %collective-permute-done.5, bf16[320,16,128]{2,0,1:T(8,128)(2,1)S(1)} %collective-permute-done.4, bf16[320,16,128]{2,0,1:T(8,128)(2,1)S(1)} %fusion.23, bf16[16,320,960]{2,1,0:T(8,128)(2,1)} %get-tuple-element.9, f32[320,16]{0,1:T(8,128)S(1)} %bitcast.106), kind=kOutput, calls=%fused_computation.32 | convolution fusion | flops 1271398400 | bytes 15093760 | tf_op jit(solution)/shard_map/hqk,khd->qhd/dot_general | solution.py:92
  224.6 1.4 copy.70
  (20 shorter events, 0.1 us)
Async XLA Ops:
  0.6 163.7 %copy-start = (bf16[320,2048]{1,0:T(8,128)(2,1)S(1)}, bf16[320,2048]{1,0:T(8,128)(2,1)}, u32[]{:S(2)}) copy-start(bf16[320,2048]{1,0:T(8,128)(2,1)} %param.13) | copy-start | bytes 3932164
  0.6 20.1 %collective-permute-start = (s32[320]{0:T(512)}, s32[320]{0:T(512)S(1)}, u32[]{:S(2)}, u32[]{:S(2)}) collective-permute-start(s32[320]{0:T(512)} %param.15), channel_id=1, source_target_pairs={{0,4},{4,8},{8,12},{1,5},{5,9},{9,13},{2,6},{6,10},{10,14},{3,7},{... | collective-permute-start | bytes 3848 | tf_op jit(solution)/shard_map/ppermute | solution.py:15
  2.1 21.9 %collective-permute-start.2 = (s32[320]{0:T(512)}, s32[320]{0:T(512)S(1)}, u32[]{:S(2)}, u32[]{:S(2)}) collective-permute-start(s32[320]{0:T(512)} %param.15), channel_id=1, source_target_pairs={{0,8},{4,12},{1,9},{5,13},{2,10},{6,14},{3,11},{7,15},{16,24},{20,... | collective-permute-start | bytes 3848 | tf_op jit(solution)/shard_map/ppermute | solution.py:15
  6.7 6.2 %copy-start.2 = (bf16[320,2048]{1,0:T(8,128)(2,1)S(1)}, bf16[320,2048]{1,0:T(8,128)(2,1)}, u32[]{:S(2)}) copy-start(bf16[320,2048]{1,0:T(8,128)(2,1)} %param.14) | copy-start | bytes 3932164
  10.2 4.4 %copy-start.3 = (s32[320]{0:T(512)S(1)}, s32[320]{0:T(512)}, u32[]{:S(2)}) copy-start(s32[320]{0:T(512)} %param.15) | copy-start | bytes 3844
  10.2 4.5 %copy-start.4 = (bf16[2048]{0:T(1024)(128)(2,1)S(1)}, bf16[2048]{0:T(1024)(128)(2,1)}, u32[]{:S(2)}) copy-start(bf16[2048]{0:T(1024)(128)(2,1)} %param.11) | copy-start | bytes 12292
  10.2 18.4 %collective-permute-start.1 = (bf16[16,128,128]{2,1,0:T(8,128)(2,1)}, bf16[16,128,128]{2,1,0:T(8,128)(2,1)S(1)}, u32[]{:S(2)}, u32[]{:S(2)}) collective-permute-start(bf16[16,128,128]{2,1,0:T(8,128)(2,1)} %fusion.47), channel_id=1, source_target_pairs={{0,4},{4,8},{8,12},{1,5},{5,9},{9,13},{2,6},{6,10},{10,14},{3,7},{... | collective-permute-start | bytes 1572872 | tf_op jit(solution)/shard_map/ppermute | solution.py:15
  11.6 40.4 %collective-permute-start.3 = (bf16[16,128,128]{2,1,0:T(8,128)(2,1)}, bf16[16,128,128]{2,1,0:T(8,128)(2,1)}, u32[]{:S(2)}, u32[]{:S(2)}) collective-permute-start(bf16[16,128,128]{2,1,0:T(8,128)(2,1)} %fusion.47), channel_id=1, source_target_pairs={{0,8},{4,12},{1,9},{5,13},{2,10},{6,14},{3,11},{7,15},{16,24},{20,... | collective-permute-start | bytes 1572872 | tf_op jit(solution)/shard_map/ppermute | solution.py:15
  13.3 54.0 %collective-permute-start.6 = (bf16[320,16,128]{2,0,1:T(8,128)(2,1)S(1)}, bf16[320,16,128]{2,0,1:T(8,128)(2,1)}, u32[]{:S(2)}, u32[]{:S(2)}) collective-permute-start(bf16[320,16,128]{2,0,1:T(8,128)(2,1)S(1)} %copy_bitcast_fusion.2), channel_id=1, source_target_pairs={{0,4},{4,8},{8,12},{1,5},{5,9},{9,13},{2,6},{6,10},{10,14},{3,7},{... | collective-permute-start | bytes 3932168 | tf_op jit(solution)/shard_map/ppermute | solution.py:15
  20.8 143.6 %collective-permute-start.7 = (bf16[320,16,128]{2,0,1:T(8,128)(2,1)S(1)}, bf16[320,16,128]{2,0,1:T(8,128)(2,1)}, u32[]{:S(2)}, u32[]{:S(2)}) collective-permute-start(bf16[320,16,128]{2,0,1:T(8,128)(2,1)S(1)} %copy_bitcast_fusion.2), channel_id=1, source_target_pairs={{0,8},{4,12},{1,9},{5,13},{2,10},{6,14},{3,11},{7,15},{16,24},{20,... | collective-permute-start | bytes 3932168 | tf_op jit(solution)/shard_map/ppermute | solution.py:15
  52.0 4.7 %copy-start.1 = (bf16[320,2048]{1,0:T(8,128)(2,1)S(1)}, bf16[320,2048]{1,0:T(8,128)(2,1)}, u32[]{:S(2)}) copy-start(bf16[320,2048]{1,0:T(8,128)(2,1)} %param.12) | copy-start | bytes 3932164
  57.6 141.3 %collective-permute-start.4 = (bf16[320,16,128]{2,0,1:T(8,128)(2,1)S(1)}, bf16[320,16,128]{2,0,1:T(8,128)(2,1)S(1)}, u32[]{:S(2)}, u32[]{:S(2)}) collective-permute-start(bf16[320,16,128]{2,0,1:T(8,128)(2,1)S(1)} %fusion.23), channel_id=1, source_target_pairs={{0,4},{4,8},{8,12},{1,5},{5,9},{9,13},{2,6},{6,10},{10,14},{3,7},{... | collective-permute-start | bytes 3932168 | tf_op jit(solution)/shard_map/ppermute | solution.py:15
  58.9 160.0 %collective-permute-start.5 = (bf16[320,16,128]{2,0,1:T(8,128)(2,1)S(1)}, bf16[320,16,128]{2,0,1:T(8,128)(2,1)S(1)}, u32[]{:S(2)}, u32[]{:S(2)}) collective-permute-start(bf16[320,16,128]{2,0,1:T(8,128)(2,1)S(1)} %fusion.23), channel_id=1, source_target_pairs={{0,8},{4,12},{1,9},{5,13},{2,10},{6,14},{3,11},{7,15},{16,24},{20,... | collective-permute-start | bytes 3932168 | tf_op jit(solution)/shard_map/ppermute | solution.py:15

commit v2 on v1

v2 whole, which is shorter than its diff:
```python
import math

import jax
import jax.numpy as jnp
from jax import lax
from jax.sharding import PartitionSpec as P

HD = 128


norm_eps = 1e-06


def shift_up(x, dist, n_seq):
    return lax.ppermute(x, "seq", [(s, s + dist) for s in range(n_seq - dist)])


def shift_down(x, dist, n_seq):
    return lax.ppermute(x, "seq", [(s + dist, s) for s in range(n_seq - dist)])


def merge(part_a, part_b):
    out_a, max_a, sum_a = part_a
    out_b, max_b, sum_b = part_b
    top = jnp.maximum(max_a, max_b)
    scale_a = jnp.exp(max_a - top)
    scale_b = jnp.exp(max_b - top)
    out = out_a * jnp.transpose(scale_a)[:, :, None] + out_b * jnp.transpose(scale_b)[:, :, None]
    return out, top, sum_a * scale_a + sum_b * scale_b


def per_device(lin_query, lin_key, lin_value, norm_gain, out_gate, soft_query, soft_key, doc_id):
    row_count = lin_query.shape[0]
    head_count = lin_query.shape[1] // HD
    n_seq = lax.axis_size("seq")
    my_index = lax.axis_index("seq")
    max_doc = n_seq * row_count // 2
    reach = min(n_seq - 1, (max_doc + row_count - 2) // row_count)
    dists = list(range(1, reach + 1))

    queries = lin_query.reshape(row_count, head_count, HD)
    key_rows = lin_key.reshape(row_count, head_count, HD)
    value_rows = lin_value.reshape(row_count, head_count, HD)
    first_doc = doc_id[0]
    last_doc = doc_id[-1]

    query_soft = soft_query.reshape(row_count, head_count, HD)
    query_blocks = [query_soft]
    for d in dists:
        query_blocks.append(shift_down(query_blocks[-1], 1, n_seq))
    query_docs = [doc_id] + [shift_down(doc_id, d, n_seq) for d in dists]

    tail_keys = jnp.where((doc_id == last_doc)[:, None, None], key_rows, jnp.zeros_like(key_rows))
    local_state = jnp.einsum(
        "thd,the->hde", tail_keys, value_rows, preferred_element_type=jnp.float32
    )
    state_bf = local_state.astype(jnp.bfloat16)
    carried = jnp.zeros_like(local_state)
    for d in dists:
        state_in = shift_up(state_bf, d, n_seq).astype(jnp.float32)
        tag_in = shift_up(last_doc[None], d, n_seq)[0]
        wanted = (my_index >= d) & (tag_in == first_doc)
        carried = carried + jnp.where(wanted, state_in, jnp.zeros_like(state_in))

    positions = jnp.arange(row_count, dtype=jnp.int32)
    causal = positions[:, None] >= positions[None, :]
    keep_local = causal & (doc_id[:, None] == doc_id[None, :])

    score_scale = 1.0 / math.sqrt(HD)
    key_soft = soft_key.reshape(row_count, head_count, HD)
    weights = []
    for d in [0] + dists:
        keep = query_docs[d][:, None] == doc_id[None, :]
        if d == 0:
            keep = keep & causal
        logits = (
            jnp.einsum(
                "qhd,khd->hqk", query_blocks[d], key_soft, preferred_element_type=jnp.float32
            )
            * score_scale
        )
        logits = jnp.where(keep[None], logits, -1e30)
        row_max = jnp.max(logits, axis=-1)
        probs = jnp.where(keep[None], jnp.exp(logits - row_max[..., None]), 0.0)
        weights.append((probs.astype(jnp.bfloat16), row_max, jnp.sum(probs, axis=-1)))

    scores = jnp.einsum("qhd,khd->hqk", queries, key_rows, preferred_element_type=jnp.float32)
    rounded = jnp.where(keep_local[None], scores, jnp.zeros_like(scores)).astype(jnp.bfloat16)
    block_term = jnp.einsum("hqk,khd->qhd", rounded, value_rows, preferred_element_type=jnp.float32)
    carried_term = jnp.einsum(
        "qhd,hde->qhe", queries.astype(jnp.float32), carried, precision=lax.Precision.HIGHEST
    )
    carried_term = jnp.where(
        (doc_id == first_doc)[:, None, None], carried_term, jnp.zeros_like(carried_term)
    )
    lin_raw = block_term + carried_term
    mean_square = jnp.mean(lin_raw * lin_raw, axis=-1, keepdims=True)
    gain_rows = norm_gain.astype(jnp.float32).reshape(head_count, HD)
    gate_rows = jax.nn.sigmoid(out_gate.astype(jnp.float32).reshape(row_count, head_count, HD))
    normed = lin_raw * lax.rsqrt(mean_square + norm_eps) * gain_rows * gate_rows
    lin_out = normed.astype(jnp.bfloat16).reshape(row_count, head_count * HD)
    value_own = lin_out.reshape(row_count, head_count, HD)

    def partial_out(d):
        probs, row_max, row_sum = weights[d]
        mixed = jnp.einsum(
            "hqk,khd->qhd", probs, value_own, preferred_element_type=jnp.float32
        )
        return mixed, row_max, row_sum

    running = None
    for d in reversed([0] + dists):
        part = partial_out(d)
        if running is not None:
            out_in, max_in, sum_in = running
            has_source = my_index >= 1
            max_in = jnp.where(has_source, max_in, -1e30)
            sum_in = jnp.where(has_source, sum_in, 0.0)
            out_in = jnp.where(has_source, out_in.astype(jnp.float32), 0.0)
            part = merge((out_in, max_in, sum_in), part)
        if d > 0:
            out_d, max_d, sum_d = part
            running = (
                shift_up(out_d.astype(jnp.bfloat16), 1, n_seq),
                shift_up(max_d, 1, n_seq),
                shift_up(sum_d, 1, n_seq),
            )
    mixed, row_max, row_sum = part
    soft_out = mixed / jnp.transpose(row_sum)[:, :, None]
    return (lin_out, soft_out.astype(jnp.bfloat16).reshape(row_count, head_count * HD))


def solution(mesh):
    return jax.shard_map(
        per_device,
        mesh=mesh,
        in_specs=(
            P(("grp", "seq"), "head"),
            P(("grp", "seq"), "head"),
            P(("grp", "seq"), "head"),
            P("head"),
            P(("grp", "seq"), "head"),
            P(("grp", "seq"), "head"),
            P(("grp", "seq"), "head"),
            P(("grp", "seq")),
        ),
        out_specs=(P(("grp", "seq"), "head"), P(("grp", "seq"), "head")),
        check_vma=False,
    )
```

time: 226 us -> 160 us (0.71)
  the two profiles are of different devices: /device:TPU:26 before, /device:TPU:0 now
where the time goes in v2:
time: 160 us; the launch traced here: 159 us
  waiting for transfers between devices  60.9 us (38%)
  starting transfers between devices  45.6 us (28%)
  matrix products  34 us (21%)
  other arithmetic  8.44 us (5%)
  local copies, waits for them, and re-layouts  6.91 us (4%)
  between operations  3.39 us (2%)
    ppermute x10, starting transfers between devices, shift_up(): return lax.ppermute(x, 'seq', [(s, s + dist) for s in range(n_seq - dist)])  40.4 us
    ppermute x10, waiting for transfers between devices, shift_up(): return lax.ppermute(x, 'seq', [(s, s + dist) for s in range(n_seq - dist)])  37.2 us
    ppermute x4, waiting for transfers between devices, shift_down(): return lax.ppermute(x, 'seq', [(s + dist, s) for s in range(n_seq - dist)])  23.7 us
    dot_general x3, matrix products, partial_out(): jnp.einsum('hqk,khd->qhd', probs, value_own, preferred_element_type=jnp.f...  12 us
    dot_general x3, matrix products, per_device(): jnp.einsum('qhd,khd->hqk', query_blocks[d], key_soft, preferred_element_t...  10.4 us
    reduce_sum x3, other arithmetic, per_device(): jnp.sum(probs, axis=-1)  5.98 us
    dot_general x1, matrix products, per_device(): jnp.einsum('hqk,khd->qhd', rounded, value_rows, preferred_element_type=jn...  5.56 us
    ppermute x4, starting transfers between devices, shift_down(): return lax.ppermute(x, 'seq', [(s + dist, s) for s in range(n_seq - dist)])  5.26 us
  transfers between devices with their start and end apart: 14, of which 5 were waited for; matrix products, arithmetic and copies ran while one was open for 22% of the time, Pallas kernels for 0%

profile of v2, /device:TPU:0, one launch (start us, length us, event | category | flops | bytes accessed | tf_op | source)
XLA Modules:
  0.0 159.2 jit_solution(15124555018280290493)
XLA Ops:
  0.7 1.5 fusion.107
  2.1 5.4 %collective-permute-start = (s32[1]{0:T(128)}, s32[1]{0:T(128)}, u32[]{:S(2)}, u32[]{:S(2)}) collective-permute-start(s32[1]{0:T(128)} %get-tuple-element.14), channel_id=1, source_target_pairs={{0,4},{4,8},{8,12},{1,5},{5,9},{9,13},{2,6},{6,10},{10,14},{3,7},{... | collective-permute-start | bytes 20 | tf_op jit(solution)/shard_map/ppermute | solution.py:15
  7.6 4.5 %collective-permute-start.2 = (s32[1]{0:T(128)}, s32[1]{0:T(128)}, u32[]{:S(2)}, u32[]{:S(2)}) collective-permute-start(s32[1]{0:T(128)} %get-tuple-element.14), channel_id=1, source_target_pairs={{0,8},{4,12},{1,9},{5,13},{2,10},{6,14},{3,11},{7,15},{16,24},{20,... | collective-permute-start | bytes 20 | tf_op jit(solution)/shard_map/ppermute | solution.py:15
  13.4 1.3 collective-permute-start.9
  14.7 2.7 %copy_bitcast_fusion.2 = bf16[320,16,128]{2,0,1:T(8,128)(2,1)} fusion(bf16[320,2048]{1,0:T(8,128)(2,1)} %param.13), kind=kLoop, calls=%fused_computation.60 | loop fusion | bytes 2621440 | tf_op jit(solution)/shard_map/reshape | solution.py:47
  17.4 1.4 collective-permute-start.5
  20.1 1.8 %fusion.65 = bf16[16,128,128]{2,1,0:T(8,128)(2,1)} fusion(pred[320]{0:T(512)(128)(4,1)S(1)} %get-tuple-element.12, bf16[320,2048]{1,0:T(8,128)(2,1)S(1)} %copy-done.5, bf16[320,2048]{1,0:T(8,128)(2,1)S(1)} %copy-done.6), kind=kOutput, calls=%fused_computation.70 | convolution fusion | flops 168689664 | bytes 3146048 | tf_op jit(solution)/shard_map/thd,the->hde/dot_general | solution.py:54
  21.9 5.2 %collective-permute-start.1 = (bf16[16,128,128]{2,1,0:T(8,128)(2,1)}, bf16[16,128,128]{2,1,0:T(8,128)(2,1)S(1)}, u32[]{:S(2)}, u32[]{:S(2)}) collective-permute-start(bf16[16,128,128]{2,1,0:T(8,128)(2,1)} %fusion.65), channel_id=1, source_target_pairs={{0,4},{4,8},{8,12},{1,5},{5,9},{9,13},{2,6},{6,10},{10,14},{3,7},{... | collective-permute-start | bytes 1572872 | tf_op jit(solution)/shard_map/ppermute | solution.py:15
  28.3 7.3 %collective-permute-start.3 = (bf16[16,128,128]{2,1,0:T(8,128)(2,1)}, bf16[16,128,128]{2,1,0:T(8,128)(2,1)}, u32[]{:S(2)}, u32[]{:S(2)}) collective-permute-start(bf16[16,128,128]{2,1,0:T(8,128)(2,1)} %fusion.65), channel_id=1, source_target_pairs={{0,8},{4,12},{1,9},{5,13},{2,10},{6,14},{3,11},{7,15},{16,24},{20,... | collective-permute-start | bytes 1572872 | tf_op jit(solution)/shard_map/ppermute | solution.py:15
  37.1 6.1 %fusion.2 = (f32[16,320]{1,0:T(8,128)S(1)}, f32[16,320,320]{1,2,0:T(8,128)}) fusion(pred[320,320]{0,1:T(8,128)(4,1)S(1)} %get-tuple-element.11, bf16[320,2048]{1,0:T(8,128)(2,1)S(1)} %copy-done, bf16[320,2048]{1,0:T(8,128)(2,1)} %param.13), kind=kOutput, calls=%fused_computation.9 | convolution fusion | flops 424340480 | bytes 9297920 | tf_op jit(solution)/shard_map/qhd,khd->hqk/dot_general | solution.py:77
  43.2 5.6 %fusion.15 = f32[16,320,128]{2,1,0:T(8,128)} fusion(pred[320,320]{0,1:T(8,128)(4,1)S(1)} %get-tuple-element.11, bf16[320,2048]{1,0:T(8,128)(2,1)} %param.10, bf16[320,2048]{1,0:T(8,128)(2,1)} %param.9, bf16[320,2048]{1,0:T(8,128)(2,1)S(1)} %copy-done.1), kind=kOutput, calls=%fused_computation.19 | convolution fusion | flops 842137600 | bytes 6656000 | tf_op jit(solution)/shard_map/hqk,khd->qhd/dot_general | solution.py:89
  48.8 1.6 %collective-permute-done.5 = bf16[320,16,128]{2,0,1:T(8,128)(2,1)} collective-permute-done((bf16[320,16,128]{2,0,1:T(8,128)(2,1)}, bf16[320,16,128]{2,0,1:T(8,128)(2,1)}, u32[]{:S(2)}, u32[]{:S(2)}) %collective-permute-start.5) | collective-permute-done | bytes 1310752 | tf_op jit(solution)/shard_map/ppermute | solution.py:19
  50.4 1.3 collective-permute-start.6
  51.7 4.2 %multiply_reduce_fusion = (f32[320,16]{0,1:T(8,128)S(1)}, f32[320,16,128]{2,0,1:T(8,128)S(1)}) fusion(bf16[16,128,128]{2,1,0:T(8,128)(2,1)} %collective-permute-done.3, bf16[16,128,128]{2,1,0:T(8,128)(2,1)S(1)} %collective-permute-done.1, pred[]{:T(512)S(6)} %and.17, pred[]{:T(512)S(6)} %and.16, pred[320]{0:T(512)(128)(4,1)S(1)} %get-tuple-element.13, ...), kind=kOutput, calls=%fused_computation.49 | convolution fusion | flops 1010560000 | bytes 7622978 | tf_op jit(solution)/shard_map/qhd,hde->qhe/dot_general | solution.py:90
  56.9 2.8 %fusion.1 = (f32[16,320]{1,0:T(8,128)S(1)}, f32[16,320,320]{1,2,0:T(8,128)S(1)}) fusion(pred[320,320]{0,1:T(8,128)(4,1)S(1)} %get-tuple-element.10, bf16[320,16,128]{2,0,1:T(8,128)(2,1)} %collective-permute-done.5, bf16[320,2048]{1,0:T(8,128)(2,1)S(1)} %copy-done), kind=kOutput, calls=%fused_computation.8 | convolution fusion | flops 424340480 | bytes 9297920 | tf_op jit(solution)/shard_map/qhd,khd->hqk/dot_general | solution.py:77
  59.7 22.1 %collective-permute-done.6 = bf16[320,16,128]{2,0,1:T(8,128)(2,1)S(1)} collective-permute-done((bf16[320,16,128]{2,0,1:T(8,128)(2,1)}, bf16[320,16,128]{2,0,1:T(8,128)(2,1)S(1)}, u32[]{:S(2)}, u32[]{:S(2)}) %collective-permute-start.6) | collective-permute-done | bytes 1310752 | tf_op jit(solution)/shard_map/ppermute | solution.py:19
  81.8 1.5 fusion
  83.4 3.8 %collective-permute-start.8 = (f32[16,320]{1,0:T(8,128)S(1)}, f32[16,320]{1,0:T(8,128)S(1)}, u32[]{:S(2)}, u32[]{:S(2)}) collective-permute-start(f32[16,320]{1,0:T(8,128)S(1)} %get-tuple-element.20), channel_id=1, source_target_pairs={{0,4},{4,8},{8,12},{1,5},{5,9},{9,13},{2,6},{6,10},{10,14},{3,7},{... | collective-permute-start | bytes 61448 | tf_op jit(solution)/shard_map/ppermute | solution.py:15
  87.2 2.8 %fusion.46 = bf16[320,16,128]{2,0,1:T(8,128)(2,1)S(1)} fusion(bf16[320,16,128]{2,0,1:T(8,128)(2,1)S(1)} %fusion.35, f32[16,320,320]{1,2,0:T(8,128)S(1)} %get-tuple-element.21, f32[16,320]{1,0:T(8,128)S(1)} %get-tuple-element.20, pred[320,320]{0,1:T(8,128)(4,1)S(1)} %get-tuple-element.9), kind=kOutput, calls=%fused_computation.51 | convolution fusion | flops 428277760 | bytes 9297920 | tf_op jit(solution)/shard_map/hqk,khd->qhd/dot_general | solution.py:106
  90.0 3.4 %collective-permute-start.7 = (bf16[320,16,128]{2,0,1:T(8,128)(2,1)S(1)}, bf16[320,16,128]{2,0,1:T(8,128)(2,1)S(1)}, u32[]{:S(2)}, u32[]{:S(2)}) collective-permute-start(bf16[320,16,128]{2,0,1:T(8,128)(2,1)S(1)} %fusion.46), channel_id=1, source_target_pairs={{0,4},{4,8},{8,12},{1,5},{5,9},{9,13},{2,6},{6,10},{10,14},{3,7},{... | collective-permute-start | bytes 3932168 | tf_op jit(solution)/shard_map/ppermute | solution.py:15
  93.5 2.0 %fusion.3 = f32[16,320]{1,0:T(8,128)S(1)} fusion(f32[16,320,320]{1,2,0:T(8,128)S(1)} %get-tuple-element.21, f32[16,320]{1,0:T(8,128)S(1)} %get-tuple-element.20, pred[320,320]{0,1:T(8,128)(4,1)S(1)} %get-tuple-element.9), kind=kLoop, calls=%fused_computation.10 | loop fusion | flops 8186880 | bytes 6696960 | tf_op jit(solution)/shard_map/reduce_sum | solution.py:85
  95.5 1.8 %collective-permute-start.12 = (f32[16,320]{1,0:T(8,128)S(1)}, f32[16,320]{1,0:T(8,128)S(1)}, u32[]{:S(2)}, u32[]{:S(2)}) collective-permute-start(f32[16,320]{1,0:T(8,128)S(1)} %fusion.3), channel_id=1, source_target_pairs={{0,4},{4,8},{8,12},{1,5},{5,9},{9,13},{2,6},{6,10},{10,14},{3,7},{... | collective-permute-start | bytes 61448 | tf_op jit(solution)/shard_map/ppermute | solution.py:15
  97.3 2.0 %fusion.5 = f32[16,320]{1,0:T(8,128)S(1)} fusion(f32[16,320,320]{1,2,0:T(8,128)S(1)} %get-tuple-element.23, f32[16,320]{1,0:T(8,128)S(1)} %get-tuple-element.22, pred[320,320]{0,1:T(8,128)(4,1)S(1)} %get-tuple-element.10), kind=kLoop, calls=%fused_computation.12 | loop fusion | flops 8186880 | bytes 6696960 | tf_op jit(solution)/shard_map/reduce_sum | solution.py:85
  99.3 19.7 %collective-permute-done.12 = f32[16,320]{1,0:T(8,128)S(1)} collective-permute-done((f32[16,320]{1,0:T(8,128)S(1)}, f32[16,320]{1,0:T(8,128)S(1)}, u32[]{:S(2)}, u32[]{:S(2)}) %collective-permute-start.12) | collective-permute-done | bytes 20512 | tf_op jit(solution)/shard_map/ppermute | solution.py:15
  119.0 4.3 %fusion.40 = bf16[320,16,128]{2,0,1:T(8,128)(2,1)S(1)} fusion(bf16[320,16,128]{2,0,1:T(8,128)(2,1)S(1)} %collective-permute-done.7, bf16[320,16,128]{2,0,1:T(8,128)(2,1)S(1)} %fusion.35, f32[16,320,320]{1,2,0:T(8,128)S(1)} %get-tuple-element.23, f32[16,320]{1,0:T(8,128)S(1)} %get-tuple-element.22, pred[320,320]{0,1:T(8,128)(4,1)S(1)} %get-tuple-element.10, ...), kind=kOutput, calls=%fused_computation.46 | convolution fusion | flops 431554560 | bytes 10649601 | tf_op jit(solution)/shard_map/hqk,khd->qhd/dot_general | solution.py:106
  123.3 4.5 %collective-permute-start.10 = (bf16[320,16,128]{2,0,1:T(8,128)(2,1)S(1)}, bf16[320,16,128]{2,0,1:T(8,128)(2,1)S(1)}, u32[]{:S(2)}, u32[]{:S(2)}) collective-permute-start(bf16[320,16,128]{2,0,1:T(8,128)(2,1)S(1)} %fusion.40), channel_id=1, source_target_pairs={{0,4},{4,8},{8,12},{1,5},{5,9},{9,13},{2,6},{6,10},{10,14},{3,7},{... | collective-permute-start | bytes 3932168 | tf_op jit(solution)/shard_map/ppermute | solution.py:15
  127.8 2.0 %fusion.7 = f32[16,320]{1,0:T(8,128)S(1)} fusion(f32[16,320,320]{1,2,0:T(8,128)S(1)} %bitcast.142, f32[16,320]{1,0:T(8,128)S(1)} %get-tuple-element.18, pred[320,320]{0,1:T(8,128)(4,1)S(1)} %get-tuple-element.11), kind=kLoop, calls=%fused_computation.14 | loop fusion | flops 8186880 | bytes 6696960 | tf_op jit(solution)/shard_map/reduce_sum | solution.py:85
  129.8 2.1 %collective-permute-start.11 = (f32[16,320]{1,0:T(8,128)S(1)}, f32[16,320]{1,0:T(8,128)S(1)}, u32[]{:S(2)}, u32[]{:S(2)}) collective-permute-start(f32[16,320]{1,0:T(8,128)S(1)} %get-tuple-element.5), channel_id=1, source_target_pairs={{0,4},{4,8},{8,12},{1,5},{5,9},{9,13},{2,6},{6,10},{10,14},{3,7},{... | collective-permute-start | bytes 61448 | tf_op jit(solution)/shard_map/ppermute | solution.py:15
  131.9 2.2 %collective-permute-start.13 = (f32[16,320]{1,0:T(8,128)S(1)}, f32[16,320]{1,0:T(8,128)S(1)}, u32[]{:S(2)}, u32[]{:S(2)}) collective-permute-start(f32[16,320]{1,0:T(8,128)S(1)} %get-tuple-element.4), channel_id=1, source_target_pairs={{0,4},{4,8},{8,12},{1,5},{5,9},{9,13},{2,6},{6,10},{10,14},{3,7},{... | collective-permute-start | bytes 61448 | tf_op jit(solution)/shard_map/ppermute | solution.py:15
  135.4 17.2 %collective-permute-done.11 = f32[16,320]{1,0:T(8,128)S(1)} collective-permute-done((f32[16,320]{1,0:T(8,128)S(1)}, f32[16,320]{1,0:T(8,128)S(1)}, u32[]{:S(2)}, u32[]{:S(2)}) %collective-permute-start.11) | collective-permute-done | bytes 20512 | tf_op jit(solution)/shard_map/ppermute | solution.py:15
  152.9 4.9 %fusion.64 = bf16[16,40,8,128]{3,2,1,0:T(8,128)(2,1)S(1)} fusion(f32[320,16]{0,1:T(8,128)S(1)} %get-tuple-element.7, f32[320,16]{0,1:T(8,128)S(1)} %get-tuple-element.8, f32[320,16]{0,1:T(8,128)S(1)} %get-tuple-element.6, bf16[320,16,128]{2,0,1:T(8,128)(2,1)S(1)} %collective-permute-done.10, pred[]{:T(512)S(6)} %ge.28, ...), kind=kOutput, calls=%fused_computation.69 | convolution fusion | flops 432209920 | bytes 10670081 | tf_op jit(solution)/shard_map/hqk,khd->qhd/dot_general | solution.py:106
  157.8 1.4 copy.102
  (38 shorter events, 5.3 us)
Async XLA Ops:
  0.6 36.5 %copy-start = (bf16[320,2048]{1,0:T(8,128)(2,1)S(1)}, bf16[320,2048]{1,0:T(8,128)(2,1)}, u32[]{:S(2)}) copy-start(bf16[320,2048]{1,0:T(8,128)(2,1)} %param.14) | copy-start | bytes 3932164
  0.6 18.2 %copy-start.3 = (s32[320]{0:T(512)S(1)}, s32[320]{0:T(512)}, u32[]{:S(2)}) copy-start(s32[320]{0:T(512)} %param.15) | copy-start | bytes 3844
  0.7 19.4 %copy-start.5 = (bf16[320,2048]{1,0:T(8,128)(2,1)S(1)}, bf16[320,2048]{1,0:T(8,128)(2,1)}, u32[]{:S(2)}) copy-start(bf16[320,2048]{1,0:T(8,128)(2,1)} %param.10) | copy-start | bytes 3932164
  0.7 19.4 %copy-start.6 = (bf16[320,2048]{1,0:T(8,128)(2,1)S(1)}, bf16[320,2048]{1,0:T(8,128)(2,1)}, u32[]{:S(2)}) copy-start(bf16[320,2048]{1,0:T(8,128)(2,1)} %param.9) | copy-start | bytes 3932164
  2.1 19.7 %collective-permute-start = (s32[1]{0:T(128)}, s32[1]{0:T(128)}, u32[]{:S(2)}, u32[]{:S(2)}) collective-permute-start(s32[1]{0:T(128)} %get-tuple-element.14), channel_id=1, source_target_pairs={{0,4},{4,8},{8,12},{1,5},{5,9},{9,13},{2,6},{6,10},{10,14},{3,7},{... | collective-permute-start | bytes 20 | tf_op jit(solution)/shard_map/ppermute | solution.py:15
  7.6 20.7 %collective-permute-start.2 = (s32[1]{0:T(128)}, s32[1]{0:T(128)}, u32[]{:S(2)}, u32[]{:S(2)}) collective-permute-start(s32[1]{0:T(128)} %get-tuple-element.14), channel_id=1, source_target_pairs={{0,8},{4,12},{1,9},{5,13},{2,10},{6,14},{3,11},{7,15},{16,24},{20,... | collective-permute-start | bytes 20 | tf_op jit(solution)/shard_map/ppermute | solution.py:15
  12.1 24.7 %collective-permute-start.4 = (s32[320]{0:T(512)}, s32[320]{0:T(512)S(1)}, u32[]{:S(2)}, u32[]{:S(2)}) collective-permute-start(s32[320]{0:T(512)} %param.15), channel_id=1, source_target_pairs={{8,0},{12,4},{9,1},{13,5},{10,2},{14,6},{11,3},{15,7},{24,16},{28,... | collective-permute-start | bytes 3848 | tf_op jit(solution)/shard_map/ppermute | solution.py:19
  13.4 23.4 %collective-permute-start.9 = (s32[320]{0:T(512)}, s32[320]{0:T(512)S(1)}, u32[]{:S(2)}, u32[]{:S(2)}) collective-permute-start(s32[320]{0:T(512)} %param.15), channel_id=1, source_target_pairs={{4,0},{8,4},{12,8},{5,1},{9,5},{13,9},{6,2},{10,6},{14,10},{7,3},{... | collective-permute-start | bytes 3848 | tf_op jit(solution)/shard_map/ppermute | solution.py:19
  17.4 4.4 %copy-start.4 = (bf16[2048]{0:T(1024)(128)(2,1)S(1)}, bf16[2048]{0:T(1024)(128)(2,1)}, u32[]{:S(2)}) copy-start(bf16[2048]{0:T(1024)(128)(2,1)} %param.11) | copy-start | bytes 12292
  17.4 32.9 %collective-permute-start.5 = (bf16[320,16,128]{2,0,1:T(8,128)(2,1)}, bf16[320,16,128]{2,0,1:T(8,128)(2,1)}, u32[]{:S(2)}, u32[]{:S(2)}) collective-permute-start(bf16[320,16,128]{2,0,1:T(8,128)(2,1)} %copy_bitcast_fusion.2), channel_id=1, source_target_pairs={{4,0},{8,4},{12,8},{5,1},{9,5},{13,9},{6,2},{10,6},{14,10},{7,3},{... | collective-permute-start | bytes 3932168 | tf_op jit(solution)/shard_map/ppermute | solution.py:19
  21.9 29.8 %collective-permute-start.1 = (bf16[16,128,128]{2,1,0:T(8,128)(2,1)}, bf16[16,128,128]{2,1,0:T(8,128)(2,1)S(1)}, u32[]{:S(2)}, u32[]{:S(2)}) collective-permute-start(bf16[16,128,128]{2,1,0:T(8,128)(2,1)} %fusion.65), channel_id=1, source_target_pairs={{0,4},{4,8},{8,12},{1,5},{5,9},{9,13},{2,6},{6,10},{10,14},{3,7},{... | collective-permute-start | bytes 1572872 | tf_op jit(solution)/shard_map/ppermute | solution.py:15
  28.3 23.3 %collective-permute-start.3 = (bf16[16,128,128]{2,1,0:T(8,128)(2,1)}, bf16[16,128,128]{2,1,0:T(8,128)(2,1)}, u32[]{:S(2)}, u32[]{:S(2)}) collective-permute-start(bf16[16,128,128]{2,1,0:T(8,128)(2,1)} %fusion.65), channel_id=1, source_target_pairs={{0,8},{4,12},{1,9},{5,13},{2,10},{6,14},{3,11},{7,15},{16,24},{20,... | collective-permute-start | bytes 1572872 | tf_op jit(solution)/shard_map/ppermute | solution.py:15
  37.1 6.1 %copy-start.1 = (bf16[320,2048]{1,0:T(8,128)(2,1)S(1)}, bf16[320,2048]{1,0:T(8,128)(2,1)}, u32[]{:S(2)}) copy-start(bf16[320,2048]{1,0:T(8,128)(2,1)} %param.8) | copy-start | bytes 3932164
  50.4 31.5 %collective-permute-start.6 = (bf16[320,16,128]{2,0,1:T(8,128)(2,1)}, bf16[320,16,128]{2,0,1:T(8,128)(2,1)S(1)}, u32[]{:S(2)}, u32[]{:S(2)}) collective-permute-start(bf16[320,16,128]{2,0,1:T(8,128)(2,1)} %collective-permute-done.5), channel_id=1, source_target_pairs={{4,0},{8,4},{12,8},{5,1},{9,5},{13,9},{6,2},{10,6},{14,10},{7,3},{... | collective-permute-start | bytes 3932168 | tf_op jit(solution)/shard_map/ppermute | solution.py:19
  51.7 4.3 %copy-start.2 = (bf16[320,2048]{1,0:T(8,128)(2,1)S(1)}, bf16[320,2048]{1,0:T(8,128)(2,1)}, u32[]{:S(2)}) copy-start(bf16[320,2048]{1,0:T(8,128)(2,1)} %param.12) | copy-start | bytes 3932164
  83.4 35.6 %collective-permute-start.8 = (f32[16,320]{1,0:T(8,128)S(1)}, f32[16,320]{1,0:T(8,128)S(1)}, u32[]{:S(2)}, u32[]{:S(2)}) collective-permute-start(f32[16,320]{1,0:T(8,128)S(1)} %get-tuple-element.20), channel_id=1, source_target_pairs={{0,4},{4,8},{8,12},{1,5},{5,9},{9,13},{2,6},{6,10},{10,14},{3,7},{... | collective-permute-start | bytes 61448 | tf_op jit(solution)/shard_map/ppermute | solution.py:15
  90.0 29.0 %collective-permute-start.7 = (bf16[320,16,128]{2,0,1:T(8,128)(2,1)S(1)}, bf16[320,16,128]{2,0,1:T(8,128)(2,1)S(1)}, u32[]{:S(2)}, u32[]{:S(2)}) collective-permute-start(bf16[320,16,128]{2,0,1:T(8,128)(2,1)S(1)} %fusion.46), channel_id=1, source_target_pairs={{0,4},{4,8},{8,12},{1,5},{5,9},{9,13},{2,6},{6,10},{10,14},{3,7},{... | collective-permute-start | bytes 3932168 | tf_op jit(solution)/shard_map/ppermute | solution.py:15
  95.5 23.5 %collective-permute-start.12 = (f32[16,320]{1,0:T(8,128)S(1)}, f32[16,320]{1,0:T(8,128)S(1)}, u32[]{:S(2)}, u32[]{:S(2)}) collective-permute-start(f32[16,320]{1,0:T(8,128)S(1)} %fusion.3), channel_id=1, source_target_pairs={{0,4},{4,8},{8,12},{1,5},{5,9},{9,13},{2,6},{6,10},{10,14},{3,7},{... | collective-permute-start | bytes 61448 | tf_op jit(solution)/shard_map/ppermute | solution.py:15
  119.0 8.8 %slice-start = ((s8[7864320]{0:T(1024)(128)(4,1)}), s8[4194304]{0:T(1024)(128)(4,1)S(1)}, s32[]{:S(2)}) async-start(s8[7864320]{0:T(1024)(128)(4,1)} %bitcast.141), calls=%async_computation | async-start | bytes 8388608
  119.0 8.8 %slice-start.1 = ((s8[7864320]{0:T(1024)(128)(4,1)}), s8[3670016]{0:T(1024)(128)(4,1)S(1)}, s32[]{:S(2)}) async-start(s8[7864320]{0:T(1024)(128)(4,1)} %bitcast.141), calls=%async_computation.1 | async-start | bytes 7340032
  123.3 29.6 %collective-permute-start.10 = (bf16[320,16,128]{2,0,1:T(8,128)(2,1)S(1)}, bf16[320,16,128]{2,0,1:T(8,128)(2,1)S(1)}, u32[]{:S(2)}, u32[]{:S(2)}) collective-permute-start(bf16[320,16,128]{2,0,1:T(8,128)(2,1)S(1)} %fusion.40), channel_id=1, source_target_pairs={{0,4},{4,8},{8,12},{1,5},{5,9},{9,13},{2,6},{6,10},{10,14},{3,7},{... | collective-permute-start | bytes 3932168 | tf_op jit(solution)/shard_map/ppermute | solution.py:15
  129.8 22.8 %collective-permute-start.11 = (f32[16,320]{1,0:T(8,128)S(1)}, f32[16,320]{1,0:T(8,128)S(1)}, u32[]{:S(2)}, u32[]{:S(2)}) collective-permute-start(f32[16,320]{1,0:T(8,128)S(1)} %get-tuple-element.5), channel_id=1, source_target_pairs={{0,4},{4,8},{8,12},{1,5},{5,9},{9,13},{2,6},{6,10},{10,14},{3,7},{... | collective-permute-start | bytes 61448 | tf_op jit(solution)/shard_map/ppermute | solution.py:15
  131.9 20.9 %collective-permute-start.13 = (f32[16,320]{1,0:T(8,128)S(1)}, f32[16,320]{1,0:T(8,128)S(1)}, u32[]{:S(2)}, u32[]{:S(2)}) collective-permute-start(f32[16,320]{1,0:T(8,128)S(1)} %get-tuple-element.4), channel_id=1, source_target_pairs={{0,4},{4,8},{8,12},{1,5},{5,9},{9,13},{2,6},{6,10},{10,14},{3,7},{... | collective-permute-start | bytes 61448 | tf_op jit(solution)/shard_map/ppermute | solution.py:15

commit v3 on v2

--- a/solution.py
+++ b/solution.py
@@ -45,20 +45,27 @@
     last_doc = doc_id[-1]
 
     query_soft = soft_query.reshape(row_count, head_count, HD)
+    doc_cols = jnp.broadcast_to(doc_id.astype(jnp.bfloat16)[:, None], (row_count, HD))
+    message = jnp.concatenate([soft_query, doc_cols], axis=1)
     query_blocks = [query_soft]
+    query_docs = [doc_id]
     for d in dists:
-        query_blocks.append(shift_down(query_blocks[-1], 1, n_seq))
-    query_docs = [doc_id] + [shift_down(doc_id, d, n_seq) for d in dists]
+        message = shift_down(message, 1, n_seq)
+        query_blocks.append(message[:, : head_count * HD].reshape(row_count, head_count, HD))
+        query_docs.append(message[:, head_count * HD].astype(jnp.int32))
 
     tail_keys = jnp.where((doc_id == last_doc)[:, None, None], key_rows, jnp.zeros_like(key_rows))
     local_state = jnp.einsum(
         "thd,the->hde", tail_keys, value_rows, preferred_element_type=jnp.float32
     )
-    state_bf = local_state.astype(jnp.bfloat16)
+    state_rows = local_state.astype(jnp.bfloat16).reshape(head_count * HD, HD)
+    tag_rows = jnp.full((8, HD), last_doc, jnp.int32).astype(jnp.bfloat16)
+    state_msg = jnp.concatenate([state_rows, tag_rows], axis=0)
     carried = jnp.zeros_like(local_state)
     for d in dists:
-        state_in = shift_up(state_bf, d, n_seq).astype(jnp.float32)
-        tag_in = shift_up(last_doc[None], d, n_seq)[0]
+        msg_in = shift_up(state_msg, d, n_seq)
+        state_in = msg_in[: head_count * HD].reshape(head_count, HD, HD).astype(jnp.float32)
+        tag_in = msg_in[head_count * HD, 0].astype(jnp.int32)
         wanted = (my_index >= d) & (tag_in == first_doc)
         carried = carried + jnp.where(wanted, state_in, jnp.zeros_like(state_in))
 
@@ -112,18 +119,17 @@
     for d in reversed([0] + dists):
         part = partial_out(d)
         if running is not None:
-            out_in, max_in, sum_in = running
+            out_in, stats_in = running
             has_source = my_index >= 1
-            max_in = jnp.where(has_source, max_in, -1e30)
-            sum_in = jnp.where(has_source, sum_in, 0.0)
+            max_in = jnp.where(has_source, stats_in[0], -1e30)
+            sum_in = jnp.where(has_source, stats_in[1], 0.0)
             out_in = jnp.where(has_source, out_in.astype(jnp.float32), 0.0)
             part = merge((out_in, max_in, sum_in), part)
         if d > 0:
             out_d, max_d, sum_d = part
             running = (
                 shift_up(out_d.astype(jnp.bfloat16), 1, n_seq),
-                shift_up(max_d, 1, n_seq),
-                shift_up(sum_d, 1, n_seq),
+                shift_up(jnp.stack([max_d, sum_d]), 1, n_seq),
             )
     mixed, row_max, row_sum = part
     soft_out = mixed / jnp.transpose(row_sum)[:, :, None]

time: 160 us -> 162 us (1.012)
  starting transfers between devices: 45.6 us -> 29.8 us
  waiting for transfers between devices: 60.9 us -> 74.2 us
  other arithmetic: 8.44 us -> 14.3 us
    ppermute x4 -> x2, waiting for transfers between devices: 23.7 us -> 37.7 us  [shift_down(): return lax.ppermute(x, 'seq', [(s + dist, s) for s in range(n_seq - dist)])]
    ppermute x10 -> x6, starting transfers between devices: 40.4 us -> 27.2 us  [shift_up(): return lax.ppermute(x, 'seq', [(s, s + dist) for s in range(n_seq - dist)])]
    dot_general x3, matrix products: 10.4 us -> 7.56 us  [per_device(): jnp.einsum('qhd,khd->hqk', query_blocks[d], key_soft, preferred_element_t...]
    reshape x1 -> x0, local copies, waits for them, and re-layouts: 2.71 us -> none  [per_device(): query_soft = soft_query.reshape(row_count, head_count, HD)]
    ppermute x4 -> x2, starting transfers between devices: 5.26 us -> 2.57 us  [shift_down(): return lax.ppermute(x, 'seq', [(s + dist, s) for s in range(n_seq - dist)])]
    eq x1 -> x3, other arithmetic: 0.27 us -> 2.34 us  [per_device(): keep = query_docs[d][:, None] == doc_id[None, :]]
    ppermute x10 -> x6, waiting for transfers between devices: 37.2 us -> 36.5 us  [shift_up(): return lax.ppermute(x, 'seq', [(s, s + dist) for s in range(n_seq - dist)])]
  transfers between devices with their start and end apart: 14 -> 8, of which waited for: 5 -> 4; matrix products, arithmetic and copies ran while one was open for 22% -> 15% of each run, Pallas kernels for 0% -> 0%
where the time goes in v3:
time: 162 us; the launch traced here: 161 us
  waiting for transfers between devices  74.2 us (46%)
  matrix products  32.7 us (20%)
  starting transfers between devices  29.8 us (18%)
  other arithmetic  14.3 us (9%)
  local copies, waits for them, and re-layouts  5.91 us (4%)
  between operations  4.26 us (3%)
    ppermute x2, waiting for transfers between devices, shift_down(): return lax.ppermute(x, 'seq', [(s + dist, s) for s in range(n_seq - dist)])  37.7 us
    ppermute x6, waiting for transfers between devices, shift_up(): return lax.ppermute(x, 'seq', [(s, s + dist) for s in range(n_seq - dist)])  36.5 us
    ppermute x6, starting transfers between devices, shift_up(): return lax.ppermute(x, 'seq', [(s, s + dist) for s in range(n_seq - dist)])  27.2 us
    dot_general x3, matrix products, partial_out(): jnp.einsum('hqk,khd->qhd', probs, value_own, preferred_element_type=jnp.f...  11.9 us
    dot_general x3, matrix products, per_device(): jnp.einsum('qhd,khd->hqk', query_blocks[d], key_soft, preferred_element_t...  7.56 us
    dot_general x1, matrix products, per_device(): jnp.einsum('hqk,khd->qhd', rounded, value_rows, preferred_element_type=jn...  6.46 us
    reduce_sum x3, other arithmetic, per_device(): jnp.sum(probs, axis=-1)  6.02 us
    dot_general x1, matrix products, per_device(): jnp.einsum('qhd,hde->qhe', queries.astype(jnp.float32), carried, precisio...  4.12 us
  transfers between devices with their start and end apart: 8, of which 4 were waited for; matrix products, arithmetic and copies ran while one was open for 15% of the time, Pallas kernels for 0%

profile of v3, /device:TPU:0, one launch (start us, length us, event | category | flops | bytes accessed | tf_op | source)
XLA Modules:
  0.0 161.1 jit_solution(690431570170279303)
XLA Ops:
  1.6 1.4 pad_maximum_fusion
  3.0 1.3 collective-permute-start.2
  5.6 1.3 broadcast_compare_fusion.3
  6.9 2.6 %fusion.72 = bf16[16,128,128]{2,1,0:T(8,128)(2,1)S(1)} fusion(pred[320]{0:T(512)(128)(4,1)S(1)} %get-tuple-element.13, bf16[320,2048]{1,0:T(8,128)(2,1)} %param.10, bf16[320,2048]{1,0:T(8,128)(2,1)} %param.9), kind=kOutput, calls=%fused_computation.79 | convolution fusion | flops 168689664 | bytes 3146048 | tf_op jit(solution)/shard_map/thd,the->hde/dot_general | solution.py:58
  9.5 6.4 %collective-permute-start = (bf16[2056,128]{1,0:T(8,128)(2,1)S(1)}, bf16[2056,128]{1,0:T(8,128)(2,1)}, u32[]{:S(2)}, u32[]{:S(2)}) collective-permute-start(bf16[2056,128]{1,0:T(8,128)(2,1)S(1)} %concatenate.6), channel_id=1, source_target_pairs={{0,4},{4,8},{8,12},{1,5},{5,9},{9,13},{2,6},{6,10},{10,14},{3,7},{... | collective-permute-start | bytes 1579016 | tf_op jit(solution)/shard_map/ppermute | solution.py:15
  15.9 6.0 %collective-permute-start.1 = (bf16[2056,128]{1,0:T(8,128)(2,1)S(1)}, bf16[2056,128]{1,0:T(8,128)(2,1)}, u32[]{:S(2)}, u32[]{:S(2)}) collective-permute-start(bf16[2056,128]{1,0:T(8,128)(2,1)S(1)} %concatenate.6), channel_id=1, source_target_pairs={{0,8},{4,12},{1,9},{5,13},{2,10},{6,14},{3,11},{7,15},{16,24},{20,... | collective-permute-start | bytes 1579016 | tf_op jit(solution)/shard_map/ppermute | solution.py:15
  21.9 16.7 %collective-permute-done.2 = bf16[320,2176]{1,0:T(8,128)(2,1)} collective-permute-done((bf16[320,2176]{1,0:T(8,128)(2,1)S(1)}, bf16[320,2176]{1,0:T(8,128)(2,1)}, u32[]{:S(2)}, u32[]{:S(2)}) %collective-permute-start.2) | collective-permute-done | bytes 1392672 | tf_op jit(solution)/shard_map/ppermute | solution.py:19
  38.6 1.3 collective-permute-start.3
  39.9 1.2 slice.56
  42.4 1.2 slice.58
  44.9 1.4 select_add_fusion
  46.3 4.1 %fusion.68 = f32[16,128,320]{1,2,0:T(8,128)} fusion(f32[16,128,128]{2,1,0:T(8,128)S(1)} %bitcast.204, bf16[320,2048]{1,0:T(8,128)(2,1)} %param.8), kind=kOutput, calls=%fused_computation.73 | convolution fusion | flops 1006632960 | bytes 4980736 | tf_op jit(solution)/shard_map/qhd,hde->qhe/dot_general | solution.py:97
  51.5 21.0 %collective-permute-done.3 = bf16[320,2176]{1,0:T(8,128)(2,1)} collective-permute-done((bf16[320,2176]{1,0:T(8,128)(2,1)}, bf16[320,2176]{1,0:T(8,128)(2,1)}, u32[]{:S(2)}, u32[]{:S(2)}) %collective-permute-start.3) | collective-permute-done | bytes 1392672 | tf_op jit(solution)/shard_map/ppermute | solution.py:19
  72.5 1.0 convert_reduce_fusion.1
  73.8 6.5 %multiply_reduce_fusion = (f32[320,16]{0,1:T(8,128)S(1)}, f32[320,16,128]{2,0,1:T(8,128)}) fusion(f32[16,128,320]{1,2,0:T(8,128)} %fusion.68, pred[320]{0:T(512)(128)(4,1)S(1)} %get-tuple-element.12, pred[320,320]{0,1:T(8,128)(4,1)S(1)} %get-tuple-element.11, bf16[320,2048]{1,0:T(8,128)(2,1)} %param.10, bf16[320,2048]{1,0:T(8,128)(2,1)} %param.9, ...), kind=kOutput, calls=%fused_computation.49 | convolution fusion | flops 844753920 | bytes 9298240 | tf_op jit(solution)/shard_map/hqk,khd->qhd/dot_general | solution.py:96
  80.3 3.0 %fusion = (f32[16,320]{1,0:T(8,128)S(1)}, f32[16,320,320]{1,2,0:T(8,128)S(1)}) fusion(pred[320,320]{0,1:T(8,128)(4,1)S(1)} %get-tuple-element.10, bf16[320,2176]{1,0:T(8,128)(2,1)} %collective-permute-done.3, bf16[320,2048]{1,0:T(8,128)(2,1)S(1)} %copy-done), kind=kOutput, calls=%fused_computation.7 | convolution fusion | flops 424340480 | bytes 9297920 | tf_op jit(solution)/shard_map/qhd,khd->hqk/dot_general | solution.py:84
  83.3 2.0 %fusion.3 = f32[16,320]{1,0:T(8,128)S(1)} fusion(f32[16,320,320]{1,2,0:T(8,128)S(1)} %get-tuple-element.23, f32[16,320]{1,0:T(8,128)S(1)} %get-tuple-element.22, pred[320,320]{0,1:T(8,128)(4,1)S(1)} %get-tuple-element.10), kind=kLoop, calls=%fused_computation.10 | loop fusion | flops 8186880 | bytes 6696960 | tf_op jit(solution)/shard_map/reduce_sum | solution.py:92
  86.3 2.8 %fusion.46 = bf16[320,16,128]{2,0,1:T(8,128)(2,1)S(1)} fusion(bf16[320,16,128]{2,0,1:T(8,128)(2,1)S(1)} %fusion.35, f32[16,320,320]{1,2,0:T(8,128)S(1)} %get-tuple-element.23, f32[16,320]{1,0:T(8,128)S(1)} %get-tuple-element.22, pred[320,320]{0,1:T(8,128)(4,1)S(1)} %get-tuple-element.10), kind=kOutput, calls=%fused_computation.51 | convolution fusion | flops 428277760 | bytes 9297920 | tf_op jit(solution)/shard_map/hqk,khd->qhd/dot_general | solution.py:113
  89.1 3.4 %collective-permute-start.4 = (bf16[320,16,128]{2,0,1:T(8,128)(2,1)S(1)}, bf16[320,16,128]{2,0,1:T(8,128)(2,1)S(1)}, u32[]{:S(2)}, u32[]{:S(2)}) collective-permute-start(bf16[320,16,128]{2,0,1:T(8,128)(2,1)S(1)} %fusion.46), channel_id=1, source_target_pairs={{0,4},{4,8},{8,12},{1,5},{5,9},{9,13},{2,6},{6,10},{10,14},{3,7},{... | collective-permute-start | bytes 3932168 | tf_op jit(solution)/shard_map/ppermute | solution.py:15
  92.5 3.6 %collective-permute-start.5 = (f32[2,16,320]{2,1,0:T(8,128)S(1)}, f32[2,16,320]{2,1,0:T(8,128)S(1)}, u32[]{:S(2)}, u32[]{:S(2)}) collective-permute-start(f32[2,16,320]{2,1,0:T(8,128)S(1)} %pad_maximum_fusion.1), channel_id=1, source_target_pairs={{0,4},{4,8},{8,12},{1,5},{5,9},{9,13},{2,6},{6,10},{10,14},{3,7},{... | collective-permute-start | bytes 122888 | tf_op jit(solution)/shard_map/ppermute | solution.py:15
  96.1 3.0 %fusion.1 = (f32[16,320]{1,0:T(8,128)S(1)}, f32[16,320,320]{1,2,0:T(8,128)S(1)}) fusion(pred[320,320]{0,1:T(8,128)(4,1)S(1)} %get-tuple-element.9, bf16[320,2176]{1,0:T(8,128)(2,1)} %collective-permute-done.2, bf16[320,2048]{1,0:T(8,128)(2,1)S(1)} %copy-done), kind=kOutput, calls=%fused_computation.8 | convolution fusion | flops 424340480 | bytes 9297920 | tf_op jit(solution)/shard_map/qhd,khd->hqk/dot_general | solution.py:84
  99.1 2.0 %fusion.5 = f32[16,320]{1,0:T(8,128)S(1)} fusion(f32[16,320,320]{1,2,0:T(8,128)S(1)} %get-tuple-element.21, f32[16,320]{1,0:T(8,128)S(1)} %get-tuple-element.20, pred[320,320]{0,1:T(8,128)(4,1)S(1)} %get-tuple-element.9), kind=kLoop, calls=%fused_computation.12 | loop fusion | flops 8186880 | bytes 6696960 | tf_op jit(solution)/shard_map/reduce_sum | solution.py:92
  101.1 1.6 %fusion.2 = (f32[16,320]{1,0:T(8,128)S(1)}, f32[16,320,320]{1,2,0:T(8,128)S(1)}) fusion(pred[320,320]{0,1:T(8,128)(4,1)S(1)} %get-tuple-element.11, bf16[320,2048]{1,0:T(8,128)(2,1)S(1)} %copy-done.3, bf16[320,2048]{1,0:T(8,128)(2,1)S(1)} %copy-done), kind=kOutput, calls=%fused_computation.9 | convolution fusion | flops 424340480 | bytes 9297920 | tf_op jit(solution)/shard_map/qhd,khd->hqk/dot_general | solution.py:84
  102.7 17.0 %collective-permute-done.5 = f32[2,16,320]{2,1,0:T(8,128)S(1)} collective-permute-done((f32[2,16,320]{2,1,0:T(8,128)S(1)}, f32[2,16,320]{2,1,0:T(8,128)S(1)}, u32[]{:S(2)}, u32[]{:S(2)}) %collective-permute-start.5) | collective-permute-done | bytes 40992 | tf_op jit(solution)/shard_map/ppermute | solution.py:15
  119.7 4.3 %fusion.40 = bf16[320,16,128]{2,0,1:T(8,128)(2,1)S(1)} fusion(bf16[320,16,128]{2,0,1:T(8,128)(2,1)S(1)} %collective-permute-done.4, bf16[320,16,128]{2,0,1:T(8,128)(2,1)S(1)} %fusion.35, f32[16,320,320]{1,2,0:T(8,128)S(1)} %get-tuple-element.21, f32[16,320]{1,0:T(8,128)S(1)} %get-tuple-element.20, pred[320,320]{0,1:T(8,128)(4,1)S(1)} %get-tuple-element.9, ...), kind=kOutput, calls=%fused_computation.46 | convolution fusion | flops 431554560 | bytes 10649601 | tf_op jit(solution)/shard_map/hqk,khd->qhd/dot_general | solution.py:113
  124.0 4.5 %collective-permute-start.6 = (bf16[320,16,128]{2,0,1:T(8,128)(2,1)S(1)}, bf16[320,16,128]{2,0,1:T(8,128)(2,1)S(1)}, u32[]{:S(2)}, u32[]{:S(2)}) collective-permute-start(bf16[320,16,128]{2,0,1:T(8,128)(2,1)S(1)} %fusion.40), channel_id=1, source_target_pairs={{0,4},{4,8},{8,12},{1,5},{5,9},{9,13},{2,6},{6,10},{10,14},{3,7},{... | collective-permute-start | bytes 3932168 | tf_op jit(solution)/shard_map/ppermute | solution.py:15
  128.5 2.0 %fusion.7 = f32[16,320]{1,0:T(8,128)S(1)} fusion(f32[16,320,320]{1,2,0:T(8,128)S(1)} %get-tuple-element.19, f32[16,320]{1,0:T(8,128)S(1)} %get-tuple-element.18, pred[320,320]{0,1:T(8,128)(4,1)S(1)} %get-tuple-element.11), kind=kLoop, calls=%fused_computation.14 | loop fusion | flops 8186880 | bytes 6696960 | tf_op jit(solution)/shard_map/reduce_sum | solution.py:92
  130.6 3.4 %collective-permute-start.7 = (f32[2,16,320]{2,1,0:T(8,128)S(1)}, f32[2,16,320]{2,1,0:T(8,128)S(1)}, u32[]{:S(2)}, u32[]{:S(2)}) collective-permute-start(f32[2,16,320]{2,1,0:T(8,128)S(1)} %pad_maximum_fusion.2), channel_id=1, source_target_pairs={{0,4},{4,8},{8,12},{1,5},{5,9},{9,13},{2,6},{6,10},{10,14},{3,7},{... | collective-permute-start | bytes 122888 | tf_op jit(solution)/shard_map/ppermute | solution.py:15
  134.0 1.3 copy_bitcast_fusion.1
  135.2 19.5 %collective-permute-done.7 = f32[2,16,320]{2,1,0:T(8,128)S(1)} collective-permute-done((f32[2,16,320]{2,1,0:T(8,128)S(1)}, f32[2,16,320]{2,1,0:T(8,128)S(1)}, u32[]{:S(2)}, u32[]{:S(2)}) %collective-permute-start.7) | collective-permute-done | bytes 40992 | tf_op jit(solution)/shard_map/ppermute | solution.py:15
  154.8 4.9 %fusion.71 = bf16[16,40,8,128]{3,2,1,0:T(8,128)(2,1)S(1)} fusion(f32[320,16]{0,1:T(8,128)S(1)} %get-tuple-element.5, f32[320,16]{0,1:T(8,128)S(1)} %get-tuple-element.6, f32[320,16]{0,1:T(8,128)S(1)} %get-tuple-element.4, bf16[320,16,128]{2,0,1:T(8,128)(2,1)S(1)} %collective-permute-done.6, pred[]{:T(512)S(6)} %ge.28, ...), kind=kOutput, calls=%fused_computation.78 | convolution fusion | flops 432209920 | bytes 10670081 | tf_op jit(solution)/shard_map/hqk,khd->qhd/dot_general | solution.py:113
  159.7 1.4 copy.124
  (32 shorter events, 4.0 us)
Async XLA Ops:
  0.6 79.7 %copy-start = (bf16[320,2048]{1,0:T(8,128)(2,1)S(1)}, bf16[320,2048]{1,0:T(8,128)(2,1)}, u32[]{:S(2)}) copy-start(bf16[320,2048]{1,0:T(8,128)(2,1)} %param.14) | copy-start | bytes 3932164
  0.6 3.7 %copy-start.5 = (s32[320]{0:T(512)S(1)}, s32[320]{0:T(512)}, u32[]{:S(2)}) copy-start(s32[320]{0:T(512)} %param.15) | copy-start | bytes 3844
  3.0 35.6 %collective-permute-start.2 = (bf16[320,2176]{1,0:T(8,128)(2,1)S(1)}, bf16[320,2176]{1,0:T(8,128)(2,1)}, u32[]{:S(2)}, u32[]{:S(2)}) collective-permute-start(bf16[320,2176]{1,0:T(8,128)(2,1)S(1)} %pad_maximum_fusion), channel_id=1, source_target_pairs={{4,0},{8,4},{12,8},{5,1},{9,5},{13,9},{6,2},{10,6},{14,10},{7,3},{... | collective-permute-start | bytes 4177928 | tf_op jit(solution)/shard_map/ppermute | solution.py:19
  6.9 33.0 %copy-start.6 = (bf16[2048]{0:T(1024)(128)(2,1)S(1)}, bf16[2048]{0:T(1024)(128)(2,1)}, u32[]{:S(2)}) copy-start(bf16[2048]{0:T(1024)(128)(2,1)} %param.11) | copy-start | bytes 12292
  9.5 30.4 %collective-permute-start = (bf16[2056,128]{1,0:T(8,128)(2,1)S(1)}, bf16[2056,128]{1,0:T(8,128)(2,1)}, u32[]{:S(2)}, u32[]{:S(2)}) collective-permute-start(bf16[2056,128]{1,0:T(8,128)(2,1)S(1)} %concatenate.6), channel_id=1, source_target_pairs={{0,4},{4,8},{8,12},{1,5},{5,9},{9,13},{2,6},{6,10},{10,14},{3,7},{... | collective-permute-start | bytes 1579016 | tf_op jit(solution)/shard_map/ppermute | solution.py:15
  15.9 26.5 %collective-permute-start.1 = (bf16[2056,128]{1,0:T(8,128)(2,1)S(1)}, bf16[2056,128]{1,0:T(8,128)(2,1)}, u32[]{:S(2)}, u32[]{:S(2)}) collective-permute-start(bf16[2056,128]{1,0:T(8,128)(2,1)S(1)} %concatenate.6), channel_id=1, source_target_pairs={{0,8},{4,12},{1,9},{5,13},{2,10},{6,14},{3,11},{7,15},{16,24},{20,... | collective-permute-start | bytes 1579016 | tf_op jit(solution)/shard_map/ppermute | solution.py:15
  38.6 33.9 %collective-permute-start.3 = (bf16[320,2176]{1,0:T(8,128)(2,1)}, bf16[320,2176]{1,0:T(8,128)(2,1)}, u32[]{:S(2)}, u32[]{:S(2)}) collective-permute-start(bf16[320,2176]{1,0:T(8,128)(2,1)} %collective-permute-done.2), channel_id=1, source_target_pairs={{4,0},{8,4},{12,8},{5,1},{9,5},{13,9},{6,2},{10,6},{14,10},{7,3},{... | collective-permute-start | bytes 4177928 | tf_op jit(solution)/shard_map/ppermute | solution.py:19
  46.3 27.5 %copy-start.4 = (bf16[320,2048]{1,0:T(8,128)(2,1)S(1)}, bf16[320,2048]{1,0:T(8,128)(2,1)}, u32[]{:S(2)}) copy-start(bf16[320,2048]{1,0:T(8,128)(2,1)} %param.8) | copy-start | bytes 3932164
  83.3 2.0 %copy-start.1 = (f32[320,16,128]{2,0,1:T(8,128)S(1)}, f32[320,16,128]{2,0,1:T(8,128)}, u32[]{:S(2)}) copy-start(f32[320,16,128]{2,0,1:T(8,128)} %get-tuple-element.17) | copy-start | bytes 7864324
  83.3 2.1 %copy-start.2 = (bf16[320,2048]{1,0:T(8,128)(2,1)S(1)}, bf16[320,2048]{1,0:T(8,128)(2,1)}, u32[]{:S(2)}) copy-start(bf16[320,2048]{1,0:T(8,128)(2,1)} %param.12) | copy-start | bytes 3932164
  89.1 30.6 %collective-permute-start.4 = (bf16[320,16,128]{2,0,1:T(8,128)(2,1)S(1)}, bf16[320,16,128]{2,0,1:T(8,128)(2,1)S(1)}, u32[]{:S(2)}, u32[]{:S(2)}) collective-permute-start(bf16[320,16,128]{2,0,1:T(8,128)(2,1)S(1)} %fusion.46), channel_id=1, source_target_pairs={{0,4},{4,8},{8,12},{1,5},{5,9},{9,13},{2,6},{6,10},{10,14},{3,7},{... | collective-permute-start | bytes 3932168 | tf_op jit(solution)/shard_map/ppermute | solution.py:15
  92.5 27.2 %collective-permute-start.5 = (f32[2,16,320]{2,1,0:T(8,128)S(1)}, f32[2,16,320]{2,1,0:T(8,128)S(1)}, u32[]{:S(2)}, u32[]{:S(2)}) collective-permute-start(f32[2,16,320]{2,1,0:T(8,128)S(1)} %pad_maximum_fusion.1), channel_id=1, source_target_pairs={{0,4},{4,8},{8,12},{1,5},{5,9},{9,13},{2,6},{6,10},{10,14},{3,7},{... | collective-permute-start | bytes 122888 | tf_op jit(solution)/shard_map/ppermute | solution.py:15
  99.0 2.0 %copy-start.3 = (bf16[320,2048]{1,0:T(8,128)(2,1)S(1)}, bf16[320,2048]{1,0:T(8,128)(2,1)}, u32[]{:S(2)}) copy-start(bf16[320,2048]{1,0:T(8,128)(2,1)} %param.13) | copy-start | bytes 3932164
  124.0 30.8 %collective-permute-start.6 = (bf16[320,16,128]{2,0,1:T(8,128)(2,1)S(1)}, bf16[320,16,128]{2,0,1:T(8,128)(2,1)S(1)}, u32[]{:S(2)}, u32[]{:S(2)}) collective-permute-start(bf16[320,16,128]{2,0,1:T(8,128)(2,1)S(1)} %fusion.40), channel_id=1, source_target_pairs={{0,4},{4,8},{8,12},{1,5},{5,9},{9,13},{2,6},{6,10},{10,14},{3,7},{... | collective-permute-start | bytes 3932168 | tf_op jit(solution)/shard_map/ppermute | solution.py:15
  130.6 24.2 %collective-permute-start.7 = (f32[2,16,320]{2,1,0:T(8,128)S(1)}, f32[2,16,320]{2,1,0:T(8,128)S(1)}, u32[]{:S(2)}, u32[]{:S(2)}) collective-permute-start(f32[2,16,320]{2,1,0:T(8,128)S(1)} %pad_maximum_fusion.2), channel_id=1, source_target_pairs={{0,4},{4,8},{8,12},{1,5},{5,9},{9,13},{2,6},{6,10},{10,14},{3,7},{... | collective-permute-start | bytes 122888 | tf_op jit(solution)/shard_map/ppermute | solution.py:15

commit v4 on v3

--- a/solution.py
+++ b/solution.py
@@ -73,6 +73,28 @@
     causal = positions[:, None] >= positions[None, :]
     keep_local = causal & (doc_id[:, None] == doc_id[None, :])
 
+    scores = jnp.einsum("qhd,khd->hqk", queries, key_rows, preferred_element_type=jnp.float32)
+    rounded = jnp.where(keep_local[None], scores, jnp.zeros_like(scores)).astype(jnp.bfloat16)
+    block_term = jnp.einsum("hqk,khd->qhd", rounded, value_rows, preferred_element_type=jnp.float32)
+    block_term = lax.optimization_barrier(block_term)
+    carried_term = jnp.einsum(
+        "qhd,hde->qhe", queries.astype(jnp.float32), carried, precision=lax.Precision.HIGHEST
+    )
+    carried_term = jnp.where(
+        (doc_id == first_doc)[:, None, None], carried_term, jnp.zeros_like(carried_term)
+    )
+    lin_raw = block_term + carried_term
+    mean_square = jnp.mean(lin_raw * lin_raw, axis=-1, keepdims=True)
+    gain_rows = norm_gain.astype(jnp.float32).reshape(head_count, HD)
+    gate_rows = jax.nn.sigmoid(out_gate.astype(jnp.float32).reshape(row_count, head_count, HD))
+    normed = lin_raw * lax.rsqrt(mean_square + norm_eps) * gain_rows * gate_rows
+    lin_out = normed.astype(jnp.bfloat16).reshape(row_count, head_count * HD)
+    if len(query_blocks) > 2:
+        tied = lax.optimization_barrier((lin_out, query_blocks[2:], query_docs[2:]))
+        lin_out = tied[0]
+        query_blocks = query_blocks[:2] + list(tied[1])
+        query_docs = query_docs[:2] + list(tied[2])
+    value_own = lin_out.reshape(row_count, head_count, HD)
     score_scale = 1.0 / math.sqrt(HD)
     key_soft = soft_key.reshape(row_count, head_count, HD)
     weights = []
@@ -90,23 +112,6 @@
         row_max = jnp.max(logits, axis=-1)
         probs = jnp.where(keep[None], jnp.exp(logits - row_max[..., None]), 0.0)
         weights.append((probs.astype(jnp.bfloat16), row_max, jnp.sum(probs, axis=-1)))
-
-    scores = jnp.einsum("qhd,khd->hqk", queries, key_rows, preferred_element_type=jnp.float32)
-    rounded = jnp.where(keep_local[None], scores, jnp.zeros_like(scores)).astype(jnp.bfloat16)
-    block_term = jnp.einsum("hqk,khd->qhd", rounded, value_rows, preferred_element_type=jnp.float32)
-    carried_term = jnp.einsum(
-        "qhd,hde->qhe", queries.astype(jnp.float32), carried, precision=lax.Precision.HIGHEST
-    )
-    carried_term = jnp.where(
-        (doc_id == first_doc)[:, None, None], carried_term, jnp.zeros_like(carried_term)
-    )
-    lin_raw = block_term + carried_term
-    mean_square = jnp.mean(lin_raw * lin_raw, axis=-1, keepdims=True)
-    gain_rows = norm_gain.astype(jnp.float32).reshape(head_count, HD)
-    gate_rows = jax.nn.sigmoid(out_gate.astype(jnp.float32).reshape(row_count, head_count, HD))
-    normed = lin_raw * lax.rsqrt(mean_square + norm_eps) * gain_rows * gate_rows
-    lin_out = normed.astype(jnp.bfloat16).reshape(row_count, head_count * HD)
-    value_own = lin_out.reshape(row_count, head_count, HD)
 
     def partial_out(d):
         probs, row_max, row_sum = weights[d]

time: 162 us -> 169 us (1.043)
  waiting for transfers between devices: 74.2 us -> 82.8 us
  matrix products: 32.7 us -> 30.6 us
    ppermute x6, waiting for transfers between devices: 36.5 us -> 44.8 us  [shift_up(): return lax.ppermute(x, 'seq', [(s, s + dist) for s in range(n_seq - dist)])]
    reshape x0 -> x2, other arithmetic: none -> 4.52 us  [the longest x1 3.6 us: per_device(): soft_out.astype(jnp.bfloat16).reshape(row_count, head_count * HD)]
    reshape x2 -> x0, local copies, waits for them, and re-layouts: 2.68 us -> none  [the longest x1 1.42 us: per_device(): soft_out.astype(jnp.bfloat16).reshape(row_count, head_count * HD)]
    dot_general x3, matrix products: 11.9 us -> 10.3 us  [partial_out(): jnp.einsum('hqk,khd->qhd', probs, value_own, preferred_element_type=jnp.f...]
  transfers between devices with their start and end apart: 8 -> 8, of which waited for: 4 -> 5; matrix products, arithmetic and copies ran while one was open for 15% -> 17% of each run, Pallas kernels for 0% -> 0%
where the time goes in v4:
time: 169 us; the launch traced here: 168 us
  waiting for transfers between devices  82.8 us (49%)
  matrix products  30.6 us (18%)
  starting transfers between devices  29.2 us (17%)
  other arithmetic  15.8 us (9%)
  local copies, waits for them, and re-layouts  5.41 us (3%)
  between operations  4.29 us (3%)
    ppermute x6, waiting for transfers between devices, shift_up(): return lax.ppermute(x, 'seq', [(s, s + dist) for s in range(n_seq - dist)])  44.8 us
    ppermute x2, waiting for transfers between devices, shift_down(): return lax.ppermute(x, 'seq', [(s + dist, s) for s in range(n_seq - dist)])  38 us
    ppermute x6, starting transfers between devices, shift_up(): return lax.ppermute(x, 'seq', [(s, s + dist) for s in range(n_seq - dist)])  26.5 us
    dot_general x3, matrix products, partial_out(): jnp.einsum('hqk,khd->qhd', probs, value_own, preferred_element_type=jnp.f...  10.3 us
    dot_general x3, matrix products, per_device(): jnp.einsum('qhd,khd->hqk', query_blocks[d], key_soft, preferred_element_t...  7.81 us
    reduce_sum x3, other arithmetic, per_device(): jnp.sum(probs, axis=-1)  5.98 us
    dot_general x1, matrix products, per_device(): jnp.einsum('hqk,khd->qhd', rounded, value_rows, preferred_element_type=jn...  5.9 us
    dot_general x1, matrix products, per_device(): jnp.einsum('qhd,hde->qhe', queries.astype(jnp.float32), carried, precisio...  3.95 us
  transfers between devices with their start and end apart: 8, of which 5 were waited for; matrix products, arithmetic and copies ran while one was open for 17% of the time, Pallas kernels for 0%

profile of v4, /device:TPU:0, one launch (start us, length us, event | category | flops | bytes accessed | tf_op | source)
XLA Modules:
  0.0 168.1 jit_solution(4790964919368799471)
XLA Ops:
  0.6 1.4 fusion.121
  2.7 2.0 %broadcast_compare_fusion.3 = (pred[320]{0:T(512)(128)(4,1)S(1)}, pred[320]{0:T(512)(128)(4,1)S(1)}) fusion(s32[320]{0:T(512)} %param.15, s32[]{:T(128)} %bitcast.1, s32[]{:T(128)} %bitcast.2), kind=kLoop, calls=%fused_computation.135 | loop fusion | flops 640 | bytes 1928 | tf_op jit(solution)/shard_map/eq | solution.py:84
  4.7 2.7 %fusion.75 = bf16[16,128,128]{2,1,0:T(8,128)(2,1)S(1)} fusion(pred[320]{0:T(512)(128)(4,1)S(1)} %get-tuple-element.18, bf16[320,2048]{1,0:T(8,128)(2,1)} %param.10, bf16[320,2048]{1,0:T(8,128)(2,1)} %param.9), kind=kOutput, calls=%fused_computation.82 | convolution fusion | flops 168689664 | bytes 3146048 | tf_op jit(solution)/shard_map/thd,the->hde/dot_general | solution.py:58
  7.4 6.7 %collective-permute-start.1 = (bf16[2056,128]{1,0:T(8,128)(2,1)S(1)}, bf16[2056,128]{1,0:T(8,128)(2,1)}, u32[]{:S(2)}, u32[]{:S(2)}) collective-permute-start(bf16[2056,128]{1,0:T(8,128)(2,1)S(1)} %concatenate.6), channel_id=1, source_target_pairs={{0,8},{4,12},{1,9},{5,13},{2,10},{6,14},{3,11},{7,15},{16,24},{20,... | collective-permute-start | bytes 1579016 | tf_op jit(solution)/shard_map/ppermute | solution.py:15
  14.2 4.3 %collective-permute-start = (bf16[2056,128]{1,0:T(8,128)(2,1)S(1)}, bf16[2056,128]{1,0:T(8,128)(2,1)}, u32[]{:S(2)}, u32[]{:S(2)}) collective-permute-start(bf16[2056,128]{1,0:T(8,128)(2,1)S(1)} %concatenate.6), channel_id=1, source_target_pairs={{0,4},{4,8},{8,12},{1,5},{5,9},{9,13},{2,6},{6,10},{10,14},{3,7},{... | collective-permute-start | bytes 1579016 | tf_op jit(solution)/shard_map/ppermute | solution.py:15
  18.7 1.3 collective-permute-start.2
  20.2 5.9 %fusion.43 = f32[320,16,128]{2,0,1:T(8,128)} fusion(pred[320,320]{0,1:T(8,128)(4,1)S(1)} %fusion.93, bf16[320,2048]{1,0:T(8,128)(2,1)} %param.10, bf16[320,2048]{1,0:T(8,128)(2,1)} %param.9, bf16[320,2048]{1,0:T(8,128)(2,1)} %param.8), kind=kOutput, calls=%fused_computation.50 | convolution fusion | flops 842137600 | bytes 6656000 | tf_op jit(solution)/shard_map/hqk,khd->qhd/dot_general | solution.py:78
  26.1 3.0 %fusion.2 = (f32[16,320]{1,0:T(8,128)S(1)}, f32[16,320,320]{1,2,0:T(8,128)S(1)}) fusion(pred[320,320]{0,1:T(8,128)(4,1)S(1)} %fusion.93, bf16[320,2048]{1,0:T(8,128)(2,1)} %param.13, bf16[320,2048]{1,0:T(8,128)(2,1)S(1)} %copy-done), kind=kOutput, calls=%fused_computation.9 | convolution fusion | flops 424340480 | bytes 9297920 | tf_op jit(solution)/shard_map/qhd,khd->hqk/dot_general | solution.py:106
  29.1 2.0 %fusion.7 = f32[16,320]{1,0:T(8,128)S(1)} fusion(f32[16,320,320]{1,2,0:T(8,128)S(1)} %get-tuple-element.24, f32[16,320]{1,0:T(8,128)S(1)} %get-tuple-element.23, pred[320,320]{0,1:T(8,128)(4,1)S(1)} %fusion.93), kind=kLoop, calls=%fused_computation.14 | loop fusion | flops 8186880 | bytes 6696960 | tf_op jit(solution)/shard_map/reduce_sum | solution.py:114
  32.1 1.2 slice.58
  34.6 1.3 collective-permute-done
  35.9 1.1 slice.56
  38.4 1.5 select_add_fusion
  39.8 12.6 %collective-permute-done.2 = bf16[320,2176]{1,0:T(8,128)(2,1)} collective-permute-done((bf16[320,2176]{1,0:T(8,128)(2,1)S(1)}, bf16[320,2176]{1,0:T(8,128)(2,1)}, u32[]{:S(2)}, u32[]{:S(2)}) %collective-permute-start.2) | collective-permute-done | bytes 1392672 | tf_op jit(solution)/shard_map/ppermute | solution.py:19
  52.4 1.5 collective-permute-start.3
  53.9 3.9 %multiply_reduce_fusion = (f32[320,16]{0,1:T(8,128)S(1)}, f32[320,16,128]{2,0,1:T(8,128)S(1)}) fusion(f32[320,16,128]{2,0,1:T(8,128)} %fusion.43, f32[16,128,128]{2,1,0:T(8,128)S(1)} %bitcast.215, pred[320]{0:T(512)(128)(4,1)S(1)} %get-tuple-element.17, bf16[320,2048]{1,0:T(8,128)(2,1)S(1)} %copy-done.5), kind=kOutput, calls=%fused_computation.49 | convolution fusion | flops 1009249280 | bytes 7622976 | tf_op jit(solution)/shard_map/qhd,hde->qhe/dot_general | solution.py:80
  58.8 1.1 convert_reduce_fusion
  60.0 25.5 %collective-permute-done.3 = bf16[320,2176]{1,0:T(8,128)(2,1)S(1)} collective-permute-done((bf16[320,2176]{1,0:T(8,128)(2,1)}, bf16[320,2176]{1,0:T(8,128)(2,1)S(1)}, u32[]{:S(2)}, u32[]{:S(2)}) %collective-permute-start.3) | collective-permute-done | bytes 1392672 | tf_op jit(solution)/shard_map/ppermute | solution.py:19
  86.3 1.9 %fusion = (f32[16,320]{1,0:T(8,128)S(1)}, f32[16,320,320]{1,2,0:T(8,128)S(1)}) fusion(pred[320,320]{0,1:T(8,128)(4,1)S(1)} %get-tuple-element.16, bf16[320,16,128]{2,1,0:T(8,128)(2,1)S(1)} %bitcast.216, bf16[320,2048]{1,0:T(8,128)(2,1)S(1)} %copy-done), kind=kOutput, calls=%fused_computation.7 | convolution fusion | flops 424340480 | bytes 9297920 | tf_op jit(solution)/shard_map/qhd,khd->hqk/dot_general | solution.py:106
  88.2 2.0 %fusion.3 = f32[16,320]{1,0:T(8,128)S(1)} fusion(f32[16,320,320]{1,2,0:T(8,128)S(1)} %get-tuple-element.28, f32[16,320]{1,0:T(8,128)S(1)} %get-tuple-element.27, pred[320,320]{0,1:T(8,128)(4,1)S(1)} %get-tuple-element.16), kind=kLoop, calls=%fused_computation.10 | loop fusion | flops 8186880 | bytes 6696960 | tf_op jit(solution)/shard_map/reduce_sum | solution.py:114
  90.2 3.1 %fusion.47 = bf16[320,16,128]{2,0,1:T(8,128)(2,1)S(1)} fusion(f32[16,320,320]{1,2,0:T(8,128)S(1)} %get-tuple-element.28, f32[16,320]{1,0:T(8,128)S(1)} %get-tuple-element.27, pred[320,320]{0,1:T(8,128)(4,1)S(1)} %get-tuple-element.16, bf16[320,2048]{1,0:T(8,128)(2,1)S(1)} %copy_bitcast_fusion.1), kind=kOutput, calls=%fused_computation.52 | convolution fusion | flops 428277760 | bytes 9297920 | tf_op jit(solution)/shard_map/hqk,khd->qhd/dot_general | solution.py:118
  93.2 4.5 %collective-permute-start.5 = (f32[2,16,320]{2,1,0:T(8,128)S(1)}, f32[2,16,320]{2,1,0:T(8,128)S(1)}, u32[]{:S(2)}, u32[]{:S(2)}) collective-permute-start(f32[2,16,320]{2,1,0:T(8,128)S(1)} %pad_maximum_fusion.1), channel_id=1, source_target_pairs={{0,4},{4,8},{8,12},{1,5},{5,9},{9,13},{2,6},{6,10},{10,14},{3,7},{... | collective-permute-start | bytes 122888 | tf_op jit(solution)/shard_map/ppermute | solution.py:15
  97.7 3.9 %collective-permute-start.4 = (bf16[320,16,128]{2,0,1:T(8,128)(2,1)S(1)}, bf16[320,16,128]{2,0,1:T(8,128)(2,1)S(1)}, u32[]{:S(2)}, u32[]{:S(2)}) collective-permute-start(bf16[320,16,128]{2,0,1:T(8,128)(2,1)S(1)} %fusion.47), channel_id=1, source_target_pairs={{0,4},{4,8},{8,12},{1,5},{5,9},{9,13},{2,6},{6,10},{10,14},{3,7},{... | collective-permute-start | bytes 3932168 | tf_op jit(solution)/shard_map/ppermute | solution.py:15
  101.7 2.9 %fusion.1 = (f32[16,320]{1,0:T(8,128)S(1)}, f32[16,320,320]{1,2,0:T(8,128)S(1)}) fusion(pred[320,320]{0,1:T(8,128)(4,1)S(1)} %get-tuple-element.15, bf16[320,2176]{1,0:T(8,128)(2,1)} %collective-permute-done.2, bf16[320,2048]{1,0:T(8,128)(2,1)S(1)} %copy-done), kind=kOutput, calls=%fused_computation.8 | convolution fusion | flops 424340480 | bytes 9297920 | tf_op jit(solution)/shard_map/qhd,khd->hqk/dot_general | solution.py:106
  104.7 2.0 %fusion.5 = f32[16,320]{1,0:T(8,128)S(1)} fusion(f32[16,320,320]{1,2,0:T(8,128)S(1)} %get-tuple-element.26, f32[16,320]{1,0:T(8,128)S(1)} %get-tuple-element.25, pred[320,320]{0,1:T(8,128)(4,1)S(1)} %get-tuple-element.15), kind=kLoop, calls=%fused_computation.12 | loop fusion | flops 8186880 | bytes 6696960 | tf_op jit(solution)/shard_map/reduce_sum | solution.py:114
  106.7 21.8 %collective-permute-done.4 = bf16[320,16,128]{2,0,1:T(8,128)(2,1)S(1)} collective-permute-done((bf16[320,16,128]{2,0,1:T(8,128)(2,1)S(1)}, bf16[320,16,128]{2,0,1:T(8,128)(2,1)S(1)}, u32[]{:S(2)}, u32[]{:S(2)}) %collective-permute-start.4) | collective-permute-done | bytes 1310752 | tf_op jit(solution)/shard_map/ppermute | solution.py:15
  128.5 4.4 %fusion.40 = bf16[320,16,128]{2,0,1:T(8,128)(2,1)S(1)} fusion(bf16[320,16,128]{2,0,1:T(8,128)(2,1)S(1)} %collective-permute-done.4, f32[16,320,320]{1,2,0:T(8,128)S(1)} %get-tuple-element.26, f32[16,320]{1,0:T(8,128)S(1)} %get-tuple-element.25, pred[320,320]{0,1:T(8,128)(4,1)S(1)} %get-tuple-element.15, f32[320,16]{0,1:T(8,128)S(1)} %get-tuple-element.9, ...), kind=kOutput, calls=%fused_computation.46 | convolution fusion | flops 431554560 | bytes 10649601 | tf_op jit(solution)/shard_map/hqk,khd->qhd/dot_general | solution.py:118
  132.9 4.5 %collective-permute-start.6 = (bf16[320,16,128]{2,0,1:T(8,128)(2,1)S(1)}, bf16[320,16,128]{2,0,1:T(8,128)(2,1)S(1)}, u32[]{:S(2)}, u32[]{:S(2)}) collective-permute-start(bf16[320,16,128]{2,0,1:T(8,128)(2,1)S(1)} %fusion.40), channel_id=1, source_target_pairs={{0,4},{4,8},{8,12},{1,5},{5,9},{9,13},{2,6},{6,10},{10,14},{3,7},{... | collective-permute-start | bytes 3932168 | tf_op jit(solution)/shard_map/ppermute | solution.py:15
  137.4 2.5 %collective-permute-start.7 = (f32[2,16,320]{2,1,0:T(8,128)S(1)}, f32[2,16,320]{2,1,0:T(8,128)S(1)}, u32[]{:S(2)}, u32[]{:S(2)}) collective-permute-start(f32[2,16,320]{2,1,0:T(8,128)S(1)} %pad_maximum_fusion.2), channel_id=1, source_target_pairs={{0,4},{4,8},{8,12},{1,5},{5,9},{9,13},{2,6},{6,10},{10,14},{3,7},{... | collective-permute-start | bytes 122888 | tf_op jit(solution)/shard_map/ppermute | solution.py:15
  139.9 2.8 %fusion.9 = f32[16,128,320]{1,2,0:T(8,128)S(1)} fusion(f32[16,320,320]{1,2,0:T(8,128)S(1)} %bitcast.214, f32[16,320]{1,0:T(8,128)S(1)} %get-tuple-element.23, pred[320,320]{0,1:T(8,128)(4,1)S(1)} %fusion.93, bf16[320,2048]{1,0:T(8,128)(2,1)S(1)} %copy_bitcast_fusion.1), kind=kOutput, calls=%fused_computation.16 | convolution fusion | flops 427622400 | bytes 10608640 | tf_op jit(solution)/shard_map/hqk,khd->qhd/dot_general | solution.py:118
  142.8 21.7 %collective-permute-done.7 = f32[2,16,320]{2,1,0:T(8,128)S(1)} collective-permute-done((f32[2,16,320]{2,1,0:T(8,128)S(1)}, f32[2,16,320]{2,1,0:T(8,128)S(1)}, u32[]{:S(2)}, u32[]{:S(2)}) %collective-permute-start.7) | collective-permute-done | bytes 40992 | tf_op jit(solution)/shard_map/ppermute | solution.py:15
  164.5 3.6 %copy_bitcast_fusion = bf16[320,2048]{1,0:T(8,128)(2,1)} fusion(f32[320,16]{0,1:T(8,128)S(1)} %get-tuple-element.11, f32[320,16]{0,1:T(8,128)S(1)} %get-tuple-element.12, f32[16,128,320]{1,2,0:T(8,128)S(1)} %fusion.9, f32[320,16]{0,1:T(8,128)S(1)} %get-tuple-element.10, bf16[320,16,128]{2,0,1:T(8,128)(2,1)S(1)} %collective-permute-done.6, pred[]{:T(512)S(6)} %ge.28), kind=kLoop, calls=%fused_computation.55 | loop fusion | flops 4587520 | bytes 5304321 | tf_op jit(solution)/shard_map/reshape | solution.py:141
  (41 shorter events, 3.3 us)
Async XLA Ops:
  0.6 25.4 %copy-start = (bf16[320,2048]{1,0:T(8,128)(2,1)S(1)}, bf16[320,2048]{1,0:T(8,128)(2,1)}, u32[]{:S(2)}) copy-start(bf16[320,2048]{1,0:T(8,128)(2,1)} %param.14) | copy-start | bytes 3932164
  4.7 13.8 %copy-start.6 = (s32[320]{0:T(512)S(1)}, s32[320]{0:T(512)}, u32[]{:S(2)}) copy-start(s32[320]{0:T(512)} %param.15) | copy-start | bytes 3844
  4.7 13.9 %copy-start.4 = (bf16[320,2048]{1,0:T(8,128)(2,1)S(1)}, bf16[320,2048]{1,0:T(8,128)(2,1)}, u32[]{:S(2)}) copy-start(bf16[320,2048]{1,0:T(8,128)(2,1)} %param.13) | copy-start | bytes 3932164
  7.4 24.7 %collective-permute-start.1 = (bf16[2056,128]{1,0:T(8,128)(2,1)S(1)}, bf16[2056,128]{1,0:T(8,128)(2,1)}, u32[]{:S(2)}, u32[]{:S(2)}) collective-permute-start(bf16[2056,128]{1,0:T(8,128)(2,1)S(1)} %concatenate.6), channel_id=1, source_target_pairs={{0,8},{4,12},{1,9},{5,13},{2,10},{6,14},{3,11},{7,15},{16,24},{20,... | collective-permute-start | bytes 1579016 | tf_op jit(solution)/shard_map/ppermute | solution.py:15
  14.2 21.7 %collective-permute-start = (bf16[2056,128]{1,0:T(8,128)(2,1)S(1)}, bf16[2056,128]{1,0:T(8,128)(2,1)}, u32[]{:S(2)}, u32[]{:S(2)}) collective-permute-start(bf16[2056,128]{1,0:T(8,128)(2,1)S(1)} %concatenate.6), channel_id=1, source_target_pairs={{0,4},{4,8},{8,12},{1,5},{5,9},{9,13},{2,6},{6,10},{10,14},{3,7},{... | collective-permute-start | bytes 1579016 | tf_op jit(solution)/shard_map/ppermute | solution.py:15
  18.7 33.7 %collective-permute-start.2 = (bf16[320,2176]{1,0:T(8,128)(2,1)S(1)}, bf16[320,2176]{1,0:T(8,128)(2,1)}, u32[]{:S(2)}, u32[]{:S(2)}) collective-permute-start(bf16[320,2176]{1,0:T(8,128)(2,1)S(1)} %pad_maximum_fusion), channel_id=1, source_target_pairs={{4,0},{8,4},{12,8},{5,1},{9,5},{13,9},{6,2},{10,6},{14,10},{7,3},{... | collective-permute-start | bytes 4177928 | tf_op jit(solution)/shard_map/ppermute | solution.py:19
  26.1 3.0 %copy-start.7 = (bf16[2048]{0:T(1024)(128)(2,1)S(1)}, bf16[2048]{0:T(1024)(128)(2,1)}, u32[]{:S(2)}) copy-start(bf16[2048]{0:T(1024)(128)(2,1)} %param.11) | copy-start | bytes 12292
  29.0 3.1 %copy-start.1 = (f32[16,320,320]{1,2,0:T(8,128)}, f32[16,320,320]{1,2,0:T(8,128)S(1)}, u32[]{:S(2)}) copy-start(f32[16,320,320]{1,2,0:T(8,128)S(1)} %get-tuple-element.24) | copy-start | bytes 19660804
  38.3 15.5 %copy-start.5 = (bf16[320,2048]{1,0:T(8,128)(2,1)S(1)}, bf16[320,2048]{1,0:T(8,128)(2,1)}, u32[]{:S(2)}) copy-start(bf16[320,2048]{1,0:T(8,128)(2,1)} %param.8) | copy-start | bytes 3932164
  52.4 33.0 %collective-permute-start.3 = (bf16[320,2176]{1,0:T(8,128)(2,1)}, bf16[320,2176]{1,0:T(8,128)(2,1)S(1)}, u32[]{:S(2)}, u32[]{:S(2)}) collective-permute-start(bf16[320,2176]{1,0:T(8,128)(2,1)} %collective-permute-done.2), channel_id=1, source_target_pairs={{4,0},{8,4},{12,8},{5,1},{9,5},{13,9},{6,2},{10,6},{14,10},{7,3},{... | collective-permute-start | bytes 4177928 | tf_op jit(solution)/shard_map/ppermute | solution.py:19
  53.9 4.0 %copy-start.2 = (bf16[320,2048]{1,0:T(8,128)(2,1)S(1)}, bf16[320,2048]{1,0:T(8,128)(2,1)}, u32[]{:S(2)}) copy-start(bf16[320,2048]{1,0:T(8,128)(2,1)} %param.12) | copy-start | bytes 3932164
  58.8 81.1 %copy-start.3 = (bf16[320,2048]{1,0:T(8,128)(2,1)}, bf16[320,2048]{1,0:T(8,128)(2,1)S(1)}, u32[]{:S(2)}) copy-start(bf16[320,2048]{1,0:T(8,128)(2,1)S(1)} %copy_bitcast_fusion.1) | copy-start | bytes 3932164
  93.2 13.4 %collective-permute-start.5 = (f32[2,16,320]{2,1,0:T(8,128)S(1)}, f32[2,16,320]{2,1,0:T(8,128)S(1)}, u32[]{:S(2)}, u32[]{:S(2)}) collective-permute-start(f32[2,16,320]{2,1,0:T(8,128)S(1)} %pad_maximum_fusion.1), channel_id=1, source_target_pairs={{0,4},{4,8},{8,12},{1,5},{5,9},{9,13},{2,6},{6,10},{10,14},{3,7},{... | collective-permute-start | bytes 122888 | tf_op jit(solution)/shard_map/ppermute | solution.py:15
  97.7 30.7 %collective-permute-start.4 = (bf16[320,16,128]{2,0,1:T(8,128)(2,1)S(1)}, bf16[320,16,128]{2,0,1:T(8,128)(2,1)S(1)}, u32[]{:S(2)}, u32[]{:S(2)}) collective-permute-start(bf16[320,16,128]{2,0,1:T(8,128)(2,1)S(1)} %fusion.47), channel_id=1, source_target_pairs={{0,4},{4,8},{8,12},{1,5},{5,9},{9,13},{2,6},{6,10},{10,14},{3,7},{... | collective-permute-start | bytes 3932168 | tf_op jit(solution)/shard_map/ppermute | solution.py:15
  104.7 35.3 %slice-start = ((s8[7864320]{0:T(1024)(128)(4,1)}), s8[4194304]{0:T(1024)(128)(4,1)S(1)}, s32[]{:S(2)}) async-start(s8[7864320]{0:T(1024)(128)(4,1)} %bitcast.213), calls=%async_computation | async-start | bytes 8388608
  128.5 11.5 %slice-start.1 = ((s8[7864320]{0:T(1024)(128)(4,1)}), s8[3670016]{0:T(1024)(128)(4,1)S(1)}, s32[]{:S(2)}) async-start(s8[7864320]{0:T(1024)(128)(4,1)} %bitcast.213), calls=%async_computation.1 | async-start | bytes 7340032
  132.9 31.6 %collective-permute-start.6 = (bf16[320,16,128]{2,0,1:T(8,128)(2,1)S(1)}, bf16[320,16,128]{2,0,1:T(8,128)(2,1)S(1)}, u32[]{:S(2)}, u32[]{:S(2)}) collective-permute-start(bf16[320,16,128]{2,0,1:T(8,128)(2,1)S(1)} %fusion.40), channel_id=1, source_target_pairs={{0,4},{4,8},{8,12},{1,5},{5,9},{9,13},{2,6},{6,10},{10,14},{3,7},{... | collective-permute-start | bytes 3932168 | tf_op jit(solution)/shard_map/ppermute | solution.py:15
  137.4 27.1 %collective-permute-start.7 = (f32[2,16,320]{2,1,0:T(8,128)S(1)}, f32[2,16,320]{2,1,0:T(8,128)S(1)}, u32[]{:S(2)}, u32[]{:S(2)}) collective-permute-start(f32[2,16,320]{2,1,0:T(8,128)S(1)} %pad_maximum_fusion.2), channel_id=1, source_target_pairs={{0,4},{4,8},{8,12},{1,5},{5,9},{9,13},{2,6},{6,10},{10,14},{3,7},{... | collective-permute-start | bytes 122888 | tf_op jit(solution)/shard_map/ppermute | solution.py:15

commit v5 on v3

v5 whole, which is shorter than its diff:
```python
import math

import jax
import jax.numpy as jnp
from jax import lax
from jax.sharding import PartitionSpec as P

HD = 128


norm_eps = 1e-06


def shift_up(x, dist, n_seq):
    return lax.ppermute(x, "seq", [(s, s + dist) for s in range(n_seq - dist)])


def shift_down(x, dist, n_seq):
    return lax.ppermute(x, "seq", [(s + dist, s) for s in range(n_seq - dist)])


def merge(part_a, part_b):
    out_a, max_a, sum_a = part_a
    out_b, max_b, sum_b = part_b
    top = jnp.maximum(max_a, max_b)
    scale_a = jnp.exp(max_a - top)
    scale_b = jnp.exp(max_b - top)
    out = out_a * jnp.transpose(scale_a)[:, :, None] + out_b * jnp.transpose(scale_b)[:, :, None]
    return out, top, sum_a * scale_a + sum_b * scale_b


def per_device(lin_query, lin_key, lin_value, norm_gain, out_gate, soft_query, soft_key, doc_id):
    row_count = lin_query.shape[0]
    head_count = lin_query.shape[1] // HD
    n_seq = lax.axis_size("seq")
    my_index = lax.axis_index("seq")
    max_doc = n_seq * row_count // 2
    reach = min(n_seq - 1, (max_doc + row_count - 2) // row_count)
    dists = list(range(1, reach + 1))
    width = head_count * HD

    queries = lin_query.reshape(row_count, head_count, HD)
    key_rows = lin_key.reshape(row_count, head_count, HD)
    value_rows = lin_value.reshape(row_count, head_count, HD)
    first_doc = doc_id[0]
    last_doc = doc_id[-1]

    doc_cols = jnp.broadcast_to(doc_id.astype(jnp.bfloat16)[:, None], (row_count, HD))

    tail_keys = jnp.where((doc_id == last_doc)[:, None, None], key_rows, jnp.zeros_like(key_rows))
    local_state = jnp.einsum(
        "thd,the->hde", tail_keys, value_rows, preferred_element_type=jnp.float32
    )
    state_rows = local_state.astype(jnp.bfloat16).reshape(width, HD)
    tag_rows = jnp.full((8, HD), last_doc, jnp.int32).astype(jnp.bfloat16)
    state_msg = jnp.concatenate([state_rows, tag_rows], axis=0)
    carried = jnp.zeros_like(local_state)
    for d in dists:
        msg_in = shift_up(state_msg, d, n_seq)
        state_in = msg_in[:width].reshape(head_count, HD, HD).astype(jnp.float32)
        tag_in = msg_in[width, 0].astype(jnp.int32)
        wanted = (my_index >= d) & (tag_in == first_doc)
        carried = carried + jnp.where(wanted, state_in, jnp.zeros_like(state_in))

    next_msg = shift_down(jnp.concatenate([soft_query, doc_cols], axis=1), 1, n_seq)
    next_queries = next_msg[:, :width].reshape(row_count, head_count, HD)
    next_docs = next_msg[:, width].astype(jnp.int32)
    key_msgs = [jnp.concatenate([soft_key, doc_cols], axis=1)]
    for d in dists[:-1]:
        key_msgs.append(shift_up(key_msgs[-1], 1, n_seq))
    key_blocks = [m[:, :width].reshape(row_count, head_count, HD) for m in key_msgs]
    key_docs = [m[:, width].astype(jnp.int32) for m in key_msgs]

    positions = jnp.arange(row_count, dtype=jnp.int32)
    causal = positions[:, None] >= positions[None, :]
    keep_local = causal & (doc_id[:, None] == doc_id[None, :])
    score_scale = 1.0 / math.sqrt(HD)

    def weights_of(query_rows, keep):
        logits = (
            jnp.einsum("qhd,khd->hqk", query_rows, key_all, preferred_element_type=jnp.float32)
            * score_scale
        )
        logits = jnp.where(keep[None], logits, -1e30)
        row_max = jnp.max(logits, axis=-1)
        probs = jnp.where(keep[None], jnp.exp(logits - row_max[..., None]), 0.0)
        return probs.astype(jnp.bfloat16), row_max, jnp.sum(probs, axis=-1)

    key_all = key_blocks[0]
    diag = weights_of(soft_query.reshape(row_count, head_count, HD), keep_local)
    key_all = jnp.concatenate(key_blocks, axis=0)
    valid = jnp.concatenate(
        [jnp.full((row_count,), my_index >= d, jnp.bool_) for d in range(len(key_blocks))]
    )
    keep_next = (next_docs[:, None] == jnp.concatenate(key_docs)[None, :]) & valid[None, :]
    ahead = weights_of(next_queries, keep_next)

    scores = jnp.einsum("qhd,khd->hqk", queries, key_rows, preferred_element_type=jnp.float32)
    rounded = jnp.where(keep_local[None], scores, jnp.zeros_like(scores)).astype(jnp.bfloat16)
    block_term = jnp.einsum("hqk,khd->qhd", rounded, value_rows, preferred_element_type=jnp.float32)
    carried_term = jnp.einsum(
        "qhd,hde->qhe", queries.astype(jnp.float32), carried, precision=lax.Precision.HIGHEST
    )
    carried_term = jnp.where(
        (doc_id == first_doc)[:, None, None], carried_term, jnp.zeros_like(carried_term)
    )
    lin_raw = block_term + carried_term
    mean_square = jnp.mean(lin_raw * lin_raw, axis=-1, keepdims=True)
    gain_rows = norm_gain.astype(jnp.float32).reshape(head_count, HD)
    gate_rows = jax.nn.sigmoid(out_gate.astype(jnp.float32).reshape(row_count, head_count, HD))
    normed = lin_raw * lax.rsqrt(mean_square + norm_eps) * gain_rows * gate_rows
    lin_out = normed.astype(jnp.bfloat16).reshape(row_count, width)

    value_blocks = [lin_out.reshape(row_count, head_count, HD)]
    for d in dists[:-1]:
        value_blocks.append(shift_up(value_blocks[-1], 1, n_seq))

    probs, ahead_max, ahead_sum = ahead
    ahead_out = jnp.zeros((row_count, head_count, HD), jnp.float32)
    for d, value_block in enumerate(value_blocks):
        ahead_out = ahead_out + jnp.einsum(
            "hqk,khd->qhd",
            probs[:, :, d * row_count : (d + 1) * row_count],
            value_block,
            preferred_element_type=jnp.float32,
        )
    out_in = shift_up(ahead_out.astype(jnp.bfloat16), 1, n_seq)
    stats_in = shift_up(jnp.stack([ahead_max, ahead_sum]), 1, n_seq)
    has_source = my_index >= 1
    max_in = jnp.where(has_source, stats_in[0], -1e30)
    sum_in = jnp.where(has_source, stats_in[1], 0.0)
    out_in = jnp.where(has_source, out_in.astype(jnp.float32), 0.0)

    diag_probs, diag_max, diag_sum = diag
    diag_out = jnp.einsum(
        "hqk,khd->qhd", diag_probs, value_blocks[0], preferred_element_type=jnp.float32
    )
    mixed, row_max, row_sum = merge((out_in, max_in, sum_in), (diag_out, diag_max, diag_sum))
    soft_out = mixed / jnp.transpose(row_sum)[:, :, None]
    return (lin_out, soft_out.astype(jnp.bfloat16).reshape(row_count, width))


def solution(mesh):
    return jax.shard_map(
        per_device,
        mesh=mesh,
        in_specs=(
            P(("grp", "seq"), "head"),
            P(("grp", "seq"), "head"),
            P(("grp", "seq"), "head"),
            P("head"),
            P(("grp", "seq"), "head"),
            P(("grp", "seq"), "head"),
            P(("grp", "seq"), "head"),
            P(("grp", "seq")),
        ),
        out_specs=(P(("grp", "seq"), "head"), P(("grp", "seq"), "head")),
        check_vma=False,
    )
```

time: 162 us -> 145 us (0.90)
  waiting for transfers between devices: 74.2 us -> 34.5 us
  starting transfers between devices: 29.8 us -> 48.2 us
  local copies, waits for them, and re-layouts: 5.91 us -> 10.9 us
  matrix products: 32.7 us -> 29.7 us
  other arithmetic: 14.3 us -> 16 us
    ppermute x2 -> x1, waiting for transfers between devices: 37.7 us -> 0.01 us  [shift_down(): return lax.ppermute(x, 'seq', [(s + dist, s) for s in range(n_seq - dist)])]
    ppermute x6, starting transfers between devices: 27.2 us -> 47 us  [shift_up(): return lax.ppermute(x, 'seq', [(s, s + dist) for s in range(n_seq - dist)])]
    reshape x2 -> x4, local copies, waits for them, and re-layouts: 2.68 us -> 5.83 us  [the longest x2 3.15 us: per_device(): m[:, :width].reshape(row_count, head_count, HD)]
    ppermute x6, waiting for transfers between devices: 36.5 us -> 34.5 us  [shift_up(): return lax.ppermute(x, 'seq', [(s, s + dist) for s in range(n_seq - dist)])]
    dot_general x6 -> x5, matrix products: 19.5 us -> 17.6 us  [the longest x2 10.1 us: weights_of(): jnp.einsum('qhd,khd->hqk', query_rows, key_all, preferred_element_type=jn...]
    slice x2 -> x3, local copies, waits for them, and re-layouts: 2.38 us -> 3.49 us  [the longest x2 2.49 us: per_device(): tag_in = msg_in[width, 0].astype(jnp.int32)]
    reduce_sum x3 -> x2, other arithmetic: 6.02 us -> 7.07 us  [weights_of(): return (probs.astype(jnp.bfloat16), row_max, jnp.sum(probs, axis=-1))]
  transfers between devices with their start and end apart: 8 -> 7, of which waited for: 4 -> 3; matrix products, arithmetic and copies ran while one was open for 15% -> 30% of each run, Pallas kernels for 0% -> 0%
where the time goes in v5:
time: 145 us; the launch traced here: 144 us
  starting transfers between devices  48.2 us (33%)
  waiting for transfers between devices  34.5 us (24%)
  matrix products  29.7 us (20%)
  other arithmetic  16 us (11%)
  local copies, waits for them, and re-layouts  10.9 us (8%)
  between operations  4.29 us (3%)
    ppermute x6, starting transfers between devices, shift_up(): return lax.ppermute(x, 'seq', [(s, s + dist) for s in range(n_seq - dist)])  47 us
    ppermute x6, waiting for transfers between devices, shift_up(): return lax.ppermute(x, 'seq', [(s, s + dist) for s in range(n_seq - dist)])  34.5 us
    dot_general x2, matrix products, weights_of(): jnp.einsum('qhd,khd->hqk', query_rows, key_all, preferred_element_type=jn...  10.1 us
    reduce_sum x2, other arithmetic, weights_of(): return (probs.astype(jnp.bfloat16), row_max, jnp.sum(probs, axis=-1))  7.07 us
    dot_general x1, matrix products, per_device(): jnp.einsum('hqk,khd->qhd', rounded, value_rows, preferred_element_type=jn...  6.55 us
    dot_general x1, matrix products, per_device(): jnp.einsum('hqk,khd->qhd', diag_probs, value_blocks[0], preferred_element...  4.78 us
    reshape x2, local copies, waits for them, and re-layouts, per_device(): m[:, :width].reshape(row_count, head_count, HD)  3.15 us
  transfers between devices with their start and end apart: 7, of which 3 were waited for; matrix products, arithmetic and copies ran while one was open for 30% of the time, Pallas kernels for 0%

profile of v5, /device:TPU:0, one launch (start us, length us, event | category | flops | bytes accessed | tf_op | source)
XLA Modules:
  0.0 143.6 jit_solution(6864918676680641831)
XLA Ops:
  0.6 1.4 fusion.83
  2.7 2.0 %broadcast_compare_fusion.1 = (pred[320]{0:T(512)(128)(4,1)S(1)}, pred[320]{0:T(512)(128)(4,1)S(1)}) fusion(s32[320]{0:T(512)} %param.15, s32[]{:T(128)} %bitcast.1, s32[]{:T(128)} %bitcast.2), kind=kLoop, calls=%fused_computation.95 | loop fusion | flops 640 | bytes 1928 | tf_op jit(solution)/shard_map/eq | solution.py:105
  4.7 2.7 %fusion.55 = bf16[16,128,128]{2,1,0:T(8,128)(2,1)S(1)} fusion(pred[320]{0:T(512)(128)(4,1)S(1)} %get-tuple-element.10, bf16[320,2048]{1,0:T(8,128)(2,1)} %param.10, bf16[320,2048]{1,0:T(8,128)(2,1)} %param.9), kind=kOutput, calls=%fused_computation.63 | convolution fusion | flops 168689664 | bytes 3146048 | tf_op jit(solution)/shard_map/thd,the->hde/dot_general | solution.py:51
  7.5 5.8 %collective-permute-start = (bf16[2056,128]{1,0:T(8,128)(2,1)S(1)}, bf16[2056,128]{1,0:T(8,128)(2,1)}, u32[]{:S(2)}, u32[]{:S(2)}) collective-permute-start(bf16[2056,128]{1,0:T(8,128)(2,1)S(1)} %concatenate.21), channel_id=1, source_target_pairs={{0,4},{4,8},{8,12},{1,5},{5,9},{9,13},{2,6},{6,10},{10,14},{3,7},{... | collective-permute-start | bytes 1579016 | tf_op jit(solution)/shard_map/ppermute | solution.py:15
  13.2 4.5 %collective-permute-start.1 = (bf16[2056,128]{1,0:T(8,128)(2,1)S(1)}, bf16[2056,128]{1,0:T(8,128)(2,1)}, u32[]{:S(2)}, u32[]{:S(2)}) collective-permute-start(bf16[2056,128]{1,0:T(8,128)(2,1)S(1)} %concatenate.21), channel_id=1, source_target_pairs={{0,8},{4,12},{1,9},{5,13},{2,10},{6,14},{3,11},{7,15},{16,24},{20,... | collective-permute-start | bytes 1579016 | tf_op jit(solution)/shard_map/ppermute | solution.py:15
  17.9 1.9 %pad_maximum_fusion.1 = (bf16[320,2176]{1,0:T(8,128)(2,1)}, bf16[320,2176]{1,0:T(8,128)(2,1)}) fusion(bf16[320,128]{1,0:T(8,128)(2,1)S(1)} %broadcast_in_dim.113, bf16[320,2048]{1,0:T(8,128)(2,1)S(1)} %copy-done.4, bf16[320,2048]{1,0:T(8,128)(2,1)S(1)} %copy-done.1), kind=kLoop, calls=%fused_computation.40 | loop fusion | flops 4874240 | bytes 5488640 | tf_op jit(solution)/shard_map/concatenate | solution.py:65
  19.8 2.5 %collective-permute-start.3 = (bf16[320,2176]{1,0:T(8,128)(2,1)}, bf16[320,2176]{1,0:T(8,128)(2,1)}, u32[]{:S(2)}, u32[]{:S(2)}) collective-permute-start(bf16[320,2176]{1,0:T(8,128)(2,1)} %get-tuple-element.5), channel_id=1, source_target_pairs={{0,4},{4,8},{8,12},{1,5},{5,9},{9,13},{2,6},{6,10},{10,14},{3,7},{... | collective-permute-start | bytes 4177928 | tf_op jit(solution)/shard_map/ppermute | solution.py:15
  22.3 1.3 collective-permute-start.2
  23.6 1.4 copy_bitcast_fusion.3
  25.2 6.0 %fusion.3 = (f32[16,320]{1,0:T(8,128)S(1)}, f32[16,320,320]{1,2,0:T(8,128)}) fusion(pred[320,320]{0,1:T(8,128)(4,1)S(1)} %fusion.67, bf16[320,2048]{1,0:T(8,128)(2,1)} %param.13, bf16[320,2048]{1,0:T(8,128)(2,1)S(1)} %copy-done.1), kind=kOutput, calls=%fused_computation.8 | convolution fusion | flops 424340480 | bytes 9297920 | tf_op jit(solution)/shard_map/qhd,khd->hqk/dot_general | solution.py:81
  31.2 1.2 slice.57
  33.7 2.3 %collective-permute-done.1 = bf16[2056,128]{1,0:T(8,128)(2,1)} collective-permute-done((bf16[2056,128]{1,0:T(8,128)(2,1)S(1)}, bf16[2056,128]{1,0:T(8,128)(2,1)}, u32[]{:S(2)}, u32[]{:S(2)}) %collective-permute-start.1) | collective-permute-done | bytes 526368 | tf_op jit(solution)/shard_map/ppermute | solution.py:15
  36.1 1.3 slice.59
  38.7 1.4 select_add_fusion
  40.1 2.8 %fusion.52 = f32[16,128,320]{1,2,0:T(8,128)} fusion(f32[16,128,128]{2,1,0:T(8,128)S(1)} %bitcast.164, bf16[320,2048]{1,0:T(8,128)(2,1)S(1)} %copy-done), kind=kOutput, calls=%fused_computation.58 | convolution fusion | flops 1006632960 | bytes 4980736 | tf_op jit(solution)/shard_map/qhd,hde->qhe/dot_general | solution.py:101
  42.9 6.6 %multiply_reduce_fusion = (f32[320,16]{0,1:T(8,128)S(1)}, f32[320,16,128]{2,0,1:T(8,128)}) fusion(f32[16,128,320]{1,2,0:T(8,128)} %fusion.52, pred[320]{0:T(512)(128)(4,1)S(1)} %get-tuple-element.9, pred[320,320]{0,1:T(8,128)(4,1)S(1)} %fusion.67, bf16[320,2048]{1,0:T(8,128)(2,1)} %param.10, bf16[320,2048]{1,0:T(8,128)(2,1)} %param.9, ...), kind=kOutput, calls=%fused_computation.38 | convolution fusion | flops 844753920 | bytes 9298240 | tf_op jit(solution)/shard_map/hqk,khd->qhd/dot_general | solution.py:100
  49.4 2.2 %fusion.22 = bf16[320,16,128]{2,0,1:T(8,128)(2,1)S(1)} fusion(f32[320,16,128]{2,0,1:T(8,128)} %get-tuple-element.14, f32[16,128]{1,0:T(8,128)S(1)} %bitcast_convert_fusion, f32[320,16]{0,1:T(8,128)S(1)} %add_rsqrt_fusion, bf16[320,2048]{1,0:T(8,128)(2,1)S(1)} %copy-done.2), kind=kLoop, calls=%fused_computation.26 | loop fusion | flops 5242880 | bytes 5271552 | tf_op jit(solution)/shard_map/convert_element_type | solution.py:112
  51.7 15.0 %collective-permute-start.4 = (bf16[320,16,128]{2,0,1:T(8,128)(2,1)S(1)}, bf16[320,16,128]{2,0,1:T(8,128)(2,1)S(1)}, u32[]{:S(2)}, u32[]{:S(2)}) collective-permute-start(bf16[320,16,128]{2,0,1:T(8,128)(2,1)S(1)} %fusion.22), channel_id=1, source_target_pairs={{0,4},{4,8},{8,12},{1,5},{5,9},{9,13},{2,6},{6,10},{10,14},{3,7},{... | collective-permute-start | bytes 3932168 | tf_op jit(solution)/shard_map/ppermute | solution.py:15
  67.8 1.0 convert_reduce_fusion
  69.1 1.8 %copy_bitcast_fusion.2 = bf16[320,16,128]{2,0,1:T(8,128)(2,1)S(1)} fusion(bf16[320,2176]{1,0:T(8,128)(2,1)} %collective-permute-done.3), kind=kLoop, calls=%fused_computation.48 | loop fusion | bytes 2621440 | tf_op jit(solution)/shard_map/reshape | solution.py:71
  70.8 4.1 %fusion = (f32[16,320]{1,0:T(8,128)S(1)}, f32[16,320,640]{2,1,0:T(8,128)S(1)}) fusion(pred[320,640]{1,0:T(8,128)(4,1)S(1)} %compare_and_fusion, bf16[320,16,128]{2,0,1:T(8,128)(2,1)S(1)} %copy_bitcast_fusion.2, bf16[320,16,128]{2,0,1:T(8,128)(2,1)S(1)} %copy-done.3, bf16[320,2176]{1,0:T(8,128)(2,1)} %collective-permute-done.2), kind=kOutput, calls=%fused_computation.2 | convolution fusion | flops 853928960 | bytes 17264640 | tf_op jit(solution)/shard_map/qhd,khd->hqk/dot_general | solution.py:81
  75.0 5.1 %fusion.1 = (f32[16,320]{1,0:T(8,128)S(1)}, bf16[16,320,640]{2,1,0:T(8,128)(2,1)S(1)}) fusion(f32[16,320,640]{2,1,0:T(8,128)S(1)} %get-tuple-element.18, f32[16,320]{1,0:T(8,128)S(1)} %get-tuple-element.17, pred[320,640]{1,0:T(8,128)(4,1)S(1)} %compare_and_fusion), kind=kLoop, calls=%fused_computation.3 | loop fusion | flops 19655680 | bytes 19906560 | tf_op jit(solution)/shard_map/reduce_sum | solution.py:87
  80.0 1.2 fusion.11
  81.3 11.6 %collective-permute-done.4 = bf16[320,16,128]{2,0,1:T(8,128)(2,1)S(1)} collective-permute-done((bf16[320,16,128]{2,0,1:T(8,128)(2,1)S(1)}, bf16[320,16,128]{2,0,1:T(8,128)(2,1)S(1)}, u32[]{:S(2)}, u32[]{:S(2)}) %collective-permute-start.4) | collective-permute-done | bytes 1310752 | tf_op jit(solution)/shard_map/ppermute | solution.py:15
  92.9 1.5 %fusion.34 = bf16[320,16,128]{2,0,1:T(8,128)(2,1)S(1)} fusion(f32[16,128,320]{1,2,0:T(8,128)S(1)} %fusion.11, bf16[320,16,128]{2,0,1:T(8,128)(2,1)S(1)} %collective-permute-done.4, bf16[16,320,640]{2,1,0:T(8,128)(2,1)S(1)} %get-tuple-element.3), kind=kOutput, calls=%fused_computation.41 | convolution fusion | flops 420741120 | bytes 9175040 | tf_op jit(solution)/shard_map/hqk,khd->qhd/dot_general | solution.py:121
  94.4 14.8 %collective-permute-start.5 = (bf16[320,16,128]{2,0,1:T(8,128)(2,1)S(1)}, bf16[320,16,128]{2,0,1:T(8,128)(2,1)S(1)}, u32[]{:S(2)}, u32[]{:S(2)}) collective-permute-start(bf16[320,16,128]{2,0,1:T(8,128)(2,1)S(1)} %fusion.34), channel_id=1, source_target_pairs={{0,4},{4,8},{8,12},{1,5},{5,9},{9,13},{2,6},{6,10},{10,14},{3,7},{... | collective-permute-start | bytes 3932168 | tf_op jit(solution)/shard_map/ppermute | solution.py:15
  109.3 2.0 %fusion.4 = f32[16,320]{1,0:T(8,128)S(1)} fusion(f32[16,320,320]{1,2,0:T(8,128)S(1)} %bitcast.163, f32[16,320]{1,0:T(8,128)S(1)} %get-tuple-element.15, pred[320,320]{0,1:T(8,128)(4,1)S(1)} %fusion.67), kind=kLoop, calls=%fused_computation.9 | loop fusion | flops 8186880 | bytes 6696960 | tf_op jit(solution)/shard_map/reduce_sum | solution.py:87
  111.3 4.3 %collective-permute-start.6 = (f32[2,16,320]{2,1,0:T(8,128)S(1)}, f32[2,16,320]{2,1,0:T(8,128)S(1)}, u32[]{:S(2)}, u32[]{:S(2)}) collective-permute-start(f32[2,16,320]{2,1,0:T(8,128)S(1)} %pad_maximum_fusion.2), channel_id=1, source_target_pairs={{0,4},{4,8},{8,12},{1,5},{5,9},{9,13},{2,6},{6,10},{10,14},{3,7},{... | collective-permute-start | bytes 122888 | tf_op jit(solution)/shard_map/ppermute | solution.py:15
  115.6 1.3 copy_bitcast_fusion.1
  116.9 20.5 %collective-permute-done.6 = f32[2,16,320]{2,1,0:T(8,128)S(1)} collective-permute-done((f32[2,16,320]{2,1,0:T(8,128)S(1)}, f32[2,16,320]{2,1,0:T(8,128)S(1)}, u32[]{:S(2)}, u32[]{:S(2)}) %collective-permute-start.6) | collective-permute-done | bytes 40992 | tf_op jit(solution)/shard_map/ppermute | solution.py:15
  137.4 4.8 %fusion.37 = bf16[16,40,8,128]{3,2,1,0:T(8,128)(2,1)S(1)} fusion(bf16[320,16,128]{2,0,1:T(8,128)(2,1)S(1)} %fusion.22, f32[16,320,320]{1,2,0:T(8,128)S(1)} %bitcast.163, f32[16,320]{1,0:T(8,128)S(1)} %get-tuple-element.15, pred[320,320]{0,1:T(8,128)(4,1)S(1)} %fusion.67, bf16[320,16,128]{2,0,1:T(8,128)(2,1)S(1)} %collective-permute-done.5, ...), kind=kOutput, calls=%fused_computation.42 | convolution fusion | flops 432209920 | bytes 10670081 | tf_op jit(solution)/shard_map/hqk,khd->qhd/dot_general | solution.py:135
  142.2 1.4 copy.95
  (36 shorter events, 1.7 us)
Async XLA Ops:
  0.6 39.5 %copy-start = (bf16[320,2048]{1,0:T(8,128)(2,1)S(1)}, bf16[320,2048]{1,0:T(8,128)(2,1)}, u32[]{:S(2)}) copy-start(bf16[320,2048]{1,0:T(8,128)(2,1)} %param.8) | copy-start | bytes 3932164
  4.7 13.1 %copy-start.5 = (s32[320]{0:T(512)S(1)}, s32[320]{0:T(512)}, u32[]{:S(2)}) copy-start(s32[320]{0:T(512)} %param.15) | copy-start | bytes 3844
  4.7 13.2 %copy-start.1 = (bf16[320,2048]{1,0:T(8,128)(2,1)S(1)}, bf16[320,2048]{1,0:T(8,128)(2,1)}, u32[]{:S(2)}) copy-start(bf16[320,2048]{1,0:T(8,128)(2,1)} %param.14) | copy-start | bytes 3932164
  4.7 13.2 %copy-start.4 = (bf16[320,2048]{1,0:T(8,128)(2,1)S(1)}, bf16[320,2048]{1,0:T(8,128)(2,1)}, u32[]{:S(2)}) copy-start(bf16[320,2048]{1,0:T(8,128)(2,1)} %param.13) | copy-start | bytes 3932164
  7.5 23.7 %collective-permute-start = (bf16[2056,128]{1,0:T(8,128)(2,1)S(1)}, bf16[2056,128]{1,0:T(8,128)(2,1)}, u32[]{:S(2)}, u32[]{:S(2)}) collective-permute-start(bf16[2056,128]{1,0:T(8,128)(2,1)S(1)} %concatenate.21), channel_id=1, source_target_pairs={{0,4},{4,8},{8,12},{1,5},{5,9},{9,13},{2,6},{6,10},{10,14},{3,7},{... | collective-permute-start | bytes 1579016 | tf_op jit(solution)/shard_map/ppermute | solution.py:15
  13.2 22.8 %collective-permute-start.1 = (bf16[2056,128]{1,0:T(8,128)(2,1)S(1)}, bf16[2056,128]{1,0:T(8,128)(2,1)}, u32[]{:S(2)}, u32[]{:S(2)}) collective-permute-start(bf16[2056,128]{1,0:T(8,128)(2,1)S(1)} %concatenate.21), channel_id=1, source_target_pairs={{0,8},{4,12},{1,9},{5,13},{2,10},{6,14},{3,11},{7,15},{16,24},{20,... | collective-permute-start | bytes 1579016 | tf_op jit(solution)/shard_map/ppermute | solution.py:15
  19.8 5.3 %copy-start.6 = (bf16[2048]{0:T(1024)(128)(2,1)S(1)}, bf16[2048]{0:T(1024)(128)(2,1)}, u32[]{:S(2)}) copy-start(bf16[2048]{0:T(1024)(128)(2,1)} %param.11) | copy-start | bytes 12292
  19.8 46.9 %collective-permute-start.3 = (bf16[320,2176]{1,0:T(8,128)(2,1)}, bf16[320,2176]{1,0:T(8,128)(2,1)}, u32[]{:S(2)}, u32[]{:S(2)}) collective-permute-start(bf16[320,2176]{1,0:T(8,128)(2,1)} %get-tuple-element.5), channel_id=1, source_target_pairs={{0,4},{4,8},{8,12},{1,5},{5,9},{9,13},{2,6},{6,10},{10,14},{3,7},{... | collective-permute-start | bytes 4177928 | tf_op jit(solution)/shard_map/ppermute | solution.py:15
  22.3 45.5 %collective-permute-start.2 = (bf16[320,2176]{1,0:T(8,128)(2,1)}, bf16[320,2176]{1,0:T(8,128)(2,1)}, u32[]{:S(2)}, u32[]{:S(2)}) collective-permute-start(bf16[320,2176]{1,0:T(8,128)(2,1)} %get-tuple-element.4), channel_id=1, source_target_pairs={{4,0},{8,4},{12,8},{5,1},{9,5},{13,9},{6,2},{10,6},{14,10},{7,3},{... | collective-permute-start | bytes 4177928 | tf_op jit(solution)/shard_map/ppermute | solution.py:19
  42.9 6.6 %copy-start.2 = (bf16[320,2048]{1,0:T(8,128)(2,1)S(1)}, bf16[320,2048]{1,0:T(8,128)(2,1)}, u32[]{:S(2)}) copy-start(bf16[320,2048]{1,0:T(8,128)(2,1)} %param.12) | copy-start | bytes 3932164
  51.7 41.2 %collective-permute-start.4 = (bf16[320,16,128]{2,0,1:T(8,128)(2,1)S(1)}, bf16[320,16,128]{2,0,1:T(8,128)(2,1)S(1)}, u32[]{:S(2)}, u32[]{:S(2)}) collective-permute-start(bf16[320,16,128]{2,0,1:T(8,128)(2,1)S(1)} %fusion.22), channel_id=1, source_target_pairs={{0,4},{4,8},{8,12},{1,5},{5,9},{9,13},{2,6},{6,10},{10,14},{3,7},{... | collective-permute-start | bytes 3932168 | tf_op jit(solution)/shard_map/ppermute | solution.py:15
  68.8 2.0 %copy-start.3 = (bf16[320,16,128]{2,0,1:T(8,128)(2,1)S(1)}, bf16[320,16,128]{2,0,1:T(8,128)(2,1)}, u32[]{:S(2)}) copy-start(bf16[320,16,128]{2,0,1:T(8,128)(2,1)} %copy_bitcast_fusion.3) | copy-start | bytes 3932164
  80.0 29.2 %slice-start = ((s8[7864320]{0:T(1024)(128)(4,1)}), s8[4194304]{0:T(1024)(128)(4,1)S(1)}, s32[]{:S(2)}) async-start(s8[7864320]{0:T(1024)(128)(4,1)} %bitcast.162), calls=%async_computation | async-start | bytes 8388608
  81.2 28.0 %slice-start.1 = ((s8[7864320]{0:T(1024)(128)(4,1)}), s8[3670016]{0:T(1024)(128)(4,1)S(1)}, s32[]{:S(2)}) async-start(s8[7864320]{0:T(1024)(128)(4,1)} %bitcast.162), calls=%async_computation.1 | async-start | bytes 7340032
  94.4 43.0 %collective-permute-start.5 = (bf16[320,16,128]{2,0,1:T(8,128)(2,1)S(1)}, bf16[320,16,128]{2,0,1:T(8,128)(2,1)S(1)}, u32[]{:S(2)}, u32[]{:S(2)}) collective-permute-start(bf16[320,16,128]{2,0,1:T(8,128)(2,1)S(1)} %fusion.34), channel_id=1, source_target_pairs={{0,4},{4,8},{8,12},{1,5},{5,9},{9,13},{2,6},{6,10},{10,14},{3,7},{... | collective-permute-start | bytes 3932168 | tf_op jit(solution)/shard_map/ppermute | solution.py:15
  111.3 26.1 %collective-permute-start.6 = (f32[2,16,320]{2,1,0:T(8,128)S(1)}, f32[2,16,320]{2,1,0:T(8,128)S(1)}, u32[]{:S(2)}, u32[]{:S(2)}) collective-permute-start(f32[2,16,320]{2,1,0:T(8,128)S(1)} %pad_maximum_fusion.2), channel_id=1, source_target_pairs={{0,4},{4,8},{8,12},{1,5},{5,9},{9,13},{2,6},{6,10},{10,14},{3,7},{... | collective-permute-start | bytes 122888 | tf_op jit(solution)/shard_map/ppermute | solution.py:15

commit v6 on v5

--- a/solution.py
+++ b/solution.py
@@ -51,16 +51,19 @@
     local_state = jnp.einsum(
         "thd,the->hde", tail_keys, value_rows, preferred_element_type=jnp.float32
     )
-    state_rows = local_state.astype(jnp.bfloat16).reshape(width, HD)
     tag_rows = jnp.full((8, HD), last_doc, jnp.int32).astype(jnp.bfloat16)
-    state_msg = jnp.concatenate([state_rows, tag_rows], axis=0)
-    carried = jnp.zeros_like(local_state)
-    for d in dists:
-        msg_in = shift_up(state_msg, d, n_seq)
+    whole_block = first_doc == last_doc
+    running = local_state
+    for stage in dists:
+        state_rows = running.astype(jnp.bfloat16).reshape(width, HD)
+        msg_in = shift_up(jnp.concatenate([state_rows, tag_rows], axis=0), 1, n_seq)
         state_in = msg_in[:width].reshape(head_count, HD, HD).astype(jnp.float32)
         tag_in = msg_in[width, 0].astype(jnp.int32)
-        wanted = (my_index >= d) & (tag_in == first_doc)
-        carried = carried + jnp.where(wanted, state_in, jnp.zeros_like(state_in))
+        joins = (my_index >= 1) & (tag_in == first_doc)
+        if stage < reach:
+            running = local_state + jnp.where(joins & whole_block, state_in, 0.0)
+        else:
+            carried = jnp.where(joins, state_in, jnp.zeros_like(state_in))
 
     next_msg = shift_down(jnp.concatenate([soft_query, doc_cols], axis=1), 1, n_seq)
     next_queries = next_msg[:, :width].reshape(row_count, head_count, HD)

time: 145 us -> 144 us (level)
  starting transfers between devices: 48.2 us -> 27.9 us
  waiting for transfers between devices: 34.5 us -> 54.1 us
  between operations: 4.29 us -> 5.8 us
    ppermute x6, starting transfers between devices: 47 us -> 26.6 us  [shift_up(): return lax.ppermute(x, 'seq', [(s, s + dist) for s in range(n_seq - dist)])]
    ppermute x6, waiting for transfers between devices: 34.5 us -> 54.1 us  [shift_up(): return lax.ppermute(x, 'seq', [(s, s + dist) for s in range(n_seq - dist)])]
  transfers between devices with their start and end apart: 7 -> 7, of which waited for: 3 -> 3; matrix products, arithmetic and copies ran while one was open for 30% -> 28% of each run, Pallas kernels for 0% -> 0%
where the time goes in v6:
time: 144 us
  waiting for transfers between devices  54.1 us (38%)
  matrix products  30.8 us (21%)
  starting transfers between devices  27.9 us (19%)
  other arithmetic  14.8 us (10%)
  local copies, waits for them, and re-layouts  10.4 us (7%)
  between operations  5.8 us (4%)
    ppermute x6, waiting for transfers between devices, shift_up(): return lax.ppermute(x, 'seq', [(s, s + dist) for s in range(n_seq - dist)])  54.1 us
    ppermute x6, starting transfers between devices, shift_up(): return lax.ppermute(x, 'seq', [(s, s + dist) for s in range(n_seq - dist)])  26.6 us
    dot_general x2, matrix products, weights_of(): jnp.einsum('qhd,khd->hqk', query_rows, key_all, preferred_element_type=jn...  10.1 us
    reduce_sum x2, other arithmetic, weights_of(): return (probs.astype(jnp.bfloat16), row_max, jnp.sum(probs, axis=-1))  7.06 us
    dot_general x1, matrix products, per_device(): jnp.einsum('hqk,khd->qhd', rounded, value_rows, preferred_element_type=jn...  5.52 us
    dot_general x1, matrix products, per_device(): jnp.einsum('hqk,khd->qhd', diag_probs, value_blocks[0], preferred_element...  4.77 us
    dot_general x1, matrix products, per_device(): jnp.einsum('qhd,hde->qhe', queries.astype(jnp.float32), carried, precisio...  3.97 us
    dot_general x1, matrix products, per_device(): jnp.einsum('thd,the->hde', tail_keys, value_rows, preferred_element_type=...  3.72 us
  transfers between devices with their start and end apart: 7, of which 3 were waited for; matrix products, arithmetic and copies ran while one was open for 28% of the time, Pallas kernels for 0%

profile of v6, /device:TPU:0, one launch (start us, length us, event | category | flops | bytes accessed | tf_op | source)
XLA Modules:
  0.0 143.8 jit_solution(11315566370928358676)
XLA Ops:
  0.6 1.5 %fusion.79 = (s32[1]{0:T(128)}, s32[1]{0:T(128)}) fusion(s32[320]{0:T(512)} %param.15), kind=kLoop, calls=%fused_computation.102 | loop fusion | bytes 16 | tf_op jit(solution)/shard_map/slice | solution.py:45
  2.8 2.1 %broadcast_compare_fusion.1 = (pred[320]{0:T(512)(128)(4,1)S(1)}, pred[320]{0:T(512)(128)(4,1)S(1)}) fusion(s32[320]{0:T(512)} %param.15, s32[]{:T(128)} %bitcast.1, s32[]{:T(128)} %bitcast.2), kind=kLoop, calls=%fused_computation.95 | loop fusion | flops 640 | bytes 1928 | tf_op jit(solution)/shard_map/eq | solution.py:108
  4.9 3.7 %fusion.80 = (bf16[16,128,128]{2,1,0:T(8,128)(2,1)S(1)}, f32[16,128,128]{2,1,0:T(8,128)}) fusion(pred[320]{0:T(512)(128)(4,1)S(1)} %get-tuple-element.10, bf16[320,2048]{1,0:T(8,128)(2,1)} %param.10, bf16[320,2048]{1,0:T(8,128)(2,1)} %param.9), kind=kOutput, calls=%fused_computation.103 | convolution fusion | flops 168689664 | bytes 4194624 | tf_op jit(solution)/shard_map/thd,the->hde/dot_general | solution.py:51
  8.6 5.8 %collective-permute-start = (bf16[2056,128]{1,0:T(8,128)(2,1)S(1)}, bf16[2056,128]{1,0:T(8,128)(2,1)}, u32[]{:S(2)}, u32[]{:S(2)}) collective-permute-start(bf16[2056,128]{1,0:T(8,128)(2,1)S(1)} %concatenate.24), channel_id=1, source_target_pairs={{0,4},{4,8},{8,12},{1,5},{5,9},{9,13},{2,6},{6,10},{10,14},{3,7},{... | collective-permute-start | bytes 1579016 | tf_op jit(solution)/shard_map/ppermute | solution.py:15
  14.5 1.9 %pad_maximum_fusion.1 = (bf16[320,2176]{1,0:T(8,128)(2,1)}, bf16[320,2176]{1,0:T(8,128)(2,1)}) fusion(bf16[320,128]{1,0:T(8,128)(2,1)S(1)} %broadcast_in_dim.119, bf16[320,2048]{1,0:T(8,128)(2,1)S(1)} %copy-done.5, bf16[320,2048]{1,0:T(8,128)(2,1)S(1)} %copy-done.2), kind=kLoop, calls=%fused_computation.40 | loop fusion | flops 4874240 | bytes 5488640 | tf_op jit(solution)/shard_map/concatenate | solution.py:68
  16.5 3.7 %collective-permute-start.3 = (bf16[320,2176]{1,0:T(8,128)(2,1)}, bf16[320,2176]{1,0:T(8,128)(2,1)}, u32[]{:S(2)}, u32[]{:S(2)}) collective-permute-start(bf16[320,2176]{1,0:T(8,128)(2,1)} %get-tuple-element.5), channel_id=1, source_target_pairs={{0,4},{4,8},{8,12},{1,5},{5,9},{9,13},{2,6},{6,10},{10,14},{3,7},{... | collective-permute-start | bytes 4177928 | tf_op jit(solution)/shard_map/ppermute | solution.py:15
  20.2 1.3 collective-permute-start.2
  21.5 1.4 copy_bitcast_fusion.3
  24.4 6.0 %fusion.3 = (f32[16,320]{1,0:T(8,128)S(1)}, f32[16,320,320]{1,2,0:T(8,128)}) fusion(pred[320,320]{0,1:T(8,128)(4,1)S(1)} %fusion.63, bf16[320,2048]{1,0:T(8,128)(2,1)} %param.13, bf16[320,2048]{1,0:T(8,128)(2,1)S(1)} %copy-done.2), kind=kOutput, calls=%fused_computation.8 | convolution fusion | flops 424340480 | bytes 9297920 | tf_op jit(solution)/shard_map/qhd,khd->hqk/dot_general | solution.py:84
  30.4 1.3 slice.57
  33.1 1.1 convert_select_fusion.1
  34.5 4.6 %collective-permute-start.1 = (bf16[2056,128]{1,0:T(8,128)(2,1)S(1)}, bf16[2056,128]{1,0:T(8,128)(2,1)S(1)}, u32[]{:S(2)}, u32[]{:S(2)}) collective-permute-start(bf16[2056,128]{1,0:T(8,128)(2,1)S(1)} %concatenate.25), channel_id=1, source_target_pairs={{0,4},{4,8},{8,12},{1,5},{5,9},{9,13},{2,6},{6,10},{10,14},{3,7},{... | collective-permute-start | bytes 1579016 | tf_op jit(solution)/shard_map/ppermute | solution.py:15
  39.1 5.5 %fusion.8 = f32[16,320,128]{2,1,0:T(8,128)} fusion(pred[320,320]{0,1:T(8,128)(4,1)S(1)} %fusion.63, bf16[320,2048]{1,0:T(8,128)(2,1)} %param.10, bf16[320,2048]{1,0:T(8,128)(2,1)} %param.9, bf16[320,2048]{1,0:T(8,128)(2,1)S(1)} %copy-done), kind=kOutput, calls=%fused_computation.12 | convolution fusion | flops 842137600 | bytes 6656000 | tf_op jit(solution)/shard_map/hqk,khd->qhd/dot_general | solution.py:103
  44.6 21.2 %collective-permute-done.1 = bf16[2056,128]{1,0:T(8,128)(2,1)S(1)} collective-permute-done((bf16[2056,128]{1,0:T(8,128)(2,1)S(1)}, bf16[2056,128]{1,0:T(8,128)(2,1)S(1)}, u32[]{:S(2)}, u32[]{:S(2)}) %collective-permute-start.1) | collective-permute-done | bytes 526368 | tf_op jit(solution)/shard_map/ppermute | solution.py:15
  67.8 4.0 %multiply_reduce_fusion = (f32[320,16]{0,1:T(8,128)S(1)}, f32[320,16,128]{2,0,1:T(8,128)S(1)}) fusion(f32[16,128,128]{2,1,0:T(8,128)S(1)} %bitcast.162, pred[320]{0:T(512)(128)(4,1)S(1)} %get-tuple-element.9, f32[16,320,128]{2,1,0:T(8,128)} %fusion.8, bf16[320,2048]{1,0:T(8,128)(2,1)S(1)} %copy-done), kind=kOutput, calls=%fused_computation.38 | convolution fusion | flops 1009249280 | bytes 7622976 | tf_op jit(solution)/shard_map/qhd,hde->qhe/dot_general | solution.py:104
  71.8 0.9 fusion.22
  72.8 4.6 %collective-permute-start.4 = (bf16[320,16,128]{2,0,1:T(8,128)(2,1)S(1)}, bf16[320,16,128]{2,0,1:T(8,128)(2,1)S(1)}, u32[]{:S(2)}, u32[]{:S(2)}) collective-permute-start(bf16[320,16,128]{2,0,1:T(8,128)(2,1)S(1)} %fusion.22), channel_id=1, source_target_pairs={{0,4},{4,8},{8,12},{1,5},{5,9},{9,13},{2,6},{6,10},{10,14},{3,7},{... | collective-permute-start | bytes 3932168 | tf_op jit(solution)/shard_map/ppermute | solution.py:15
  77.4 1.0 slice_reduce_fusion
  78.5 1.0 convert_reduce_fusion
  79.8 1.8 %copy_bitcast_fusion.2 = bf16[320,16,128]{2,0,1:T(8,128)(2,1)S(1)} fusion(bf16[320,2176]{1,0:T(8,128)(2,1)} %collective-permute-done.3), kind=kLoop, calls=%fused_computation.48 | loop fusion | bytes 2621440 | tf_op jit(solution)/shard_map/reshape | solution.py:74
  81.6 4.1 %fusion = (f32[16,320]{1,0:T(8,128)S(1)}, f32[16,320,640]{2,1,0:T(8,128)S(1)}) fusion(pred[320,640]{1,0:T(8,128)(4,1)S(1)} %compare_and_fusion, bf16[320,16,128]{2,0,1:T(8,128)(2,1)S(1)} %copy_bitcast_fusion.2, bf16[320,16,128]{2,0,1:T(8,128)(2,1)S(1)} %copy-done.4, bf16[320,2176]{1,0:T(8,128)(2,1)} %collective-permute-done.2), kind=kOutput, calls=%fused_computation.2 | convolution fusion | flops 853928960 | bytes 17264640 | tf_op jit(solution)/shard_map/qhd,khd->hqk/dot_general | solution.py:84
  85.7 5.1 %fusion.1 = (f32[16,320]{1,0:T(8,128)S(1)}, bf16[16,320,640]{2,1,0:T(8,128)(2,1)S(1)}) fusion(f32[16,320,640]{2,1,0:T(8,128)S(1)} %get-tuple-element.20, f32[16,320]{1,0:T(8,128)S(1)} %get-tuple-element.19, pred[320,640]{1,0:T(8,128)(4,1)S(1)} %compare_and_fusion), kind=kLoop, calls=%fused_computation.3 | loop fusion | flops 19655680 | bytes 19906560 | tf_op jit(solution)/shard_map/reduce_sum | solution.py:90
  90.8 1.2 fusion.11
  92.0 12.3 %collective-permute-done.4 = bf16[320,16,128]{2,0,1:T(8,128)(2,1)S(1)} collective-permute-done((bf16[320,16,128]{2,0,1:T(8,128)(2,1)S(1)}, bf16[320,16,128]{2,0,1:T(8,128)(2,1)S(1)}, u32[]{:S(2)}, u32[]{:S(2)}) %collective-permute-start.4) | collective-permute-done | bytes 1310752 | tf_op jit(solution)/shard_map/ppermute | solution.py:15
  104.3 1.5 %fusion.34 = bf16[320,16,128]{2,0,1:T(8,128)(2,1)S(1)} fusion(f32[16,128,320]{1,2,0:T(8,128)S(1)} %fusion.11, bf16[320,16,128]{2,0,1:T(8,128)(2,1)S(1)} %collective-permute-done.4, bf16[16,320,640]{2,1,0:T(8,128)(2,1)S(1)} %get-tuple-element.3), kind=kOutput, calls=%fused_computation.41 | convolution fusion | flops 420741120 | bytes 9175040 | tf_op jit(solution)/shard_map/hqk,khd->qhd/dot_general | solution.py:124
  105.8 4.5 %collective-permute-start.5 = (bf16[320,16,128]{2,0,1:T(8,128)(2,1)S(1)}, bf16[320,16,128]{2,0,1:T(8,128)(2,1)S(1)}, u32[]{:S(2)}, u32[]{:S(2)}) collective-permute-start(bf16[320,16,128]{2,0,1:T(8,128)(2,1)S(1)} %fusion.34), channel_id=1, source_target_pairs={{0,4},{4,8},{8,12},{1,5},{5,9},{9,13},{2,6},{6,10},{10,14},{3,7},{... | collective-permute-start | bytes 3932168 | tf_op jit(solution)/shard_map/ppermute | solution.py:15
  110.3 2.0 %fusion.4 = f32[16,320]{1,0:T(8,128)S(1)} fusion(f32[16,320,320]{1,2,0:T(8,128)S(1)} %bitcast.161, f32[16,320]{1,0:T(8,128)S(1)} %get-tuple-element.17, pred[320,320]{0,1:T(8,128)(4,1)S(1)} %fusion.63), kind=kLoop, calls=%fused_computation.9 | loop fusion | flops 8186880 | bytes 6696960 | tf_op jit(solution)/shard_map/reduce_sum | solution.py:90
  112.4 3.4 %collective-permute-start.6 = (f32[2,16,320]{2,1,0:T(8,128)S(1)}, f32[2,16,320]{2,1,0:T(8,128)S(1)}, u32[]{:S(2)}, u32[]{:S(2)}) collective-permute-start(f32[2,16,320]{2,1,0:T(8,128)S(1)} %pad_maximum_fusion.2), channel_id=1, source_target_pairs={{0,4},{4,8},{8,12},{1,5},{5,9},{9,13},{2,6},{6,10},{10,14},{3,7},{... | collective-permute-start | bytes 122888 | tf_op jit(solution)/shard_map/ppermute | solution.py:15
  115.8 1.3 copy_bitcast_fusion.1
  117.0 20.5 %collective-permute-done.6 = f32[2,16,320]{2,1,0:T(8,128)S(1)} collective-permute-done((f32[2,16,320]{2,1,0:T(8,128)S(1)}, f32[2,16,320]{2,1,0:T(8,128)S(1)}, u32[]{:S(2)}, u32[]{:S(2)}) %collective-permute-start.6) | collective-permute-done | bytes 40992 | tf_op jit(solution)/shard_map/ppermute | solution.py:15
  137.6 4.8 %fusion.37 = bf16[16,40,8,128]{3,2,1,0:T(8,128)(2,1)S(1)} fusion(bf16[320,16,128]{2,0,1:T(8,128)(2,1)S(1)} %fusion.22, f32[16,320,320]{1,2,0:T(8,128)S(1)} %bitcast.161, f32[16,320]{1,0:T(8,128)S(1)} %get-tuple-element.17, pred[320,320]{0,1:T(8,128)(4,1)S(1)} %fusion.63, bf16[320,16,128]{2,0,1:T(8,128)(2,1)S(1)} %collective-permute-done.5, ...), kind=kOutput, calls=%fused_computation.42 | convolution fusion | flops 432209920 | bytes 10670081 | tf_op jit(solution)/shard_map/hqk,khd->qhd/dot_general | solution.py:138
  142.3 1.4 copy.95
  (43 shorter events, 1.5 us)
Async XLA Ops:
  0.6 38.5 %copy-start = (bf16[320,2048]{1,0:T(8,128)(2,1)S(1)}, bf16[320,2048]{1,0:T(8,128)(2,1)}, u32[]{:S(2)}) copy-start(bf16[320,2048]{1,0:T(8,128)(2,1)} %param.8) | copy-start | bytes 3932164
  4.8 9.6 %copy-start.7 = (s32[320]{0:T(512)S(1)}, s32[320]{0:T(512)}, u32[]{:S(2)}) copy-start(s32[320]{0:T(512)} %param.15) | copy-start | bytes 3844
  4.8 9.7 %copy-start.2 = (bf16[320,2048]{1,0:T(8,128)(2,1)S(1)}, bf16[320,2048]{1,0:T(8,128)(2,1)}, u32[]{:S(2)}) copy-start(bf16[320,2048]{1,0:T(8,128)(2,1)} %param.14) | copy-start | bytes 3932164
  4.8 9.7 %copy-start.5 = (bf16[320,2048]{1,0:T(8,128)(2,1)S(1)}, bf16[320,2048]{1,0:T(8,128)(2,1)}, u32[]{:S(2)}) copy-start(bf16[320,2048]{1,0:T(8,128)(2,1)} %param.13) | copy-start | bytes 3932164
  8.6 21.8 %collective-permute-start = (bf16[2056,128]{1,0:T(8,128)(2,1)S(1)}, bf16[2056,128]{1,0:T(8,128)(2,1)}, u32[]{:S(2)}, u32[]{:S(2)}) collective-permute-start(bf16[2056,128]{1,0:T(8,128)(2,1)S(1)} %concatenate.24), channel_id=1, source_target_pairs={{0,4},{4,8},{8,12},{1,5},{5,9},{9,13},{2,6},{6,10},{10,14},{3,7},{... | collective-permute-start | bytes 1579016 | tf_op jit(solution)/shard_map/ppermute | solution.py:15
  16.5 61.0 %collective-permute-start.3 = (bf16[320,2176]{1,0:T(8,128)(2,1)}, bf16[320,2176]{1,0:T(8,128)(2,1)}, u32[]{:S(2)}, u32[]{:S(2)}) collective-permute-start(bf16[320,2176]{1,0:T(8,128)(2,1)} %get-tuple-element.5), channel_id=1, source_target_pairs={{0,4},{4,8},{8,12},{1,5},{5,9},{9,13},{2,6},{6,10},{10,14},{3,7},{... | collective-permute-start | bytes 4177928 | tf_op jit(solution)/shard_map/ppermute | solution.py:15
  20.2 58.3 %collective-permute-start.2 = (bf16[320,2176]{1,0:T(8,128)(2,1)}, bf16[320,2176]{1,0:T(8,128)(2,1)}, u32[]{:S(2)}, u32[]{:S(2)}) collective-permute-start(bf16[320,2176]{1,0:T(8,128)(2,1)} %get-tuple-element.4), channel_id=1, source_target_pairs={{4,0},{8,4},{12,8},{5,1},{9,5},{13,9},{6,2},{10,6},{14,10},{7,3},{... | collective-permute-start | bytes 4177928 | tf_op jit(solution)/shard_map/ppermute | solution.py:19
  30.4 3.8 %copy-start.6 = (f32[16,128,128]{2,1,0:T(8,128)S(1)}, f32[16,128,128]{2,1,0:T(8,128)}, u32[]{:S(2)}) copy-start(f32[16,128,128]{2,1,0:T(8,128)} %get-tuple-element.14) | copy-start | bytes 3145732
  34.3 4.8 %copy-start.8 = (bf16[2048]{0:T(1024)(128)(2,1)S(1)}, bf16[2048]{0:T(1024)(128)(2,1)}, u32[]{:S(2)}) copy-start(bf16[2048]{0:T(1024)(128)(2,1)} %param.11) | copy-start | bytes 12292
  34.5 31.4 %collective-permute-start.1 = (bf16[2056,128]{1,0:T(8,128)(2,1)S(1)}, bf16[2056,128]{1,0:T(8,128)(2,1)S(1)}, u32[]{:S(2)}, u32[]{:S(2)}) collective-permute-start(bf16[2056,128]{1,0:T(8,128)(2,1)S(1)} %concatenate.25), channel_id=1, source_target_pairs={{0,4},{4,8},{8,12},{1,5},{5,9},{9,13},{2,6},{6,10},{10,14},{3,7},{... | collective-permute-start | bytes 1579016 | tf_op jit(solution)/shard_map/ppermute | solution.py:15
  67.8 4.0 %copy-start.3 = (bf16[320,2048]{1,0:T(8,128)(2,1)S(1)}, bf16[320,2048]{1,0:T(8,128)(2,1)}, u32[]{:S(2)}) copy-start(bf16[320,2048]{1,0:T(8,128)(2,1)} %param.12) | copy-start | bytes 3932164
  72.8 31.5 %collective-permute-start.4 = (bf16[320,16,128]{2,0,1:T(8,128)(2,1)S(1)}, bf16[320,16,128]{2,0,1:T(8,128)(2,1)S(1)}, u32[]{:S(2)}, u32[]{:S(2)}) collective-permute-start(bf16[320,16,128]{2,0,1:T(8,128)(2,1)S(1)} %fusion.22), channel_id=1, source_target_pairs={{0,4},{4,8},{8,12},{1,5},{5,9},{9,13},{2,6},{6,10},{10,14},{3,7},{... | collective-permute-start | bytes 3932168 | tf_op jit(solution)/shard_map/ppermute | solution.py:15
  79.6 2.0 %copy-start.4 = (bf16[320,16,128]{2,0,1:T(8,128)(2,1)S(1)}, bf16[320,16,128]{2,0,1:T(8,128)(2,1)}, u32[]{:S(2)}) copy-start(bf16[320,16,128]{2,0,1:T(8,128)(2,1)} %copy_bitcast_fusion.3) | copy-start | bytes 3932164
  90.8 19.6 %slice-start = ((s8[7864320]{0:T(1024)(128)(4,1)}), s8[4194304]{0:T(1024)(128)(4,1)S(1)}, s32[]{:S(2)}) async-start(s8[7864320]{0:T(1024)(128)(4,1)} %bitcast.160), calls=%async_computation | async-start | bytes 8388608
  92.0 18.4 %slice-start.1 = ((s8[7864320]{0:T(1024)(128)(4,1)}), s8[3670016]{0:T(1024)(128)(4,1)S(1)}, s32[]{:S(2)}) async-start(s8[7864320]{0:T(1024)(128)(4,1)} %bitcast.160), calls=%async_computation.1 | async-start | bytes 7340032
  105.8 31.7 %collective-permute-start.5 = (bf16[320,16,128]{2,0,1:T(8,128)(2,1)S(1)}, bf16[320,16,128]{2,0,1:T(8,128)(2,1)S(1)}, u32[]{:S(2)}, u32[]{:S(2)}) collective-permute-start(bf16[320,16,128]{2,0,1:T(8,128)(2,1)S(1)} %fusion.34), channel_id=1, source_target_pairs={{0,4},{4,8},{8,12},{1,5},{5,9},{9,13},{2,6},{6,10},{10,14},{3,7},{... | collective-permute-start | bytes 3932168 | tf_op jit(solution)/shard_map/ppermute | solution.py:15
  112.4 25.2 %collective-permute-start.6 = (f32[2,16,320]{2,1,0:T(8,128)S(1)}, f32[2,16,320]{2,1,0:T(8,128)S(1)}, u32[]{:S(2)}, u32[]{:S(2)}) collective-permute-start(f32[2,16,320]{2,1,0:T(8,128)S(1)} %pad_maximum_fusion.2), channel_id=1, source_target_pairs={{0,4},{4,8},{8,12},{1,5},{5,9},{9,13},{2,6},{6,10},{10,14},{3,7},{... | collective-permute-start | bytes 122888 | tf_op jit(solution)/shard_map/ppermute | solution.py:15
  137.5 6.2 %copy-start.1 = (bf16[320,2048]{1,0:T(8,128)(2,1)S(1)}, bf16[320,2048]{1,0:T(8,128)(2,1)}, u32[]{:S(2)}) copy-start(bf16[320,2048]{1,0:T(8,128)(2,1)} %param.8) | copy-start | bytes 3932164

commit v7 on v6

--- a/solution.py
+++ b/solution.py
@@ -68,7 +68,8 @@
     next_msg = shift_down(jnp.concatenate([soft_query, doc_cols], axis=1), 1, n_seq)
     next_queries = next_msg[:, :width].reshape(row_count, head_count, HD)
     next_docs = next_msg[:, width].astype(jnp.int32)
-    key_msgs = [jnp.concatenate([soft_key, doc_cols], axis=1)]
+    key_first, _ = lax.optimization_barrier((jnp.concatenate([soft_key, doc_cols], axis=1), carried))
+    key_msgs = [key_first]
     for d in dists[:-1]:
         key_msgs.append(shift_up(key_msgs[-1], 1, n_seq))
     key_blocks = [m[:, :width].reshape(row_count, head_count, HD) for m in key_msgs]

time: 144 us -> 148 us (1.028)
  waiting for transfers between devices: 54.1 us -> 62 us
  matrix products: 30.8 us -> 27.8 us
  local copies, waits for them, and re-layouts: 10.4 us -> 7.8 us
  starting transfers between devices: 27.9 us -> 29.5 us
    ppermute x6, waiting for transfers between devices: 54.1 us -> 62 us  [shift_up(): return lax.ppermute(x, 'seq', [(s, s + dist) for s in range(n_seq - dist)])]
    dot_general x2, matrix products: 10.1 us -> 5.75 us  [weights_of(): jnp.einsum('qhd,khd->hqk', query_rows, key_all, preferred_element_type=jn...]
    reshape x2, local copies, waits for them, and re-layouts: 3.15 us -> 0.67 us  [per_device(): m[:, :width].reshape(row_count, head_count, HD)]
    ppermute x6, starting transfers between devices: 26.6 us -> 28.2 us  [shift_up(): return lax.ppermute(x, 'seq', [(s, s + dist) for s in range(n_seq - dist)])]
  transfers between devices with their start and end apart: 7 -> 7, of which waited for: 3 -> 5; matrix products, arithmetic and copies ran while one was open for 28% -> 23% of each run, Pallas kernels for 0% -> 0%
where the time goes in v7:
time: 148 us
  waiting for transfers between devices  62 us (42%)
  starting transfers between devices  29.5 us (20%)
  matrix products  27.8 us (19%)
  other arithmetic  15.2 us (10%)
  local copies, waits for them, and re-layouts  7.8 us (5%)
  between operations  5.39 us (4%)
    ppermute x6, waiting for transfers between devices, shift_up(): return lax.ppermute(x, 'seq', [(s, s + dist) for s in range(n_seq - dist)])  62 us
    ppermute x6, starting transfers between devices, shift_up(): return lax.ppermute(x, 'seq', [(s, s + dist) for s in range(n_seq - dist)])  28.2 us
    reduce_sum x2, other arithmetic, weights_of(): return (probs.astype(jnp.bfloat16), row_max, jnp.sum(probs, axis=-1))  7.07 us
    dot_general x2, matrix products, weights_of(): jnp.einsum('qhd,khd->hqk', query_rows, key_all, preferred_element_type=jn...  5.75 us
    dot_general x1, matrix products, per_device(): jnp.einsum('hqk,khd->qhd', rounded, value_rows, preferred_element_type=jn...  5.47 us
    dot_general x1, matrix products, per_device(): jnp.einsum('hqk,khd->qhd', diag_probs, value_blocks[0], preferred_element...  4.87 us
    dot_general x2, matrix products, per_device(): jnp.einsum('hqk,khd->qhd', probs[:, :, d * row_count:(d + 1) * row_count]...  4.03 us
    dot_general x1, matrix products, per_device(): jnp.einsum('qhd,hde->qhe', queries.astype(jnp.float32), carried, precisio...  3.95 us
  transfers between devices with their start and end apart: 7, of which 5 were waited for; matrix products, arithmetic and copies ran while one was open for 23% of the time, Pallas kernels for 0%

profile of v7, /device:TPU:0, one launch (start us, length us, event | category | flops | bytes accessed | tf_op | source)
XLA Modules:
  0.0 147.7 jit_solution(4330110162770190645)
XLA Ops:
  0.6 1.4 fusion.79
  2.7 1.9 %broadcast_compare_fusion.1 = (pred[320]{0:T(512)(128)(4,1)S(1)}, pred[320]{0:T(512)(128)(4,1)S(1)}) fusion(s32[320]{0:T(512)} %param.15, s32[]{:T(128)} %bitcast.1, s32[]{:T(128)} %bitcast.2), kind=kLoop, calls=%fused_computation.97 | loop fusion | flops 640 | bytes 1928 | tf_op jit(solution)/shard_map/eq | solution.py:109
  4.6 3.7 %fusion.80 = (bf16[16,128,128]{2,1,0:T(8,128)(2,1)S(1)}, f32[16,128,128]{2,1,0:T(8,128)}) fusion(pred[320]{0:T(512)(128)(4,1)S(1)} %get-tuple-element.12, bf16[320,2048]{1,0:T(8,128)(2,1)} %param.10, bf16[320,2048]{1,0:T(8,128)(2,1)} %param.9), kind=kOutput, calls=%fused_computation.105 | convolution fusion | flops 168689664 | bytes 4194624 | tf_op jit(solution)/shard_map/thd,the->hde/dot_general | solution.py:51
  8.4 5.7 %collective-permute-start = (bf16[2056,128]{1,0:T(8,128)(2,1)S(1)}, bf16[2056,128]{1,0:T(8,128)(2,1)}, u32[]{:S(2)}, u32[]{:S(2)}) collective-permute-start(bf16[2056,128]{1,0:T(8,128)(2,1)S(1)} %concatenate.24), channel_id=1, source_target_pairs={{0,4},{4,8},{8,12},{1,5},{5,9},{9,13},{2,6},{6,10},{10,14},{3,7},{... | collective-permute-start | bytes 1579016 | tf_op jit(solution)/shard_map/ppermute | solution.py:15
  14.2 1.3 pad_maximum_fusion.1
  15.6 1.3 collective-permute-start.2
  18.3 6.3 %collective-permute-done = bf16[2056,128]{1,0:T(8,128)(2,1)} collective-permute-done((bf16[2056,128]{1,0:T(8,128)(2,1)S(1)}, bf16[2056,128]{1,0:T(8,128)(2,1)}, u32[]{:S(2)}, u32[]{:S(2)}) %collective-permute-start) | collective-permute-done | bytes 526368 | tf_op jit(solution)/shard_map/ppermute | solution.py:15
  24.5 1.2 slice.64
  27.0 1.2 convert_select_fusion.1
  28.6 5.3 %collective-permute-start.1 = (bf16[2056,128]{1,0:T(8,128)(2,1)S(1)}, bf16[2056,128]{1,0:T(8,128)(2,1)}, u32[]{:S(2)}, u32[]{:S(2)}) collective-permute-start(bf16[2056,128]{1,0:T(8,128)(2,1)S(1)} %concatenate.25), channel_id=1, source_target_pairs={{0,4},{4,8},{8,12},{1,5},{5,9},{9,13},{2,6},{6,10},{10,14},{3,7},{... | collective-permute-start | bytes 1579016 | tf_op jit(solution)/shard_map/ppermute | solution.py:15
  33.9 5.5 %fusion.8 = f32[16,320,128]{2,1,0:T(8,128)} fusion(pred[320,320]{0,1:T(8,128)(4,1)S(1)} %fusion.63, bf16[320,2048]{1,0:T(8,128)(2,1)} %param.10, bf16[320,2048]{1,0:T(8,128)(2,1)} %param.9, bf16[320,2048]{1,0:T(8,128)(2,1)S(1)} %copy-done), kind=kOutput, calls=%fused_computation.12 | convolution fusion | flops 842137600 | bytes 6656000 | tf_op jit(solution)/shard_map/hqk,khd->qhd/dot_general | solution.py:104
  39.4 4.0 %collective-permute-done.1 = bf16[2056,128]{1,0:T(8,128)(2,1)} collective-permute-done((bf16[2056,128]{1,0:T(8,128)(2,1)S(1)}, bf16[2056,128]{1,0:T(8,128)(2,1)}, u32[]{:S(2)}, u32[]{:S(2)}) %collective-permute-start.1) | collective-permute-done | bytes 526368 | tf_op jit(solution)/shard_map/ppermute | solution.py:15
  43.4 1.2 slice.66
  45.9 1.1 convert_select_fusion
  47.0 4.6 %collective-permute-start.3 = (bf16[320,2176]{1,0:T(8,128)(2,1)S(1)}, bf16[320,2176]{1,0:T(8,128)(2,1)S(1)}, u32[]{:S(2)}, u32[]{:S(2)}) collective-permute-start(bf16[320,2176]{1,0:T(8,128)(2,1)S(1)} %get-tuple-element.3), channel_id=1, source_target_pairs={{0,4},{4,8},{8,12},{1,5},{5,9},{9,13},{2,6},{6,10},{10,14},{3,7},{... | collective-permute-start | bytes 4177928 | tf_op jit(solution)/shard_map/ppermute | solution.py:15
  51.6 4.0 %multiply_reduce_fusion = (f32[320,16]{0,1:T(8,128)S(1)}, f32[320,16,128]{2,0,1:T(8,128)S(1)}) fusion(f32[16,128,128]{2,1,0:T(8,128)S(1)} %bitcast.174, pred[320]{0:T(512)(128)(4,1)S(1)} %get-tuple-element.11, f32[16,320,128]{2,1,0:T(8,128)} %fusion.8, bf16[320,2048]{1,0:T(8,128)(2,1)S(1)} %copy-done), kind=kOutput, calls=%fused_computation.38 | convolution fusion | flops 1009249280 | bytes 7622976 | tf_op jit(solution)/shard_map/qhd,hde->qhe/dot_general | solution.py:105
  56.6 4.6 %collective-permute-start.4 = (bf16[320,16,128]{2,0,1:T(8,128)(2,1)S(1)}, bf16[320,16,128]{2,0,1:T(8,128)(2,1)}, u32[]{:S(2)}, u32[]{:S(2)}) collective-permute-start(bf16[320,16,128]{2,0,1:T(8,128)(2,1)S(1)} %fusion.22), channel_id=1, source_target_pairs={{0,4},{4,8},{8,12},{1,5},{5,9},{9,13},{2,6},{6,10},{10,14},{3,7},{... | collective-permute-start | bytes 3932168 | tf_op jit(solution)/shard_map/ppermute | solution.py:15
  61.7 1.6 %fusion.3 = (f32[16,320]{1,0:T(8,128)S(1)}, f32[16,320,320]{2,1,0:T(8,128)S(1)}) fusion(pred[320,320]{0,1:T(8,128)(4,1)S(1)} %fusion.63, bf16[320,2176]{1,0:T(8,128)(2,1)S(1)} %get-tuple-element.3, bf16[320,2048]{1,0:T(8,128)(2,1)S(1)} %copy-done.5), kind=kOutput, calls=%fused_computation.8 | convolution fusion | flops 424340480 | bytes 9318400 | tf_op jit(solution)/shard_map/qhd,khd->hqk/dot_general | solution.py:85
  63.3 1.0 convert_reduce_fusion
  64.3 18.2 %collective-permute-done.3 = bf16[320,2176]{1,0:T(8,128)(2,1)S(1)} collective-permute-done((bf16[320,2176]{1,0:T(8,128)(2,1)S(1)}, bf16[320,2176]{1,0:T(8,128)(2,1)S(1)}, u32[]{:S(2)}, u32[]{:S(2)}) %collective-permute-start.3) | collective-permute-done | bytes 1392672 | tf_op jit(solution)/shard_map/ppermute | solution.py:15
  83.3 4.1 %fusion = (f32[16,320]{1,0:T(8,128)S(1)}, f32[16,320,640]{2,1,0:T(8,128)S(1)}) fusion(pred[320,640]{1,0:T(8,128)(4,1)S(1)} %compare_and_fusion, bf16[320,16,128]{2,0,1:T(8,128)(2,1)S(1)} %copy_bitcast_fusion.2, bf16[320,16,128]{2,0,1:T(8,128)(2,1)S(1)} %copy_bitcast_fusion.3, bf16[320,2176]{1,0:T(8,128)(2,1)} %collective-permute-done.2), kind=kOutput, calls=%fused_computation.2 | convolution fusion | flops 853928960 | bytes 17264640 | tf_op jit(solution)/shard_map/qhd,khd->hqk/dot_general | solution.py:85
  87.4 5.1 %fusion.1 = (f32[16,320]{1,0:T(8,128)S(1)}, bf16[16,320,640]{2,1,0:T(8,128)(2,1)S(1)}) fusion(f32[16,320,640]{2,1,0:T(8,128)S(1)} %get-tuple-element.22, f32[16,320]{1,0:T(8,128)S(1)} %get-tuple-element.21, pred[320,640]{1,0:T(8,128)(4,1)S(1)} %compare_and_fusion), kind=kLoop, calls=%fused_computation.3 | loop fusion | flops 19655680 | bytes 19906560 | tf_op jit(solution)/shard_map/reduce_sum | solution.py:91
  92.5 1.2 fusion.11
  93.7 13.9 %collective-permute-done.4 = bf16[320,16,128]{2,0,1:T(8,128)(2,1)} collective-permute-done((bf16[320,16,128]{2,0,1:T(8,128)(2,1)S(1)}, bf16[320,16,128]{2,0,1:T(8,128)(2,1)}, u32[]{:S(2)}, u32[]{:S(2)}) %collective-permute-start.4) | collective-permute-done | bytes 1310752 | tf_op jit(solution)/shard_map/ppermute | solution.py:15
  107.6 2.8 %fusion.34 = bf16[320,16,128]{2,0,1:T(8,128)(2,1)S(1)} fusion(f32[16,128,320]{1,2,0:T(8,128)S(1)} %fusion.11, bf16[320,16,128]{2,0,1:T(8,128)(2,1)} %collective-permute-done.4, bf16[16,320,640]{2,1,0:T(8,128)(2,1)S(1)} %get-tuple-element.5), kind=kOutput, calls=%fused_computation.41 | convolution fusion | flops 420741120 | bytes 9175040 | tf_op jit(solution)/shard_map/hqk,khd->qhd/dot_general | solution.py:125
  110.5 4.6 %collective-permute-start.5 = (bf16[320,16,128]{2,0,1:T(8,128)(2,1)S(1)}, bf16[320,16,128]{2,0,1:T(8,128)(2,1)S(1)}, u32[]{:S(2)}, u32[]{:S(2)}) collective-permute-start(bf16[320,16,128]{2,0,1:T(8,128)(2,1)S(1)} %fusion.34), channel_id=1, source_target_pairs={{0,4},{4,8},{8,12},{1,5},{5,9},{9,13},{2,6},{6,10},{10,14},{3,7},{... | collective-permute-start | bytes 3932168 | tf_op jit(solution)/shard_map/ppermute | solution.py:15
  115.0 2.0 %fusion.4 = f32[16,320]{1,0:T(8,128)S(1)} fusion(f32[16,320,320]{2,1,0:T(8,128)S(1)} %get-tuple-element.20, f32[16,320]{1,0:T(8,128)S(1)} %get-tuple-element.19, pred[320,320]{0,1:T(8,128)(4,1)S(1)} %fusion.63), kind=kLoop, calls=%fused_computation.9 | loop fusion | flops 8186880 | bytes 6696960 | tf_op jit(solution)/shard_map/reduce_sum | solution.py:91
  117.0 3.4 %collective-permute-start.6 = (f32[2,16,320]{2,1,0:T(8,128)S(1)}, f32[2,16,320]{2,1,0:T(8,128)S(1)}, u32[]{:S(2)}, u32[]{:S(2)}) collective-permute-start(f32[2,16,320]{2,1,0:T(8,128)S(1)} %pad_maximum_fusion.2), channel_id=1, source_target_pairs={{0,4},{4,8},{8,12},{1,5},{5,9},{9,13},{2,6},{6,10},{10,14},{3,7},{... | collective-permute-start | bytes 122888 | tf_op jit(solution)/shard_map/ppermute | solution.py:15
  120.5 1.3 copy_bitcast_fusion.1
  121.7 19.6 %collective-permute-done.6 = f32[2,16,320]{2,1,0:T(8,128)S(1)} collective-permute-done((f32[2,16,320]{2,1,0:T(8,128)S(1)}, f32[2,16,320]{2,1,0:T(8,128)S(1)}, u32[]{:S(2)}, u32[]{:S(2)}) %collective-permute-start.6) | collective-permute-done | bytes 40992 | tf_op jit(solution)/shard_map/ppermute | solution.py:15
  141.4 4.9 %fusion.37 = bf16[16,40,8,128]{3,2,1,0:T(8,128)(2,1)S(1)} fusion(bf16[320,16,128]{2,0,1:T(8,128)(2,1)S(1)} %fusion.22, f32[16,320,320]{2,1,0:T(8,128)S(1)} %get-tuple-element.20, f32[16,320]{1,0:T(8,128)S(1)} %get-tuple-element.19, pred[320,320]{0,1:T(8,128)(4,1)S(1)} %fusion.63, bf16[320,16,128]{2,0,1:T(8,128)(2,1)S(1)} %collective-permute-done.5, ...), kind=kOutput, calls=%fused_computation.42 | convolution fusion | flops 432209920 | bytes 10670081 | tf_op jit(solution)/shard_map/hqk,khd->qhd/dot_general | solution.py:139
  146.2 1.4 copy.95
  (39 shorter events, 2.8 us)
Async XLA Ops:
  0.6 33.3 %copy-start = (bf16[320,2048]{1,0:T(8,128)(2,1)S(1)}, bf16[320,2048]{1,0:T(8,128)(2,1)}, u32[]{:S(2)}) copy-start(bf16[320,2048]{1,0:T(8,128)(2,1)} %param.8) | copy-start | bytes 3932164
  4.6 9.5 %copy-start.7 = (s32[320]{0:T(512)S(1)}, s32[320]{0:T(512)}, u32[]{:S(2)}) copy-start(s32[320]{0:T(512)} %param.15) | copy-start | bytes 3844
  4.6 9.6 %copy-start.3 = (bf16[320,2048]{1,0:T(8,128)(2,1)S(1)}, bf16[320,2048]{1,0:T(8,128)(2,1)}, u32[]{:S(2)}) copy-start(bf16[320,2048]{1,0:T(8,128)(2,1)} %param.14) | copy-start | bytes 3932164
  4.6 9.6 %copy-start.4 = (bf16[320,2048]{1,0:T(8,128)(2,1)S(1)}, bf16[320,2048]{1,0:T(8,128)(2,1)}, u32[]{:S(2)}) copy-start(bf16[320,2048]{1,0:T(8,128)(2,1)} %param.13) | copy-start | bytes 3932164
  8.4 16.1 %collective-permute-start = (bf16[2056,128]{1,0:T(8,128)(2,1)S(1)}, bf16[2056,128]{1,0:T(8,128)(2,1)}, u32[]{:S(2)}, u32[]{:S(2)}) collective-permute-start(bf16[2056,128]{1,0:T(8,128)(2,1)S(1)} %concatenate.24), channel_id=1, source_target_pairs={{0,4},{4,8},{8,12},{1,5},{5,9},{9,13},{2,6},{6,10},{10,14},{3,7},{... | collective-permute-start | bytes 1579016 | tf_op jit(solution)/shard_map/ppermute | solution.py:15
  15.6 47.7 %collective-permute-start.2 = (bf16[320,2176]{1,0:T(8,128)(2,1)}, bf16[320,2176]{1,0:T(8,128)(2,1)}, u32[]{:S(2)}, u32[]{:S(2)}) collective-permute-start(bf16[320,2176]{1,0:T(8,128)(2,1)} %get-tuple-element.6), channel_id=1, source_target_pairs={{4,0},{8,4},{12,8},{5,1},{9,5},{13,9},{6,2},{10,6},{14,10},{7,3},{... | collective-permute-start | bytes 4177928 | tf_op jit(solution)/shard_map/ppermute | solution.py:19
  27.0 1.4 copy-start.6
  28.4 5.5 %copy-start.8 = (bf16[2048]{0:T(1024)(128)(2,1)S(1)}, bf16[2048]{0:T(1024)(128)(2,1)}, u32[]{:S(2)}) copy-start(bf16[2048]{0:T(1024)(128)(2,1)} %param.11) | copy-start | bytes 12292
  28.6 14.8 %collective-permute-start.1 = (bf16[2056,128]{1,0:T(8,128)(2,1)S(1)}, bf16[2056,128]{1,0:T(8,128)(2,1)}, u32[]{:S(2)}, u32[]{:S(2)}) collective-permute-start(bf16[2056,128]{1,0:T(8,128)(2,1)S(1)} %concatenate.25), channel_id=1, source_target_pairs={{0,4},{4,8},{8,12},{1,5},{5,9},{9,13},{2,6},{6,10},{10,14},{3,7},{... | collective-permute-start | bytes 1579016 | tf_op jit(solution)/shard_map/ppermute | solution.py:15
  47.0 35.5 %collective-permute-start.3 = (bf16[320,2176]{1,0:T(8,128)(2,1)S(1)}, bf16[320,2176]{1,0:T(8,128)(2,1)S(1)}, u32[]{:S(2)}, u32[]{:S(2)}) collective-permute-start(bf16[320,2176]{1,0:T(8,128)(2,1)S(1)} %get-tuple-element.3), channel_id=1, source_target_pairs={{0,4},{4,8},{8,12},{1,5},{5,9},{9,13},{2,6},{6,10},{10,14},{3,7},{... | collective-permute-start | bytes 4177928 | tf_op jit(solution)/shard_map/ppermute | solution.py:15
  51.6 4.0 %copy-start.2 = (bf16[320,2048]{1,0:T(8,128)(2,1)S(1)}, bf16[320,2048]{1,0:T(8,128)(2,1)}, u32[]{:S(2)}) copy-start(bf16[320,2048]{1,0:T(8,128)(2,1)} %param.12) | copy-start | bytes 3932164
  56.6 5.1 %copy-start.5 = (bf16[320,2048]{1,0:T(8,128)(2,1)S(1)}, bf16[320,2048]{1,0:T(8,128)(2,1)}, u32[]{:S(2)}) copy-start(bf16[320,2048]{1,0:T(8,128)(2,1)} %param.13) | copy-start | bytes 3932164
  56.6 51.0 %collective-permute-start.4 = (bf16[320,16,128]{2,0,1:T(8,128)(2,1)S(1)}, bf16[320,16,128]{2,0,1:T(8,128)(2,1)}, u32[]{:S(2)}, u32[]{:S(2)}) collective-permute-start(bf16[320,16,128]{2,0,1:T(8,128)(2,1)S(1)} %fusion.22), channel_id=1, source_target_pairs={{0,4},{4,8},{8,12},{1,5},{5,9},{9,13},{2,6},{6,10},{10,14},{3,7},{... | collective-permute-start | bytes 3932168 | tf_op jit(solution)/shard_map/ppermute | solution.py:15
  110.5 30.9 %collective-permute-start.5 = (bf16[320,16,128]{2,0,1:T(8,128)(2,1)S(1)}, bf16[320,16,128]{2,0,1:T(8,128)(2,1)S(1)}, u32[]{:S(2)}, u32[]{:S(2)}) collective-permute-start(bf16[320,16,128]{2,0,1:T(8,128)(2,1)S(1)} %fusion.34), channel_id=1, source_target_pairs={{0,4},{4,8},{8,12},{1,5},{5,9},{9,13},{2,6},{6,10},{10,14},{3,7},{... | collective-permute-start | bytes 3932168 | tf_op jit(solution)/shard_map/ppermute | solution.py:15
  117.0 24.3 %collective-permute-start.6 = (f32[2,16,320]{2,1,0:T(8,128)S(1)}, f32[2,16,320]{2,1,0:T(8,128)S(1)}, u32[]{:S(2)}, u32[]{:S(2)}) collective-permute-start(f32[2,16,320]{2,1,0:T(8,128)S(1)} %pad_maximum_fusion.2), channel_id=1, source_target_pairs={{0,4},{4,8},{8,12},{1,5},{5,9},{9,13},{2,6},{6,10},{10,14},{3,7},{... | collective-permute-start | bytes 122888 | tf_op jit(solution)/shard_map/ppermute | solution.py:15
  141.3 6.3 %copy-start.1 = (bf16[320,2048]{1,0:T(8,128)(2,1)S(1)}, bf16[320,2048]{1,0:T(8,128)(2,1)}, u32[]{:S(2)}) copy-start(bf16[320,2048]{1,0:T(8,128)(2,1)} %param.8) | copy-start | bytes 3932164

commit v8 on v6

--- a/solution.py
+++ b/solution.py
@@ -65,21 +65,36 @@
         else:
             carried = jnp.where(joins, state_in, jnp.zeros_like(state_in))
 
-    next_msg = shift_down(jnp.concatenate([soft_query, doc_cols], axis=1), 1, n_seq)
-    next_queries = next_msg[:, :width].reshape(row_count, head_count, HD)
-    next_docs = next_msg[:, width].astype(jnp.int32)
-    key_msgs = [jnp.concatenate([soft_key, doc_cols], axis=1)]
+    split = head_count // 2
+    query_msg = jnp.concatenate([soft_query, doc_cols], axis=1)
+    query_msgs = [query_msg]
+    for d in dists:
+        if d == 2:
+            query_msg = jnp.concatenate([query_msg[:, split * HD : width], query_msg[:, width:]], axis=1)
+        query_msg = shift_down(query_msg, 1, n_seq)
+        query_msgs.append(query_msg)
+    far_width = (head_count - split) * HD
+    next_queries = query_msgs[1][:, :width].reshape(row_count, head_count, HD)
+    next_docs = query_msgs[1][:, width].astype(jnp.int32)
+    far_queries = [next_queries[:, split:]] + [
+        m[:, :far_width].reshape(row_count, head_count - split, HD) for m in query_msgs[2:]
+    ]
+    far_docs = [next_docs] + [m[:, far_width].astype(jnp.int32) for m in query_msgs[2:]]
+
+    near_key = jnp.concatenate([soft_key[:, : split * HD], doc_cols], axis=1)
+    key_msgs = [near_key]
     for d in dists[:-1]:
         key_msgs.append(shift_up(key_msgs[-1], 1, n_seq))
-    key_blocks = [m[:, :width].reshape(row_count, head_count, HD) for m in key_msgs]
-    key_docs = [m[:, width].astype(jnp.int32) for m in key_msgs]
+    key_blocks = [m[:, : split * HD].reshape(row_count, split, HD) for m in key_msgs]
+    key_docs = [m[:, split * HD].astype(jnp.int32) for m in key_msgs]
 
     positions = jnp.arange(row_count, dtype=jnp.int32)
     causal = positions[:, None] >= positions[None, :]
     keep_local = causal & (doc_id[:, None] == doc_id[None, :])
     score_scale = 1.0 / math.sqrt(HD)
-
-    def weights_of(query_rows, keep):
+    key_soft = soft_key.reshape(row_count, head_count, HD)
+
+    def weights_of(query_rows, key_all, keep):
         logits = (
             jnp.einsum("qhd,khd->hqk", query_rows, key_all, preferred_element_type=jnp.float32)
             * score_scale
@@ -89,14 +104,16 @@
         probs = jnp.where(keep[None], jnp.exp(logits - row_max[..., None]), 0.0)
         return probs.astype(jnp.bfloat16), row_max, jnp.sum(probs, axis=-1)
 
-    key_all = key_blocks[0]
-    diag = weights_of(soft_query.reshape(row_count, head_count, HD), keep_local)
-    key_all = jnp.concatenate(key_blocks, axis=0)
+    diag = weights_of(soft_query.reshape(row_count, head_count, HD), key_soft, keep_local)
     valid = jnp.concatenate(
         [jnp.full((row_count,), my_index >= d, jnp.bool_) for d in range(len(key_blocks))]
     )
     keep_next = (next_docs[:, None] == jnp.concatenate(key_docs)[None, :]) & valid[None, :]
-    ahead = weights_of(next_queries, keep_next)
+    near = weights_of(next_queries[:, :split], jnp.concatenate(key_blocks, axis=0), keep_next)
+    far = [
+        weights_of(far_queries[i], key_soft[:, split:], far_docs[i][:, None] == doc_id[None, :])
+        for i in range(reach)
+    ]
 
     scores = jnp.einsum("qhd,khd->hqk", queries, key_rows, preferred_element_type=jnp.float32)
     rounded = jnp.where(keep_local[None], scores, jnp.zeros_like(scores)).astype(jnp.bfloat16)
@@ -114,31 +131,55 @@
     normed = lin_raw * lax.rsqrt(mean_square + norm_eps) * gain_rows * gate_rows
     lin_out = normed.astype(jnp.bfloat16).reshape(row_count, width)
 
-    value_blocks = [lin_out.reshape(row_count, head_count, HD)]
-    for d in dists[:-1]:
-        value_blocks.append(shift_up(value_blocks[-1], 1, n_seq))
-
-    probs, ahead_max, ahead_sum = ahead
-    ahead_out = jnp.zeros((row_count, head_count, HD), jnp.float32)
-    for d, value_block in enumerate(value_blocks):
-        ahead_out = ahead_out + jnp.einsum(
-            "hqk,khd->qhd",
-            probs[:, :, d * row_count : (d + 1) * row_count],
-            value_block,
-            preferred_element_type=jnp.float32,
-        )
-    out_in = shift_up(ahead_out.astype(jnp.bfloat16), 1, n_seq)
-    stats_in = shift_up(jnp.stack([ahead_max, ahead_sum]), 1, n_seq)
+    value_own = lin_out.reshape(row_count, head_count, HD)
     has_source = my_index >= 1
-    max_in = jnp.where(has_source, stats_in[0], -1e30)
-    sum_in = jnp.where(has_source, stats_in[1], 0.0)
-    out_in = jnp.where(has_source, out_in.astype(jnp.float32), 0.0)
+
+    def received(msg, stats):
+        max_in = jnp.where(has_source, stats[0], -1e30)
+        sum_in = jnp.where(has_source, stats[1], 0.0)
+        return jnp.where(has_source, msg.astype(jnp.float32), 0.0), max_in, sum_in
+
+    def mix(weights, value_block):
+        return jnp.einsum("hqk,khd->qhd", weights, value_block, preferred_element_type=jnp.float32)
+
+    near_values = [value_own[:, :split]]
+    far_running = None
+    for s in dists:
+        d = reach + 1 - s
+        far_probs, far_max, far_sum = far[d - 1]
+        far_part = (mix(far_probs, value_own[:, split:]), far_max, far_sum)
+        if far_running is not None:
+            far_part = merge(far_running, far_part)
+        if s < reach:
+            near_msg = near_values[-1]
+        else:
+            probs, near_max, near_sum = near
+            near_out = jnp.zeros((row_count, split, HD), jnp.float32)
+            for k, value_block in enumerate(near_values):
+                near_out = near_out + mix(
+                    probs[:, :, k * row_count : (k + 1) * row_count], value_block
+                )
+            near_msg = near_out
+            far_part = (
+                jnp.concatenate([near_out, far_part[0]], axis=1),
+                jnp.concatenate([near_max, far_part[1]], axis=0),
+                jnp.concatenate([near_sum, far_part[2]], axis=0),
+            )
+        if s < reach:
+            msg = jnp.concatenate([near_msg.astype(jnp.bfloat16), far_part[0].astype(jnp.bfloat16)], axis=1)
+        else:
+            msg = far_part[0].astype(jnp.bfloat16)
+        msg_in = shift_up(msg, 1, n_seq)
+        stats_in = shift_up(jnp.stack([far_part[1], far_part[2]]), 1, n_seq)
+        if s < reach:
+            near_values.append(msg_in[:, :split])
+            far_running = received(msg_in[:, split:], stats_in)
+        else:
+            running_in = received(msg_in, stats_in)
 
     diag_probs, diag_max, diag_sum = diag
-    diag_out = jnp.einsum(
-        "hqk,khd->qhd", diag_probs, value_blocks[0], preferred_element_type=jnp.float32
-    )
-    mixed, row_max, row_sum = merge((out_in, max_in, sum_in), (diag_out, diag_max, diag_sum))
+    diag_out = mix(diag_probs, value_own)
+    mixed, row_max, row_sum = merge(running_in, (diag_out, diag_max, diag_sum))
     soft_out = mixed / jnp.transpose(row_sum)[:, :, None]
     return (lin_out, soft_out.astype(jnp.bfloat16).reshape(row_count, width))
 

time: 144 us -> 167 us (1.16)
  waiting for transfers between devices: 54.1 us -> 66.4 us
  local copies, waits for them, and re-layouts: 10.4 us -> 18.4 us
  matrix products: 30.8 us -> 27.5 us
  other arithmetic: 14.8 us -> 17.4 us
  starting transfers between devices: 27.9 us -> 30.3 us
    ppermute x1 -> x2, waiting for transfers between devices: 0.01 us -> 11.2 us  [shift_down(): return lax.ppermute(x, 'seq', [(s + dist, s) for s in range(n_seq - dist)])]
    dot_general x2 -> x4, matrix products: 10.1 us -> 4.86 us  [weights_of(): jnp.einsum('qhd,khd->hqk', query_rows, key_all, preferred_element_type=jn...]
    unnamed x22 -> x47, local copies, waits for them, and re-layouts: 0.06 us -> 5.04 us
    dot_general x3 -> x5, matrix products: 7.47 us -> 9.81 us  [mix(): jnp.einsum('hqk,khd->qhd', weights, value_block, preferred_element_type=j...]
    reshape x2 -> x3, local copies, waits for them, and re-layouts: 3.15 us -> 4.41 us  [the longest x2 3.01 us: per_device(): m[:, :split * HD].reshape(row_count, split, HD)]
    ppermute x6 -> x7, waiting for transfers between devices: 54.1 us -> 55.2 us  [shift_up(): return lax.ppermute(x, 'seq', [(s, s + dist) for s in range(n_seq - dist)])]
    ppermute x6 -> x7, starting transfers between devices: 26.6 us -> 27.6 us  [shift_up(): return lax.ppermute(x, 'seq', [(s, s + dist) for s in range(n_seq - dist)])]
    reduce_sum x2 -> x4, other arithmetic: 7.06 us -> 7.69 us  [weights_of(): return (probs.astype(jnp.bfloat16), row_max, jnp.sum(probs, axis=-1))]
  transfers between devices with their start and end apart: 7 -> 9, of which waited for: 3 -> 5; matrix products, arithmetic and copies ran while one was open for 28% -> 19% of each run, Pallas kernels for 0% -> 0%
where the time goes in v8:
time: 167 us; the launch traced here: 166 us
  waiting for transfers between devices  66.4 us (40%)
  starting transfers between devices  30.3 us (18%)
  matrix products  27.5 us (16%)
  local copies, waits for them, and re-layouts  18.4 us (11%)
  other arithmetic  17.4 us (10%)
  between operations  5.63 us (3%)
    ppermute x7, waiting for transfers between devices, shift_up(): return lax.ppermute(x, 'seq', [(s, s + dist) for s in range(n_seq - dist)])  55.2 us
    ppermute x7, starting transfers between devices, shift_up(): return lax.ppermute(x, 'seq', [(s, s + dist) for s in range(n_seq - dist)])  27.6 us
    ppermute x2, waiting for transfers between devices, shift_down(): return lax.ppermute(x, 'seq', [(s + dist, s) for s in range(n_seq - dist)])  11.2 us
    dot_general x5, matrix products, mix(): jnp.einsum('hqk,khd->qhd', weights, value_block, preferred_element_type=j...  9.81 us
    reduce_sum x4, other arithmetic, weights_of(): return (probs.astype(jnp.bfloat16), row_max, jnp.sum(probs, axis=-1))  7.69 us
    dot_general x1, matrix products, per_device(): jnp.einsum('hqk,khd->qhd', rounded, value_rows, preferred_element_type=jn...  5.49 us
    unnamed x47, local copies, waits for them, and re-layouts  5.04 us
    dot_general x4, matrix products, weights_of(): jnp.einsum('qhd,khd->hqk', query_rows, key_all, preferred_element_type=jn...  4.86 us
  transfers between devices with their start and end apart: 9, of which 5 were waited for; matrix products, arithmetic and copies ran while one was open for 19% of the time, Pallas kernels for 0%

profile of v8, /device:TPU:0, one launch (start us, length us, event | category | flops | bytes accessed | tf_op | source)
XLA Modules:
  0.0 165.7 jit_solution(8330654782733559247)
XLA Ops:
  1.5 1.3 slice_bitcast_fusion.3
  3.9 5.8 %collective-permute-start.3 = (bf16[320,1152]{1,0:T(8,128)(2,1)}, bf16[320,1152]{1,0:T(8,128)(2,1)}, u32[]{:S(2)}, u32[]{:S(2)}) collective-permute-start(bf16[320,1152]{1,0:T(8,128)(2,1)} %pad_maximum_fusion.3), channel_id=1, source_target_pairs={{0,4},{4,8},{8,12},{1,5},{5,9},{9,13},{2,6},{6,10},{10,14},{3,7},{... | collective-permute-start | bytes 2211848 | tf_op jit(solution)/shard_map/ppermute | solution.py:15
  10.9 1.9 %broadcast_compare_fusion.3 = (pred[320]{0:T(512)(128)(4,1)}, pred[320]{0:T(512)(128)(4,1)S(1)}) fusion(s32[320]{0:T(512)S(1)} %copy-done.12, s32[]{:T(128)} %bitcast.1, s32[]{:T(128)} %bitcast.2), kind=kLoop, calls=%fused_computation.151 | loop fusion | flops 640 | bytes 1928 | tf_op jit(solution)/shard_map/eq | solution.py:125
  12.8 3.4 %fusion.141 = (bf16[16,128,128]{2,1,0:T(8,128)(2,1)S(1)}, f32[16,128,128]{2,1,0:T(8,128)}) fusion(pred[320]{0:T(512)(128)(4,1)S(1)} %get-tuple-element.19, bf16[320,2048]{1,0:T(8,128)(2,1)S(1)} %copy-done.21, bf16[320,2048]{1,0:T(8,128)(2,1)} %param.9), kind=kOutput, calls=%fused_computation.168 | convolution fusion | flops 168689664 | bytes 4194624 | tf_op jit(solution)/shard_map/thd,the->hde/dot_general | solution.py:51
  17.0 3.4 %collective-permute-start = (bf16[2056,128]{1,0:T(8,128)(2,1)}, bf16[2056,128]{1,0:T(8,128)(2,1)}, u32[]{:S(2)}, u32[]{:S(2)}) collective-permute-start(bf16[2056,128]{1,0:T(8,128)(2,1)} %concatenate.40), channel_id=1, source_target_pairs={{0,4},{4,8},{8,12},{1,5},{5,9},{9,13},{2,6},{6,10},{10,14},{3,7},{... | collective-permute-start | bytes 1579016 | tf_op jit(solution)/shard_map/ppermute | solution.py:15
  21.6 1.3 collective-permute-start.2
  24.2 1.4 copy_bitcast_fusion.2
  25.6 10.5 %collective-permute-done = bf16[2056,128]{1,0:T(8,128)(2,1)} collective-permute-done((bf16[2056,128]{1,0:T(8,128)(2,1)}, bf16[2056,128]{1,0:T(8,128)(2,1)}, u32[]{:S(2)}, u32[]{:S(2)}) %collective-permute-start) | collective-permute-done | bytes 526368 | tf_op jit(solution)/shard_map/ppermute | solution.py:15
  39.9 4.4 %collective-permute-start.1 = (bf16[2056,128]{1,0:T(8,128)(2,1)S(1)}, bf16[2056,128]{1,0:T(8,128)(2,1)S(1)}, u32[]{:S(2)}, u32[]{:S(2)}) collective-permute-start(bf16[2056,128]{1,0:T(8,128)(2,1)S(1)} %concatenate.41), channel_id=1, source_target_pairs={{0,4},{4,8},{8,12},{1,5},{5,9},{9,13},{2,6},{6,10},{10,14},{3,7},{... | collective-permute-start | bytes 1579016 | tf_op jit(solution)/shard_map/ppermute | solution.py:15
  47.6 2.0 %copy_bitcast_fusion.3 = bf16[320,8,128]{2,0,1:T(8,128)(2,1)} fusion(bf16[320,1152]{1,0:T(8,128)(2,1)} %collective-permute-done.3), kind=kLoop, calls=%fused_computation.101 | loop fusion | bytes 1310720 | tf_op jit(solution)/shard_map/reshape | solution.py:88
  49.7 5.0 %collective-permute-done.1 = bf16[2056,128]{1,0:T(8,128)(2,1)S(1)} collective-permute-done((bf16[2056,128]{1,0:T(8,128)(2,1)S(1)}, bf16[2056,128]{1,0:T(8,128)(2,1)S(1)}, u32[]{:S(2)}, u32[]{:S(2)}) %collective-permute-start.1) | collective-permute-done | bytes 526368 | tf_op jit(solution)/shard_map/ppermute | solution.py:15
  56.6 1.4 slice_bitcast_fusion
  58.5 1.3 concatenate.53
  59.7 1.5 collective-permute-start.4
  62.5 1.5 fusion.1
  64.0 3.6 %fusion.4 = (f32[8,320]{1,0:T(8,128)S(1)}, bf16[8,320,640]{2,1,0:T(8,128)(2,1)}) fusion(f32[8,320,640]{2,1,0:T(8,128)S(1)} %get-tuple-element.33, f32[8,320]{1,0:T(8,128)S(1)} %get-tuple-element.32, pred[320,640]{1,0:T(8,128)(4,1)S(1)} %compare_and_fusion), kind=kLoop, calls=%fused_computation.9 | loop fusion | flops 9827840 | bytes 10055680 | tf_op jit(solution)/shard_map/reduce_sum | solution.py:105
  67.7 11.2 %collective-permute-done.4 = bf16[320,1152]{1,0:T(8,128)(2,1)S(1)} collective-permute-done((bf16[320,1152]{1,0:T(8,128)(2,1)S(1)}, bf16[320,1152]{1,0:T(8,128)(2,1)S(1)}, u32[]{:S(2)}, u32[]{:S(2)}) %collective-permute-start.4) | collective-permute-done | bytes 737312 | tf_op jit(solution)/shard_map/ppermute | solution.py:19
  79.8 5.5 %fusion.8 = f32[16,320,128]{2,1,0:T(8,128)} fusion(pred[320,320]{0,1:T(8,128)(4,1)S(1)} %get-tuple-element.17, bf16[320,2048]{1,0:T(8,128)(2,1)} %param.10, bf16[320,2048]{1,0:T(8,128)(2,1)} %param.9, bf16[320,2048]{1,0:T(8,128)(2,1)S(1)} %copy-done), kind=kOutput, calls=%fused_computation.12 | convolution fusion | flops 842137600 | bytes 6656000 | tf_op jit(solution)/shard_map/hqk,khd->qhd/dot_general | solution.py:120
  85.3 4.0 %multiply_reduce_fusion = (f32[320,16]{0,1:T(8,128)S(1)}, f32[320,16,128]{2,0,1:T(8,128)S(1)}) fusion(f32[16,128,128]{2,1,0:T(8,128)S(1)} %bitcast.202, pred[320]{0:T(512)(128)(4,1)S(1)} %copy-done.20, f32[16,320,128]{2,1,0:T(8,128)} %fusion.8, bf16[320,2048]{1,0:T(8,128)(2,1)S(1)} %copy-done), kind=kOutput, calls=%fused_computation.39 | convolution fusion | flops 1009249280 | bytes 7622976 | tf_op jit(solution)/shard_map/qhd,hde->qhe/dot_general | solution.py:121
  92.6 1.4 fusion.82
  94.1 3.6 %collective-permute-start.6 = (f32[2,8,320]{2,1,0:T(8,128)S(1)}, f32[2,8,320]{2,1,0:T(8,128)S(1)}, u32[]{:S(2)}, u32[]{:S(2)}) collective-permute-start(f32[2,8,320]{2,1,0:T(8,128)S(1)} %pad_maximum_fusion.5), channel_id=1, source_target_pairs={{0,4},{4,8},{8,12},{1,5},{5,9},{9,13},{2,6},{6,10},{10,14},{3,7},{... | collective-permute-start | bytes 61448 | tf_op jit(solution)/shard_map/ppermute | solution.py:15
  97.9 3.7 %collective-permute-start.5 = (bf16[320,16,128]{2,0,1:T(8,128)(2,1)S(1)}, bf16[320,16,128]{2,0,1:T(8,128)(2,1)S(1)}, u32[]{:S(2)}, u32[]{:S(2)}) collective-permute-start(bf16[320,16,128]{2,0,1:T(8,128)(2,1)S(1)} %pad_maximum_fusion.1), channel_id=1, source_target_pairs={{0,4},{4,8},{8,12},{1,5},{5,9},{9,13},{2,6},{6,10},{10,14},{3,7},{... | collective-permute-start | bytes 3932168 | tf_op jit(solution)/shard_map/ppermute | solution.py:15
  104.1 1.7 %fusion = (f32[16,320]{1,0:T(8,128)S(1)}, f32[16,320,320]{1,2,0:T(8,128)S(1)}) fusion(pred[320,320]{0,1:T(8,128)(4,1)S(1)} %get-tuple-element.17, bf16[320,2048]{1,0:T(8,128)(2,1)S(1)} %copy-done.7, bf16[320,2048]{1,0:T(8,128)(2,1)S(1)} %copy-done.4), kind=kOutput, calls=%fused_computation.3 | convolution fusion | flops 424340480 | bytes 9297920 | tf_op jit(solution)/shard_map/qhd,khd->hqk/dot_general | solution.py:99
  106.8 19.8 %collective-permute-done.5 = bf16[320,16,128]{2,0,1:T(8,128)(2,1)S(1)} collective-permute-done((bf16[320,16,128]{2,0,1:T(8,128)(2,1)S(1)}, bf16[320,16,128]{2,0,1:T(8,128)(2,1)S(1)}, u32[]{:S(2)}, u32[]{:S(2)}) %collective-permute-start.5) | collective-permute-done | bytes 1310752 | tf_op jit(solution)/shard_map/ppermute | solution.py:15
  127.4 2.0 %add_convert_fusion = bf16[320,8,128]{2,0,1:T(8,128)(2,1)S(1)} fusion(bf16[320,16,128]{2,0,1:T(8,128)(2,1)S(1)} %collective-permute-done.5, f32[320,8]{0,1:T(8,128)S(1)} %get-tuple-element.14, bf16[320,16,128]{2,0,1:T(8,128)(2,1)S(1)} %fusion.24, f32[8,320,320]{1,2,0:T(8,128)S(1)} %get-tuple-element.31, f32[8,320]{1,0:T(8,128)S(1)} %get-tuple-element.30, ...), kind=kOutput, calls=%fused_computation.83 | convolution fusion | flops 215777280 | bytes 6031361 | tf_op jit(solution)/shard_map/hqk,khd->qhd/dot_general | solution.py:143
  129.5 4.5 %collective-permute-start.7 = (bf16[320,16,128]{2,0,1:T(8,128)(2,1)S(1)}, bf16[320,16,128]{2,0,1:T(8,128)(2,1)S(1)}, u32[]{:S(2)}, u32[]{:S(2)}) collective-permute-start(bf16[320,16,128]{2,0,1:T(8,128)(2,1)S(1)} %pad_maximum_fusion.2), channel_id=1, source_target_pairs={{0,4},{4,8},{8,12},{1,5},{5,9},{9,13},{2,6},{6,10},{10,14},{3,7},{... | collective-permute-start | bytes 3932168 | tf_op jit(solution)/shard_map/ppermute | solution.py:15
  134.0 2.0 %fusion.2 = f32[16,320]{1,0:T(8,128)S(1)} fusion(f32[16,320,320]{1,2,0:T(8,128)S(1)} %get-tuple-element.27, f32[16,320]{1,0:T(8,128)S(1)} %get-tuple-element.26, pred[320,320]{0,1:T(8,128)(4,1)S(1)} %get-tuple-element.17), kind=kLoop, calls=%fused_computation.7 | loop fusion | flops 8186880 | bytes 6696960 | tf_op jit(solution)/shard_map/reduce_sum | solution.py:105
  136.1 2.1 %collective-permute-start.8 = (f32[2,16,320]{2,1,0:T(8,128)S(1)}, f32[2,16,320]{2,1,0:T(8,128)S(1)}, u32[]{:S(2)}, u32[]{:S(2)}) collective-permute-start(f32[2,16,320]{2,1,0:T(8,128)S(1)} %pad_maximum_fusion.4), channel_id=1, source_target_pairs={{0,4},{4,8},{8,12},{1,5},{5,9},{9,13},{2,6},{6,10},{10,14},{3,7},{... | collective-permute-start | bytes 122888 | tf_op jit(solution)/shard_map/ppermute | solution.py:15
  138.2 1.3 copy_bitcast_fusion.1
  139.4 19.9 %collective-permute-done.8 = f32[2,16,320]{2,1,0:T(8,128)S(1)} collective-permute-done((f32[2,16,320]{2,1,0:T(8,128)S(1)}, f32[2,16,320]{2,1,0:T(8,128)S(1)}, u32[]{:S(2)}, u32[]{:S(2)}) %collective-permute-start.8) | collective-permute-done | bytes 40992 | tf_op jit(solution)/shard_map/ppermute | solution.py:15
  159.3 4.9 %fusion.57 = bf16[16,40,8,128]{3,2,1,0:T(8,128)(2,1)S(1)} fusion(bf16[320,16,128]{2,0,1:T(8,128)(2,1)S(1)} %fusion.24, f32[16,320,320]{1,2,0:T(8,128)S(1)} %get-tuple-element.27, f32[16,320]{1,0:T(8,128)S(1)} %get-tuple-element.26, pred[320,320]{0,1:T(8,128)(4,1)S(1)} %get-tuple-element.17, bf16[320,16,128]{2,0,1:T(8,128)(2,1)S(1)} %collective-permute-done.7, ...), kind=kOutput, calls=%fused_computation.59 | convolution fusion | flops 432209920 | bytes 10670081 | tf_op jit(solution)/shard_map/hqk,khd->qhd/dot_general | solution.py:143
  164.2 1.4 copy.117
  (90 shorter events, 21.3 us)
Async XLA Ops:
  0.6 79.2 %copy-start = (bf16[320,2048]{1,0:T(8,128)(2,1)S(1)}, bf16[320,2048]{1,0:T(8,128)(2,1)}, u32[]{:S(2)}) copy-start(bf16[320,2048]{1,0:T(8,128)(2,1)} %param.8) | copy-start | bytes 3932164
  0.6 9.0 %copy-start.12 = (s32[320]{0:T(512)S(1)}, s32[320]{0:T(512)}, u32[]{:S(2)}) copy-start(s32[320]{0:T(512)} %param.15) | copy-start | bytes 3844
  0.7 12.1 %copy-start.21 = (bf16[320,2048]{1,0:T(8,128)(2,1)S(1)}, bf16[320,2048]{1,0:T(8,128)(2,1)}, u32[]{:S(2)}) copy-start(bf16[320,2048]{1,0:T(8,128)(2,1)} %param.10) | copy-start | bytes 3932164
  1.5 11.3 %copy-start.14 = (bf16[320]{0:T(512)(128)(2,1)}, bf16[320]{0:T(512)(128)(2,1)S(1)}, u32[]{:S(2)}) copy-start(bf16[320]{0:T(512)(128)(2,1)S(1)} %convert_element_type.93) | copy-start | bytes 1924
  3.9 42.0 %collective-permute-start.3 = (bf16[320,1152]{1,0:T(8,128)(2,1)}, bf16[320,1152]{1,0:T(8,128)(2,1)}, u32[]{:S(2)}, u32[]{:S(2)}) collective-permute-start(bf16[320,1152]{1,0:T(8,128)(2,1)} %pad_maximum_fusion.3), channel_id=1, source_target_pairs={{0,4},{4,8},{8,12},{1,5},{5,9},{9,13},{2,6},{6,10},{10,14},{3,7},{... | collective-permute-start | bytes 2211848 | tf_op jit(solution)/shard_map/ppermute | solution.py:15
  12.8 7.6 %copy-start.6 = (bf16[320,2048]{1,0:T(8,128)(2,1)S(1)}, bf16[320,2048]{1,0:T(8,128)(2,1)}, u32[]{:S(2)}) copy-start(bf16[320,2048]{1,0:T(8,128)(2,1)} %param.13) | copy-start | bytes 3932164
  16.1 8.0 %copy-start.3 = (bf16[320,2048]{1,0:T(8,128)(2,1)S(1)}, bf16[320,2048]{1,0:T(8,128)(2,1)}, u32[]{:S(2)}) copy-start(bf16[320,2048]{1,0:T(8,128)(2,1)} %param.14) | copy-start | bytes 3932164
  17.0 19.1 %collective-permute-start = (bf16[2056,128]{1,0:T(8,128)(2,1)}, bf16[2056,128]{1,0:T(8,128)(2,1)}, u32[]{:S(2)}, u32[]{:S(2)}) collective-permute-start(bf16[2056,128]{1,0:T(8,128)(2,1)} %concatenate.40), channel_id=1, source_target_pairs={{0,4},{4,8},{8,12},{1,5},{5,9},{9,13},{2,6},{6,10},{10,14},{3,7},{... | collective-permute-start | bytes 1579016 | tf_op jit(solution)/shard_map/ppermute | solution.py:15
  21.6 34.9 %collective-permute-start.2 = (bf16[320,2176]{1,0:T(8,128)(2,1)}, bf16[320,2176]{1,0:T(8,128)(2,1)}, u32[]{:S(2)}, u32[]{:S(2)}) collective-permute-start(bf16[320,2176]{1,0:T(8,128)(2,1)} %pad_maximum_fusion), channel_id=1, source_target_pairs={{4,0},{8,4},{12,8},{5,1},{9,5},{13,9},{6,2},{10,6},{14,10},{7,3},{... | collective-permute-start | bytes 4177928 | tf_op jit(solution)/shard_map/ppermute | solution.py:19
  25.6 14.2 %copy-start.9 = (f32[16,128,128]{2,1,0:T(8,128)S(1)}, f32[16,128,128]{2,1,0:T(8,128)}, u32[]{:S(2)}) copy-start(f32[16,128,128]{2,1,0:T(8,128)} %get-tuple-element.23) | copy-start | bytes 3145732
  39.7 4.6 %copy-start.19 = (bf16[2048]{0:T(1024)(128)(2,1)S(1)}, bf16[2048]{0:T(1024)(128)(2,1)}, u32[]{:S(2)}) copy-start(bf16[2048]{0:T(1024)(128)(2,1)} %param.11) | copy-start | bytes 12292
  39.9 7.0 %copy-start.15 = (bf16[320]{0:T(512)(128)(2,1)S(1)}, bf16[320]{0:T(512)(128)(2,1)}, u32[]{:S(2)}) copy-start(bf16[320]{0:T(512)(128)(2,1)} %copy-done.14) | copy-start | bytes 1924
  39.9 14.7 %collective-permute-start.1 = (bf16[2056,128]{1,0:T(8,128)(2,1)S(1)}, bf16[2056,128]{1,0:T(8,128)(2,1)S(1)}, u32[]{:S(2)}, u32[]{:S(2)}) collective-permute-start(bf16[2056,128]{1,0:T(8,128)(2,1)S(1)} %concatenate.41), channel_id=1, source_target_pairs={{0,4},{4,8},{8,12},{1,5},{5,9},{9,13},{2,6},{6,10},{10,14},{3,7},{... | collective-permute-start | bytes 1579016 | tf_op jit(solution)/shard_map/ppermute | solution.py:15
  58.3 3.9 %copy-start.13 = (s32[640]{0:T(1024)S(1)}, s32[640]{0:T(1024)}, u32[]{:S(2)}) copy-start(s32[640]{0:T(1024)} %maximum_convert_fusion) | copy-start | bytes 7684
  58.3 3.9 %copy-start.18 = (pred[640]{0:T(1024)(128)(4,1)S(1)}, pred[640]{0:T(1024)(128)(4,1)}, u32[]{:S(2)}) copy-start(pred[640]{0:T(1024)(128)(4,1)} %concatenate.46) | copy-start | bytes 1924
  58.4 4.1 %copy-start.10 = (bf16[40,8,8,128]{3,2,0,1:T(8,128)(2,1)S(1)}, bf16[40,8,8,128]{3,2,0,1:T(8,128)(2,1)}, u32[]{:S(2)}) copy-start(bf16[40,8,8,128]{3,2,0,1:T(8,128)(2,1)} %copy.118) | copy-start | bytes 1966084
  58.4 4.1 %copy-start.11 = (bf16[320,8,128]{2,0,1:T(8,128)(2,1)S(1)}, bf16[320,8,128]{2,0,1:T(8,128)(2,1)}, u32[]{:S(2)}) copy-start(bf16[320,8,128]{2,0,1:T(8,128)(2,1)} %copy_bitcast_fusion.3) | copy-start | bytes 1966084
  59.7 19.2 %collective-permute-start.4 = (bf16[320,1152]{1,0:T(8,128)(2,1)S(1)}, bf16[320,1152]{1,0:T(8,128)(2,1)S(1)}, u32[]{:S(2)}, u32[]{:S(2)}) collective-permute-start(bf16[320,1152]{1,0:T(8,128)(2,1)S(1)} %concatenate.53), channel_id=1, source_target_pairs={{4,0},{8,4},{12,8},{5,1},{9,5},{13,9},{6,2},{10,6},{14,10},{7,3},{... | collective-permute-start | bytes 2211848 | tf_op jit(solution)/shard_map/ppermute | solution.py:19
  78.9 0.9 copy-start.16
  79.8 5.5 %copy-start.20 = (pred[320]{0:T(512)(128)(4,1)S(1)}, pred[320]{0:T(512)(128)(4,1)}, u32[]{:S(2)}) copy-start(pred[320]{0:T(512)(128)(4,1)} %get-tuple-element.18) | copy-start | bytes 964
  85.3 4.0 %copy-start.5 = (bf16[320,2048]{1,0:T(8,128)(2,1)S(1)}, bf16[320,2048]{1,0:T(8,128)(2,1)}, u32[]{:S(2)}) copy-start(bf16[320,2048]{1,0:T(8,128)(2,1)} %param.12) | copy-start | bytes 3932164
  89.3 1.3 copy-start.8
  89.3 1.5 copy-start.17
  94.1 12.6 %collective-permute-start.6 = (f32[2,8,320]{2,1,0:T(8,128)S(1)}, f32[2,8,320]{2,1,0:T(8,128)S(1)}, u32[]{:S(2)}, u32[]{:S(2)}) collective-permute-start(f32[2,8,320]{2,1,0:T(8,128)S(1)} %pad_maximum_fusion.5), channel_id=1, source_target_pairs={{0,4},{4,8},{8,12},{1,5},{5,9},{9,13},{2,6},{6,10},{10,14},{3,7},{... | collective-permute-start | bytes 61448 | tf_op jit(solution)/shard_map/ppermute | solution.py:15
  97.9 28.7 %collective-permute-start.5 = (bf16[320,16,128]{2,0,1:T(8,128)(2,1)S(1)}, bf16[320,16,128]{2,0,1:T(8,128)(2,1)S(1)}, u32[]{:S(2)}, u32[]{:S(2)}) collective-permute-start(bf16[320,16,128]{2,0,1:T(8,128)(2,1)S(1)} %pad_maximum_fusion.1), channel_id=1, source_target_pairs={{0,4},{4,8},{8,12},{1,5},{5,9},{9,13},{2,6},{6,10},{10,14},{3,7},{... | collective-permute-start | bytes 3932168 | tf_op jit(solution)/shard_map/ppermute | solution.py:15
  102.4 1.3 copy-start.4
  102.4 1.7 %copy-start.7 = (bf16[320,2048]{1,0:T(8,128)(2,1)S(1)}, bf16[320,2048]{1,0:T(8,128)(2,1)}, u32[]{:S(2)}) copy-start(bf16[320,2048]{1,0:T(8,128)(2,1)} %param.13) | copy-start | bytes 3932164
  104.1 1.9 %copy-start.2 = (bf16[8,320,640]{2,1,0:T(8,128)(2,1)S(1)}, bf16[8,320,640]{2,1,0:T(8,128)(2,1)}, u32[]{:S(2)}) copy-start(bf16[8,320,640]{2,1,0:T(8,128)(2,1)} %get-tuple-element.5) | copy-start | bytes 9830404
  129.5 29.8 %collective-permute-start.7 = (bf16[320,16,128]{2,0,1:T(8,128)(2,1)S(1)}, bf16[320,16,128]{2,0,1:T(8,128)(2,1)S(1)}, u32[]{:S(2)}, u32[]{:S(2)}) collective-permute-start(bf16[320,16,128]{2,0,1:T(8,128)(2,1)S(1)} %pad_maximum_fusion.2), channel_id=1, source_target_pairs={{0,4},{4,8},{8,12},{1,5},{5,9},{9,13},{2,6},{6,10},{10,14},{3,7},{... | collective-permute-start | bytes 3932168 | tf_op jit(solution)/shard_map/ppermute | solution.py:15
  136.1 23.2 %collective-permute-start.8 = (f32[2,16,320]{2,1,0:T(8,128)S(1)}, f32[2,16,320]{2,1,0:T(8,128)S(1)}, u32[]{:S(2)}, u32[]{:S(2)}) collective-permute-start(f32[2,16,320]{2,1,0:T(8,128)S(1)} %pad_maximum_fusion.4), channel_id=1, source_target_pairs={{0,4},{4,8},{8,12},{1,5},{5,9},{9,13},{2,6},{6,10},{10,14},{3,7},{... | collective-permute-start | bytes 122888 | tf_op jit(solution)/shard_map/ppermute | solution.py:15
  159.3 6.3 %copy-start.1 = (bf16[320,2048]{1,0:T(8,128)(2,1)S(1)}, bf16[320,2048]{1,0:T(8,128)(2,1)}, u32[]{:S(2)}) copy-start(bf16[320,2048]{1,0:T(8,128)(2,1)} %param.8) | copy-start | bytes 3932164

commit v9 on v6

--- a/solution.py
+++ b/solution.py
@@ -27,6 +27,66 @@
     scale_b = jnp.exp(max_b - top)
     out = out_a * jnp.transpose(scale_a)[:, :, None] + out_b * jnp.transpose(scale_b)[:, :, None]
     return out, top, sum_a * scale_a + sum_b * scale_b
+
+
+def general_softmax(soft_query, soft_key, doc_id, doc_cols, lin_out, diag, reach, n_seq, my_index):
+    row_count, width = soft_query.shape
+    head_count = width // HD
+    dists = list(range(1, reach + 1))
+    score_scale = 1.0 / math.sqrt(HD)
+
+    def weights_of(query_rows, keep):
+        logits = (
+            jnp.einsum("qhd,khd->hqk", query_rows, key_all, preferred_element_type=jnp.float32)
+            * score_scale
+        )
+        logits = jnp.where(keep[None], logits, -1e30)
+        row_max = jnp.max(logits, axis=-1)
+        probs = jnp.where(keep[None], jnp.exp(logits - row_max[..., None]), 0.0)
+        return probs.astype(jnp.bfloat16), row_max, jnp.sum(probs, axis=-1)
+
+    next_msg = shift_down(jnp.concatenate([soft_query, doc_cols], axis=1), 1, n_seq)
+    next_queries = next_msg[:, :width].reshape(row_count, head_count, HD)
+    next_docs = next_msg[:, width].astype(jnp.int32)
+    key_msgs = [jnp.concatenate([soft_key, doc_cols], axis=1)]
+    for d in dists[:-1]:
+        key_msgs.append(shift_up(key_msgs[-1], 1, n_seq))
+    key_blocks = [m[:, :width].reshape(row_count, head_count, HD) for m in key_msgs]
+    key_docs = [m[:, width].astype(jnp.int32) for m in key_msgs]
+
+    key_all = jnp.concatenate(key_blocks, axis=0)
+    valid = jnp.concatenate(
+        [jnp.full((row_count,), my_index >= d, jnp.bool_) for d in range(len(key_blocks))]
+    )
+    keep_next = (next_docs[:, None] == jnp.concatenate(key_docs)[None, :]) & valid[None, :]
+    ahead = weights_of(next_queries, keep_next)
+
+    value_blocks = [lin_out.reshape(row_count, head_count, HD)]
+    for d in dists[:-1]:
+        value_blocks.append(shift_up(value_blocks[-1], 1, n_seq))
+
+    probs, ahead_max, ahead_sum = ahead
+    ahead_out = jnp.zeros((row_count, head_count, HD), jnp.float32)
+    for d, value_block in enumerate(value_blocks):
+        ahead_out = ahead_out + jnp.einsum(
+            "hqk,khd->qhd",
+            probs[:, :, d * row_count : (d + 1) * row_count],
+            value_block,
+            preferred_element_type=jnp.float32,
+        )
+    out_in = shift_up(ahead_out.astype(jnp.bfloat16), 1, n_seq)
+    stats_in = shift_up(jnp.stack([ahead_max, ahead_sum]), 1, n_seq)
+    has_source = my_index >= 1
+    max_in = jnp.where(has_source, stats_in[0], -1e30)
+    sum_in = jnp.where(has_source, stats_in[1], 0.0)
+    out_in = jnp.where(has_source, out_in.astype(jnp.float32), 0.0)
+
+    diag_probs, diag_max, diag_sum = diag
+    diag_out = jnp.einsum(
+        "hqk,khd->qhd", diag_probs, value_blocks[0], preferred_element_type=jnp.float32
+    )
+    mixed, row_max, row_sum = merge((out_in, max_in, sum_in), (diag_out, diag_max, diag_sum))
+    return mixed, row_max, row_sum
 
 
 def per_device(lin_query, lin_key, lin_value, norm_gain, out_gate, soft_query, soft_key, doc_id):
@@ -65,38 +125,10 @@
         else:
             carried = jnp.where(joins, state_in, jnp.zeros_like(state_in))
 
-    next_msg = shift_down(jnp.concatenate([soft_query, doc_cols], axis=1), 1, n_seq)
-    next_queries = next_msg[:, :width].reshape(row_count, head_count, HD)
-    next_docs = next_msg[:, width].astype(jnp.int32)
-    key_msgs = [jnp.concatenate([soft_key, doc_cols], axis=1)]
-    for d in dists[:-1]:
-        key_msgs.append(shift_up(key_msgs[-1], 1, n_seq))
-    key_blocks = [m[:, :width].reshape(row_count, head_count, HD) for m in key_msgs]
-    key_docs = [m[:, width].astype(jnp.int32) for m in key_msgs]
-
     positions = jnp.arange(row_count, dtype=jnp.int32)
     causal = positions[:, None] >= positions[None, :]
     keep_local = causal & (doc_id[:, None] == doc_id[None, :])
     score_scale = 1.0 / math.sqrt(HD)
-
-    def weights_of(query_rows, keep):
-        logits = (
-            jnp.einsum("qhd,khd->hqk", query_rows, key_all, preferred_element_type=jnp.float32)
-            * score_scale
-        )
-        logits = jnp.where(keep[None], logits, -1e30)
-        row_max = jnp.max(logits, axis=-1)
-        probs = jnp.where(keep[None], jnp.exp(logits - row_max[..., None]), 0.0)
-        return probs.astype(jnp.bfloat16), row_max, jnp.sum(probs, axis=-1)
-
-    key_all = key_blocks[0]
-    diag = weights_of(soft_query.reshape(row_count, head_count, HD), keep_local)
-    key_all = jnp.concatenate(key_blocks, axis=0)
-    valid = jnp.concatenate(
-        [jnp.full((row_count,), my_index >= d, jnp.bool_) for d in range(len(key_blocks))]
-    )
-    keep_next = (next_docs[:, None] == jnp.concatenate(key_docs)[None, :]) & valid[None, :]
-    ahead = weights_of(next_queries, keep_next)
 
     scores = jnp.einsum("qhd,khd->hqk", queries, key_rows, preferred_element_type=jnp.float32)
     rounded = jnp.where(keep_local[None], scores, jnp.zeros_like(scores)).astype(jnp.bfloat16)
@@ -114,31 +146,89 @@
     normed = lin_raw * lax.rsqrt(mean_square + norm_eps) * gain_rows * gate_rows
     lin_out = normed.astype(jnp.bfloat16).reshape(row_count, width)
 
-    value_blocks = [lin_out.reshape(row_count, head_count, HD)]
-    for d in dists[:-1]:
-        value_blocks.append(shift_up(value_blocks[-1], 1, n_seq))
-
-    probs, ahead_max, ahead_sum = ahead
-    ahead_out = jnp.zeros((row_count, head_count, HD), jnp.float32)
-    for d, value_block in enumerate(value_blocks):
-        ahead_out = ahead_out + jnp.einsum(
-            "hqk,khd->qhd",
-            probs[:, :, d * row_count : (d + 1) * row_count],
-            value_block,
-            preferred_element_type=jnp.float32,
-        )
-    out_in = shift_up(ahead_out.astype(jnp.bfloat16), 1, n_seq)
-    stats_in = shift_up(jnp.stack([ahead_max, ahead_sum]), 1, n_seq)
+    def weights_of(query_rows, key_all, keep):
+        logits = (
+            jnp.einsum("qhd,khd->hqk", query_rows, key_all, preferred_element_type=jnp.float32)
+            * score_scale
+        )
+        logits = jnp.where(keep[None], logits, -1e30)
+        row_max = jnp.max(logits, axis=-1)
+        probs = jnp.where(keep[None], jnp.exp(logits - row_max[..., None]), 0.0)
+        return probs.astype(jnp.bfloat16), row_max, jnp.sum(probs, axis=-1)
+
+    def mix(weights, value_block):
+        return jnp.einsum("hqk,khd->qhd", weights, value_block, preferred_element_type=jnp.float32)
+
     has_source = my_index >= 1
-    max_in = jnp.where(has_source, stats_in[0], -1e30)
-    sum_in = jnp.where(has_source, stats_in[1], 0.0)
-    out_in = jnp.where(has_source, out_in.astype(jnp.float32), 0.0)
-
-    diag_probs, diag_max, diag_sum = diag
-    diag_out = jnp.einsum(
-        "hqk,khd->qhd", diag_probs, value_blocks[0], preferred_element_type=jnp.float32
-    )
-    mixed, row_max, row_sum = merge((out_in, max_in, sum_in), (diag_out, diag_max, diag_sum))
+    query_soft = soft_query.reshape(row_count, head_count, HD)
+    key_soft = soft_key.reshape(row_count, head_count, HD)
+    value_own = lin_out.reshape(row_count, head_count, HD)
+    diag = weights_of(query_soft, key_soft, keep_local)
+    window = (max_doc - row_count + 1) // 2
+    if reach == 2 and n_seq >= 3 and 0 < window < row_count:
+        cut = row_count - window
+        query_msg = shift_down(jnp.concatenate([soft_query, doc_cols], axis=1), 1, n_seq)
+        next_queries = query_msg[:, :width].reshape(row_count, head_count, HD)
+        next_docs = query_msg[:, width].astype(jnp.int32)
+        far_msg = shift_down(query_msg[:window], 1, n_seq)
+        far_queries = far_msg[:, :width].reshape(window, head_count, HD)
+        far_docs = far_msg[:, width].astype(jnp.int32)
+        key_msg = shift_up(jnp.concatenate([soft_key, doc_cols], axis=1)[cut:], 1, n_seq)
+        tail_keys_soft = key_msg[:, :width].reshape(window, head_count, HD)
+        tail_docs = key_msg[:, width].astype(jnp.int32)
+        below_tail = has_source & (tail_docs[0] != tail_docs[-1])
+        own_tail = doc_id[cut] != doc_id[-1]
+
+        far_probs, far_max, far_sum = weights_of(
+            far_queries, key_soft, far_docs[:, None] == doc_id[None, :]
+        )
+        far_out = mix(far_probs, value_own)
+        stage_msg = jnp.where(own_tail, value_own[cut:], far_out.astype(jnp.bfloat16))
+        stage_in = shift_up(stage_msg, 1, n_seq)
+        stats_in = shift_up(jnp.stack([far_max, far_sum]), 1, n_seq)
+
+        keep_next = jnp.concatenate(
+            [
+                next_docs[:, None] == doc_id[None, :],
+                (next_docs[:, None] == tail_docs[None, :]) & below_tail,
+            ],
+            axis=1,
+        )
+        probs, next_max, next_sum = weights_of(
+            next_queries, jnp.concatenate([key_soft, tail_keys_soft], axis=0), keep_next
+        )
+        tail_values = jnp.where(below_tail, stage_in, jnp.zeros_like(stage_in))
+        next_out = mix(probs[:, :, :row_count], value_own) + mix(probs[:, :, row_count:], tail_values)
+        use_far = has_source & jnp.logical_not(below_tail)
+        pad = row_count - window
+        far_in = (
+            jnp.concatenate(
+                [jnp.where(use_far, stage_in.astype(jnp.float32), 0.0),
+                 jnp.zeros((pad, head_count, HD), jnp.float32)], axis=0
+            ),
+            jnp.concatenate(
+                [jnp.where(use_far, stats_in[0], -1e30),
+                 jnp.full((head_count, pad), -1e30, jnp.float32)], axis=1
+            ),
+            jnp.concatenate(
+                [jnp.where(use_far, stats_in[1], 0.0),
+                 jnp.zeros((head_count, pad), jnp.float32)], axis=1
+            ),
+        )
+        next_out, next_max, next_sum = merge(far_in, (next_out, next_max, next_sum))
+        out_in = shift_up(next_out.astype(jnp.bfloat16), 1, n_seq)
+        stats_in = shift_up(jnp.stack([next_max, next_sum]), 1, n_seq)
+        running_in = (
+            jnp.where(has_source, out_in.astype(jnp.float32), 0.0),
+            jnp.where(has_source, stats_in[0], -1e30),
+            jnp.where(has_source, stats_in[1], 0.0),
+        )
+        diag_probs, diag_max, diag_sum = diag
+        mixed, row_max, row_sum = merge(running_in, (mix(diag_probs, value_own), diag_max, diag_sum))
+    else:
+        mixed, row_max, row_sum = general_softmax(
+            soft_query, soft_key, doc_id, doc_cols, lin_out, diag, reach, n_seq, my_index
+        )
     soft_out = mixed / jnp.transpose(row_sum)[:, :, None]
     return (lin_out, soft_out.astype(jnp.bfloat16).reshape(row_count, width))
 

time: 144 us -> 153 us (1.062)
  waiting for transfers between devices: 54.1 us -> 43.8 us
  other arithmetic: 14.8 us -> 22 us
  starting transfers between devices: 27.9 us -> 32.7 us
  local copies, waits for them, and re-layouts: 10.4 us -> 12.8 us
  between operations: 5.8 us -> 8.19 us
    ppermute x6 -> x7, waiting for transfers between devices: 54.1 us -> 37.9 us  [shift_up(): return lax.ppermute(x, 'seq', [(s, s + dist) for s in range(n_seq - dist)])]
    ppermute x1 -> x2, waiting for transfers between devices: 0.01 us -> 5.97 us  [shift_down(): return lax.ppermute(x, 'seq', [(s + dist, s) for s in range(n_seq - dist)])]
    convert_element_type x0 -> x3, other arithmetic: none -> 5.05 us  [the longest x1 4.34 us: weights_of(): return (probs.astype(jnp.bfloat16), row_max, jnp.sum(probs, axis=-1))]
    reduce_sum x2, other arithmetic: 7.06 us -> 3.58 us  [weights_of(): return (probs.astype(jnp.bfloat16), row_max, jnp.sum(probs, axis=-1))]
    ppermute x6 -> x7, starting transfers between devices: 26.6 us -> 30 us  [shift_up(): return lax.ppermute(x, 'seq', [(s, s + dist) for s in range(n_seq - dist)])]
    dot_general x3 -> x4, matrix products: 7.47 us -> 9.98 us  [mix(): jnp.einsum('hqk,khd->qhd', weights, value_block, preferred_element_type=j...]
    select_n x1, other arithmetic: 0.07 us -> 2.08 us  [per_device(): carried = jnp.where(joins, state_in, jnp.zeros_like(state_in))]
    dot_general x1, matrix products: 3.97 us -> 2.18 us  [per_device(): jnp.einsum('qhd,hde->qhe', queries.astype(jnp.float32), carried, precisio...]
  transfers between devices with their start and end apart: 7 -> 9, of which waited for: 3 -> 5; matrix products, arithmetic and copies ran while one was open for 28% -> 20% of each run, Pallas kernels for 0% -> 0%
where the time goes in v9:
time: 153 us; the launch traced here: 152 us
  waiting for transfers between devices  43.8 us (29%)
  starting transfers between devices  32.7 us (21%)
  matrix products  32.3 us (21%)
  other arithmetic  22 us (14%)
  local copies, waits for them, and re-layouts  12.8 us (8%)
  between operations  8.19 us (5%)
    ppermute x7, waiting for transfers between devices, shift_up(): return lax.ppermute(x, 'seq', [(s, s + dist) for s in range(n_seq - dist)])  37.9 us
    ppermute x7, starting transfers between devices, shift_up(): return lax.ppermute(x, 'seq', [(s, s + dist) for s in range(n_seq - dist)])  30 us
    dot_general x3, matrix products, weights_of(): jnp.einsum('qhd,khd->hqk', query_rows, key_all, preferred_element_type=jn...  10.9 us
    dot_general x4, matrix products, mix(): jnp.einsum('hqk,khd->qhd', weights, value_block, preferred_element_type=j...  9.98 us
    ppermute x2, waiting for transfers between devices, shift_down(): return lax.ppermute(x, 'seq', [(s + dist, s) for s in range(n_seq - dist)])  5.97 us
    dot_general x1, matrix products, per_device(): jnp.einsum('hqk,khd->qhd', rounded, value_rows, preferred_element_type=jn...  5.58 us
    convert_element_type x1, other arithmetic, weights_of(): return (probs.astype(jnp.bfloat16), row_max, jnp.sum(probs, axis=-1))  4.34 us
    dot_general x1, matrix products, per_device(): jnp.einsum('thd,the->hde', tail_keys, value_rows, preferred_element_type=...  3.67 us
  transfers between devices with their start and end apart: 9, of which 5 were waited for; matrix products, arithmetic and copies ran while one was open for 20% of the time, Pallas kernels for 0%

profile of v9, /device:TPU:0, one launch (start us, length us, event | category | flops | bytes accessed | tf_op | source)
XLA Modules:
  0.0 151.9 jit_solution(14469377795763095183)
XLA Ops:
  0.6 1.5 fusion.111
  2.8 2.5 %broadcast_compare_fusion.3 = (pred[320]{0:T(512)(128)(4,1)}, pred[320]{0:T(512)(128)(4,1)S(1)}) fusion(s32[320]{0:T(512)} %param.15, s32[]{:T(128)} %bitcast.1, s32[]{:T(128)} %bitcast.2), kind=kLoop, calls=%fused_computation.135 | loop fusion | flops 640 | bytes 1928 | tf_op jit(solution)/shard_map/eq | solution.py:140
  5.3 3.7 %fusion.112 = (bf16[16,128,128]{2,1,0:T(8,128)(2,1)S(1)}, f32[16,128,128]{2,1,0:T(8,128)}) fusion(pred[320]{0:T(512)(128)(4,1)S(1)} %get-tuple-element.21, bf16[320,2048]{1,0:T(8,128)(2,1)} %param.10, bf16[320,2048]{1,0:T(8,128)(2,1)} %param.9), kind=kOutput, calls=%fused_computation.148 | convolution fusion | flops 168689664 | bytes 4194624 | tf_op jit(solution)/shard_map/thd,the->hde/dot_general | solution.py:111
  9.8 5.9 %collective-permute-start = (bf16[2056,128]{1,0:T(8,128)(2,1)}, bf16[2056,128]{1,0:T(8,128)(2,1)}, u32[]{:S(2)}, u32[]{:S(2)}) collective-permute-start(bf16[2056,128]{1,0:T(8,128)(2,1)} %concatenate.27), channel_id=1, source_target_pairs={{0,4},{4,8},{8,12},{1,5},{5,9},{9,13},{2,6},{6,10},{10,14},{3,7},{... | collective-permute-start | bytes 1579016 | tf_op jit(solution)/shard_map/ppermute | solution.py:15
  17.0 1.3 collective-permute-start.3
  19.2 4.6 %collective-permute-start.2 = (bf16[160,2176]{1,0:T(8,128)(2,1)}, bf16[160,2176]{1,0:T(8,128)(2,1)S(1)}, u32[]{:S(2)}, u32[]{:S(2)}) collective-permute-start(bf16[160,2176]{1,0:T(8,128)(2,1)} %pad_maximum_fusion.1), channel_id=1, source_target_pairs={{0,4},{4,8},{8,12},{1,5},{5,9},{9,13},{2,6},{6,10},{10,14},{3,7},{... | collective-permute-start | bytes 2088968 | tf_op jit(solution)/shard_map/ppermute | solution.py:15
  27.0 1.4 copy_bitcast_fusion.2
  28.4 1.3 slice.99
  32.1 1.4 add_convert_fusion
  34.3 4.3 %collective-permute-start.1 = (bf16[2056,128]{1,0:T(8,128)(2,1)}, bf16[2056,128]{1,0:T(8,128)(2,1)}, u32[]{:S(2)}, u32[]{:S(2)}) collective-permute-start(bf16[2056,128]{1,0:T(8,128)(2,1)} %concatenate.28), channel_id=1, source_target_pairs={{0,4},{4,8},{8,12},{1,5},{5,9},{9,13},{2,6},{6,10},{10,14},{3,7},{... | collective-permute-start | bytes 1579016 | tf_op jit(solution)/shard_map/ppermute | solution.py:15
  38.6 3.8 %collective-permute-done.2 = bf16[160,2176]{1,0:T(8,128)(2,1)S(1)} collective-permute-done((bf16[160,2176]{1,0:T(8,128)(2,1)}, bf16[160,2176]{1,0:T(8,128)(2,1)S(1)}, u32[]{:S(2)}, u32[]{:S(2)}) %collective-permute-start.2) | collective-permute-done | bytes 696352 | tf_op jit(solution)/shard_map/ppermute | solution.py:15
  46.1 6.5 %collective-permute-done.1 = bf16[2056,128]{1,0:T(8,128)(2,1)} collective-permute-done((bf16[2056,128]{1,0:T(8,128)(2,1)}, bf16[2056,128]{1,0:T(8,128)(2,1)}, u32[]{:S(2)}, u32[]{:S(2)}) %collective-permute-start.1) | collective-permute-done | bytes 526368 | tf_op jit(solution)/shard_map/ppermute | solution.py:15
  55.0 2.1 %convert_select_fusion.1 = f32[2048,128]{1,0:T(8,128)} fusion(bf16[2056,128]{1,0:T(8,128)(2,1)} %collective-permute-done.1, pred[]{:T(512)S(6)} %and.32), kind=kLoop, calls=%fused_computation.81 | loop fusion | flops 524288 | bytes 1572865 | tf_op jit(solution)/shard_map/jit(_where)/select_n | solution.py:126
  58.6 6.0 %fusion.3 = (f32[16,320]{1,0:T(8,128)S(1)}, f32[16,320,320]{1,2,0:T(8,128)}) fusion(pred[320,320]{0,1:T(8,128)(4,1)S(1)} %copy.19, bf16[320,2048]{1,0:T(8,128)(2,1)} %param.13, bf16[320,2048]{1,0:T(8,128)(2,1)S(1)} %copy-done.2), kind=kOutput, calls=%fused_computation.8 | convolution fusion | flops 424340480 | bytes 9297920 | tf_op jit(solution)/shard_map/qhd,khd->hqk/dot_general | solution.py:151
  64.6 5.6 %fusion.8 = f32[16,320,128]{2,1,0:T(8,128)} fusion(pred[320,320]{0,1:T(8,128)(4,1)S(1)} %copy.19, bf16[320,2048]{1,0:T(8,128)(2,1)} %param.10, bf16[320,2048]{1,0:T(8,128)(2,1)} %param.9, bf16[320,2048]{1,0:T(8,128)(2,1)S(1)} %copy-done), kind=kOutput, calls=%fused_computation.12 | convolution fusion | flops 842137600 | bytes 6656000 | tf_op jit(solution)/shard_map/hqk,khd->qhd/dot_general | solution.py:135
  72.1 1.5 collective-permute-start.4
  73.8 3.9 %fusion = (f32[16,320]{1,0:T(8,128)S(1)}, f32[16,320,480]{2,1,0:T(8,128)S(1)}) fusion(pred[320,480]{1,0:T(8,128)(4,1)S(1)} %pad_add_fusion, bf16[160,16,128]{2,0,1:T(8,128)(2,1)S(1)} %copy-done.7, bf16[320,16,128]{2,0,1:T(8,128)(2,1)} %copy_bitcast_fusion.2, bf16[320,2176]{1,0:T(8,128)(2,1)} %collective-permute-done.3), kind=kOutput, calls=%fused_computation.2 | convolution fusion | flops 640445440 | bytes 13281280 | tf_op jit(solution)/shard_map/qhd,khd->hqk/dot_general | solution.py:151
  77.7 4.3 %fusion.2 = (bf16[16,320,480]{2,1,0:T(8,128)(2,1)S(1)}, f32[16,320]{1,0:T(8,128)S(1)}) fusion(f32[16,320,480]{2,1,0:T(8,128)S(1)} %get-tuple-element.29, f32[16,320]{1,0:T(8,128)S(1)} %get-tuple-element.28, pred[320,480]{1,0:T(8,128)(4,1)S(1)} %pad_add_fusion), kind=kLoop, calls=%fused_computation.7 | loop fusion | flops 14740480 | bytes 14940160 | tf_op jit(solution)/shard_map/convert_element_type | solution.py:157
  82.1 2.2 %multiply_reduce_fusion = (f32[320,16]{0,1:T(8,128)S(1)}, f32[320,16,128]{2,0,1:T(8,128)S(1)}) fusion(f32[16,128,128]{2,1,0:T(8,128)S(1)} %bitcast.199, pred[320]{0:T(512)(128)(4,1)S(1)} %copy-done.11, f32[16,320,128]{2,1,0:T(8,128)S(1)} %copy-done.4, bf16[320,2048]{1,0:T(8,128)(2,1)S(1)} %copy-done), kind=kOutput, calls=%fused_computation.41 | convolution fusion | flops 1009249280 | bytes 7622976 | tf_op jit(solution)/shard_map/qhd,hde->qhe/dot_general | solution.py:136
  85.3 6.0 %collective-permute-done.4 = bf16[160,2176]{1,0:T(8,128)(2,1)S(1)} collective-permute-done((bf16[160,2176]{1,0:T(8,128)(2,1)S(1)}, bf16[160,2176]{1,0:T(8,128)(2,1)S(1)}, u32[]{:S(2)}, u32[]{:S(2)}) %collective-permute-start.4) | collective-permute-done | bytes 696352 | tf_op jit(solution)/shard_map/ppermute | solution.py:19
  92.5 1.6 %fusion.21 = f32[16,160]{1,0:T(8,128)S(1)} fusion(f32[16,160,320]{2,1,0:T(8,128)S(1)} %get-tuple-element.31, f32[16,160]{1,0:T(8,128)S(1)} %get-tuple-element.30, pred[160,320]{1,0:T(8,128)(4,1)S(1)} %broadcast_compare_fusion.1), kind=kLoop, calls=%fused_computation.26 | loop fusion | flops 4093440 | bytes 3348480 | tf_op jit(solution)/shard_map/reduce_sum | solution.py:157
  94.1 1.5 fusion.73
  95.6 3.7 %collective-permute-start.5 = (bf16[160,16,128]{2,0,1:T(8,128)(2,1)S(1)}, bf16[160,16,128]{2,0,1:T(8,128)(2,1)S(1)}, u32[]{:S(2)}, u32[]{:S(2)}) collective-permute-start(bf16[160,16,128]{2,0,1:T(8,128)(2,1)S(1)} %fusion.73), channel_id=1, source_target_pairs={{0,4},{4,8},{8,12},{1,5},{5,9},{9,13},{2,6},{6,10},{10,14},{3,7},{... | collective-permute-start | bytes 1966088 | tf_op jit(solution)/shard_map/ppermute | solution.py:15
  99.3 3.4 %collective-permute-start.6 = (f32[2,16,160]{2,1,0:T(8,128)S(1)}, f32[2,16,160]{2,1,0:T(8,128)S(1)}, u32[]{:S(2)}, u32[]{:S(2)}) collective-permute-start(f32[2,16,160]{2,1,0:T(8,128)S(1)} %pad_maximum_fusion.3), channel_id=1, source_target_pairs={{0,4},{4,8},{8,12},{1,5},{5,9},{9,13},{2,6},{6,10},{10,14},{3,7},{... | collective-permute-start | bytes 61448 | tf_op jit(solution)/shard_map/ppermute | solution.py:15
  103.9 8.2 %collective-permute-done.6 = f32[2,16,160]{2,1,0:T(8,128)S(1)} collective-permute-done((f32[2,16,160]{2,1,0:T(8,128)S(1)}, f32[2,16,160]{2,1,0:T(8,128)S(1)}, u32[]{:S(2)}, u32[]{:S(2)}) %collective-permute-start.6) | collective-permute-done | bytes 20512 | tf_op jit(solution)/shard_map/ppermute | solution.py:15
  112.3 2.4 %fusion.30 = bf16[320,16,128]{2,0,1:T(8,128)(2,1)S(1)} fusion(f32[16,128,320]{1,2,0:T(8,128)S(1)} %fusion.9, f32[160,16,128]{2,0,1:T(8,128)S(1)} %convert_select_fusion, bf16[16,320,480]{2,1,0:T(8,128)(2,1)S(1)} %get-tuple-element.2, f32[320,16]{0,1:T(8,128)S(1)} %get-tuple-element.12, f32[320,16]{0,1:T(8,128)S(1)} %get-tuple-element.9, ...), kind=kOutput, calls=%fused_computation.38 | convolution fusion | flops 213319680 | bytes 8568833 | tf_op jit(solution)/shard_map/hqk,khd->qhd/dot_general | solution.py:160
  114.7 4.7 %collective-permute-start.7 = (bf16[320,16,128]{2,0,1:T(8,128)(2,1)S(1)}, bf16[320,16,128]{2,0,1:T(8,128)(2,1)S(1)}, u32[]{:S(2)}, u32[]{:S(2)}) collective-permute-start(bf16[320,16,128]{2,0,1:T(8,128)(2,1)S(1)} %fusion.30), channel_id=1, source_target_pairs={{0,4},{4,8},{8,12},{1,5},{5,9},{9,13},{2,6},{6,10},{10,14},{3,7},{... | collective-permute-start | bytes 3932168 | tf_op jit(solution)/shard_map/ppermute | solution.py:15
  119.5 2.0 %fusion.4 = f32[16,320]{1,0:T(8,128)S(1)} fusion(f32[16,320,320]{1,2,0:T(8,128)S(1)} %bitcast.198, f32[16,320]{1,0:T(8,128)S(1)} %get-tuple-element.26, pred[320,320]{0,1:T(8,128)(4,1)S(1)} %copy.19), kind=kLoop, calls=%fused_computation.9 | loop fusion | flops 8186880 | bytes 6696960 | tf_op jit(solution)/shard_map/reduce_sum | solution.py:157
  121.5 3.4 %collective-permute-start.8 = (f32[2,16,320]{2,1,0:T(8,128)S(1)}, f32[2,16,320]{2,1,0:T(8,128)S(1)}, u32[]{:S(2)}, u32[]{:S(2)}) collective-permute-start(f32[2,16,320]{2,1,0:T(8,128)S(1)} %pad_maximum_fusion.2), channel_id=1, source_target_pairs={{0,4},{4,8},{8,12},{1,5},{5,9},{9,13},{2,6},{6,10},{10,14},{3,7},{... | collective-permute-start | bytes 122888 | tf_op jit(solution)/shard_map/ppermute | solution.py:15
  126.1 19.4 %collective-permute-done.8 = f32[2,16,320]{2,1,0:T(8,128)S(1)} collective-permute-done((f32[2,16,320]{2,1,0:T(8,128)S(1)}, f32[2,16,320]{2,1,0:T(8,128)S(1)}, u32[]{:S(2)}, u32[]{:S(2)}) %collective-permute-start.8) | collective-permute-done | bytes 40992 | tf_op jit(solution)/shard_map/ppermute | solution.py:15
  145.5 4.9 %fusion.61 = bf16[16,40,8,128]{3,2,1,0:T(8,128)(2,1)S(1)} fusion(f32[320,16]{0,1:T(8,128)S(1)} %get-tuple-element.7, f32[320,16]{0,1:T(8,128)S(1)} %get-tuple-element.8, f32[320,16]{0,1:T(8,128)S(1)} %get-tuple-element.6, bf16[320,16,128]{2,0,1:T(8,128)(2,1)S(1)} %collective-permute-done.7, pred[]{:T(512)S(6)} %ge.25, ...), kind=kOutput, calls=%fused_computation.72 | convolution fusion | flops 432209920 | bytes 10670081 | tf_op jit(solution)/shard_map/hqk,khd->qhd/dot_general | solution.py:160
  150.4 1.4 copy.112
  (65 shorter events, 17.5 us)
Async XLA Ops:
  0.6 64.0 %copy-start = (bf16[320,2048]{1,0:T(8,128)(2,1)S(1)}, bf16[320,2048]{1,0:T(8,128)(2,1)}, u32[]{:S(2)}) copy-start(bf16[320,2048]{1,0:T(8,128)(2,1)} %param.8) | copy-start | bytes 3932164
  5.3 10.4 %copy-start.8 = (s32[320]{0:T(512)S(1)}, s32[320]{0:T(512)}, u32[]{:S(2)}) copy-start(s32[320]{0:T(512)} %param.15) | copy-start | bytes 3844
  5.3 10.5 %copy-start.6 = (bf16[320,2048]{1,0:T(8,128)(2,1)S(1)}, bf16[320,2048]{1,0:T(8,128)(2,1)}, u32[]{:S(2)}) copy-start(bf16[320,2048]{1,0:T(8,128)(2,1)} %param.13) | copy-start | bytes 3932164
  9.0 9.4 %copy-start.2 = (bf16[320,2048]{1,0:T(8,128)(2,1)S(1)}, bf16[320,2048]{1,0:T(8,128)(2,1)}, u32[]{:S(2)}) copy-start(bf16[320,2048]{1,0:T(8,128)(2,1)} %param.14) | copy-start | bytes 3932164
  9.8 16.6 %copy-start.10 = (bf16[2048]{0:T(1024)(128)(2,1)S(1)}, bf16[2048]{0:T(1024)(128)(2,1)}, u32[]{:S(2)}) copy-start(bf16[2048]{0:T(1024)(128)(2,1)} %param.11) | copy-start | bytes 12292
  9.8 18.6 %collective-permute-start = (bf16[2056,128]{1,0:T(8,128)(2,1)}, bf16[2056,128]{1,0:T(8,128)(2,1)}, u32[]{:S(2)}, u32[]{:S(2)}) collective-permute-start(bf16[2056,128]{1,0:T(8,128)(2,1)} %concatenate.27), channel_id=1, source_target_pairs={{0,4},{4,8},{8,12},{1,5},{5,9},{9,13},{2,6},{6,10},{10,14},{3,7},{... | collective-permute-start | bytes 1579016 | tf_op jit(solution)/shard_map/ppermute | solution.py:15
  17.0 40.1 %collective-permute-start.3 = (bf16[320,2176]{1,0:T(8,128)(2,1)}, bf16[320,2176]{1,0:T(8,128)(2,1)}, u32[]{:S(2)}, u32[]{:S(2)}) collective-permute-start(bf16[320,2176]{1,0:T(8,128)(2,1)} %pad_maximum_fusion), channel_id=1, source_target_pairs={{4,0},{8,4},{12,8},{5,1},{9,5},{13,9},{6,2},{10,6},{14,10},{7,3},{... | collective-permute-start | bytes 4177928 | tf_op jit(solution)/shard_map/ppermute | solution.py:19
  19.2 23.2 %collective-permute-start.2 = (bf16[160,2176]{1,0:T(8,128)(2,1)}, bf16[160,2176]{1,0:T(8,128)(2,1)S(1)}, u32[]{:S(2)}, u32[]{:S(2)}) collective-permute-start(bf16[160,2176]{1,0:T(8,128)(2,1)} %pad_maximum_fusion.1), channel_id=1, source_target_pairs={{0,4},{4,8},{8,12},{1,5},{5,9},{9,13},{2,6},{6,10},{10,14},{3,7},{... | collective-permute-start | bytes 2088968 | tf_op jit(solution)/shard_map/ppermute | solution.py:15
  34.3 18.3 %collective-permute-start.1 = (bf16[2056,128]{1,0:T(8,128)(2,1)}, bf16[2056,128]{1,0:T(8,128)(2,1)}, u32[]{:S(2)}, u32[]{:S(2)}) collective-permute-start(bf16[2056,128]{1,0:T(8,128)(2,1)} %concatenate.28), channel_id=1, source_target_pairs={{0,4},{4,8},{8,12},{1,5},{5,9},{9,13},{2,6},{6,10},{10,14},{3,7},{... | collective-permute-start | bytes 1579016 | tf_op jit(solution)/shard_map/ppermute | solution.py:15
  64.6 9.2 %copy-start.7 = (bf16[160,16,128]{2,0,1:T(8,128)(2,1)S(1)}, bf16[160,16,128]{2,0,1:T(8,128)(2,1)}, u32[]{:S(2)}) copy-start(bf16[160,16,128]{2,0,1:T(8,128)(2,1)} %copy_bitcast_fusion.3) | copy-start | bytes 1966084
  72.1 19.1 %collective-permute-start.4 = (bf16[160,2176]{1,0:T(8,128)(2,1)S(1)}, bf16[160,2176]{1,0:T(8,128)(2,1)S(1)}, u32[]{:S(2)}, u32[]{:S(2)}) collective-permute-start(bf16[160,2176]{1,0:T(8,128)(2,1)S(1)} %slice.107), channel_id=1, source_target_pairs={{4,0},{8,4},{12,8},{5,1},{9,5},{13,9},{6,2},{10,6},{14,10},{7,3},{... | collective-permute-start | bytes 2088968 | tf_op jit(solution)/shard_map/ppermute | solution.py:19
  77.7 4.4 %copy-start.3 = (f32[2048,128]{1,0:T(8,128)S(1)}, f32[2048,128]{1,0:T(8,128)}, u32[]{:S(2)}) copy-start(f32[2048,128]{1,0:T(8,128)} %convert_select_fusion.1) | copy-start | bytes 3145732
  77.7 4.4 %copy-start.4 = (f32[16,320,128]{2,1,0:T(8,128)S(1)}, f32[16,320,128]{2,1,0:T(8,128)}, u32[]{:S(2)}) copy-start(f32[16,320,128]{2,1,0:T(8,128)} %fusion.8) | copy-start | bytes 7864324
  77.7 4.4 %copy-start.11 = (pred[320]{0:T(512)(128)(4,1)S(1)}, pred[320]{0:T(512)(128)(4,1)}, u32[]{:S(2)}) copy-start(pred[320]{0:T(512)(128)(4,1)} %get-tuple-element.20) | copy-start | bytes 964
  82.1 2.2 %copy-start.5 = (bf16[320,2048]{1,0:T(8,128)(2,1)S(1)}, bf16[320,2048]{1,0:T(8,128)(2,1)}, u32[]{:S(2)}) copy-start(bf16[320,2048]{1,0:T(8,128)(2,1)} %param.12) | copy-start | bytes 3932164
  82.1 2.2 %copy-start.9 = (f32[16,128]{1,0:T(8,128)S(1)}, f32[16,128]{1,0:T(8,128)}, u32[]{:S(2)}) copy-start(f32[16,128]{1,0:T(8,128)} %bitcast_convert_fusion) | copy-start | bytes 24580
  95.6 16.6 %collective-permute-start.5 = (bf16[160,16,128]{2,0,1:T(8,128)(2,1)S(1)}, bf16[160,16,128]{2,0,1:T(8,128)(2,1)S(1)}, u32[]{:S(2)}, u32[]{:S(2)}) collective-permute-start(bf16[160,16,128]{2,0,1:T(8,128)(2,1)S(1)} %fusion.73), channel_id=1, source_target_pairs={{0,4},{4,8},{8,12},{1,5},{5,9},{9,13},{2,6},{6,10},{10,14},{3,7},{... | collective-permute-start | bytes 1966088 | tf_op jit(solution)/shard_map/ppermute | solution.py:15
  99.3 12.8 %collective-permute-start.6 = (f32[2,16,160]{2,1,0:T(8,128)S(1)}, f32[2,16,160]{2,1,0:T(8,128)S(1)}, u32[]{:S(2)}, u32[]{:S(2)}) collective-permute-start(f32[2,16,160]{2,1,0:T(8,128)S(1)} %pad_maximum_fusion.3), channel_id=1, source_target_pairs={{0,4},{4,8},{8,12},{1,5},{5,9},{9,13},{2,6},{6,10},{10,14},{3,7},{... | collective-permute-start | bytes 61448 | tf_op jit(solution)/shard_map/ppermute | solution.py:15
  102.7 16.7 %slice-start = ((s8[7864320]{0:T(1024)(128)(4,1)}), s8[4194304]{0:T(1024)(128)(4,1)S(1)}, s32[]{:S(2)}) async-start(s8[7864320]{0:T(1024)(128)(4,1)} %bitcast.197), calls=%async_computation | async-start | bytes 8388608
  112.1 7.3 %slice-start.1 = ((s8[7864320]{0:T(1024)(128)(4,1)}), s8[3670016]{0:T(1024)(128)(4,1)S(1)}, s32[]{:S(2)}) async-start(s8[7864320]{0:T(1024)(128)(4,1)} %bitcast.197), calls=%async_computation.1 | async-start | bytes 7340032
  114.7 30.8 %collective-permute-start.7 = (bf16[320,16,128]{2,0,1:T(8,128)(2,1)S(1)}, bf16[320,16,128]{2,0,1:T(8,128)(2,1)S(1)}, u32[]{:S(2)}, u32[]{:S(2)}) collective-permute-start(bf16[320,16,128]{2,0,1:T(8,128)(2,1)S(1)} %fusion.30), channel_id=1, source_target_pairs={{0,4},{4,8},{8,12},{1,5},{5,9},{9,13},{2,6},{6,10},{10,14},{3,7},{... | collective-permute-start | bytes 3932168 | tf_op jit(solution)/shard_map/ppermute | solution.py:15
  121.5 24.0 %collective-permute-start.8 = (f32[2,16,320]{2,1,0:T(8,128)S(1)}, f32[2,16,320]{2,1,0:T(8,128)S(1)}, u32[]{:S(2)}, u32[]{:S(2)}) collective-permute-start(f32[2,16,320]{2,1,0:T(8,128)S(1)} %pad_maximum_fusion.2), channel_id=1, source_target_pairs={{0,4},{4,8},{8,12},{1,5},{5,9},{9,13},{2,6},{6,10},{10,14},{3,7},{... | collective-permute-start | bytes 122888 | tf_op jit(solution)/shard_map/ppermute | solution.py:15
  145.5 6.3 %copy-start.1 = (bf16[320,2048]{1,0:T(8,128)(2,1)S(1)}, bf16[320,2048]{1,0:T(8,128)(2,1)}, u32[]{:S(2)}) copy-start(bf16[320,2048]{1,0:T(8,128)(2,1)} %param.8) | copy-start | bytes 3932164

commit v10 on v9

--- a/solution.py
+++ b/solution.py
@@ -130,6 +130,22 @@
     keep_local = causal & (doc_id[:, None] == doc_id[None, :])
     score_scale = 1.0 / math.sqrt(HD)
 
+    def weights_of(query_rows, key_all, keep):
+        logits = (
+            jnp.einsum("qhd,khd->hqk", query_rows, key_all, preferred_element_type=jnp.float32)
+            * score_scale
+        )
+        logits = jnp.where(keep[None], logits, -1e30)
+        row_max = jnp.max(logits, axis=-1)
+        probs = jnp.where(keep[None], jnp.exp(logits - row_max[..., None]), 0.0)
+        return probs.astype(jnp.bfloat16), row_max, jnp.sum(probs, axis=-1)
+
+    query_soft = soft_query.reshape(row_count, head_count, HD)
+    key_soft = soft_key.reshape(row_count, head_count, HD)
+    diag = weights_of(query_soft, key_soft, keep_local)
+    if reach == 2:
+        carried, diag = lax.optimization_barrier((carried, diag))
+
     scores = jnp.einsum("qhd,khd->hqk", queries, key_rows, preferred_element_type=jnp.float32)
     rounded = jnp.where(keep_local[None], scores, jnp.zeros_like(scores)).astype(jnp.bfloat16)
     block_term = jnp.einsum("hqk,khd->qhd", rounded, value_rows, preferred_element_type=jnp.float32)
@@ -146,24 +162,11 @@
     normed = lin_raw * lax.rsqrt(mean_square + norm_eps) * gain_rows * gate_rows
     lin_out = normed.astype(jnp.bfloat16).reshape(row_count, width)
 
-    def weights_of(query_rows, key_all, keep):
-        logits = (
-            jnp.einsum("qhd,khd->hqk", query_rows, key_all, preferred_element_type=jnp.float32)
-            * score_scale
-        )
-        logits = jnp.where(keep[None], logits, -1e30)
-        row_max = jnp.max(logits, axis=-1)
-        probs = jnp.where(keep[None], jnp.exp(logits - row_max[..., None]), 0.0)
-        return probs.astype(jnp.bfloat16), row_max, jnp.sum(probs, axis=-1)
-
     def mix(weights, value_block):
         return jnp.einsum("hqk,khd->qhd", weights, value_block, preferred_element_type=jnp.float32)
 
     has_source = my_index >= 1
-    query_soft = soft_query.reshape(row_count, head_count, HD)
-    key_soft = soft_key.reshape(row_count, head_count, HD)
     value_own = lin_out.reshape(row_count, head_count, HD)
-    diag = weights_of(query_soft, key_soft, keep_local)
     window = (max_doc - row_count + 1) // 2
     if reach == 2 and n_seq >= 3 and 0 < window < row_count:
         cut = row_count - window
@@ -171,6 +174,10 @@
         next_queries = query_msg[:, :width].reshape(row_count, head_count, HD)
         next_docs = query_msg[:, width].astype(jnp.int32)
         far_msg = shift_down(query_msg[:window], 1, n_seq)
+        lin_out, query_msg = lax.optimization_barrier((lin_out, query_msg))
+        value_own = lin_out.reshape(row_count, head_count, HD)
+        next_queries = query_msg[:, :width].reshape(row_count, head_count, HD)
+        next_docs = query_msg[:, width].astype(jnp.int32)
         far_queries = far_msg[:, :width].reshape(window, head_count, HD)
         far_docs = far_msg[:, width].astype(jnp.int32)
         key_msg = shift_up(jnp.concatenate([soft_key, doc_cols], axis=1)[cut:], 1, n_seq)

time: 153 us -> 156 us (1.020)
  other arithmetic: 22 us -> 25.3 us
    reduce_sum x2, other arithmetic: 3.58 us -> 7.41 us  [weights_of(): return (probs.astype(jnp.bfloat16), row_max, jnp.sum(probs, axis=-1))]
    reshape x0 -> x1, other arithmetic: none -> 2.53 us  [per_device(): lin_out = normed.astype(jnp.bfloat16).reshape(row_count, width)]
  transfers between devices with their start and end apart: 9 -> 9, of which waited for: 5 -> 4; matrix products, arithmetic and copies ran while one was open for 20% -> 35% of each run, Pallas kernels for 0% -> 0%
where the time goes in v10:
time: 156 us; the launch traced here: 155 us
  waiting for transfers between devices  45 us (29%)
  matrix products  33.8 us (22%)
  starting transfers between devices  31.5 us (20%)
  other arithmetic  25.3 us (16%)
  local copies, waits for them, and re-layouts  11.8 us (8%)
  between operations  7.78 us (5%)
    ppermute x7, waiting for transfers between devices, shift_up(): return lax.ppermute(x, 'seq', [(s, s + dist) for s in range(n_seq - dist)])  38.7 us
    ppermute x7, starting transfers between devices, shift_up(): return lax.ppermute(x, 'seq', [(s, s + dist) for s in range(n_seq - dist)])  28.8 us
    dot_general x3, matrix products, weights_of(): jnp.einsum('qhd,khd->hqk', query_rows, key_all, preferred_element_type=jn...  12.2 us
    dot_general x4, matrix products, mix(): jnp.einsum('hqk,khd->qhd', weights, value_block, preferred_element_type=j...  8.87 us
    reduce_sum x2, other arithmetic, weights_of(): return (probs.astype(jnp.bfloat16), row_max, jnp.sum(probs, axis=-1))  7.41 us
    dot_general x1, matrix products, per_device(): jnp.einsum('hqk,khd->qhd', rounded, value_rows, preferred_element_type=jn...  6.41 us
    ppermute x2, waiting for transfers between devices, shift_down(): return lax.ppermute(x, 'seq', [(s + dist, s) for s in range(n_seq - dist)])  6.3 us
    convert_element_type x1, other arithmetic, weights_of(): return (probs.astype(jnp.bfloat16), row_max, jnp.sum(probs, axis=-1))  4.35 us
  transfers between devices with their start and end apart: 9, of which 4 were waited for; matrix products, arithmetic and copies ran while one was open for 35% of the time, Pallas kernels for 0%

profile of v10, /device:TPU:0, one launch (start us, length us, event | category | flops | bytes accessed | tf_op | source)
XLA Modules:
  0.0 155.3 jit_solution(10299380451191663350)
XLA Ops:
  1.6 2.0 %pad_maximum_fusion.1 = bf16[160,2176]{1,0:T(8,128)(2,1)} fusion(bf16[320,128]{1,0:T(8,128)(2,1)S(1)} %broadcast_in_dim.159, bf16[320,2048]{1,0:T(8,128)(2,1)} %param.14), kind=kLoop, calls=%fused_computation.88 | loop fusion | flops 1392640 | bytes 2088960 | tf_op jit(solution)/shard_map/concatenate | solution.py:183
  3.6 5.0 %collective-permute-start.3 = (bf16[160,2176]{1,0:T(8,128)(2,1)}, bf16[160,2176]{1,0:T(8,128)(2,1)S(1)}, u32[]{:S(2)}, u32[]{:S(2)}) collective-permute-start(bf16[160,2176]{1,0:T(8,128)(2,1)} %pad_maximum_fusion.1), channel_id=1, source_target_pairs={{0,4},{4,8},{8,12},{1,5},{5,9},{9,13},{2,6},{6,10},{10,14},{3,7},{... | collective-permute-start | bytes 2088968 | tf_op jit(solution)/shard_map/ppermute | solution.py:15
  8.6 1.2 pad_maximum_fusion
  9.8 1.3 collective-permute-start.2
  13.5 3.7 %fusion.117 = (bf16[16,128,128]{2,1,0:T(8,128)(2,1)S(1)}, f32[16,128,128]{2,1,0:T(8,128)}) fusion(pred[320]{0:T(512)(128)(4,1)S(1)} %get-tuple-element.33, bf16[320,2048]{1,0:T(8,128)(2,1)} %param.10, bf16[320,2048]{1,0:T(8,128)(2,1)} %param.9), kind=kOutput, calls=%fused_computation.149 | convolution fusion | flops 168689664 | bytes 4194624 | tf_op jit(solution)/shard_map/thd,the->hde/dot_general | solution.py:111
  18.0 5.3 %collective-permute-start = (bf16[2056,128]{1,0:T(8,128)(2,1)}, bf16[2056,128]{1,0:T(8,128)(2,1)}, u32[]{:S(2)}, u32[]{:S(2)}) collective-permute-start(bf16[2056,128]{1,0:T(8,128)(2,1)} %concatenate.27), channel_id=1, source_target_pairs={{0,4},{4,8},{8,12},{1,5},{5,9},{9,13},{2,6},{6,10},{10,14},{3,7},{... | collective-permute-start | bytes 1579016 | tf_op jit(solution)/shard_map/ppermute | solution.py:15
  24.7 1.4 copy_bitcast_fusion.2
  27.3 6.0 %fusion.3 = (f32[16,320]{1,0:T(8,128)S(1)}, f32[16,320,320]{1,2,0:T(8,128)}) fusion(pred[320,320]{0,1:T(8,128)(4,1)S(1)} %fusion.90, bf16[320,2048]{1,0:T(8,128)(2,1)S(1)} %copy-done.2, bf16[320,2048]{1,0:T(8,128)(2,1)} %param.13), kind=kOutput, calls=%fused_computation.8 | convolution fusion | flops 424340480 | bytes 9297920 | tf_op jit(solution)/shard_map/qhd,khd->hqk/dot_general | solution.py:135
  33.3 5.8 %fusion.4 = (f32[16,320]{1,0:T(8,128)S(1)}, bf16[16,320,320]{1,2,0:T(8,128)(2,1)}) fusion(f32[16,320,320]{1,2,0:T(8,128)} %get-tuple-element.37, f32[16,320]{1,0:T(8,128)S(1)} %get-tuple-element.11, pred[320,320]{0,1:T(8,128)(4,1)S(1)} %fusion.90), kind=kLoop, calls=%fused_computation.9 | loop fusion | flops 9825280 | bytes 9973760 | tf_op jit(solution)/shard_map/reduce_sum | solution.py:141
  41.5 1.2 convert_select_fusion.2
  43.8 3.4 %collective-permute-start.1 = (bf16[2056,128]{1,0:T(8,128)(2,1)}, bf16[2056,128]{1,0:T(8,128)(2,1)}, u32[]{:S(2)}, u32[]{:S(2)}) collective-permute-start(bf16[2056,128]{1,0:T(8,128)(2,1)} %concatenate.28), channel_id=1, source_target_pairs={{0,4},{4,8},{8,12},{1,5},{5,9},{9,13},{2,6},{6,10},{10,14},{3,7},{... | collective-permute-start | bytes 1579016 | tf_op jit(solution)/shard_map/ppermute | solution.py:15
  50.8 6.4 %collective-permute-done.1 = bf16[2056,128]{1,0:T(8,128)(2,1)} collective-permute-done((bf16[2056,128]{1,0:T(8,128)(2,1)}, bf16[2056,128]{1,0:T(8,128)(2,1)}, u32[]{:S(2)}, u32[]{:S(2)}) %collective-permute-start.1) | collective-permute-done | bytes 526368 | tf_op jit(solution)/shard_map/ppermute | solution.py:15
  60.7 2.7 %fusion.57 = f32[16,128,320]{1,2,0:T(8,128)} fusion(f32[16,128,128]{2,1,0:T(8,128)S(1)} %bitcast.231, bf16[320,2048]{1,0:T(8,128)(2,1)S(1)} %copy-done), kind=kOutput, calls=%fused_computation.67 | convolution fusion | flops 1006632960 | bytes 4980736 | tf_op jit(solution)/shard_map/qhd,hde->qhe/dot_general | solution.py:152
  63.4 6.4 %multiply_reduce_fusion = (f32[320,16]{0,1:T(8,128)S(1)}, f32[320,16,128]{2,0,1:T(8,128)}) fusion(f32[16,128,320]{1,2,0:T(8,128)} %fusion.57, pred[320]{0:T(512)(128)(4,1)S(1)} %get-tuple-element.32, pred[320,320]{0,1:T(8,128)(4,1)S(1)} %fusion.90, bf16[320,2048]{1,0:T(8,128)(2,1)} %param.10, bf16[320,2048]{1,0:T(8,128)(2,1)} %param.9, ...), kind=kOutput, calls=%fused_computation.35 | convolution fusion | flops 844753920 | bytes 9298240 | tf_op jit(solution)/shard_map/hqk,khd->qhd/dot_general | solution.py:151
  69.9 2.5 %copy_bitcast_fusion.1 = bf16[320,2048]{1,0:T(8,128)(2,1)S(1)} fusion(f32[320,16,128]{2,0,1:T(8,128)} %get-tuple-element.39, f32[16,128]{1,0:T(8,128)S(1)} %bitcast_convert_fusion, f32[320,16]{0,1:T(8,128)S(1)} %add_rsqrt_fusion, bf16[320,2048]{1,0:T(8,128)(2,1)} %param.12), kind=kLoop, calls=%fused_computation.50 | loop fusion | flops 5242880 | bytes 5271552 | tf_op jit(solution)/shard_map/reshape | solution.py:163
  72.4 1.6 %slice.110 = bf16[160,2176]{1,0:T(8,128)(2,1)S(1)} slice(bf16[320,2176]{1,0:T(8,128)(2,1)} %collective-permute-done.2), slice={[0:160], [0:2176]} | slice | bytes 1392640 | tf_op jit(solution)/shard_map/slice | solution.py:176
  74.0 1.5 collective-permute-start.4
  77.8 4.1 %fusion = (f32[16,320]{1,0:T(8,128)S(1)}, f32[16,320,480]{2,1,0:T(8,128)S(1)}) fusion(pred[320,480]{1,0:T(8,128)(4,1)} %copy.35, bf16[160,16,128]{2,0,1:T(8,128)(2,1)} %copy_bitcast_fusion.3, bf16[320,16,128]{2,0,1:T(8,128)(2,1)} %copy_bitcast_fusion.2, bf16[320,2176]{1,0:T(8,128)(2,1)} %collective-permute-done.2), kind=kOutput, calls=%fused_computation.2 | convolution fusion | flops 640445440 | bytes 13291520 | tf_op jit(solution)/shard_map/qhd,khd->hqk/dot_general | solution.py:135
  82.0 4.3 %fusion.2 = (bf16[16,320,480]{2,1,0:T(8,128)(2,1)S(1)}, f32[16,320]{1,0:T(8,128)S(1)}) fusion(f32[16,320,480]{2,1,0:T(8,128)S(1)} %get-tuple-element.41, f32[16,320]{1,0:T(8,128)S(1)} %get-tuple-element.40, pred[320,480]{1,0:T(8,128)(4,1)S(1)} %copy-done.8), kind=kLoop, calls=%fused_computation.7 | loop fusion | flops 14740480 | bytes 14940160 | tf_op jit(solution)/shard_map/convert_element_type | solution.py:141
  86.3 6.3 %collective-permute-done.4 = bf16[160,2176]{1,0:T(8,128)(2,1)} collective-permute-done((bf16[160,2176]{1,0:T(8,128)(2,1)S(1)}, bf16[160,2176]{1,0:T(8,128)(2,1)}, u32[]{:S(2)}, u32[]{:S(2)}) %collective-permute-start.4) | collective-permute-done | bytes 696352 | tf_op jit(solution)/shard_map/ppermute | solution.py:19
  93.6 2.1 %fusion.11 = (f32[16,160]{1,0:T(8,128)S(1)}, f32[16,160,320]{2,1,0:T(8,128)S(1)}) fusion(pred[160,320]{1,0:T(8,128)(4,1)S(1)} %broadcast_compare_fusion.1, bf16[320,2048]{1,0:T(8,128)(2,1)S(1)} %copy-done.2, bf16[160,2176]{1,0:T(8,128)(2,1)} %collective-permute-done.4), kind=kOutput, calls=%fused_computation.18 | convolution fusion | flops 212170240 | bytes 5304320 | tf_op jit(solution)/shard_map/qhd,khd->hqk/dot_general | solution.py:135
  95.7 1.6 %fusion.14 = f32[16,160]{1,0:T(8,128)S(1)} fusion(f32[16,160,320]{2,1,0:T(8,128)S(1)} %get-tuple-element.43, f32[16,160]{1,0:T(8,128)S(1)} %get-tuple-element.42, pred[160,320]{1,0:T(8,128)(4,1)S(1)} %broadcast_compare_fusion.1), kind=kLoop, calls=%fused_computation.20 | loop fusion | flops 4093440 | bytes 3348480 | tf_op jit(solution)/shard_map/reduce_sum | solution.py:141
  97.3 4.4 %collective-permute-start.6 = (f32[2,16,160]{2,1,0:T(8,128)S(1)}, f32[2,16,160]{2,1,0:T(8,128)S(1)}, u32[]{:S(2)}, u32[]{:S(2)}) collective-permute-start(f32[2,16,160]{2,1,0:T(8,128)S(1)} %pad_maximum_fusion.3), channel_id=1, source_target_pairs={{0,4},{4,8},{8,12},{1,5},{5,9},{9,13},{2,6},{6,10},{10,14},{3,7},{... | collective-permute-start | bytes 61448 | tf_op jit(solution)/shard_map/ppermute | solution.py:15
  101.7 1.6 %fusion.74 = bf16[160,16,128]{2,0,1:T(8,128)(2,1)S(1)} fusion(f32[16,160,320]{2,1,0:T(8,128)S(1)} %get-tuple-element.43, f32[16,160]{1,0:T(8,128)S(1)} %get-tuple-element.42, pred[160,320]{1,0:T(8,128)(4,1)S(1)} %broadcast_compare_fusion.1, pred[]{:T(512)S(6)} %ne.12, bf16[320,2048]{1,0:T(8,128)(2,1)S(1)} %copy_bitcast_fusion.1), kind=kOutput, calls=%fused_computation.80 | convolution fusion | flops 214466560 | bytes 6631425 | tf_op jit(solution)/shard_map/hqk,khd->qhd/dot_general | solution.py:166
  103.3 3.7 %collective-permute-start.5 = (bf16[160,16,128]{2,0,1:T(8,128)(2,1)S(1)}, bf16[160,16,128]{2,0,1:T(8,128)(2,1)S(1)}, u32[]{:S(2)}, u32[]{:S(2)}) collective-permute-start(bf16[160,16,128]{2,0,1:T(8,128)(2,1)S(1)} %fusion.74), channel_id=1, source_target_pairs={{0,4},{4,8},{8,12},{1,5},{5,9},{9,13},{2,6},{6,10},{10,14},{3,7},{... | collective-permute-start | bytes 1966088 | tf_op jit(solution)/shard_map/ppermute | solution.py:15
  108.2 9.7 %collective-permute-done.5 = bf16[160,16,128]{2,0,1:T(8,128)(2,1)S(1)} collective-permute-done((bf16[160,16,128]{2,0,1:T(8,128)(2,1)S(1)}, bf16[160,16,128]{2,0,1:T(8,128)(2,1)S(1)}, u32[]{:S(2)}, u32[]{:S(2)}) %collective-permute-start.5) | collective-permute-done | bytes 655392 | tf_op jit(solution)/shard_map/ppermute | solution.py:15
  118.1 2.4 %fusion.23 = bf16[320,16,128]{2,0,1:T(8,128)(2,1)S(1)} fusion(f32[16,128,320]{1,2,0:T(8,128)S(1)} %fusion.7, f32[160,16,128]{2,0,1:T(8,128)S(1)} %convert_select_fusion, bf16[16,320,480]{2,1,0:T(8,128)(2,1)S(1)} %get-tuple-element.14, f32[320,16]{0,1:T(8,128)S(1)} %get-tuple-element.26, f32[320,16]{0,1:T(8,128)S(1)} %get-tuple-element.23, ...), kind=kOutput, calls=%fused_computation.32 | convolution fusion | flops 213319680 | bytes 8568833 | tf_op jit(solution)/shard_map/hqk,khd->qhd/dot_general | solution.py:166
  120.5 4.5 %collective-permute-start.7 = (bf16[320,16,128]{2,0,1:T(8,128)(2,1)S(1)}, bf16[320,16,128]{2,0,1:T(8,128)(2,1)S(1)}, u32[]{:S(2)}, u32[]{:S(2)}) collective-permute-start(bf16[320,16,128]{2,0,1:T(8,128)(2,1)S(1)} %fusion.23), channel_id=1, source_target_pairs={{0,4},{4,8},{8,12},{1,5},{5,9},{9,13},{2,6},{6,10},{10,14},{3,7},{... | collective-permute-start | bytes 3932168 | tf_op jit(solution)/shard_map/ppermute | solution.py:15
  125.0 2.5 %collective-permute-start.8 = (f32[2,16,320]{2,1,0:T(8,128)S(1)}, f32[2,16,320]{2,1,0:T(8,128)S(1)}, u32[]{:S(2)}, u32[]{:S(2)}) collective-permute-start(f32[2,16,320]{2,1,0:T(8,128)S(1)} %pad_maximum_fusion.2), channel_id=1, source_target_pairs={{0,4},{4,8},{8,12},{1,5},{5,9},{9,13},{2,6},{6,10},{10,14},{3,7},{... | collective-permute-start | bytes 122888 | tf_op jit(solution)/shard_map/ppermute | solution.py:15
  127.5 22.6 %collective-permute-done.8 = f32[2,16,320]{2,1,0:T(8,128)S(1)} collective-permute-done((f32[2,16,320]{2,1,0:T(8,128)S(1)}, f32[2,16,320]{2,1,0:T(8,128)S(1)}, u32[]{:S(2)}, u32[]{:S(2)}) %collective-permute-start.8) | collective-permute-done | bytes 40992 | tf_op jit(solution)/shard_map/ppermute | solution.py:15
  150.1 3.7 %fusion.60 = bf16[16,40,8,128]{3,2,1,0:T(8,128)(2,1)S(1)} fusion(f32[320,16]{0,1:T(8,128)S(1)} %get-tuple-element.21, f32[320,16]{0,1:T(8,128)S(1)} %get-tuple-element.22, f32[320,16]{0,1:T(8,128)S(1)} %get-tuple-element.20, bf16[320,16,128]{2,0,1:T(8,128)(2,1)S(1)} %collective-permute-done.7, pred[]{:T(512)S(6)} %ge.25, ...), kind=kOutput, calls=%fused_computation.72 | convolution fusion | flops 424017920 | bytes 7270401 | tf_op jit(solution)/shard_map/hqk,khd->qhd/dot_general | solution.py:166
  153.9 1.4 copy.143
  (60 shorter events, 15.2 us)
Async XLA Ops:
  0.6 60.1 %copy-start = (bf16[320,2048]{1,0:T(8,128)(2,1)S(1)}, bf16[320,2048]{1,0:T(8,128)(2,1)}, u32[]{:S(2)}) copy-start(bf16[320,2048]{1,0:T(8,128)(2,1)} %param.8) | copy-start | bytes 3932164
  0.6 8.0 %copy-start.6 = (bf16[320,2048]{1,0:T(8,128)(2,1)S(1)}, bf16[320,2048]{1,0:T(8,128)(2,1)}, u32[]{:S(2)}) copy-start(bf16[320,2048]{1,0:T(8,128)(2,1)} %param.13) | copy-start | bytes 3932164
  1.6 9.5 %copy-start.9 = (s32[320]{0:T(512)S(1)}, s32[320]{0:T(512)}, u32[]{:S(2)}) copy-start(s32[320]{0:T(512)} %param.15) | copy-start | bytes 3844
  3.6 43.6 %collective-permute-start.3 = (bf16[160,2176]{1,0:T(8,128)(2,1)}, bf16[160,2176]{1,0:T(8,128)(2,1)S(1)}, u32[]{:S(2)}, u32[]{:S(2)}) collective-permute-start(bf16[160,2176]{1,0:T(8,128)(2,1)} %pad_maximum_fusion.1), channel_id=1, source_target_pairs={{0,4},{4,8},{8,12},{1,5},{5,9},{9,13},{2,6},{6,10},{10,14},{3,7},{... | collective-permute-start | bytes 2088968 | tf_op jit(solution)/shard_map/ppermute | solution.py:15
  9.8 62.6 %collective-permute-start.2 = (bf16[320,2176]{1,0:T(8,128)(2,1)}, bf16[320,2176]{1,0:T(8,128)(2,1)}, u32[]{:S(2)}, u32[]{:S(2)}) collective-permute-start(bf16[320,2176]{1,0:T(8,128)(2,1)} %pad_maximum_fusion), channel_id=1, source_target_pairs={{4,0},{8,4},{12,8},{5,1},{9,5},{13,9},{6,2},{10,6},{14,10},{7,3},{... | collective-permute-start | bytes 4177928 | tf_op jit(solution)/shard_map/ppermute | solution.py:19
  13.5 11.2 %copy-start.2 = (bf16[320,2048]{1,0:T(8,128)(2,1)S(1)}, bf16[320,2048]{1,0:T(8,128)(2,1)}, u32[]{:S(2)}) copy-start(bf16[320,2048]{1,0:T(8,128)(2,1)} %param.14) | copy-start | bytes 3932164
  17.2 10.1 %copy-start.10 = (bf16[2048]{0:T(1024)(128)(2,1)S(1)}, bf16[2048]{0:T(1024)(128)(2,1)}, u32[]{:S(2)}) copy-start(bf16[2048]{0:T(1024)(128)(2,1)} %param.11) | copy-start | bytes 12292
  18.0 21.1 %collective-permute-start = (bf16[2056,128]{1,0:T(8,128)(2,1)}, bf16[2056,128]{1,0:T(8,128)(2,1)}, u32[]{:S(2)}, u32[]{:S(2)}) collective-permute-start(bf16[2056,128]{1,0:T(8,128)(2,1)} %concatenate.27), channel_id=1, source_target_pairs={{0,4},{4,8},{8,12},{1,5},{5,9},{9,13},{2,6},{6,10},{10,14},{3,7},{... | collective-permute-start | bytes 1579016 | tf_op jit(solution)/shard_map/ppermute | solution.py:15
  41.5 1.4 copy-start.7
  43.8 13.3 %collective-permute-start.1 = (bf16[2056,128]{1,0:T(8,128)(2,1)}, bf16[2056,128]{1,0:T(8,128)(2,1)}, u32[]{:S(2)}, u32[]{:S(2)}) collective-permute-start(bf16[2056,128]{1,0:T(8,128)(2,1)} %concatenate.28), channel_id=1, source_target_pairs={{0,4},{4,8},{8,12},{1,5},{5,9},{9,13},{2,6},{6,10},{10,14},{3,7},{... | collective-permute-start | bytes 1579016 | tf_op jit(solution)/shard_map/ppermute | solution.py:15
  69.8 6.9 %copy-start.11 = (s32[160]{0:T(256)S(1)}, s32[160]{0:T(256)}, u32[]{:S(2)}) copy-start(s32[160]{0:T(256)} %fusion.103) | copy-start | bytes 1924
  72.4 34.6 %copy-start.4 = (bf16[320,2048]{1,0:T(8,128)(2,1)}, bf16[320,2048]{1,0:T(8,128)(2,1)S(1)}, u32[]{:S(2)}) copy-start(bf16[320,2048]{1,0:T(8,128)(2,1)S(1)} %copy_bitcast_fusion.1) | copy-start | bytes 3932164
  74.0 18.6 %collective-permute-start.4 = (bf16[160,2176]{1,0:T(8,128)(2,1)S(1)}, bf16[160,2176]{1,0:T(8,128)(2,1)}, u32[]{:S(2)}, u32[]{:S(2)}) collective-permute-start(bf16[160,2176]{1,0:T(8,128)(2,1)S(1)} %slice.110), channel_id=1, source_target_pairs={{4,0},{8,4},{12,8},{5,1},{9,5},{13,9},{6,2},{10,6},{14,10},{7,3},{... | collective-permute-start | bytes 2088968 | tf_op jit(solution)/shard_map/ppermute | solution.py:19
  77.8 4.1 %copy-start.8 = (pred[320,480]{1,0:T(8,128)(4,1)S(1)}, pred[320,480]{1,0:T(8,128)(4,1)}, u32[]{:S(2)}) copy-start(pred[320,480]{1,0:T(8,128)(4,1)} %copy.35) | copy-start | bytes 460804
  97.3 10.8 %collective-permute-start.6 = (f32[2,16,160]{2,1,0:T(8,128)S(1)}, f32[2,16,160]{2,1,0:T(8,128)S(1)}, u32[]{:S(2)}, u32[]{:S(2)}) collective-permute-start(f32[2,16,160]{2,1,0:T(8,128)S(1)} %pad_maximum_fusion.3), channel_id=1, source_target_pairs={{0,4},{4,8},{8,12},{1,5},{5,9},{9,13},{2,6},{6,10},{10,14},{3,7},{... | collective-permute-start | bytes 61448 | tf_op jit(solution)/shard_map/ppermute | solution.py:15
  103.3 14.7 %collective-permute-start.5 = (bf16[160,16,128]{2,0,1:T(8,128)(2,1)S(1)}, bf16[160,16,128]{2,0,1:T(8,128)(2,1)S(1)}, u32[]{:S(2)}, u32[]{:S(2)}) collective-permute-start(bf16[160,16,128]{2,0,1:T(8,128)(2,1)S(1)} %fusion.74), channel_id=1, source_target_pairs={{0,4},{4,8},{8,12},{1,5},{5,9},{9,13},{2,6},{6,10},{10,14},{3,7},{... | collective-permute-start | bytes 1966088 | tf_op jit(solution)/shard_map/ppermute | solution.py:15
  118.0 32.1 %copy-start.3 = (bf16[16,320,320]{1,2,0:T(8,128)(2,1)S(1)}, bf16[16,320,320]{1,2,0:T(8,128)(2,1)}, u32[]{:S(2)}) copy-start(bf16[16,320,320]{1,2,0:T(8,128)(2,1)} %get-tuple-element.12) | copy-start | bytes 9830404
  118.1 32.1 %copy-start.5 = (bf16[320,2048]{1,0:T(8,128)(2,1)S(1)}, bf16[320,2048]{1,0:T(8,128)(2,1)}, u32[]{:S(2)}) copy-start(bf16[320,2048]{1,0:T(8,128)(2,1)} %copy-done.4) | copy-start | bytes 3932164
  120.5 29.6 %collective-permute-start.7 = (bf16[320,16,128]{2,0,1:T(8,128)(2,1)S(1)}, bf16[320,16,128]{2,0,1:T(8,128)(2,1)S(1)}, u32[]{:S(2)}, u32[]{:S(2)}) collective-permute-start(bf16[320,16,128]{2,0,1:T(8,128)(2,1)S(1)} %fusion.23), channel_id=1, source_target_pairs={{0,4},{4,8},{8,12},{1,5},{5,9},{9,13},{2,6},{6,10},{10,14},{3,7},{... | collective-permute-start | bytes 3932168 | tf_op jit(solution)/shard_map/ppermute | solution.py:15
  125.0 25.1 %collective-permute-start.8 = (f32[2,16,320]{2,1,0:T(8,128)S(1)}, f32[2,16,320]{2,1,0:T(8,128)S(1)}, u32[]{:S(2)}, u32[]{:S(2)}) collective-permute-start(f32[2,16,320]{2,1,0:T(8,128)S(1)} %pad_maximum_fusion.2), channel_id=1, source_target_pairs={{0,4},{4,8},{8,12},{1,5},{5,9},{9,13},{2,6},{6,10},{10,14},{3,7},{... | collective-permute-start | bytes 122888 | tf_op jit(solution)/shard_map/ppermute | solution.py:15
  150.1 5.2 %copy-start.1 = (bf16[320,2048]{1,0:T(8,128)(2,1)S(1)}, bf16[320,2048]{1,0:T(8,128)(2,1)}, u32[]{:S(2)}) copy-start(bf16[320,2048]{1,0:T(8,128)(2,1)} %param.8) | copy-start | bytes 3932164

commit v11 on v10

--- a/solution.py
+++ b/solution.py
@@ -174,10 +174,6 @@
         next_queries = query_msg[:, :width].reshape(row_count, head_count, HD)
         next_docs = query_msg[:, width].astype(jnp.int32)
         far_msg = shift_down(query_msg[:window], 1, n_seq)
-        lin_out, query_msg = lax.optimization_barrier((lin_out, query_msg))
-        value_own = lin_out.reshape(row_count, head_count, HD)
-        next_queries = query_msg[:, :width].reshape(row_count, head_count, HD)
-        next_docs = query_msg[:, width].astype(jnp.int32)
         far_queries = far_msg[:, :width].reshape(window, head_count, HD)
         far_docs = far_msg[:, width].astype(jnp.int32)
         key_msg = shift_up(jnp.concatenate([soft_key, doc_cols], axis=1)[cut:], 1, n_seq)

time: 156 us -> 158 us (1.013)
  other arithmetic: 25.3 us -> 32.3 us
  matrix products: 33.8 us -> 27.9 us
  starting transfers between devices: 31.5 us -> 35.1 us
  waiting for transfers between devices: 45 us -> 42 us
    ppermute x2, waiting for transfers between devices: 6.3 us -> 0.01 us  [shift_down(): return lax.ppermute(x, 'seq', [(s + dist, s) for s in range(n_seq - dist)])]
    ppermute x7, starting transfers between devices: 28.8 us -> 32.4 us  [shift_up(): return lax.ppermute(x, 'seq', [(s, s + dist) for s in range(n_seq - dist)])]
    dot_general x3, matrix products: 12.2 us -> 8.74 us  [weights_of(): jnp.einsum('qhd,khd->hqk', query_rows, key_all, preferred_element_type=jn...]
    ppermute x7, waiting for transfers between devices: 38.7 us -> 42 us  [shift_up(): return lax.ppermute(x, 'seq', [(s, s + dist) for s in range(n_seq - dist)])]
    convert_element_type x0 -> x1, other arithmetic: none -> 2.54 us  [per_device(): lin_out = normed.astype(jnp.bfloat16).reshape(row_count, width)]
    dot_general x4, matrix products: 8.87 us -> 6.45 us  [mix(): jnp.einsum('hqk,khd->qhd', weights, value_block, preferred_element_type=j...]
    reduce_sum x2, other arithmetic: 7.41 us -> 5.2 us  [weights_of(): return (probs.astype(jnp.bfloat16), row_max, jnp.sum(probs, axis=-1))]
    convert_element_type x1, other arithmetic: 4.35 us -> 5.94 us  [weights_of(): return (probs.astype(jnp.bfloat16), row_max, jnp.sum(probs, axis=-1))]
where the time goes in v11:
time: 158 us; the launch traced here: 157 us
  waiting for transfers between devices  42 us (27%)
  starting transfers between devices  35.1 us (22%)
  other arithmetic  32.3 us (20%)
  matrix products  27.9 us (18%)
  local copies, waits for them, and re-layouts  11.3 us (7%)
  between operations  7.98 us (5%)
    ppermute x7, waiting for transfers between devices, shift_up(): return lax.ppermute(x, 'seq', [(s, s + dist) for s in range(n_seq - dist)])  42 us
    ppermute x7, starting transfers between devices, shift_up(): return lax.ppermute(x, 'seq', [(s, s + dist) for s in range(n_seq - dist)])  32.4 us
    dot_general x3, matrix products, weights_of(): jnp.einsum('qhd,khd->hqk', query_rows, key_all, preferred_element_type=jn...  8.74 us
    dot_general x4, matrix products, mix(): jnp.einsum('hqk,khd->qhd', weights, value_block, preferred_element_type=j...  6.45 us
    dot_general x1, matrix products, per_device(): jnp.einsum('hqk,khd->qhd', rounded, value_rows, preferred_element_type=jn...  6.39 us
    convert_element_type x1, other arithmetic, weights_of(): return (probs.astype(jnp.bfloat16), row_max, jnp.sum(probs, axis=-1))  5.94 us
    reduce_sum x2, other arithmetic, weights_of(): return (probs.astype(jnp.bfloat16), row_max, jnp.sum(probs, axis=-1))  5.2 us
    dot_general x1, matrix products, per_device(): jnp.einsum('thd,the->hde', tail_keys, value_rows, preferred_element_type=...  3.67 us
  transfers between devices with their start and end apart: 9, of which 4 were waited for; matrix products, arithmetic and copies ran while one was open for 35% of the time, Pallas kernels for 0%

profile of v11, /device:TPU:0, one launch (start us, length us, event | category | flops | bytes accessed | tf_op | source)
XLA Modules:
  0.0 156.6 jit_solution(17220787317972863903)
XLA Ops:
  1.6 2.0 %pad_maximum_fusion.1 = bf16[160,2176]{1,0:T(8,128)(2,1)} fusion(bf16[320,128]{1,0:T(8,128)(2,1)S(1)} %broadcast_in_dim.159, bf16[320,2048]{1,0:T(8,128)(2,1)} %param.14), kind=kLoop, calls=%fused_computation.80 | loop fusion | flops 1392640 | bytes 2088960 | tf_op jit(solution)/shard_map/concatenate | solution.py:179
  3.5 5.0 %collective-permute-start.2 = (bf16[160,2176]{1,0:T(8,128)(2,1)}, bf16[160,2176]{1,0:T(8,128)(2,1)S(1)}, u32[]{:S(2)}, u32[]{:S(2)}) collective-permute-start(bf16[160,2176]{1,0:T(8,128)(2,1)} %pad_maximum_fusion.1), channel_id=1, source_target_pairs={{0,4},{4,8},{8,12},{1,5},{5,9},{9,13},{2,6},{6,10},{10,14},{3,7},{... | collective-permute-start | bytes 2088968 | tf_op jit(solution)/shard_map/ppermute | solution.py:15
  8.5 1.4 fusion.102
  10.6 2.5 %broadcast_compare_fusion.3 = (pred[320]{0:T(512)(128)(4,1)}, pred[320]{0:T(512)(128)(4,1)S(1)}) fusion(s32[320]{0:T(512)} %param.15, s32[]{:T(128)} %bitcast.1, s32[]{:T(128)} %bitcast.2), kind=kLoop, calls=%fused_computation.130 | loop fusion | flops 640 | bytes 1928 | tf_op jit(solution)/shard_map/eq | solution.py:156
  13.1 3.7 %fusion.103 = (bf16[16,128,128]{2,1,0:T(8,128)(2,1)S(1)}, f32[16,128,128]{2,1,0:T(8,128)}) fusion(pred[320]{0:T(512)(128)(4,1)S(1)} %get-tuple-element.31, bf16[320,2048]{1,0:T(8,128)(2,1)} %param.10, bf16[320,2048]{1,0:T(8,128)(2,1)} %param.9), kind=kOutput, calls=%fused_computation.140 | convolution fusion | flops 168689664 | bytes 4194624 | tf_op jit(solution)/shard_map/thd,the->hde/dot_general | solution.py:111
  17.6 4.2 %collective-permute-start = (bf16[2056,128]{1,0:T(8,128)(2,1)}, bf16[2056,128]{1,0:T(8,128)(2,1)}, u32[]{:S(2)}, u32[]{:S(2)}) collective-permute-start(bf16[2056,128]{1,0:T(8,128)(2,1)} %concatenate.27), channel_id=1, source_target_pairs={{0,4},{4,8},{8,12},{1,5},{5,9},{9,13},{2,6},{6,10},{10,14},{3,7},{... | collective-permute-start | bytes 1579016 | tf_op jit(solution)/shard_map/ppermute | solution.py:15
  27.5 1.4 copy_bitcast_fusion.2
  28.9 6.0 %collective-permute-done = bf16[2056,128]{1,0:T(8,128)(2,1)} collective-permute-done((bf16[2056,128]{1,0:T(8,128)(2,1)}, bf16[2056,128]{1,0:T(8,128)(2,1)}, u32[]{:S(2)}, u32[]{:S(2)}) %collective-permute-start) | collective-permute-done | bytes 526368 | tf_op jit(solution)/shard_map/ppermute | solution.py:15
  38.4 1.3 add_convert_fusion
  40.6 5.2 %collective-permute-start.1 = (bf16[2056,128]{1,0:T(8,128)(2,1)}, bf16[2056,128]{1,0:T(8,128)(2,1)}, u32[]{:S(2)}, u32[]{:S(2)}) collective-permute-start(bf16[2056,128]{1,0:T(8,128)(2,1)} %concatenate.28), channel_id=1, source_target_pairs={{0,4},{4,8},{8,12},{1,5},{5,9},{9,13},{2,6},{6,10},{10,14},{3,7},{... | collective-permute-start | bytes 1579016 | tf_op jit(solution)/shard_map/ppermute | solution.py:15
  48.7 6.9 %collective-permute-done.1 = bf16[2056,128]{1,0:T(8,128)(2,1)} collective-permute-done((bf16[2056,128]{1,0:T(8,128)(2,1)}, bf16[2056,128]{1,0:T(8,128)(2,1)}, u32[]{:S(2)}, u32[]{:S(2)}) %collective-permute-start.1) | collective-permute-done | bytes 526368 | tf_op jit(solution)/shard_map/ppermute | solution.py:15
  58.1 2.1 %convert_select_fusion.1 = f32[2048,128]{1,0:T(8,128)} fusion(bf16[2056,128]{1,0:T(8,128)(2,1)} %collective-permute-done.1, pred[]{:T(512)S(6)} %and.32), kind=kLoop, calls=%fused_computation.76 | loop fusion | flops 524288 | bytes 1572865 | tf_op jit(solution)/shard_map/jit(_where)/select_n | solution.py:126
  63.7 1.5 collective-permute-start.4
  65.2 3.0 %fusion.3 = (f32[16,320]{1,0:T(8,128)S(1)}, f32[16,320,320]{1,2,0:T(8,128)S(1)}) fusion(pred[320,320]{0,1:T(8,128)(4,1)} %get-tuple-element.29, bf16[320,2048]{1,0:T(8,128)(2,1)S(1)} %copy-done.3, bf16[320,2048]{1,0:T(8,128)(2,1)} %param.13), kind=kOutput, calls=%fused_computation.8 | convolution fusion | flops 424340480 | bytes 9297920 | tf_op jit(solution)/shard_map/qhd,khd->hqk/dot_general | solution.py:135
  68.3 3.6 %fusion.4 = (f32[16,320]{1,0:T(8,128)S(1)}, bf16[16,320,320]{1,2,0:T(8,128)(2,1)}) fusion(f32[16,320,320]{1,2,0:T(8,128)S(1)} %get-tuple-element.35, f32[16,320]{1,0:T(8,128)S(1)} %get-tuple-element.7, pred[320,320]{0,1:T(8,128)(4,1)S(1)} %copy-done.8), kind=kLoop, calls=%fused_computation.9 | loop fusion | flops 9825280 | bytes 9973760 | tf_op jit(solution)/shard_map/reduce_sum | solution.py:141
  71.9 3.7 %fusion = (f32[16,320]{1,0:T(8,128)S(1)}, f32[16,320,480]{2,1,0:T(8,128)S(1)}) fusion(pred[320,480]{1,0:T(8,128)(4,1)S(1)} %copy.30, bf16[160,16,128]{2,0,1:T(8,128)(2,1)S(1)} %copy-done.7, bf16[320,16,128]{2,0,1:T(8,128)(2,1)S(1)} %copy-done.6, bf16[320,2176]{1,0:T(8,128)(2,1)} %collective-permute-done.3), kind=kOutput, calls=%fused_computation.2 | convolution fusion | flops 640445440 | bytes 13281280 | tf_op jit(solution)/shard_map/qhd,khd->hqk/dot_general | solution.py:135
  75.6 5.9 %fusion.2 = (bf16[16,320,480]{2,1,0:T(8,128)(2,1)}, f32[16,320]{1,0:T(8,128)}) fusion(f32[16,320,480]{2,1,0:T(8,128)S(1)} %get-tuple-element.39, f32[16,320]{1,0:T(8,128)S(1)} %get-tuple-element.38, pred[320,480]{1,0:T(8,128)(4,1)S(1)} %copy.30), kind=kLoop, calls=%fused_computation.7 | loop fusion | flops 14740480 | bytes 14940160 | tf_op jit(solution)/shard_map/convert_element_type | solution.py:141
  81.5 2.7 %fusion.52 = f32[16,128,320]{1,2,0:T(8,128)} fusion(f32[16,128,128]{2,1,0:T(8,128)S(1)} %bitcast.205, bf16[320,2048]{1,0:T(8,128)(2,1)S(1)} %copy-done), kind=kOutput, calls=%fused_computation.62 | convolution fusion | flops 1006632960 | bytes 4980736 | tf_op jit(solution)/shard_map/qhd,hde->qhe/dot_general | solution.py:152
  84.2 6.4 %multiply_reduce_fusion = (f32[320,16]{0,1:T(8,128)S(1)}, f32[320,16,128]{2,0,1:T(8,128)}) fusion(f32[16,128,320]{1,2,0:T(8,128)} %fusion.52, pred[320]{0:T(512)(128)(4,1)S(1)} %copy-done.15, pred[320,320]{0,1:T(8,128)(4,1)S(1)} %copy-done.9, bf16[320,2048]{1,0:T(8,128)(2,1)} %param.10, bf16[320,2048]{1,0:T(8,128)(2,1)} %param.9, ...), kind=kOutput, calls=%fused_computation.35 | convolution fusion | flops 844753920 | bytes 9298240 | tf_op jit(solution)/shard_map/hqk,khd->qhd/dot_general | solution.py:151
  90.6 2.5 %fusion.16 = bf16[320,16,128]{2,0,1:T(8,128)(2,1)S(1)} fusion(f32[320,16,128]{2,0,1:T(8,128)} %get-tuple-element.37, f32[16,128]{1,0:T(8,128)S(1)} %copy-done.13, f32[320,16]{0,1:T(8,128)S(1)} %add_rsqrt_fusion, bf16[320,2048]{1,0:T(8,128)(2,1)} %param.12), kind=kLoop, calls=%fused_computation.23 | loop fusion | flops 5242880 | bytes 5271552 | tf_op jit(solution)/shard_map/convert_element_type | solution.py:163
  94.2 2.1 %fusion.11 = (f32[16,160]{1,0:T(8,128)S(1)}, f32[16,160,320]{2,1,0:T(8,128)S(1)}) fusion(pred[160,320]{1,0:T(8,128)(4,1)S(1)} %broadcast_compare_fusion.1, bf16[320,2048]{1,0:T(8,128)(2,1)S(1)} %copy-done.3, bf16[160,2176]{1,0:T(8,128)(2,1)} %collective-permute-done.4), kind=kOutput, calls=%fused_computation.18 | convolution fusion | flops 212170240 | bytes 5304320 | tf_op jit(solution)/shard_map/qhd,khd->hqk/dot_general | solution.py:135
  96.3 1.6 %fusion.14 = f32[16,160]{1,0:T(8,128)S(1)} fusion(f32[16,160,320]{2,1,0:T(8,128)S(1)} %get-tuple-element.41, f32[16,160]{1,0:T(8,128)S(1)} %get-tuple-element.40, pred[160,320]{1,0:T(8,128)(4,1)S(1)} %broadcast_compare_fusion.1), kind=kLoop, calls=%fused_computation.20 | loop fusion | flops 4093440 | bytes 3348480 | tf_op jit(solution)/shard_map/reduce_sum | solution.py:141
  97.9 5.3 %collective-permute-start.6 = (f32[2,16,160]{2,1,0:T(8,128)S(1)}, f32[2,16,160]{2,1,0:T(8,128)S(1)}, u32[]{:S(2)}, u32[]{:S(2)}) collective-permute-start(f32[2,16,160]{2,1,0:T(8,128)S(1)} %pad_maximum_fusion.3), channel_id=1, source_target_pairs={{0,4},{4,8},{8,12},{1,5},{5,9},{9,13},{2,6},{6,10},{10,14},{3,7},{... | collective-permute-start | bytes 61448 | tf_op jit(solution)/shard_map/ppermute | solution.py:15
  103.2 1.5 fusion.67
  104.7 4.2 %collective-permute-start.5 = (bf16[160,16,128]{2,0,1:T(8,128)(2,1)S(1)}, bf16[160,16,128]{2,0,1:T(8,128)(2,1)S(1)}, u32[]{:S(2)}, u32[]{:S(2)}) collective-permute-start(bf16[160,16,128]{2,0,1:T(8,128)(2,1)S(1)} %fusion.67), channel_id=1, source_target_pairs={{0,4},{4,8},{8,12},{1,5},{5,9},{9,13},{2,6},{6,10},{10,14},{3,7},{... | collective-permute-start | bytes 1966088 | tf_op jit(solution)/shard_map/ppermute | solution.py:15
  110.2 10.1 %collective-permute-done.5 = bf16[160,16,128]{2,0,1:T(8,128)(2,1)S(1)} collective-permute-done((bf16[160,16,128]{2,0,1:T(8,128)(2,1)S(1)}, bf16[160,16,128]{2,0,1:T(8,128)(2,1)S(1)}, u32[]{:S(2)}, u32[]{:S(2)}) %collective-permute-start.5) | collective-permute-done | bytes 655392 | tf_op jit(solution)/shard_map/ppermute | solution.py:15
  120.4 2.4 %fusion.23 = bf16[320,16,128]{2,0,1:T(8,128)(2,1)S(1)} fusion(f32[16,128,320]{1,2,0:T(8,128)S(1)} %fusion.7, f32[160,16,128]{2,0,1:T(8,128)S(1)} %convert_select_fusion, bf16[16,320,480]{2,1,0:T(8,128)(2,1)S(1)} %bitcast.204, f32[320,16]{0,1:T(8,128)S(1)} %get-tuple-element.22, f32[320,16]{0,1:T(8,128)S(1)} %get-tuple-element.19, ...), kind=kOutput, calls=%fused_computation.32 | convolution fusion | flops 213319680 | bytes 8568833 | tf_op jit(solution)/shard_map/hqk,khd->qhd/dot_general | solution.py:166
  122.8 4.5 %collective-permute-start.7 = (bf16[320,16,128]{2,0,1:T(8,128)(2,1)S(1)}, bf16[320,16,128]{2,0,1:T(8,128)(2,1)S(1)}, u32[]{:S(2)}, u32[]{:S(2)}) collective-permute-start(bf16[320,16,128]{2,0,1:T(8,128)(2,1)S(1)} %fusion.23), channel_id=1, source_target_pairs={{0,4},{4,8},{8,12},{1,5},{5,9},{9,13},{2,6},{6,10},{10,14},{3,7},{... | collective-permute-start | bytes 3932168 | tf_op jit(solution)/shard_map/ppermute | solution.py:15
  128.5 4.1 %collective-permute-start.8 = (f32[2,16,320]{2,1,0:T(8,128)S(1)}, f32[2,16,320]{2,1,0:T(8,128)S(1)}, u32[]{:S(2)}, u32[]{:S(2)}) collective-permute-start(f32[2,16,320]{2,1,0:T(8,128)S(1)} %pad_maximum_fusion.2), channel_id=1, source_target_pairs={{0,4},{4,8},{8,12},{1,5},{5,9},{9,13},{2,6},{6,10},{10,14},{3,7},{... | collective-permute-start | bytes 122888 | tf_op jit(solution)/shard_map/ppermute | solution.py:15
  132.6 1.4 fusion.108
  134.0 19.0 %collective-permute-done.8 = f32[2,16,320]{2,1,0:T(8,128)S(1)} collective-permute-done((f32[2,16,320]{2,1,0:T(8,128)S(1)}, f32[2,16,320]{2,1,0:T(8,128)S(1)}, u32[]{:S(2)}, u32[]{:S(2)}) %collective-permute-start.8) | collective-permute-done | bytes 40992 | tf_op jit(solution)/shard_map/ppermute | solution.py:15
  153.0 3.6 %copy_bitcast_fusion = bf16[320,2048]{1,0:T(8,128)(2,1)} fusion(f32[320,16]{0,1:T(8,128)S(1)} %get-tuple-element.17, f32[320,16]{0,1:T(8,128)S(1)} %get-tuple-element.18, f32[16,128,320]{1,2,0:T(8,128)S(1)} %fusion.108, f32[320,16]{0,1:T(8,128)S(1)} %get-tuple-element.16, bf16[320,16,128]{2,0,1:T(8,128)(2,1)S(1)} %collective-permute-done.7, pred[]{:T(512)S(6)} %ge.25), kind=kLoop, calls=%fused_computation.48 | loop fusion | flops 4587520 | bytes 5304321 | tf_op jit(solution)/shard_map/reshape | solution.py:236
  (73 shorter events, 18.0 us)
Async XLA Ops:
  0.6 80.9 %copy-start = (bf16[320,2048]{1,0:T(8,128)(2,1)S(1)}, bf16[320,2048]{1,0:T(8,128)(2,1)}, u32[]{:S(2)}) copy-start(bf16[320,2048]{1,0:T(8,128)(2,1)} %param.8) | copy-start | bytes 3932164
  3.5 42.2 %collective-permute-start.2 = (bf16[160,2176]{1,0:T(8,128)(2,1)}, bf16[160,2176]{1,0:T(8,128)(2,1)S(1)}, u32[]{:S(2)}, u32[]{:S(2)}) collective-permute-start(bf16[160,2176]{1,0:T(8,128)(2,1)} %pad_maximum_fusion.1), channel_id=1, source_target_pairs={{0,4},{4,8},{8,12},{1,5},{5,9},{9,13},{2,6},{6,10},{10,14},{3,7},{... | collective-permute-start | bytes 2088968 | tf_op jit(solution)/shard_map/ppermute | solution.py:15
  13.1 8.8 %copy-start.5 = (bf16[320,2048]{1,0:T(8,128)(2,1)S(1)}, bf16[320,2048]{1,0:T(8,128)(2,1)}, u32[]{:S(2)}) copy-start(bf16[320,2048]{1,0:T(8,128)(2,1)} %param.13) | copy-start | bytes 3932164
  16.8 10.1 %copy-start.14 = (bf16[2048]{0:T(1024)(128)(2,1)S(1)}, bf16[2048]{0:T(1024)(128)(2,1)}, u32[]{:S(2)}) copy-start(bf16[2048]{0:T(1024)(128)(2,1)} %param.11) | copy-start | bytes 12292
  16.8 10.7 %copy-start.3 = (bf16[320,2048]{1,0:T(8,128)(2,1)S(1)}, bf16[320,2048]{1,0:T(8,128)(2,1)}, u32[]{:S(2)}) copy-start(bf16[320,2048]{1,0:T(8,128)(2,1)} %param.14) | copy-start | bytes 3932164
  17.6 17.3 %collective-permute-start = (bf16[2056,128]{1,0:T(8,128)(2,1)}, bf16[2056,128]{1,0:T(8,128)(2,1)}, u32[]{:S(2)}, u32[]{:S(2)}) collective-permute-start(bf16[2056,128]{1,0:T(8,128)(2,1)} %concatenate.27), channel_id=1, source_target_pairs={{0,4},{4,8},{8,12},{1,5},{5,9},{9,13},{2,6},{6,10},{10,14},{3,7},{... | collective-permute-start | bytes 1579016 | tf_op jit(solution)/shard_map/ppermute | solution.py:15
  23.0 37.2 %collective-permute-start.3 = (bf16[320,2176]{1,0:T(8,128)(2,1)}, bf16[320,2176]{1,0:T(8,128)(2,1)}, u32[]{:S(2)}, u32[]{:S(2)}) collective-permute-start(bf16[320,2176]{1,0:T(8,128)(2,1)} %pad_maximum_fusion), channel_id=1, source_target_pairs={{4,0},{8,4},{12,8},{5,1},{9,5},{13,9},{6,2},{10,6},{14,10},{7,3},{... | collective-permute-start | bytes 4177928 | tf_op jit(solution)/shard_map/ppermute | solution.py:19
  39.8 21.5 %copy-start.11 = (s32[320]{0:T(512)S(1)}, s32[320]{0:T(512)}, u32[]{:S(2)}) copy-start(s32[320]{0:T(512)} %param.15) | copy-start | bytes 3844
  40.6 15.0 %collective-permute-start.1 = (bf16[2056,128]{1,0:T(8,128)(2,1)}, bf16[2056,128]{1,0:T(8,128)(2,1)}, u32[]{:S(2)}, u32[]{:S(2)}) collective-permute-start(bf16[2056,128]{1,0:T(8,128)(2,1)} %concatenate.28), channel_id=1, source_target_pairs={{0,4},{4,8},{8,12},{1,5},{5,9},{9,13},{2,6},{6,10},{10,14},{3,7},{... | collective-permute-start | bytes 1579016 | tf_op jit(solution)/shard_map/ppermute | solution.py:15
  63.7 29.4 %collective-permute-start.4 = (bf16[160,2176]{1,0:T(8,128)(2,1)S(1)}, bf16[160,2176]{1,0:T(8,128)(2,1)}, u32[]{:S(2)}, u32[]{:S(2)}) collective-permute-start(bf16[160,2176]{1,0:T(8,128)(2,1)S(1)} %slice.107), channel_id=1, source_target_pairs={{4,0},{8,4},{12,8},{5,1},{9,5},{13,9},{6,2},{10,6},{14,10},{7,3},{... | collective-permute-start | bytes 2088968 | tf_op jit(solution)/shard_map/ppermute | solution.py:19
  65.2 3.0 %copy-start.8 = (pred[320,320]{0,1:T(8,128)(4,1)S(1)}, pred[320,320]{0,1:T(8,128)(4,1)}, u32[]{:S(2)}) copy-start(pred[320,320]{0,1:T(8,128)(4,1)} %get-tuple-element.29) | copy-start | bytes 307204
  68.2 3.7 %copy-start.6 = (bf16[320,16,128]{2,0,1:T(8,128)(2,1)S(1)}, bf16[320,16,128]{2,0,1:T(8,128)(2,1)}, u32[]{:S(2)}) copy-start(bf16[320,16,128]{2,0,1:T(8,128)(2,1)} %copy_bitcast_fusion.2) | copy-start | bytes 3932164
  68.3 3.6 %copy-start.7 = (bf16[160,16,128]{2,0,1:T(8,128)(2,1)S(1)}, bf16[160,16,128]{2,0,1:T(8,128)(2,1)}, u32[]{:S(2)}) copy-start(bf16[160,16,128]{2,0,1:T(8,128)(2,1)} %copy_bitcast_fusion.3) | copy-start | bytes 1966084
  75.6 6.0 %copy-start.4 = (f32[2048,128]{1,0:T(8,128)S(1)}, f32[2048,128]{1,0:T(8,128)}, u32[]{:S(2)}) copy-start(f32[2048,128]{1,0:T(8,128)} %convert_select_fusion.1) | copy-start | bytes 3145732
  81.5 2.7 %copy-start.9 = (pred[320,320]{0,1:T(8,128)(4,1)S(1)}, pred[320,320]{0,1:T(8,128)(4,1)}, u32[]{:S(2)}) copy-start(pred[320,320]{0,1:T(8,128)(4,1)} %get-tuple-element.29) | copy-start | bytes 307204
  81.5 2.7 %copy-start.15 = (pred[320]{0:T(512)(128)(4,1)S(1)}, pred[320]{0:T(512)(128)(4,1)}, u32[]{:S(2)}) copy-start(pred[320]{0:T(512)(128)(4,1)} %get-tuple-element.30) | copy-start | bytes 964
  84.2 6.4 %copy-start.13 = (f32[16,128]{1,0:T(8,128)S(1)}, f32[16,128]{1,0:T(8,128)}, u32[]{:S(2)}) copy-start(f32[16,128]{1,0:T(8,128)} %bitcast_convert_fusion) | copy-start | bytes 24580
  90.6 3.5 %copy-start.12 = (s32[320]{0:T(512)S(1)}, s32[320]{0:T(512)}, u32[]{:S(2)}) copy-start(s32[320]{0:T(512)} %param.15) | copy-start | bytes 3844
  97.9 11.0 %slice-start = ((s8[5242880]{0:T(1024)(128)(4,1)}), s8[4194304]{0:T(1024)(128)(4,1)S(1)}, s32[]{:S(2)}) async-start(s8[5242880]{0:T(1024)(128)(4,1)} %bitcast.203), calls=%async_computation | async-start | bytes 8388608
  97.9 11.0 %slice-start.1 = ((s8[5242880]{0:T(1024)(128)(4,1)}), s8[1048576]{0:T(1024)(128)(4,1)S(1)}, s32[]{:S(2)}) async-start(s8[5242880]{0:T(1024)(128)(4,1)} %bitcast.203), calls=%async_computation.1 | async-start | bytes 2097152
  97.9 12.2 %collective-permute-start.6 = (f32[2,16,160]{2,1,0:T(8,128)S(1)}, f32[2,16,160]{2,1,0:T(8,128)S(1)}, u32[]{:S(2)}, u32[]{:S(2)}) collective-permute-start(f32[2,16,160]{2,1,0:T(8,128)S(1)} %pad_maximum_fusion.3), channel_id=1, source_target_pairs={{0,4},{4,8},{8,12},{1,5},{5,9},{9,13},{2,6},{6,10},{10,14},{3,7},{... | collective-permute-start | bytes 61448 | tf_op jit(solution)/shard_map/ppermute | solution.py:15
  104.7 15.5 %collective-permute-start.5 = (bf16[160,16,128]{2,0,1:T(8,128)(2,1)S(1)}, bf16[160,16,128]{2,0,1:T(8,128)(2,1)S(1)}, u32[]{:S(2)}, u32[]{:S(2)}) collective-permute-start(bf16[160,16,128]{2,0,1:T(8,128)(2,1)S(1)} %fusion.67), channel_id=1, source_target_pairs={{0,4},{4,8},{8,12},{1,5},{5,9},{9,13},{2,6},{6,10},{10,14},{3,7},{... | collective-permute-start | bytes 1966088 | tf_op jit(solution)/shard_map/ppermute | solution.py:15
  108.9 1.2 copy-start.10
  120.4 12.3 %copy-start.2 = (bf16[16,320,320]{1,2,0:T(8,128)(2,1)S(1)}, bf16[16,320,320]{1,2,0:T(8,128)(2,1)}, u32[]{:S(2)}) copy-start(bf16[16,320,320]{1,2,0:T(8,128)(2,1)} %get-tuple-element.8) | copy-start | bytes 9830404
  122.8 30.2 %collective-permute-start.7 = (bf16[320,16,128]{2,0,1:T(8,128)(2,1)S(1)}, bf16[320,16,128]{2,0,1:T(8,128)(2,1)S(1)}, u32[]{:S(2)}, u32[]{:S(2)}) collective-permute-start(bf16[320,16,128]{2,0,1:T(8,128)(2,1)S(1)} %fusion.23), channel_id=1, source_target_pairs={{0,4},{4,8},{8,12},{1,5},{5,9},{9,13},{2,6},{6,10},{10,14},{3,7},{... | collective-permute-start | bytes 3932168 | tf_op jit(solution)/shard_map/ppermute | solution.py:15
  128.5 24.4 %collective-permute-start.8 = (f32[2,16,320]{2,1,0:T(8,128)S(1)}, f32[2,16,320]{2,1,0:T(8,128)S(1)}, u32[]{:S(2)}, u32[]{:S(2)}) collective-permute-start(f32[2,16,320]{2,1,0:T(8,128)S(1)} %pad_maximum_fusion.2), channel_id=1, source_target_pairs={{0,4},{4,8},{8,12},{1,5},{5,9},{9,13},{2,6},{6,10},{10,14},{3,7},{... | collective-permute-start | bytes 122888 | tf_op jit(solution)/shard_map/ppermute | solution.py:15
  153.0 3.6 %copy-start.1 = (bf16[320,2048]{1,0:T(8,128)(2,1)S(1)}, bf16[320,2048]{1,0:T(8,128)(2,1)}, u32[]{:S(2)}) copy-start(bf16[320,2048]{1,0:T(8,128)(2,1)} %param.8) | copy-start | bytes 3932164

commit v12 on v6

--- a/solution.py
+++ b/solution.py
@@ -114,32 +114,37 @@
     normed = lin_raw * lax.rsqrt(mean_square + norm_eps) * gain_rows * gate_rows
     lin_out = normed.astype(jnp.bfloat16).reshape(row_count, width)
 
-    value_blocks = [lin_out.reshape(row_count, head_count, HD)]
-    for d in dists[:-1]:
-        value_blocks.append(shift_up(value_blocks[-1], 1, n_seq))
-
+    value_own = lin_out.reshape(row_count, head_count, HD)
     probs, ahead_max, ahead_sum = ahead
-    ahead_out = jnp.zeros((row_count, head_count, HD), jnp.float32)
-    for d, value_block in enumerate(value_blocks):
-        ahead_out = ahead_out + jnp.einsum(
-            "hqk,khd->qhd",
-            probs[:, :, d * row_count : (d + 1) * row_count],
-            value_block,
-            preferred_element_type=jnp.float32,
+    diag_probs, diag_max, diag_sum = diag
+    has_source = my_index >= 1
+    half = head_count // 2
+    pieces = []
+    for lo, hi in ((0, half), (half, head_count)):
+        value_blocks = [value_own[:, lo:hi]]
+        for d in dists[:-1]:
+            value_blocks.append(shift_up(value_blocks[-1], 1, n_seq))
+        ahead_out = jnp.zeros((row_count, hi - lo, HD), jnp.float32)
+        for d, value_block in enumerate(value_blocks):
+            ahead_out = ahead_out + jnp.einsum(
+                "hqk,khd->qhd",
+                probs[lo:hi, :, d * row_count : (d + 1) * row_count],
+                value_block,
+                preferred_element_type=jnp.float32,
+            )
+        out_in = shift_up(ahead_out.astype(jnp.bfloat16), 1, n_seq)
+        stats_in = shift_up(jnp.stack([ahead_max[lo:hi], ahead_sum[lo:hi]]), 1, n_seq)
+        max_in = jnp.where(has_source, stats_in[0], -1e30)
+        sum_in = jnp.where(has_source, stats_in[1], 0.0)
+        out_in = jnp.where(has_source, out_in.astype(jnp.float32), 0.0)
+        diag_out = jnp.einsum(
+            "hqk,khd->qhd", diag_probs[lo:hi], value_blocks[0], preferred_element_type=jnp.float32
         )
-    out_in = shift_up(ahead_out.astype(jnp.bfloat16), 1, n_seq)
-    stats_in = shift_up(jnp.stack([ahead_max, ahead_sum]), 1, n_seq)
-    has_source = my_index >= 1
-    max_in = jnp.where(has_source, stats_in[0], -1e30)
-    sum_in = jnp.where(has_source, stats_in[1], 0.0)
-    out_in = jnp.where(has_source, out_in.astype(jnp.float32), 0.0)
-
-    diag_probs, diag_max, diag_sum = diag
-    diag_out = jnp.einsum(
-        "hqk,khd->qhd", diag_probs, value_blocks[0], preferred_element_type=jnp.float32
-    )
-    mixed, row_max, row_sum = merge((out_in, max_in, sum_in), (diag_out, diag_max, diag_sum))
-    soft_out = mixed / jnp.transpose(row_sum)[:, :, None]
+        mixed, row_max, row_sum = merge(
+            (out_in, max_in, sum_in), (diag_out, diag_max[lo:hi], diag_sum[lo:hi])
+        )
+        pieces.append(mixed / jnp.transpose(row_sum)[:, :, None])
+    soft_out = jnp.concatenate(pieces, axis=1)
     return (lin_out, soft_out.astype(jnp.bfloat16).reshape(row_count, width))
 
 

time: 144 us -> 137 us (0.951)
  waiting for transfers between devices: 54.1 us -> 37.1 us
  starting transfers between devices: 27.9 us -> 35.5 us
  other arithmetic: 14.8 us -> 19.6 us
  local copies, waits for them, and re-layouts: 10.4 us -> 8.93 us
    ppermute x6 -> x9, waiting for transfers between devices: 54.1 us -> 37.1 us  [shift_up(): return lax.ppermute(x, 'seq', [(s, s + dist) for s in range(n_seq - dist)])]
    ppermute x6 -> x9, starting transfers between devices: 26.6 us -> 34.2 us  [shift_up(): return lax.ppermute(x, 'seq', [(s, s + dist) for s in range(n_seq - dist)])]
    convert_element_type x0 -> x2, other arithmetic: none -> 6.43 us  [the longest x1 5.17 us: weights_of(): return (probs.astype(jnp.bfloat16), row_max, jnp.sum(probs, axis=-1))]
    reduce_sum x2 -> x1, other arithmetic: 7.06 us -> 5.75 us  [weights_of(): return (probs.astype(jnp.bfloat16), row_max, jnp.sum(probs, axis=-1))]
    dot_general x3 -> x6, matrix products: 7.47 us -> 6.4 us  [the longest x2 3.42 us: per_device(): jnp.einsum('hqk,khd->qhd', diag_probs[lo:hi], value_blocks[0], preferred_...]
  transfers between devices with their start and end apart: 7 -> 10, of which waited for: 3 -> 4; matrix products, arithmetic and copies ran while one was open for 28% -> 35% of each run, Pallas kernels for 0% -> 0%
where the time goes in v12:
time: 137 us; the launch traced here: 136 us
  waiting for transfers between devices  37.1 us (27%)
  starting transfers between devices  35.5 us (26%)
  matrix products  29.7 us (22%)
  other arithmetic  19.6 us (14%)
  local copies, waits for them, and re-layouts  8.93 us (7%)
  between operations  5.29 us (4%)
    ppermute x9, waiting for transfers between devices, shift_up(): return lax.ppermute(x, 'seq', [(s, s + dist) for s in range(n_seq - dist)])  37.1 us
    ppermute x9, starting transfers between devices, shift_up(): return lax.ppermute(x, 'seq', [(s, s + dist) for s in range(n_seq - dist)])  34.2 us
    dot_general x2, matrix products, weights_of(): jnp.einsum('qhd,khd->hqk', query_rows, key_all, preferred_element_type=jn...  10.1 us
    reduce_sum x1, other arithmetic, weights_of(): return (probs.astype(jnp.bfloat16), row_max, jnp.sum(probs, axis=-1))  5.75 us
    dot_general x1, matrix products, per_device(): jnp.einsum('hqk,khd->qhd', rounded, value_rows, preferred_element_type=jn...  5.48 us
    convert_element_type x1, other arithmetic, weights_of(): return (probs.astype(jnp.bfloat16), row_max, jnp.sum(probs, axis=-1))  5.17 us
    dot_general x1, matrix products, per_device(): jnp.einsum('qhd,hde->qhe', queries.astype(jnp.float32), carried, precisio...  3.98 us
    dot_general x1, matrix products, per_device(): jnp.einsum('thd,the->hde', tail_keys, value_rows, preferred_element_type=...  3.72 us
  transfers between devices with their start and end apart: 10, of which 4 were waited for; matrix products, arithmetic and copies ran while one was open for 35% of the time, Pallas kernels for 0%

profile of v12, /device:TPU:0, one launch (start us, length us, event | category | flops | bytes accessed | tf_op | source)
XLA Modules:
  0.0 136.1 jit_solution(12018320520641821138)
XLA Ops:
  0.6 1.4 %fusion.106 = (s32[1]{0:T(128)}, s32[1]{0:T(128)}) fusion(s32[320]{0:T(512)} %param.15), kind=kLoop, calls=%fused_computation.130 | loop fusion | bytes 16 | tf_op jit(solution)/shard_map/slice | solution.py:45
  2.7 1.9 %broadcast_compare_fusion.1 = (pred[320]{0:T(512)(128)(4,1)S(1)}, pred[320]{0:T(512)(128)(4,1)S(1)}) fusion(s32[320]{0:T(512)} %param.15, s32[]{:T(128)} %bitcast.1, s32[]{:T(128)} %bitcast.2), kind=kLoop, calls=%fused_computation.123 | loop fusion | flops 640 | bytes 1928 | tf_op jit(solution)/shard_map/eq | solution.py:108
  4.6 3.7 %fusion.107 = (bf16[16,128,128]{2,1,0:T(8,128)(2,1)S(1)}, f32[16,128,128]{2,1,0:T(8,128)}) fusion(pred[320]{0:T(512)(128)(4,1)S(1)} %get-tuple-element.21, bf16[320,2048]{1,0:T(8,128)(2,1)} %param.10, bf16[320,2048]{1,0:T(8,128)(2,1)} %param.9), kind=kOutput, calls=%fused_computation.131 | convolution fusion | flops 168689664 | bytes 4194624 | tf_op jit(solution)/shard_map/thd,the->hde/dot_general | solution.py:51
  8.3 5.7 %collective-permute-start = (bf16[2056,128]{1,0:T(8,128)(2,1)S(1)}, bf16[2056,128]{1,0:T(8,128)(2,1)}, u32[]{:S(2)}, u32[]{:S(2)}) collective-permute-start(bf16[2056,128]{1,0:T(8,128)(2,1)S(1)} %concatenate.28), channel_id=1, source_target_pairs={{0,4},{4,8},{8,12},{1,5},{5,9},{9,13},{2,6},{6,10},{10,14},{3,7},{... | collective-permute-start | bytes 1579016 | tf_op jit(solution)/shard_map/ppermute | solution.py:15
  14.2 1.8 %pad_maximum_fusion.1 = (bf16[320,2176]{1,0:T(8,128)(2,1)}, bf16[320,2176]{1,0:T(8,128)(2,1)}) fusion(bf16[320,128]{1,0:T(8,128)(2,1)S(1)} %broadcast_in_dim.125, bf16[320,2048]{1,0:T(8,128)(2,1)S(1)} %copy-done.6, bf16[320,2048]{1,0:T(8,128)(2,1)S(1)} %copy-done.2), kind=kLoop, calls=%fused_computation.37 | loop fusion | flops 4874240 | bytes 5488640 | tf_op jit(solution)/shard_map/concatenate | solution.py:68
  16.0 3.8 %collective-permute-start.3 = (bf16[320,2176]{1,0:T(8,128)(2,1)}, bf16[320,2176]{1,0:T(8,128)(2,1)}, u32[]{:S(2)}, u32[]{:S(2)}) collective-permute-start(bf16[320,2176]{1,0:T(8,128)(2,1)} %get-tuple-element.9), channel_id=1, source_target_pairs={{0,4},{4,8},{8,12},{1,5},{5,9},{9,13},{2,6},{6,10},{10,14},{3,7},{... | collective-permute-start | bytes 4177928 | tf_op jit(solution)/shard_map/ppermute | solution.py:15
  19.8 1.3 collective-permute-start.2
  22.5 1.4 %copy_bitcast_fusion.3 = bf16[320,16,128]{2,0,1:T(8,128)(2,1)} fusion(bf16[320,2048]{1,0:T(8,128)(2,1)S(1)} %copy-done.2), kind=kLoop, calls=%fused_computation.52 | loop fusion | bytes 2621440 | tf_op jit(solution)/shard_map/reshape | solution.py:74
  23.9 6.0 %fusion.3 = (f32[16,320]{1,0:T(8,128)S(1)}, f32[16,320,320]{1,2,0:T(8,128)}) fusion(pred[320,320]{0,1:T(8,128)(4,1)S(1)} %fusion.81, bf16[320,2048]{1,0:T(8,128)(2,1)} %param.13, bf16[320,2048]{1,0:T(8,128)(2,1)S(1)} %copy-done.2), kind=kOutput, calls=%fused_computation.8 | convolution fusion | flops 424340480 | bytes 9297920 | tf_op jit(solution)/shard_map/qhd,khd->hqk/dot_general | solution.py:84
  29.9 5.7 %fusion.4 = (f32[16,320]{1,0:T(8,128)S(1)}, bf16[16,320,320]{1,2,0:T(8,128)(2,1)}) fusion(f32[16,320,320]{1,2,0:T(8,128)} %get-tuple-element.29, f32[16,320]{1,0:T(8,128)S(1)} %get-tuple-element.28, pred[320,320]{0,1:T(8,128)(4,1)S(1)} %fusion.81), kind=kLoop, calls=%fused_computation.9 | loop fusion | flops 9825280 | bytes 9973760 | tf_op jit(solution)/shard_map/reduce_sum | solution.py:90
  35.6 1.3 slice.121
  38.1 1.1 convert_select_fusion.1
  39.5 4.6 %collective-permute-start.1 = (bf16[2056,128]{1,0:T(8,128)(2,1)S(1)}, bf16[2056,128]{1,0:T(8,128)(2,1)S(1)}, u32[]{:S(2)}, u32[]{:S(2)}) collective-permute-start(bf16[2056,128]{1,0:T(8,128)(2,1)S(1)} %concatenate.29), channel_id=1, source_target_pairs={{0,4},{4,8},{8,12},{1,5},{5,9},{9,13},{2,6},{6,10},{10,14},{3,7},{... | collective-permute-start | bytes 1579016 | tf_op jit(solution)/shard_map/ppermute | solution.py:15
  44.1 5.5 %fusion.6 = f32[16,320,128]{2,1,0:T(8,128)} fusion(pred[320,320]{0,1:T(8,128)(4,1)S(1)} %fusion.81, bf16[320,2048]{1,0:T(8,128)(2,1)} %param.10, bf16[320,2048]{1,0:T(8,128)(2,1)} %param.9, bf16[320,2048]{1,0:T(8,128)(2,1)S(1)} %copy-done), kind=kOutput, calls=%fused_computation.11 | convolution fusion | flops 842137600 | bytes 6656000 | tf_op jit(solution)/shard_map/hqk,khd->qhd/dot_general | solution.py:103
  49.6 16.0 %collective-permute-done.1 = bf16[2056,128]{1,0:T(8,128)(2,1)S(1)} collective-permute-done((bf16[2056,128]{1,0:T(8,128)(2,1)S(1)}, bf16[2056,128]{1,0:T(8,128)(2,1)S(1)}, u32[]{:S(2)}, u32[]{:S(2)}) %collective-permute-start.1) | collective-permute-done | bytes 526368 | tf_op jit(solution)/shard_map/ppermute | solution.py:15
  67.4 4.0 %multiply_reduce_fusion = (f32[320,16]{0,1:T(8,128)S(1)}, f32[320,16,128]{2,0,1:T(8,128)S(1)}) fusion(f32[16,128,128]{2,1,0:T(8,128)S(1)} %bitcast.191, pred[320]{0:T(512)(128)(4,1)S(1)} %get-tuple-element.20, f32[16,320,128]{2,1,0:T(8,128)} %fusion.6, bf16[320,2048]{1,0:T(8,128)(2,1)S(1)} %copy-done), kind=kOutput, calls=%fused_computation.23 | convolution fusion | flops 1009249280 | bytes 7622976 | tf_op jit(solution)/shard_map/qhd,hde->qhe/dot_general | solution.py:104
  72.5 4.4 %collective-permute-start.4 = (bf16[320,8,128]{2,0,1:T(8,128)(2,1)S(1)}, bf16[320,8,128]{2,0,1:T(8,128)(2,1)S(1)}, u32[]{:S(2)}, u32[]{:S(2)}) collective-permute-start(bf16[320,8,128]{2,0,1:T(8,128)(2,1)S(1)} %get-tuple-element.6), channel_id=1, source_target_pairs={{0,4},{4,8},{8,12},{1,5},{5,9},{9,13},{2,6},{6,10},{10,14},{3,7},{... | collective-permute-start | bytes 1966088 | tf_op jit(solution)/shard_map/ppermute | solution.py:15
  76.9 3.7 %collective-permute-start.7 = (bf16[320,8,128]{2,0,1:T(8,128)(2,1)S(1)}, bf16[320,8,128]{2,0,1:T(8,128)(2,1)S(1)}, u32[]{:S(2)}, u32[]{:S(2)}) collective-permute-start(bf16[320,8,128]{2,0,1:T(8,128)(2,1)S(1)} %get-tuple-element.7), channel_id=1, source_target_pairs={{0,4},{4,8},{8,12},{1,5},{5,9},{9,13},{2,6},{6,10},{10,14},{3,7},{... | collective-permute-start | bytes 1966088 | tf_op jit(solution)/shard_map/ppermute | solution.py:15
  80.6 1.3 copy_bitcast_fusion.1
  82.9 1.0 convert_reduce_fusion
  84.2 1.8 %copy_bitcast_fusion.2 = bf16[320,16,128]{2,0,1:T(8,128)(2,1)S(1)} fusion(bf16[320,2176]{1,0:T(8,128)(2,1)} %collective-permute-done.3), kind=kLoop, calls=%fused_computation.51 | loop fusion | bytes 2621440 | tf_op jit(solution)/shard_map/reshape | solution.py:74
  85.9 4.1 %fusion = (f32[16,320]{1,0:T(8,128)S(1)}, f32[16,320,640]{2,1,0:T(8,128)S(1)}) fusion(pred[320,640]{1,0:T(8,128)(4,1)S(1)} %compare_and_fusion, bf16[320,16,128]{2,0,1:T(8,128)(2,1)S(1)} %copy_bitcast_fusion.2, bf16[320,16,128]{2,0,1:T(8,128)(2,1)S(1)} %copy-done.5, bf16[320,2176]{1,0:T(8,128)(2,1)} %collective-permute-done.2), kind=kOutput, calls=%fused_computation.2 | convolution fusion | flops 853928960 | bytes 17264640 | tf_op jit(solution)/shard_map/qhd,khd->hqk/dot_general | solution.py:84
  90.1 5.2 %fusion.2 = (bf16[16,320,640]{2,1,0:T(8,128)(2,1)S(1)}, f32[16,320]{1,0:T(8,128)S(1)}) fusion(f32[16,320,640]{2,1,0:T(8,128)S(1)} %get-tuple-element.31, f32[16,320]{1,0:T(8,128)S(1)} %get-tuple-element.30, pred[320,640]{1,0:T(8,128)(4,1)S(1)} %compare_and_fusion), kind=kLoop, calls=%fused_computation.4 | loop fusion | flops 19655680 | bytes 19906560 | tf_op jit(solution)/shard_map/convert_element_type | solution.py:90
  95.3 3.5 %collective-permute-start.9 = (f32[2,8,320]{2,1,0:T(8,128)S(1)}, f32[2,8,320]{2,1,0:T(8,128)S(1)}, u32[]{:S(2)}, u32[]{:S(2)}) collective-permute-start(f32[2,8,320]{2,1,0:T(8,128)S(1)} %pad_maximum_fusion.3), channel_id=1, source_target_pairs={{0,4},{4,8},{8,12},{1,5},{5,9},{9,13},{2,6},{6,10},{10,14},{3,7},{... | collective-permute-start | bytes 61448 | tf_op jit(solution)/shard_map/ppermute | solution.py:15
  100.9 2.0 %collective-permute-start.5 = (bf16[320,8,128]{2,0,1:T(8,128)(2,1)S(1)}, bf16[320,8,128]{2,0,1:T(8,128)(2,1)S(1)}, u32[]{:S(2)}, u32[]{:S(2)}) collective-permute-start(bf16[320,8,128]{2,0,1:T(8,128)(2,1)S(1)} %fusion.66), channel_id=1, source_target_pairs={{0,4},{4,8},{8,12},{1,5},{5,9},{9,13},{2,6},{6,10},{10,14},{3,7},{... | collective-permute-start | bytes 1966088 | tf_op jit(solution)/shard_map/ppermute | solution.py:15
  102.9 2.1 %collective-permute-start.6 = (f32[2,8,320]{2,1,0:T(8,128)S(1)}, f32[2,8,320]{2,1,0:T(8,128)S(1)}, u32[]{:S(2)}, u32[]{:S(2)}) collective-permute-start(f32[2,8,320]{2,1,0:T(8,128)S(1)} %pad_maximum_fusion.2), channel_id=1, source_target_pairs={{0,4},{4,8},{8,12},{1,5},{5,9},{9,13},{2,6},{6,10},{10,14},{3,7},{... | collective-permute-start | bytes 61448 | tf_op jit(solution)/shard_map/ppermute | solution.py:15
  106.9 4.4 %collective-permute-start.8 = (bf16[320,8,128]{2,0,1:T(8,128)(2,1)S(1)}, bf16[320,8,128]{2,0,1:T(8,128)(2,1)S(1)}, u32[]{:S(2)}, u32[]{:S(2)}) collective-permute-start(bf16[320,8,128]{2,0,1:T(8,128)(2,1)S(1)} %fusion.69), channel_id=1, source_target_pairs={{0,4},{4,8},{8,12},{1,5},{5,9},{9,13},{2,6},{6,10},{10,14},{3,7},{... | collective-permute-start | bytes 1966088 | tf_op jit(solution)/shard_map/ppermute | solution.py:15
  111.3 9.8 %collective-permute-done.6 = f32[2,8,320]{2,1,0:T(8,128)S(1)} collective-permute-done((f32[2,8,320]{2,1,0:T(8,128)S(1)}, f32[2,8,320]{2,1,0:T(8,128)S(1)}, u32[]{:S(2)}, u32[]{:S(2)}) %collective-permute-start.6) | collective-permute-done | bytes 20512 | tf_op jit(solution)/shard_map/ppermute | solution.py:15
  121.2 1.7 %divide_convert_fusion.1 = bf16[320,8,128]{2,0,1:T(8,128)(2,1)S(1)} fusion(bf16[320,8,128]{2,0,1:T(8,128)(2,1)S(1)} %collective-permute-done.5, f32[320,8]{0,1:T(8,128)S(1)} %get-tuple-element.11, f32[320,8]{0,1:T(8,128)S(1)} %get-tuple-element.10, pred[]{:T(512)S(6)} %ge.29, f32[320,8]{0,1:T(8,128)S(1)} %get-tuple-element.15, ...), kind=kOutput, calls=%fused_computation.66 | convolution fusion | flops 212008960 | bytes 4624385 | tf_op jit(solution)/shard_map/hqk,khd->qhd/dot_general | solution.py:140
  122.9 10.2 %collective-permute-done.8 = bf16[320,8,128]{2,0,1:T(8,128)(2,1)S(1)} collective-permute-done((bf16[320,8,128]{2,0,1:T(8,128)(2,1)S(1)}, bf16[320,8,128]{2,0,1:T(8,128)(2,1)S(1)}, u32[]{:S(2)}, u32[]{:S(2)}) %collective-permute-start.8) | collective-permute-done | bytes 655392 | tf_op jit(solution)/shard_map/ppermute | solution.py:15
  133.1 1.7 %divide_convert_fusion = bf16[320,8,128]{2,0,1:T(8,128)(2,1)S(1)} fusion(bf16[320,8,128]{2,0,1:T(8,128)(2,1)S(1)} %collective-permute-done.8, f32[320,8]{0,1:T(8,128)S(1)} %get-tuple-element.12, f32[320,8]{0,1:T(8,128)S(1)} %get-tuple-element.14, pred[]{:T(512)S(6)} %ge.29, f32[320,8]{0,1:T(8,128)S(1)} %get-tuple-element.13, ...), kind=kOutput, calls=%fused_computation.65 | convolution fusion | flops 212008960 | bytes 4624385 | tf_op jit(solution)/shard_map/hqk,khd->qhd/dot_general | solution.py:140
  134.8 1.3 copy_bitcast_fusion
  (53 shorter events, 7.5 us)
Async XLA Ops:
  0.6 43.5 %copy-start = (bf16[320,2048]{1,0:T(8,128)(2,1)S(1)}, bf16[320,2048]{1,0:T(8,128)(2,1)}, u32[]{:S(2)}) copy-start(bf16[320,2048]{1,0:T(8,128)(2,1)} %param.8) | copy-start | bytes 3932164
  4.6 9.5 %copy-start.8 = (s32[320]{0:T(512)S(1)}, s32[320]{0:T(512)}, u32[]{:S(2)}) copy-start(s32[320]{0:T(512)} %param.15) | copy-start | bytes 3844
  4.6 9.6 %copy-start.2 = (bf16[320,2048]{1,0:T(8,128)(2,1)S(1)}, bf16[320,2048]{1,0:T(8,128)(2,1)}, u32[]{:S(2)}) copy-start(bf16[320,2048]{1,0:T(8,128)(2,1)} %param.14) | copy-start | bytes 3932164
  4.6 9.6 %copy-start.6 = (bf16[320,2048]{1,0:T(8,128)(2,1)S(1)}, bf16[320,2048]{1,0:T(8,128)(2,1)}, u32[]{:S(2)}) copy-start(bf16[320,2048]{1,0:T(8,128)(2,1)} %param.13) | copy-start | bytes 3932164
  8.3 27.3 %collective-permute-start = (bf16[2056,128]{1,0:T(8,128)(2,1)S(1)}, bf16[2056,128]{1,0:T(8,128)(2,1)}, u32[]{:S(2)}, u32[]{:S(2)}) collective-permute-start(bf16[2056,128]{1,0:T(8,128)(2,1)S(1)} %concatenate.28), channel_id=1, source_target_pairs={{0,4},{4,8},{8,12},{1,5},{5,9},{9,13},{2,6},{6,10},{10,14},{3,7},{... | collective-permute-start | bytes 1579016 | tf_op jit(solution)/shard_map/ppermute | solution.py:15
  16.0 65.8 %collective-permute-start.3 = (bf16[320,2176]{1,0:T(8,128)(2,1)}, bf16[320,2176]{1,0:T(8,128)(2,1)}, u32[]{:S(2)}, u32[]{:S(2)}) collective-permute-start(bf16[320,2176]{1,0:T(8,128)(2,1)} %get-tuple-element.9), channel_id=1, source_target_pairs={{0,4},{4,8},{8,12},{1,5},{5,9},{9,13},{2,6},{6,10},{10,14},{3,7},{... | collective-permute-start | bytes 4177928 | tf_op jit(solution)/shard_map/ppermute | solution.py:15
  19.8 63.1 %collective-permute-start.2 = (bf16[320,2176]{1,0:T(8,128)(2,1)}, bf16[320,2176]{1,0:T(8,128)(2,1)}, u32[]{:S(2)}, u32[]{:S(2)}) collective-permute-start(bf16[320,2176]{1,0:T(8,128)(2,1)} %get-tuple-element.8), channel_id=1, source_target_pairs={{4,0},{8,4},{12,8},{5,1},{9,5},{13,9},{6,2},{10,6},{14,10},{7,3},{... | collective-permute-start | bytes 4177928 | tf_op jit(solution)/shard_map/ppermute | solution.py:19
  35.6 3.6 %copy-start.7 = (f32[16,128,128]{2,1,0:T(8,128)S(1)}, f32[16,128,128]{2,1,0:T(8,128)}, u32[]{:S(2)}) copy-start(f32[16,128,128]{2,1,0:T(8,128)} %get-tuple-element.25) | copy-start | bytes 3145732
  39.2 4.8 %copy-start.9 = (bf16[2048]{0:T(1024)(128)(2,1)S(1)}, bf16[2048]{0:T(1024)(128)(2,1)}, u32[]{:S(2)}) copy-start(bf16[2048]{0:T(1024)(128)(2,1)} %param.11) | copy-start | bytes 12292
  39.5 26.1 %collective-permute-start.1 = (bf16[2056,128]{1,0:T(8,128)(2,1)S(1)}, bf16[2056,128]{1,0:T(8,128)(2,1)S(1)}, u32[]{:S(2)}, u32[]{:S(2)}) collective-permute-start(bf16[2056,128]{1,0:T(8,128)(2,1)S(1)} %concatenate.29), channel_id=1, source_target_pairs={{0,4},{4,8},{8,12},{1,5},{5,9},{9,13},{2,6},{6,10},{10,14},{3,7},{... | collective-permute-start | bytes 1579016 | tf_op jit(solution)/shard_map/ppermute | solution.py:15
  67.4 4.0 %copy-start.4 = (bf16[320,2048]{1,0:T(8,128)(2,1)S(1)}, bf16[320,2048]{1,0:T(8,128)(2,1)}, u32[]{:S(2)}) copy-start(bf16[320,2048]{1,0:T(8,128)(2,1)} %param.12) | copy-start | bytes 3932164
  72.5 27.6 %collective-permute-start.4 = (bf16[320,8,128]{2,0,1:T(8,128)(2,1)S(1)}, bf16[320,8,128]{2,0,1:T(8,128)(2,1)S(1)}, u32[]{:S(2)}, u32[]{:S(2)}) collective-permute-start(bf16[320,8,128]{2,0,1:T(8,128)(2,1)S(1)} %get-tuple-element.6), channel_id=1, source_target_pairs={{0,4},{4,8},{8,12},{1,5},{5,9},{9,13},{2,6},{6,10},{10,14},{3,7},{... | collective-permute-start | bytes 1966088 | tf_op jit(solution)/shard_map/ppermute | solution.py:15
  76.9 29.2 %collective-permute-start.7 = (bf16[320,8,128]{2,0,1:T(8,128)(2,1)S(1)}, bf16[320,8,128]{2,0,1:T(8,128)(2,1)S(1)}, u32[]{:S(2)}, u32[]{:S(2)}) collective-permute-start(bf16[320,8,128]{2,0,1:T(8,128)(2,1)S(1)} %get-tuple-element.7), channel_id=1, source_target_pairs={{0,4},{4,8},{8,12},{1,5},{5,9},{9,13},{2,6},{6,10},{10,14},{3,7},{... | collective-permute-start | bytes 1966088 | tf_op jit(solution)/shard_map/ppermute | solution.py:15
  84.2 1.8 %copy-start.5 = (bf16[320,16,128]{2,0,1:T(8,128)(2,1)S(1)}, bf16[320,16,128]{2,0,1:T(8,128)(2,1)}, u32[]{:S(2)}) copy-start(bf16[320,16,128]{2,0,1:T(8,128)(2,1)} %copy_bitcast_fusion.3) | copy-start | bytes 3932164
  95.3 16.1 %collective-permute-start.9 = (f32[2,8,320]{2,1,0:T(8,128)S(1)}, f32[2,8,320]{2,1,0:T(8,128)S(1)}, u32[]{:S(2)}, u32[]{:S(2)}) collective-permute-start(f32[2,8,320]{2,1,0:T(8,128)S(1)} %pad_maximum_fusion.3), channel_id=1, source_target_pairs={{0,4},{4,8},{8,12},{1,5},{5,9},{9,13},{2,6},{6,10},{10,14},{3,7},{... | collective-permute-start | bytes 61448 | tf_op jit(solution)/shard_map/ppermute | solution.py:15
  100.9 20.3 %collective-permute-start.5 = (bf16[320,8,128]{2,0,1:T(8,128)(2,1)S(1)}, bf16[320,8,128]{2,0,1:T(8,128)(2,1)S(1)}, u32[]{:S(2)}, u32[]{:S(2)}) collective-permute-start(bf16[320,8,128]{2,0,1:T(8,128)(2,1)S(1)} %fusion.66), channel_id=1, source_target_pairs={{0,4},{4,8},{8,12},{1,5},{5,9},{9,13},{2,6},{6,10},{10,14},{3,7},{... | collective-permute-start | bytes 1966088 | tf_op jit(solution)/shard_map/ppermute | solution.py:15
  102.9 18.3 %copy-start.3 = (bf16[16,320,320]{1,2,0:T(8,128)(2,1)S(1)}, bf16[16,320,320]{1,2,0:T(8,128)(2,1)}, u32[]{:S(2)}) copy-start(bf16[16,320,320]{1,2,0:T(8,128)(2,1)} %get-tuple-element.5) | copy-start | bytes 9830404
  102.9 18.2 %collective-permute-start.6 = (f32[2,8,320]{2,1,0:T(8,128)S(1)}, f32[2,8,320]{2,1,0:T(8,128)S(1)}, u32[]{:S(2)}, u32[]{:S(2)}) collective-permute-start(f32[2,8,320]{2,1,0:T(8,128)S(1)} %pad_maximum_fusion.2), channel_id=1, source_target_pairs={{0,4},{4,8},{8,12},{1,5},{5,9},{9,13},{2,6},{6,10},{10,14},{3,7},{... | collective-permute-start | bytes 61448 | tf_op jit(solution)/shard_map/ppermute | solution.py:15
  106.9 26.2 %collective-permute-start.8 = (bf16[320,8,128]{2,0,1:T(8,128)(2,1)S(1)}, bf16[320,8,128]{2,0,1:T(8,128)(2,1)S(1)}, u32[]{:S(2)}, u32[]{:S(2)}) collective-permute-start(bf16[320,8,128]{2,0,1:T(8,128)(2,1)S(1)} %fusion.69), channel_id=1, source_target_pairs={{0,4},{4,8},{8,12},{1,5},{5,9},{9,13},{2,6},{6,10},{10,14},{3,7},{... | collective-permute-start | bytes 1966088 | tf_op jit(solution)/shard_map/ppermute | solution.py:15
  133.1 3.0 %copy-start.1 = (bf16[320,2048]{1,0:T(8,128)(2,1)S(1)}, bf16[320,2048]{1,0:T(8,128)(2,1)}, u32[]{:S(2)}) copy-start(bf16[320,2048]{1,0:T(8,128)(2,1)} %param.8) | copy-start | bytes 3932164

commit v13 on v12

--- a/solution.py
+++ b/solution.py
@@ -118,9 +118,10 @@
     probs, ahead_max, ahead_sum = ahead
     diag_probs, diag_max, diag_sum = diag
     has_source = my_index >= 1
-    half = head_count // 2
+    group = head_count // 4 if head_count % 4 == 0 else head_count // 2
     pieces = []
-    for lo, hi in ((0, half), (half, head_count)):
+    for lo in range(0, head_count, group):
+        hi = min(lo + group, head_count)
         value_blocks = [value_own[:, lo:hi]]
         for d in dists[:-1]:
             value_blocks.append(shift_up(value_blocks[-1], 1, n_seq))

time: 137 us -> 139 us (1.015)
  starting transfers between devices: 35.5 us -> 47.4 us
  waiting for transfers between devices: 37.1 us -> 25.6 us
    ppermute x9 -> x15, starting transfers between devices: 34.2 us -> 46.1 us  [shift_up(): return lax.ppermute(x, 'seq', [(s, s + dist) for s in range(n_seq - dist)])]
    ppermute x9 -> x15, waiting for transfers between devices: 37.1 us -> 25.6 us  [shift_up(): return lax.ppermute(x, 'seq', [(s, s + dist) for s in range(n_seq - dist)])]
    dot_general x4 -> x8, matrix products: 2.99 us -> 3.67 us  [per_device(): jnp.einsum('hqk,khd->qhd', probs[lo:hi, :, d * row_count:(d + 1) * row_co...]
    dot_general x2 -> x4, matrix products: 3.42 us -> 3.59 us  [per_device(): jnp.einsum('hqk,khd->qhd', diag_probs[lo:hi], value_blocks[0], preferred_...]
  transfers between devices with their start and end apart: 10 -> 16, of which waited for: 4 -> 4; matrix products, arithmetic and copies ran while one was open for 35% -> 36% of each run, Pallas kernels for 0% -> 0%
where the time goes in v13:
time: 139 us; the launch traced here: 138 us
  starting transfers between devices  47.4 us (34%)
  matrix products  30.5 us (22%)
  waiting for transfers between devices  25.6 us (18%)
  other arithmetic  19.8 us (14%)
  local copies, waits for them, and re-layouts  8.99 us (6%)
  between operations  5.78 us (4%)
    ppermute x15, starting transfers between devices, shift_up(): return lax.ppermute(x, 'seq', [(s, s + dist) for s in range(n_seq - dist)])  46.1 us
    ppermute x15, waiting for transfers between devices, shift_up(): return lax.ppermute(x, 'seq', [(s, s + dist) for s in range(n_seq - dist)])  25.6 us
    dot_general x2, matrix products, weights_of(): jnp.einsum('qhd,khd->hqk', query_rows, key_all, preferred_element_type=jn...  10.1 us
    reduce_sum x1, other arithmetic, weights_of(): return (probs.astype(jnp.bfloat16), row_max, jnp.sum(probs, axis=-1))  5.84 us
    dot_general x1, matrix products, per_device(): jnp.einsum('hqk,khd->qhd', rounded, value_rows, preferred_element_type=jn...  5.46 us
    convert_element_type x1, other arithmetic, weights_of(): return (probs.astype(jnp.bfloat16), row_max, jnp.sum(probs, axis=-1))  5.11 us
    dot_general x1, matrix products, per_device(): jnp.einsum('qhd,hde->qhe', queries.astype(jnp.float32), carried, precisio...  3.97 us
    dot_general x1, matrix products, per_device(): jnp.einsum('thd,the->hde', tail_keys, value_rows, preferred_element_type=...  3.72 us
  transfers between devices with their start and end apart: 16, of which 4 were waited for; matrix products, arithmetic and copies ran while one was open for 36% of the time, Pallas kernels for 0%

profile of v13, /device:TPU:0, one launch (start us, length us, event | category | flops | bytes accessed | tf_op | source)
XLA Modules:
  0.0 138.2 jit_solution(5974476260891168607)
XLA Ops:
  0.6 1.4 %fusion.112 = (s32[1]{0:T(128)}, s32[1]{0:T(128)}) fusion(s32[320]{0:T(512)} %param.15), kind=kLoop, calls=%fused_computation.182 | loop fusion | bytes 16 | tf_op jit(solution)/shard_map/slice | solution.py:45
  2.7 2.0 %broadcast_compare_fusion.1 = (pred[320]{0:T(512)(128)(4,1)S(1)}, pred[320]{0:T(512)(128)(4,1)S(1)}) fusion(s32[320]{0:T(512)} %param.15, s32[]{:T(128)} %bitcast.1, s32[]{:T(128)} %bitcast.2), kind=kLoop, calls=%fused_computation.165 | loop fusion | flops 640 | bytes 1928 | tf_op jit(solution)/shard_map/eq | solution.py:108
  4.7 3.7 %fusion.113 = (bf16[16,128,128]{2,1,0:T(8,128)(2,1)S(1)}, f32[16,128,128]{2,1,0:T(8,128)}) fusion(pred[320]{0:T(512)(128)(4,1)S(1)} %get-tuple-element.37, bf16[320,2048]{1,0:T(8,128)(2,1)} %param.10, bf16[320,2048]{1,0:T(8,128)(2,1)} %param.9), kind=kOutput, calls=%fused_computation.183 | convolution fusion | flops 168689664 | bytes 4194624 | tf_op jit(solution)/shard_map/thd,the->hde/dot_general | solution.py:51
  8.4 5.7 %collective-permute-start = (bf16[2056,128]{1,0:T(8,128)(2,1)S(1)}, bf16[2056,128]{1,0:T(8,128)(2,1)}, u32[]{:S(2)}, u32[]{:S(2)}) collective-permute-start(bf16[2056,128]{1,0:T(8,128)(2,1)S(1)} %concatenate.28), channel_id=1, source_target_pairs={{0,4},{4,8},{8,12},{1,5},{5,9},{9,13},{2,6},{6,10},{10,14},{3,7},{... | collective-permute-start | bytes 1579016 | tf_op jit(solution)/shard_map/ppermute | solution.py:15
  14.3 1.9 %pad_maximum_fusion.1 = (bf16[320,2176]{1,0:T(8,128)(2,1)}, bf16[320,2176]{1,0:T(8,128)(2,1)}) fusion(bf16[320,128]{1,0:T(8,128)(2,1)S(1)} %broadcast_in_dim.137, bf16[320,2048]{1,0:T(8,128)(2,1)S(1)} %copy-done.6, bf16[320,2048]{1,0:T(8,128)(2,1)S(1)} %copy-done.2), kind=kLoop, calls=%fused_computation.25 | loop fusion | flops 4874240 | bytes 5488640 | tf_op jit(solution)/shard_map/concatenate | solution.py:68
  16.1 3.8 %collective-permute-start.3 = (bf16[320,2176]{1,0:T(8,128)(2,1)}, bf16[320,2176]{1,0:T(8,128)(2,1)}, u32[]{:S(2)}, u32[]{:S(2)}) collective-permute-start(bf16[320,2176]{1,0:T(8,128)(2,1)} %get-tuple-element.11), channel_id=1, source_target_pairs={{0,4},{4,8},{8,12},{1,5},{5,9},{9,13},{2,6},{6,10},{10,14},{3,7},{... | collective-permute-start | bytes 4177928 | tf_op jit(solution)/shard_map/ppermute | solution.py:15
  20.0 1.3 collective-permute-start.2
  22.7 1.4 %copy_bitcast_fusion.3 = bf16[320,16,128]{2,0,1:T(8,128)(2,1)} fusion(bf16[320,2048]{1,0:T(8,128)(2,1)S(1)} %copy-done.2), kind=kLoop, calls=%fused_computation.32 | loop fusion | bytes 2621440 | tf_op jit(solution)/shard_map/reshape | solution.py:74
  24.1 6.0 %fusion.3 = (f32[16,320]{1,0:T(8,128)S(1)}, f32[16,320,320]{1,2,0:T(8,128)}) fusion(pred[320,320]{0,1:T(8,128)(4,1)S(1)} %fusion.67, bf16[320,2048]{1,0:T(8,128)(2,1)} %param.13, bf16[320,2048]{1,0:T(8,128)(2,1)S(1)} %copy-done.2), kind=kOutput, calls=%fused_computation.8 | convolution fusion | flops 424340480 | bytes 9297920 | tf_op jit(solution)/shard_map/qhd,khd->hqk/dot_general | solution.py:84
  30.1 5.8 %fusion.4 = (f32[16,320]{1,0:T(8,128)S(1)}, bf16[16,320,320]{1,2,0:T(8,128)(2,1)}) fusion(f32[16,320,320]{1,2,0:T(8,128)} %get-tuple-element.45, f32[16,320]{1,0:T(8,128)S(1)} %get-tuple-element.44, pred[320,320]{0,1:T(8,128)(4,1)S(1)} %fusion.67), kind=kLoop, calls=%fused_computation.9 | loop fusion | flops 9825280 | bytes 9973760 | tf_op jit(solution)/shard_map/reduce_sum | solution.py:90
  35.9 1.3 slice.201
  39.9 4.6 %collective-permute-start.1 = (bf16[2056,128]{1,0:T(8,128)(2,1)S(1)}, bf16[2056,128]{1,0:T(8,128)(2,1)S(1)}, u32[]{:S(2)}, u32[]{:S(2)}) collective-permute-start(bf16[2056,128]{1,0:T(8,128)(2,1)S(1)} %concatenate.29), channel_id=1, source_target_pairs={{0,4},{4,8},{8,12},{1,5},{5,9},{9,13},{2,6},{6,10},{10,14},{3,7},{... | collective-permute-start | bytes 1579016 | tf_op jit(solution)/shard_map/ppermute | solution.py:15
  44.6 5.5 %fusion.6 = f32[16,320,128]{2,1,0:T(8,128)} fusion(pred[320,320]{0,1:T(8,128)(4,1)S(1)} %fusion.67, bf16[320,2048]{1,0:T(8,128)(2,1)} %param.10, bf16[320,2048]{1,0:T(8,128)(2,1)} %param.9, bf16[320,2048]{1,0:T(8,128)(2,1)S(1)} %copy-done), kind=kOutput, calls=%fused_computation.11 | convolution fusion | flops 842137600 | bytes 6656000 | tf_op jit(solution)/shard_map/hqk,khd->qhd/dot_general | solution.py:103
  50.1 15.6 %collective-permute-done.1 = bf16[2056,128]{1,0:T(8,128)(2,1)S(1)} collective-permute-done((bf16[2056,128]{1,0:T(8,128)(2,1)S(1)}, bf16[2056,128]{1,0:T(8,128)(2,1)S(1)}, u32[]{:S(2)}, u32[]{:S(2)}) %collective-permute-start.1) | collective-permute-done | bytes 526368 | tf_op jit(solution)/shard_map/ppermute | solution.py:15
  67.6 4.0 %multiply_reduce_fusion = (f32[320,16]{0,1:T(8,128)S(1)}, f32[320,16,128]{2,0,1:T(8,128)S(1)}) fusion(f32[16,128,128]{2,1,0:T(8,128)S(1)} %bitcast.267, pred[320]{0:T(512)(128)(4,1)S(1)} %get-tuple-element.36, f32[16,320,128]{2,1,0:T(8,128)} %fusion.6, bf16[320,2048]{1,0:T(8,128)(2,1)S(1)} %copy-done), kind=kOutput, calls=%fused_computation.23 | convolution fusion | flops 1009249280 | bytes 7622976 | tf_op jit(solution)/shard_map/qhd,hde->qhe/dot_general | solution.py:104
  72.6 4.4 %collective-permute-start.4 = (bf16[320,4,128]{2,0,1:T(8,128)(2,1)S(1)}, bf16[320,4,128]{2,0,1:T(8,128)(2,1)S(1)}, u32[]{:S(2)}, u32[]{:S(2)}) collective-permute-start(bf16[320,4,128]{2,0,1:T(8,128)(2,1)S(1)} %get-tuple-element.6), channel_id=1, source_target_pairs={{0,4},{4,8},{8,12},{1,5},{5,9},{9,13},{2,6},{6,10},{10,14},{3,7},{... | collective-permute-start | bytes 983048 | tf_op jit(solution)/shard_map/ppermute | solution.py:15
  77.1 3.5 %collective-permute-start.7 = (bf16[320,4,128]{2,0,1:T(8,128)(2,1)S(1)}, bf16[320,4,128]{2,0,1:T(8,128)(2,1)S(1)}, u32[]{:S(2)}, u32[]{:S(2)}) collective-permute-start(bf16[320,4,128]{2,0,1:T(8,128)(2,1)S(1)} %get-tuple-element.9), channel_id=1, source_target_pairs={{0,4},{4,8},{8,12},{1,5},{5,9},{9,13},{2,6},{6,10},{10,14},{3,7},{... | collective-permute-start | bytes 983048 | tf_op jit(solution)/shard_map/ppermute | solution.py:15
  80.5 3.5 %collective-permute-start.10 = (bf16[320,4,128]{2,0,1:T(8,128)(2,1)S(1)}, bf16[320,4,128]{2,0,1:T(8,128)(2,1)S(1)}, u32[]{:S(2)}, u32[]{:S(2)}) collective-permute-start(bf16[320,4,128]{2,0,1:T(8,128)(2,1)S(1)} %get-tuple-element.8), channel_id=1, source_target_pairs={{0,4},{4,8},{8,12},{1,5},{5,9},{9,13},{2,6},{6,10},{10,14},{3,7},{... | collective-permute-start | bytes 983048 | tf_op jit(solution)/shard_map/ppermute | solution.py:15
  85.3 2.1 %collective-permute-start.13 = (bf16[320,4,128]{2,0,1:T(8,128)(2,1)S(1)}, bf16[320,4,128]{2,0,1:T(8,128)(2,1)S(1)}, u32[]{:S(2)}, u32[]{:S(2)}) collective-permute-start(bf16[320,4,128]{2,0,1:T(8,128)(2,1)S(1)} %get-tuple-element.7), channel_id=1, source_target_pairs={{0,4},{4,8},{8,12},{1,5},{5,9},{9,13},{2,6},{6,10},{10,14},{3,7},{... | collective-permute-start | bytes 983048 | tf_op jit(solution)/shard_map/ppermute | solution.py:15
  89.7 1.8 %copy_bitcast_fusion.2 = bf16[320,16,128]{2,0,1:T(8,128)(2,1)S(1)} fusion(bf16[320,2176]{1,0:T(8,128)(2,1)} %collective-permute-done.3), kind=kLoop, calls=%fused_computation.31 | loop fusion | bytes 2621440 | tf_op jit(solution)/shard_map/reshape | solution.py:74
  91.5 4.1 %fusion = (f32[16,320]{1,0:T(8,128)S(1)}, f32[16,320,640]{2,1,0:T(8,128)S(1)}) fusion(pred[320,640]{1,0:T(8,128)(4,1)S(1)} %compare_and_fusion, bf16[320,16,128]{2,0,1:T(8,128)(2,1)S(1)} %copy_bitcast_fusion.2, bf16[320,16,128]{2,0,1:T(8,128)(2,1)S(1)} %copy-done.5, bf16[320,2176]{1,0:T(8,128)(2,1)} %collective-permute-done.2), kind=kOutput, calls=%fused_computation.2 | convolution fusion | flops 853928960 | bytes 17264640 | tf_op jit(solution)/shard_map/qhd,khd->hqk/dot_general | solution.py:84
  95.6 5.1 %fusion.2 = (bf16[16,320,640]{2,1,0:T(8,128)(2,1)S(1)}, f32[16,320]{1,0:T(8,128)S(1)}) fusion(f32[16,320,640]{2,1,0:T(8,128)S(1)} %get-tuple-element.47, f32[16,320]{1,0:T(8,128)S(1)} %get-tuple-element.46, pred[320,640]{1,0:T(8,128)(4,1)S(1)} %compare_and_fusion), kind=kLoop, calls=%fused_computation.4 | loop fusion | flops 19655680 | bytes 19906560 | tf_op jit(solution)/shard_map/convert_element_type | solution.py:90
  102.1 1.9 %collective-permute-start.5 = (bf16[320,4,128]{2,0,1:T(8,128)(2,1)S(1)}, bf16[320,4,128]{2,0,1:T(8,128)(2,1)S(1)}, u32[]{:S(2)}, u32[]{:S(2)}) collective-permute-start(bf16[320,4,128]{2,0,1:T(8,128)(2,1)S(1)} %fusion.41), channel_id=1, source_target_pairs={{0,4},{4,8},{8,12},{1,5},{5,9},{9,13},{2,6},{6,10},{10,14},{3,7},{... | collective-permute-start | bytes 983048 | tf_op jit(solution)/shard_map/ppermute | solution.py:15
  104.1 1.9 %collective-permute-start.9 = (f32[2,4,320]{2,1,0:T(4,128)S(1)}, f32[2,4,320]{2,1,0:T(4,128)S(1)}, u32[]{:S(2)}, u32[]{:S(2)}) collective-permute-start(f32[2,4,320]{2,1,0:T(4,128)S(1)} %pad_maximum_fusion.3), channel_id=1, source_target_pairs={{0,4},{4,8},{8,12},{1,5},{5,9},{9,13},{2,6},{6,10},{10,14},{3,7},{... | collective-permute-start | bytes 30728 | tf_op jit(solution)/shard_map/ppermute | solution.py:15
  106.4 1.9 %collective-permute-start.12 = (f32[2,4,320]{2,1,0:T(4,128)S(1)}, f32[2,4,320]{2,1,0:T(4,128)S(1)}, u32[]{:S(2)}, u32[]{:S(2)}) collective-permute-start(f32[2,4,320]{2,1,0:T(4,128)S(1)} %pad_maximum_fusion.4), channel_id=1, source_target_pairs={{0,4},{4,8},{8,12},{1,5},{5,9},{9,13},{2,6},{6,10},{10,14},{3,7},{... | collective-permute-start | bytes 30728 | tf_op jit(solution)/shard_map/ppermute | solution.py:15
  109.3 1.9 %collective-permute-start.15 = (f32[2,4,320]{2,1,0:T(4,128)S(1)}, f32[2,4,320]{2,1,0:T(4,128)S(1)}, u32[]{:S(2)}, u32[]{:S(2)}) collective-permute-start(f32[2,4,320]{2,1,0:T(4,128)S(1)} %pad_maximum_fusion.5), channel_id=1, source_target_pairs={{0,4},{4,8},{8,12},{1,5},{5,9},{9,13},{2,6},{6,10},{10,14},{3,7},{... | collective-permute-start | bytes 30728 | tf_op jit(solution)/shard_map/ppermute | solution.py:15
  111.8 2.1 %collective-permute-start.6 = (f32[2,4,320]{2,1,0:T(4,128)S(1)}, f32[2,4,320]{2,1,0:T(4,128)S(1)}, u32[]{:S(2)}, u32[]{:S(2)}) collective-permute-start(f32[2,4,320]{2,1,0:T(4,128)S(1)} %pad_maximum_fusion.2), channel_id=1, source_target_pairs={{0,4},{4,8},{8,12},{1,5},{5,9},{9,13},{2,6},{6,10},{10,14},{3,7},{... | collective-permute-start | bytes 30728 | tf_op jit(solution)/shard_map/ppermute | solution.py:15
  114.4 1.9 %collective-permute-start.8 = (bf16[320,4,128]{2,0,1:T(8,128)(2,1)S(1)}, bf16[320,4,128]{2,0,1:T(8,128)(2,1)S(1)}, u32[]{:S(2)}, u32[]{:S(2)}) collective-permute-start(bf16[320,4,128]{2,0,1:T(8,128)(2,1)S(1)} %fusion.40), channel_id=1, source_target_pairs={{0,4},{4,8},{8,12},{1,5},{5,9},{9,13},{2,6},{6,10},{10,14},{3,7},{... | collective-permute-start | bytes 983048 | tf_op jit(solution)/shard_map/ppermute | solution.py:15
  116.3 3.4 %collective-permute-start.11 = (bf16[320,4,128]{2,0,1:T(8,128)(2,1)S(1)}, bf16[320,4,128]{2,0,1:T(8,128)(2,1)S(1)}, u32[]{:S(2)}, u32[]{:S(2)}) collective-permute-start(bf16[320,4,128]{2,0,1:T(8,128)(2,1)S(1)} %fusion.39), channel_id=1, source_target_pairs={{0,4},{4,8},{8,12},{1,5},{5,9},{9,13},{2,6},{6,10},{10,14},{3,7},{... | collective-permute-start | bytes 983048 | tf_op jit(solution)/shard_map/ppermute | solution.py:15
  119.8 3.5 %collective-permute-start.14 = (bf16[320,4,128]{2,0,1:T(8,128)(2,1)S(1)}, bf16[320,4,128]{2,0,1:T(8,128)(2,1)S(1)}, u32[]{:S(2)}, u32[]{:S(2)}) collective-permute-start(bf16[320,4,128]{2,0,1:T(8,128)(2,1)S(1)} %fusion.38), channel_id=1, source_target_pairs={{0,4},{4,8},{8,12},{1,5},{5,9},{9,13},{2,6},{6,10},{10,14},{3,7},{... | collective-permute-start | bytes 983048 | tf_op jit(solution)/shard_map/ppermute | solution.py:15
  125.4 6.1 %collective-permute-done.11 = bf16[320,4,128]{2,0,1:T(8,128)(2,1)S(1)} collective-permute-done((bf16[320,4,128]{2,0,1:T(8,128)(2,1)S(1)}, bf16[320,4,128]{2,0,1:T(8,128)(2,1)S(1)}, u32[]{:S(2)}, u32[]{:S(2)}) %collective-permute-start.11) | collective-permute-done | bytes 327712 | tf_op jit(solution)/shard_map/ppermute | solution.py:15
  132.4 3.6 %collective-permute-done.14 = bf16[320,4,128]{2,0,1:T(8,128)(2,1)S(1)} collective-permute-done((bf16[320,4,128]{2,0,1:T(8,128)(2,1)S(1)}, bf16[320,4,128]{2,0,1:T(8,128)(2,1)S(1)}, u32[]{:S(2)}, u32[]{:S(2)}) %collective-permute-start.14) | collective-permute-done | bytes 327712 | tf_op jit(solution)/shard_map/ppermute | solution.py:15
  (74 shorter events, 15.7 us)
Async XLA Ops:
  0.6 44.0 %copy-start = (bf16[320,2048]{1,0:T(8,128)(2,1)S(1)}, bf16[320,2048]{1,0:T(8,128)(2,1)}, u32[]{:S(2)}) copy-start(bf16[320,2048]{1,0:T(8,128)(2,1)} %param.8) | copy-start | bytes 3932164
  4.7 9.5 %copy-start.8 = (s32[320]{0:T(512)S(1)}, s32[320]{0:T(512)}, u32[]{:S(2)}) copy-start(s32[320]{0:T(512)} %param.15) | copy-start | bytes 3844
  4.7 9.6 %copy-start.2 = (bf16[320,2048]{1,0:T(8,128)(2,1)S(1)}, bf16[320,2048]{1,0:T(8,128)(2,1)}, u32[]{:S(2)}) copy-start(bf16[320,2048]{1,0:T(8,128)(2,1)} %param.14) | copy-start | bytes 3932164
  4.7 9.6 %copy-start.6 = (bf16[320,2048]{1,0:T(8,128)(2,1)S(1)}, bf16[320,2048]{1,0:T(8,128)(2,1)}, u32[]{:S(2)}) copy-start(bf16[320,2048]{1,0:T(8,128)(2,1)} %param.13) | copy-start | bytes 3932164
  8.4 27.5 %collective-permute-start = (bf16[2056,128]{1,0:T(8,128)(2,1)S(1)}, bf16[2056,128]{1,0:T(8,128)(2,1)}, u32[]{:S(2)}, u32[]{:S(2)}) collective-permute-start(bf16[2056,128]{1,0:T(8,128)(2,1)S(1)} %concatenate.28), channel_id=1, source_target_pairs={{0,4},{4,8},{8,12},{1,5},{5,9},{9,13},{2,6},{6,10},{10,14},{3,7},{... | collective-permute-start | bytes 1579016 | tf_op jit(solution)/shard_map/ppermute | solution.py:15
  16.1 69.1 %collective-permute-start.3 = (bf16[320,2176]{1,0:T(8,128)(2,1)}, bf16[320,2176]{1,0:T(8,128)(2,1)}, u32[]{:S(2)}, u32[]{:S(2)}) collective-permute-start(bf16[320,2176]{1,0:T(8,128)(2,1)} %get-tuple-element.11), channel_id=1, source_target_pairs={{0,4},{4,8},{8,12},{1,5},{5,9},{9,13},{2,6},{6,10},{10,14},{3,7},{... | collective-permute-start | bytes 4177928 | tf_op jit(solution)/shard_map/ppermute | solution.py:15
  20.0 68.5 %collective-permute-start.2 = (bf16[320,2176]{1,0:T(8,128)(2,1)}, bf16[320,2176]{1,0:T(8,128)(2,1)}, u32[]{:S(2)}, u32[]{:S(2)}) collective-permute-start(bf16[320,2176]{1,0:T(8,128)(2,1)} %get-tuple-element.10), channel_id=1, source_target_pairs={{4,0},{8,4},{12,8},{5,1},{9,5},{13,9},{6,2},{10,6},{14,10},{7,3},{... | collective-permute-start | bytes 4177928 | tf_op jit(solution)/shard_map/ppermute | solution.py:19
  35.9 3.8 %copy-start.7 = (f32[16,128,128]{2,1,0:T(8,128)S(1)}, f32[16,128,128]{2,1,0:T(8,128)}, u32[]{:S(2)}) copy-start(f32[16,128,128]{2,1,0:T(8,128)} %get-tuple-element.41) | copy-start | bytes 3145732
  39.7 4.8 %copy-start.9 = (bf16[2048]{0:T(1024)(128)(2,1)S(1)}, bf16[2048]{0:T(1024)(128)(2,1)}, u32[]{:S(2)}) copy-start(bf16[2048]{0:T(1024)(128)(2,1)} %param.11) | copy-start | bytes 12292
  39.9 25.8 %collective-permute-start.1 = (bf16[2056,128]{1,0:T(8,128)(2,1)S(1)}, bf16[2056,128]{1,0:T(8,128)(2,1)S(1)}, u32[]{:S(2)}, u32[]{:S(2)}) collective-permute-start(bf16[2056,128]{1,0:T(8,128)(2,1)S(1)} %concatenate.29), channel_id=1, source_target_pairs={{0,4},{4,8},{8,12},{1,5},{5,9},{9,13},{2,6},{6,10},{10,14},{3,7},{... | collective-permute-start | bytes 1579016 | tf_op jit(solution)/shard_map/ppermute | solution.py:15
  67.6 4.0 %copy-start.4 = (bf16[320,2048]{1,0:T(8,128)(2,1)S(1)}, bf16[320,2048]{1,0:T(8,128)(2,1)}, u32[]{:S(2)}) copy-start(bf16[320,2048]{1,0:T(8,128)(2,1)} %param.12) | copy-start | bytes 3932164
  72.6 29.0 %collective-permute-start.4 = (bf16[320,4,128]{2,0,1:T(8,128)(2,1)S(1)}, bf16[320,4,128]{2,0,1:T(8,128)(2,1)S(1)}, u32[]{:S(2)}, u32[]{:S(2)}) collective-permute-start(bf16[320,4,128]{2,0,1:T(8,128)(2,1)S(1)} %get-tuple-element.6), channel_id=1, source_target_pairs={{0,4},{4,8},{8,12},{1,5},{5,9},{9,13},{2,6},{6,10},{10,14},{3,7},{... | collective-permute-start | bytes 983048 | tf_op jit(solution)/shard_map/ppermute | solution.py:15
  77.1 29.4 %collective-permute-start.7 = (bf16[320,4,128]{2,0,1:T(8,128)(2,1)S(1)}, bf16[320,4,128]{2,0,1:T(8,128)(2,1)S(1)}, u32[]{:S(2)}, u32[]{:S(2)}) collective-permute-start(bf16[320,4,128]{2,0,1:T(8,128)(2,1)S(1)} %get-tuple-element.9), channel_id=1, source_target_pairs={{0,4},{4,8},{8,12},{1,5},{5,9},{9,13},{2,6},{6,10},{10,14},{3,7},{... | collective-permute-start | bytes 983048 | tf_op jit(solution)/shard_map/ppermute | solution.py:15
  80.5 28.8 %collective-permute-start.10 = (bf16[320,4,128]{2,0,1:T(8,128)(2,1)S(1)}, bf16[320,4,128]{2,0,1:T(8,128)(2,1)S(1)}, u32[]{:S(2)}, u32[]{:S(2)}) collective-permute-start(bf16[320,4,128]{2,0,1:T(8,128)(2,1)S(1)} %get-tuple-element.8), channel_id=1, source_target_pairs={{0,4},{4,8},{8,12},{1,5},{5,9},{9,13},{2,6},{6,10},{10,14},{3,7},{... | collective-permute-start | bytes 983048 | tf_op jit(solution)/shard_map/ppermute | solution.py:15
  85.3 26.5 %collective-permute-start.13 = (bf16[320,4,128]{2,0,1:T(8,128)(2,1)S(1)}, bf16[320,4,128]{2,0,1:T(8,128)(2,1)S(1)}, u32[]{:S(2)}, u32[]{:S(2)}) collective-permute-start(bf16[320,4,128]{2,0,1:T(8,128)(2,1)S(1)} %get-tuple-element.7), channel_id=1, source_target_pairs={{0,4},{4,8},{8,12},{1,5},{5,9},{9,13},{2,6},{6,10},{10,14},{3,7},{... | collective-permute-start | bytes 983048 | tf_op jit(solution)/shard_map/ppermute | solution.py:15
  89.5 2.0 %copy-start.5 = (bf16[320,16,128]{2,0,1:T(8,128)(2,1)S(1)}, bf16[320,16,128]{2,0,1:T(8,128)(2,1)}, u32[]{:S(2)}) copy-start(bf16[320,16,128]{2,0,1:T(8,128)(2,1)} %copy_bitcast_fusion.3) | copy-start | bytes 3932164
  102.1 21.2 %collective-permute-start.5 = (bf16[320,4,128]{2,0,1:T(8,128)(2,1)S(1)}, bf16[320,4,128]{2,0,1:T(8,128)(2,1)S(1)}, u32[]{:S(2)}, u32[]{:S(2)}) collective-permute-start(bf16[320,4,128]{2,0,1:T(8,128)(2,1)S(1)} %fusion.41), channel_id=1, source_target_pairs={{0,4},{4,8},{8,12},{1,5},{5,9},{9,13},{2,6},{6,10},{10,14},{3,7},{... | collective-permute-start | bytes 983048 | tf_op jit(solution)/shard_map/ppermute | solution.py:15
  104.1 10.3 %collective-permute-start.9 = (f32[2,4,320]{2,1,0:T(4,128)S(1)}, f32[2,4,320]{2,1,0:T(4,128)S(1)}, u32[]{:S(2)}, u32[]{:S(2)}) collective-permute-start(f32[2,4,320]{2,1,0:T(4,128)S(1)} %pad_maximum_fusion.3), channel_id=1, source_target_pairs={{0,4},{4,8},{8,12},{1,5},{5,9},{9,13},{2,6},{6,10},{10,14},{3,7},{... | collective-permute-start | bytes 30728 | tf_op jit(solution)/shard_map/ppermute | solution.py:15
  106.4 9.9 %collective-permute-start.12 = (f32[2,4,320]{2,1,0:T(4,128)S(1)}, f32[2,4,320]{2,1,0:T(4,128)S(1)}, u32[]{:S(2)}, u32[]{:S(2)}) collective-permute-start(f32[2,4,320]{2,1,0:T(4,128)S(1)} %pad_maximum_fusion.4), channel_id=1, source_target_pairs={{0,4},{4,8},{8,12},{1,5},{5,9},{9,13},{2,6},{6,10},{10,14},{3,7},{... | collective-permute-start | bytes 30728 | tf_op jit(solution)/shard_map/ppermute | solution.py:15
  109.3 10.4 %collective-permute-start.15 = (f32[2,4,320]{2,1,0:T(4,128)S(1)}, f32[2,4,320]{2,1,0:T(4,128)S(1)}, u32[]{:S(2)}, u32[]{:S(2)}) collective-permute-start(f32[2,4,320]{2,1,0:T(4,128)S(1)} %pad_maximum_fusion.5), channel_id=1, source_target_pairs={{0,4},{4,8},{8,12},{1,5},{5,9},{9,13},{2,6},{6,10},{10,14},{3,7},{... | collective-permute-start | bytes 30728 | tf_op jit(solution)/shard_map/ppermute | solution.py:15
  111.3 12.1 %copy-start.3 = (bf16[16,320,320]{1,2,0:T(8,128)(2,1)S(1)}, bf16[16,320,320]{1,2,0:T(8,128)(2,1)}, u32[]{:S(2)}) copy-start(bf16[16,320,320]{1,2,0:T(8,128)(2,1)} %get-tuple-element.5) | copy-start | bytes 9830404
  111.8 11.5 %collective-permute-start.6 = (f32[2,4,320]{2,1,0:T(4,128)S(1)}, f32[2,4,320]{2,1,0:T(4,128)S(1)}, u32[]{:S(2)}, u32[]{:S(2)}) collective-permute-start(f32[2,4,320]{2,1,0:T(4,128)S(1)} %pad_maximum_fusion.2), channel_id=1, source_target_pairs={{0,4},{4,8},{8,12},{1,5},{5,9},{9,13},{2,6},{6,10},{10,14},{3,7},{... | collective-permute-start | bytes 30728 | tf_op jit(solution)/shard_map/ppermute | solution.py:15
  114.4 10.1 %collective-permute-start.8 = (bf16[320,4,128]{2,0,1:T(8,128)(2,1)S(1)}, bf16[320,4,128]{2,0,1:T(8,128)(2,1)S(1)}, u32[]{:S(2)}, u32[]{:S(2)}) collective-permute-start(bf16[320,4,128]{2,0,1:T(8,128)(2,1)S(1)} %fusion.40), channel_id=1, source_target_pairs={{0,4},{4,8},{8,12},{1,5},{5,9},{9,13},{2,6},{6,10},{10,14},{3,7},{... | collective-permute-start | bytes 983048 | tf_op jit(solution)/shard_map/ppermute | solution.py:15
  116.3 15.1 %collective-permute-start.11 = (bf16[320,4,128]{2,0,1:T(8,128)(2,1)S(1)}, bf16[320,4,128]{2,0,1:T(8,128)(2,1)S(1)}, u32[]{:S(2)}, u32[]{:S(2)}) collective-permute-start(bf16[320,4,128]{2,0,1:T(8,128)(2,1)S(1)} %fusion.39), channel_id=1, source_target_pairs={{0,4},{4,8},{8,12},{1,5},{5,9},{9,13},{2,6},{6,10},{10,14},{3,7},{... | collective-permute-start | bytes 983048 | tf_op jit(solution)/shard_map/ppermute | solution.py:15
  119.8 16.2 %collective-permute-start.14 = (bf16[320,4,128]{2,0,1:T(8,128)(2,1)S(1)}, bf16[320,4,128]{2,0,1:T(8,128)(2,1)S(1)}, u32[]{:S(2)}, u32[]{:S(2)}) collective-permute-start(bf16[320,4,128]{2,0,1:T(8,128)(2,1)S(1)} %fusion.38), channel_id=1, source_target_pairs={{0,4},{4,8},{8,12},{1,5},{5,9},{9,13},{2,6},{6,10},{10,14},{3,7},{... | collective-permute-start | bytes 983048 | tf_op jit(solution)/shard_map/ppermute | solution.py:15
  136.0 2.2 %copy-start.1 = (bf16[320,2048]{1,0:T(8,128)(2,1)S(1)}, bf16[320,2048]{1,0:T(8,128)(2,1)}, u32[]{:S(2)}) copy-start(bf16[320,2048]{1,0:T(8,128)(2,1)} %param.8) | copy-start | bytes 3932164

commit v14 on v12

--- a/solution.py
+++ b/solution.py
@@ -98,30 +98,36 @@
     keep_next = (next_docs[:, None] == jnp.concatenate(key_docs)[None, :]) & valid[None, :]
     ahead = weights_of(next_queries, keep_next)
 
-    scores = jnp.einsum("qhd,khd->hqk", queries, key_rows, preferred_element_type=jnp.float32)
-    rounded = jnp.where(keep_local[None], scores, jnp.zeros_like(scores)).astype(jnp.bfloat16)
-    block_term = jnp.einsum("hqk,khd->qhd", rounded, value_rows, preferred_element_type=jnp.float32)
-    carried_term = jnp.einsum(
-        "qhd,hde->qhe", queries.astype(jnp.float32), carried, precision=lax.Precision.HIGHEST
-    )
-    carried_term = jnp.where(
-        (doc_id == first_doc)[:, None, None], carried_term, jnp.zeros_like(carried_term)
-    )
-    lin_raw = block_term + carried_term
-    mean_square = jnp.mean(lin_raw * lin_raw, axis=-1, keepdims=True)
-    gain_rows = norm_gain.astype(jnp.float32).reshape(head_count, HD)
-    gate_rows = jax.nn.sigmoid(out_gate.astype(jnp.float32).reshape(row_count, head_count, HD))
-    normed = lin_raw * lax.rsqrt(mean_square + norm_eps) * gain_rows * gate_rows
-    lin_out = normed.astype(jnp.bfloat16).reshape(row_count, width)
+    def lightning(lo, hi):
+        q, k, v = queries[:, lo:hi], key_rows[:, lo:hi], value_rows[:, lo:hi]
+        scores = jnp.einsum("qhd,khd->hqk", q, k, preferred_element_type=jnp.float32)
+        rounded = jnp.where(keep_local[None], scores, jnp.zeros_like(scores)).astype(jnp.bfloat16)
+        block_term = jnp.einsum("hqk,khd->qhd", rounded, v, preferred_element_type=jnp.float32)
+        carried_term = jnp.einsum(
+            "qhd,hde->qhe", q.astype(jnp.float32), carried[lo:hi], precision=lax.Precision.HIGHEST
+        )
+        carried_term = jnp.where(
+            (doc_id == first_doc)[:, None, None], carried_term, jnp.zeros_like(carried_term)
+        )
+        lin_raw = block_term + carried_term
+        mean_square = jnp.mean(lin_raw * lin_raw, axis=-1, keepdims=True)
+        gain_rows = norm_gain.astype(jnp.float32).reshape(head_count, HD)[lo:hi]
+        gate_rows = jax.nn.sigmoid(
+            out_gate.astype(jnp.float32).reshape(row_count, head_count, HD)[:, lo:hi]
+        )
+        normed = lin_raw * lax.rsqrt(mean_square + norm_eps) * gain_rows * gate_rows
+        return normed.astype(jnp.bfloat16)
 
-    value_own = lin_out.reshape(row_count, head_count, HD)
     probs, ahead_max, ahead_sum = ahead
     diag_probs, diag_max, diag_sum = diag
     has_source = my_index >= 1
     half = head_count // 2
     pieces = []
+    lin_pieces = []
     for lo, hi in ((0, half), (half, head_count)):
-        value_blocks = [value_own[:, lo:hi]]
+        value_half = lightning(lo, hi)
+        lin_pieces.append(value_half)
+        value_blocks = [value_half]
         for d in dists[:-1]:
             value_blocks.append(shift_up(value_blocks[-1], 1, n_seq))
         ahead_out = jnp.zeros((row_count, hi - lo, HD), jnp.float32)
@@ -145,6 +151,7 @@
         )
         pieces.append(mixed / jnp.transpose(row_sum)[:, :, None])
     soft_out = jnp.concatenate(pieces, axis=1)
+    lin_out = jnp.concatenate(lin_pieces, axis=1).reshape(row_count, width)
     return (lin_out, soft_out.astype(jnp.bfloat16).reshape(row_count, width))
 
 

time: 137 us -> 149 us (1.088)
  local copies, waits for them, and re-layouts: 8.93 us -> 18.5 us
  other arithmetic: 19.6 us -> 26.1 us
  waiting for transfers between devices: 37.1 us -> 32.4 us
  matrix products: 29.7 us -> 32.9 us
  starting transfers between devices: 35.5 us -> 33.1 us
    unnamed x20 -> x47, local copies, waits for them, and re-layouts: 0.05 us -> 5.24 us
    ppermute x9, waiting for transfers between devices: 37.1 us -> 32.4 us  [shift_up(): return lax.ppermute(x, 'seq', [(s, s + dist) for s in range(n_seq - dist)])]
    convert_element_type x1 -> x3, other arithmetic: 0.93 us -> 3.69 us  [the longest x2 3.68 us: lightning(): return normed.astype(jnp.bfloat16)]
    slice x1 -> x4, local copies, waits for them, and re-layouts: 0.09 us -> 2.57 us  [the longest x1 1.52 us: lightning(): q, k, v = (queries[:, lo:hi], key_rows[:, lo:hi], value_rows[:, lo:hi])]
    ppermute x9, starting transfers between devices: 34.2 us -> 31.8 us  [shift_up(): return lax.ppermute(x, 'seq', [(s, s + dist) for s in range(n_seq - dist)])]
    dot_general x2 -> x4, matrix products: 9.46 us -> 11.2 us  [the longest x2 7.73 us: lightning(): jnp.einsum('hqk,khd->qhd', rounded, v, preferred_element_type=jnp.float32)]
  transfers between devices with their start and end apart: 10 -> 10, of which waited for: 4 -> 3; matrix products, arithmetic and copies ran while one was open for 35% -> 42% of each run, Pallas kernels for 0% -> 0%
where the time goes in v14:
time: 149 us; the launch traced here: 148 us
  starting transfers between devices  33.1 us (22%)
  matrix products  32.9 us (22%)
  waiting for transfers between devices  32.4 us (22%)
  other arithmetic  26.1 us (18%)
  local copies, waits for them, and re-layouts  18.5 us (12%)
  between operations  5.44 us (4%)
    ppermute x9, waiting for transfers between devices, shift_up(): return lax.ppermute(x, 'seq', [(s, s + dist) for s in range(n_seq - dist)])  32.4 us
    ppermute x9, starting transfers between devices, shift_up(): return lax.ppermute(x, 'seq', [(s, s + dist) for s in range(n_seq - dist)])  31.8 us
    dot_general x2, matrix products, weights_of(): jnp.einsum('qhd,khd->hqk', query_rows, key_all, preferred_element_type=jn...  10.5 us
    dot_general x2, matrix products, lightning(): jnp.einsum('hqk,khd->qhd', rounded, v, preferred_element_type=jnp.float32)  7.73 us
    reduce_sum x1, other arithmetic, weights_of(): return (probs.astype(jnp.bfloat16), row_max, jnp.sum(probs, axis=-1))  6.34 us
    unnamed x47, local copies, waits for them, and re-layouts  5.24 us
    convert_element_type x1, other arithmetic, weights_of(): return (probs.astype(jnp.bfloat16), row_max, jnp.sum(probs, axis=-1))  5.1 us
    dot_general x4, matrix products, per_device(): jnp.einsum('hqk,khd->qhd', probs[lo:hi, :, d * row_count:(d + 1) * row_co...  4.07 us
  transfers between devices with their start and end apart: 10, of which 3 were waited for; matrix products, arithmetic and copies ran while one was open for 42% of the time, Pallas kernels for 0%

profile of v14, /device:TPU:0, one launch (start us, length us, event | category | flops | bytes accessed | tf_op | source)
XLA Modules:
  0.0 148.4 jit_solution(7633621436546140449)
XLA Ops:
  0.6 1.4 fusion.118
  2.7 2.5 %broadcast_compare_fusion.1 = (pred[320]{0:T(512)(128)(4,1)}, pred[320]{0:T(512)(128)(4,1)S(1)}) fusion(s32[320]{0:T(512)} %param.15, s32[]{:T(128)} %bitcast.1, s32[]{:T(128)} %bitcast.2), kind=kLoop, calls=%fused_computation.142 | loop fusion | flops 640 | bytes 1928 | tf_op jit(solution)/shard_map/eq | solution.py:110
  5.2 3.3 %fusion.119 = (bf16[16,128,128]{2,1,0:T(8,128)(2,1)S(1)}, f32[16,128,128]{2,1,0:T(8,128)}) fusion(pred[320]{0:T(512)(128)(4,1)S(1)} %get-tuple-element.29, bf16[320,2048]{1,0:T(8,128)(2,1)} %param.9, bf16[320,2048]{1,0:T(8,128)(2,1)S(1)} %copy-done), kind=kOutput, calls=%fused_computation.152 | convolution fusion | flops 168689664 | bytes 4194624 | tf_op jit(solution)/shard_map/thd,the->hde/dot_general | solution.py:51
  9.4 5.8 %collective-permute-start = (bf16[2056,128]{1,0:T(8,128)(2,1)}, bf16[2056,128]{1,0:T(8,128)(2,1)}, u32[]{:S(2)}, u32[]{:S(2)}) collective-permute-start(bf16[2056,128]{1,0:T(8,128)(2,1)} %concatenate.31), channel_id=1, source_target_pairs={{0,4},{4,8},{8,12},{1,5},{5,9},{9,13},{2,6},{6,10},{10,14},{3,7},{... | collective-permute-start | bytes 1579016 | tf_op jit(solution)/shard_map/ppermute | solution.py:15
  15.9 1.8 %pad_maximum_fusion.1 = (bf16[320,2176]{1,0:T(8,128)(2,1)}, bf16[320,2176]{1,0:T(8,128)(2,1)}) fusion(bf16[320,128]{1,0:T(8,128)(2,1)S(1)} %broadcast_in_dim.130, bf16[320,2048]{1,0:T(8,128)(2,1)S(1)} %copy-done.11, bf16[320,2048]{1,0:T(8,128)(2,1)S(1)} %copy-done.2), kind=kLoop, calls=%fused_computation.30 | loop fusion | flops 4874240 | bytes 5488640 | tf_op jit(solution)/shard_map/concatenate | solution.py:68
  17.7 3.7 %collective-permute-start.3 = (bf16[320,2176]{1,0:T(8,128)(2,1)}, bf16[320,2176]{1,0:T(8,128)(2,1)}, u32[]{:S(2)}, u32[]{:S(2)}) collective-permute-start(bf16[320,2176]{1,0:T(8,128)(2,1)} %get-tuple-element.15), channel_id=1, source_target_pairs={{0,4},{4,8},{8,12},{1,5},{5,9},{9,13},{2,6},{6,10},{10,14},{3,7},{... | collective-permute-start | bytes 4177928 | tf_op jit(solution)/shard_map/ppermute | solution.py:15
  24.2 1.4 copy_bitcast_fusion.3
  29.8 1.5 %fusion.115 = (bf16[320,8,128]{2,1,0:T(8,128)(2,1)}, bf16[320,8,128]{2,1,0:T(8,128)(2,1)}, bf16[320,8,128]{2,1,0:T(8,128)(2,1)S(1)}, bf16[320,8,128]{2,1,0:T(8,128)(2,1)}) fusion(bf16[320,16,128]{2,1,0:T(8,128)(2,1)S(1)} %bitcast.179, bf16[320,16,128]{2,1,0:T(8,128)(2,1)S(1)} %bitcast.180), kind=kLoop, calls=%fused_computation.148 | loop fusion | bytes 5242880 | tf_op jit(solution)/shard_map/slice | solution.py:102
  33.4 6.4 %fusion.3 = (f32[16,320]{1,0:T(8,128)S(1)}, f32[16,320,320]{1,2,0:T(8,128)}) fusion(pred[320,320]{0,1:T(8,128)(4,1)S(1)} %fusion.91, bf16[320,2048]{1,0:T(8,128)(2,1)} %param.13, bf16[320,2048]{1,0:T(8,128)(2,1)} %param.14), kind=kOutput, calls=%fused_computation.7 | convolution fusion | flops 424340480 | bytes 9297920 | tf_op jit(solution)/shard_map/qhd,khd->hqk/dot_general | solution.py:84
  43.8 4.6 %collective-permute-start.1 = (bf16[2056,128]{1,0:T(8,128)(2,1)S(1)}, bf16[2056,128]{1,0:T(8,128)(2,1)S(1)}, u32[]{:S(2)}, u32[]{:S(2)}) collective-permute-start(bf16[2056,128]{1,0:T(8,128)(2,1)S(1)} %concatenate.32), channel_id=1, source_target_pairs={{0,4},{4,8},{8,12},{1,5},{5,9},{9,13},{2,6},{6,10},{10,14},{3,7},{... | collective-permute-start | bytes 1579016 | tf_op jit(solution)/shard_map/ppermute | solution.py:15
  48.4 6.3 %fusion.4 = (f32[16,320]{1,0:T(8,128)}, bf16[16,320,320]{1,2,0:T(8,128)(2,1)}) fusion(f32[16,320,320]{1,2,0:T(8,128)} %get-tuple-element.39, f32[16,320]{1,0:T(8,128)S(1)} %get-tuple-element.38, pred[320,320]{0,1:T(8,128)(4,1)S(1)} %fusion.91), kind=kLoop, calls=%fused_computation.8 | loop fusion | flops 9825280 | bytes 9973760 | tf_op jit(solution)/shard_map/reduce_sum | solution.py:90
  54.7 12.2 %collective-permute-done.1 = bf16[2056,128]{1,0:T(8,128)(2,1)S(1)} collective-permute-done((bf16[2056,128]{1,0:T(8,128)(2,1)S(1)}, bf16[2056,128]{1,0:T(8,128)(2,1)S(1)}, u32[]{:S(2)}, u32[]{:S(2)}) %collective-permute-start.1) | collective-permute-done | bytes 526368 | tf_op jit(solution)/shard_map/ppermute | solution.py:15
  71.6 1.7 %fusion.46 = f32[320,8,128]{2,0,1:T(8,128)} fusion(f32[8,128,128]{2,1,0:T(8,128)S(1)} %bitcast.184, pred[320]{0:T(512)(128)(4,1)S(1)} %copy-done.19, bf16[320,8,128]{2,1,0:T(8,128)(2,1)S(1)} %get-tuple-element.42), kind=kOutput, calls=%fused_computation.44 | convolution fusion | flops 503644160 | bytes 2490688 | tf_op jit(solution)/shard_map/qhd,hde->qhe/dot_general | solution.py:106
  73.3 4.0 %multiply_reduce_fusion = (f32[320,8]{0,1:T(8,128)S(1)}, f32[320,8,128]{2,0,1:T(8,128)}) fusion(f32[320,8,128]{2,0,1:T(8,128)} %fusion.46, bf16[320,16,128]{2,0,1:T(8,128)(2,1)} %copy_bitcast_fusion.4, pred[320,320]{1,0:T(8,128)(4,1)S(1)} %copy.15, bf16[320,8,128]{2,1,0:T(8,128)(2,1)} %get-tuple-element.9, bf16[320,8,128]{2,1,0:T(8,128)(2,1)S(1)} %get-tuple-element.42), kind=kOutput, calls=%fused_computation.78 | convolution fusion | flops 422049280 | bytes 4700160 | tf_op jit(solution)/shard_map/hqk,khd->qhd/dot_general | solution.py:105
  77.3 1.9 %fusion.70 = bf16[320,8,128]{2,0,1:T(8,128)(2,1)S(1)} fusion(f32[320,8,128]{2,1,0:T(8,128)S(1)} %get-tuple-element.7, f32[320,8,128]{2,0,1:T(8,128)} %get-tuple-element.35, f32[8,128]{1,0:T(8,128)S(1)} %get-tuple-element.27, f32[320,8]{0,1:T(8,128)S(1)} %add_rsqrt_fusion), kind=kLoop, calls=%fused_computation.81 | loop fusion | flops 2293760 | bytes 3291136 | tf_op jit(solution)/shard_map/convert_element_type | solution.py:119
  79.2 5.4 %collective-permute-start.7 = (bf16[320,8,128]{2,0,1:T(8,128)(2,1)S(1)}, bf16[320,8,128]{2,0,1:T(8,128)(2,1)}, u32[]{:S(2)}, u32[]{:S(2)}) collective-permute-start(bf16[320,8,128]{2,0,1:T(8,128)(2,1)S(1)} %fusion.70), channel_id=1, source_target_pairs={{0,4},{4,8},{8,12},{1,5},{5,9},{9,13},{2,6},{6,10},{10,14},{3,7},{... | collective-permute-start | bytes 1966088 | tf_op jit(solution)/shard_map/ppermute | solution.py:15
  84.6 1.7 %fusion.47 = f32[320,8,128]{2,0,1:T(8,128)} fusion(f32[8,128,128]{2,1,0:T(8,128)S(1)} %bitcast.183, pred[320]{0:T(512)(128)(4,1)S(1)} %copy-done.19, bf16[320,8,128]{2,1,0:T(8,128)(2,1)S(1)} %copy-done.4), kind=kOutput, calls=%fused_computation.46 | convolution fusion | flops 503644160 | bytes 2490688 | tf_op jit(solution)/shard_map/qhd,hde->qhe/dot_general | solution.py:106
  86.4 3.8 %multiply_reduce_fusion.1 = (f32[320,8]{0,1:T(8,128)S(1)}, f32[320,8,128]{2,0,1:T(8,128)}) fusion(f32[320,8,128]{2,0,1:T(8,128)} %fusion.47, bf16[320,16,128]{2,0,1:T(8,128)(2,1)} %copy_bitcast_fusion.4, pred[320,320]{1,0:T(8,128)(4,1)S(1)} %copy.15, bf16[320,8,128]{2,1,0:T(8,128)(2,1)S(1)} %copy-done.13, bf16[320,8,128]{2,1,0:T(8,128)(2,1)S(1)} %copy-done.5), kind=kOutput, calls=%fused_computation.79 | convolution fusion | flops 422049280 | bytes 4700160 | tf_op jit(solution)/shard_map/hqk,khd->qhd/dot_general | solution.py:105
  90.1 1.8 %fusion.69 = bf16[320,8,128]{2,0,1:T(8,128)(2,1)S(1)} fusion(f32[320,8,128]{2,1,0:T(8,128)S(1)} %get-tuple-element.6, f32[320,8,128]{2,0,1:T(8,128)} %get-tuple-element.37, f32[8,128]{1,0:T(8,128)S(1)} %get-tuple-element.26, f32[320,8]{0,1:T(8,128)S(1)} %add_rsqrt_fusion.1), kind=kLoop, calls=%fused_computation.80 | loop fusion | flops 2293760 | bytes 3291136 | tf_op jit(solution)/shard_map/convert_element_type | solution.py:119
  92.0 2.9 %collective-permute-start.4 = (bf16[320,8,128]{2,0,1:T(8,128)(2,1)S(1)}, bf16[320,8,128]{2,0,1:T(8,128)(2,1)S(1)}, u32[]{:S(2)}, u32[]{:S(2)}) collective-permute-start(bf16[320,8,128]{2,0,1:T(8,128)(2,1)S(1)} %fusion.69), channel_id=1, source_target_pairs={{0,4},{4,8},{8,12},{1,5},{5,9},{9,13},{2,6},{6,10},{10,14},{3,7},{... | collective-permute-start | bytes 1966088 | tf_op jit(solution)/shard_map/ppermute | solution.py:15
  98.4 1.8 %copy_bitcast_fusion.2 = bf16[320,16,128]{2,0,1:T(8,128)(2,1)S(1)} fusion(bf16[320,2176]{1,0:T(8,128)(2,1)} %collective-permute-done.3), kind=kLoop, calls=%fused_computation.54 | loop fusion | bytes 2621440 | tf_op jit(solution)/shard_map/reshape | solution.py:74
  100.2 4.1 %fusion = (f32[16,320]{1,0:T(8,128)S(1)}, f32[16,320,640]{2,1,0:T(8,128)S(1)}) fusion(pred[320,640]{1,0:T(8,128)(4,1)S(1)} %compare_and_fusion, bf16[320,16,128]{2,0,1:T(8,128)(2,1)S(1)} %copy_bitcast_fusion.2, bf16[320,16,128]{2,0,1:T(8,128)(2,1)S(1)} %copy-done.9, bf16[320,2176]{1,0:T(8,128)(2,1)} %collective-permute-done.2), kind=kOutput, calls=%fused_computation.2 | convolution fusion | flops 853928960 | bytes 17264640 | tf_op jit(solution)/shard_map/qhd,khd->hqk/dot_general | solution.py:84
  104.3 5.1 %fusion.2 = (bf16[16,320,640]{2,1,0:T(8,128)(2,1)S(1)}, f32[16,320]{1,0:T(8,128)S(1)}) fusion(f32[16,320,640]{2,1,0:T(8,128)S(1)} %get-tuple-element.41, f32[16,320]{1,0:T(8,128)S(1)} %get-tuple-element.40, pred[320,640]{1,0:T(8,128)(4,1)S(1)} %compare_and_fusion), kind=kLoop, calls=%fused_computation.4 | loop fusion | flops 19655680 | bytes 19906560 | tf_op jit(solution)/shard_map/convert_element_type | solution.py:90
  109.5 3.4 %collective-permute-start.6 = (f32[2,8,320]{2,1,0:T(8,128)S(1)}, f32[2,8,320]{2,1,0:T(8,128)S(1)}, u32[]{:S(2)}, u32[]{:S(2)}) collective-permute-start(f32[2,8,320]{2,1,0:T(8,128)S(1)} %pad_maximum_fusion.2), channel_id=1, source_target_pairs={{0,4},{4,8},{8,12},{1,5},{5,9},{9,13},{2,6},{6,10},{10,14},{3,7},{... | collective-permute-start | bytes 61448 | tf_op jit(solution)/shard_map/ppermute | solution.py:15
  114.3 1.9 %fusion.75 = bf16[320,8,128]{2,0,1:T(8,128)(2,1)S(1)} fusion(f32[8,128,320]{1,2,0:T(8,128)S(1)} %fusion.14, bf16[320,8,128]{2,0,1:T(8,128)(2,1)} %collective-permute-done.7, bf16[16,320,640]{2,1,0:T(8,128)(2,1)S(1)} %get-tuple-element.2), kind=kOutput, calls=%fused_computation.84 | convolution fusion | flops 210370560 | bytes 4587520 | tf_op jit(solution)/shard_map/hqk,khd->qhd/dot_general | solution.py:135
  116.2 2.0 %collective-permute-start.8 = (bf16[320,8,128]{2,0,1:T(8,128)(2,1)S(1)}, bf16[320,8,128]{2,0,1:T(8,128)(2,1)S(1)}, u32[]{:S(2)}, u32[]{:S(2)}) collective-permute-start(bf16[320,8,128]{2,0,1:T(8,128)(2,1)S(1)} %fusion.75), channel_id=1, source_target_pairs={{0,4},{4,8},{8,12},{1,5},{5,9},{9,13},{2,6},{6,10},{10,14},{3,7},{... | collective-permute-start | bytes 1966088 | tf_op jit(solution)/shard_map/ppermute | solution.py:15
  118.2 2.1 %collective-permute-start.9 = (f32[2,8,320]{2,1,0:T(8,128)S(1)}, f32[2,8,320]{2,1,0:T(8,128)S(1)}, u32[]{:S(2)}, u32[]{:S(2)}) collective-permute-start(f32[2,8,320]{2,1,0:T(8,128)S(1)} %pad_maximum_fusion.3), channel_id=1, source_target_pairs={{0,4},{4,8},{8,12},{1,5},{5,9},{9,13},{2,6},{6,10},{10,14},{3,7},{... | collective-permute-start | bytes 61448 | tf_op jit(solution)/shard_map/ppermute | solution.py:15
  121.2 2.0 %collective-permute-start.5 = (bf16[320,8,128]{2,0,1:T(8,128)(2,1)S(1)}, bf16[320,8,128]{2,0,1:T(8,128)(2,1)S(1)}, u32[]{:S(2)}, u32[]{:S(2)}) collective-permute-start(bf16[320,8,128]{2,0,1:T(8,128)(2,1)S(1)} %fusion.72), channel_id=1, source_target_pairs={{0,4},{4,8},{8,12},{1,5},{5,9},{9,13},{2,6},{6,10},{10,14},{3,7},{... | collective-permute-start | bytes 1966088 | tf_op jit(solution)/shard_map/ppermute | solution.py:15
  123.2 10.7 %collective-permute-done.9 = f32[2,8,320]{2,1,0:T(8,128)S(1)} collective-permute-done((f32[2,8,320]{2,1,0:T(8,128)S(1)}, f32[2,8,320]{2,1,0:T(8,128)S(1)}, u32[]{:S(2)}, u32[]{:S(2)}) %collective-permute-start.9) | collective-permute-done | bytes 20512 | tf_op jit(solution)/shard_map/ppermute | solution.py:15
  133.9 1.9 %divide_convert_fusion = bf16[320,8,128]{2,0,1:T(8,128)(2,1)S(1)} fusion(bf16[320,8,128]{2,0,1:T(8,128)(2,1)S(1)} %collective-permute-done.8, f32[320,8]{0,1:T(8,128)S(1)} %get-tuple-element.18, f32[320,8]{0,1:T(8,128)S(1)} %get-tuple-element.20, pred[]{:T(512)S(6)} %ge.29, f32[320,8]{0,1:T(8,128)S(1)} %get-tuple-element.19, ...), kind=kOutput, calls=%fused_computation.76 | convolution fusion | flops 212008960 | bytes 3969025 | tf_op jit(solution)/shard_map/hqk,khd->qhd/dot_general | solution.py:146
  135.8 9.5 %collective-permute-done.5 = bf16[320,8,128]{2,0,1:T(8,128)(2,1)S(1)} collective-permute-done((bf16[320,8,128]{2,0,1:T(8,128)(2,1)S(1)}, bf16[320,8,128]{2,0,1:T(8,128)(2,1)S(1)}, u32[]{:S(2)}, u32[]{:S(2)}) %collective-permute-start.5) | collective-permute-done | bytes 655392 | tf_op jit(solution)/shard_map/ppermute | solution.py:15
  145.3 1.9 %divide_convert_fusion.1 = bf16[320,8,128]{2,0,1:T(8,128)(2,1)S(1)} fusion(bf16[320,8,128]{2,0,1:T(8,128)(2,1)S(1)} %collective-permute-done.5, f32[320,8]{0,1:T(8,128)S(1)} %get-tuple-element.17, f32[320,8]{0,1:T(8,128)S(1)} %get-tuple-element.16, pred[]{:T(512)S(6)} %ge.29, f32[320,8]{0,1:T(8,128)S(1)} %get-tuple-element.21, ...), kind=kOutput, calls=%fused_computation.77 | convolution fusion | flops 212008960 | bytes 3969025 | tf_op jit(solution)/shard_map/hqk,khd->qhd/dot_general | solution.py:146
  (90 shorter events, 22.6 us)
Async XLA Ops:
  0.6 4.6 %copy-start = (bf16[320,2048]{1,0:T(8,128)(2,1)S(1)}, bf16[320,2048]{1,0:T(8,128)(2,1)}, u32[]{:S(2)}) copy-start(bf16[320,2048]{1,0:T(8,128)(2,1)} %param.10) | copy-start | bytes 3932164
  5.2 10.0 %copy-start.16 = (s32[320]{0:T(512)S(1)}, s32[320]{0:T(512)}, u32[]{:S(2)}) copy-start(s32[320]{0:T(512)} %param.15) | copy-start | bytes 3844
  5.2 10.7 %copy-start.2 = (bf16[320,2048]{1,0:T(8,128)(2,1)S(1)}, bf16[320,2048]{1,0:T(8,128)(2,1)}, u32[]{:S(2)}) copy-start(bf16[320,2048]{1,0:T(8,128)(2,1)} %param.14) | copy-start | bytes 3932164
  5.2 10.7 %copy-start.11 = (bf16[320,2048]{1,0:T(8,128)(2,1)S(1)}, bf16[320,2048]{1,0:T(8,128)(2,1)}, u32[]{:S(2)}) copy-start(bf16[320,2048]{1,0:T(8,128)(2,1)} %param.13) | copy-start | bytes 3932164
  9.4 30.4 %collective-permute-start = (bf16[2056,128]{1,0:T(8,128)(2,1)}, bf16[2056,128]{1,0:T(8,128)(2,1)}, u32[]{:S(2)}, u32[]{:S(2)}) collective-permute-start(bf16[2056,128]{1,0:T(8,128)(2,1)} %concatenate.31), channel_id=1, source_target_pairs={{0,4},{4,8},{8,12},{1,5},{5,9},{9,13},{2,6},{6,10},{10,14},{3,7},{... | collective-permute-start | bytes 1579016 | tf_op jit(solution)/shard_map/ppermute | solution.py:15
  15.2 0.6 copy-start.17
  17.7 78.4 %collective-permute-start.3 = (bf16[320,2176]{1,0:T(8,128)(2,1)}, bf16[320,2176]{1,0:T(8,128)(2,1)}, u32[]{:S(2)}, u32[]{:S(2)}) collective-permute-start(bf16[320,2176]{1,0:T(8,128)(2,1)} %get-tuple-element.15), channel_id=1, source_target_pairs={{0,4},{4,8},{8,12},{1,5},{5,9},{9,13},{2,6},{6,10},{10,14},{3,7},{... | collective-permute-start | bytes 4177928 | tf_op jit(solution)/shard_map/ppermute | solution.py:15
  21.4 75.8 %collective-permute-start.2 = (bf16[320,2176]{1,0:T(8,128)(2,1)}, bf16[320,2176]{1,0:T(8,128)(2,1)}, u32[]{:S(2)}, u32[]{:S(2)}) collective-permute-start(bf16[320,2176]{1,0:T(8,128)(2,1)} %get-tuple-element.14), channel_id=1, source_target_pairs={{4,0},{8,4},{12,8},{5,1},{9,5},{13,9},{6,2},{10,6},{14,10},{7,3},{... | collective-permute-start | bytes 4177928 | tf_op jit(solution)/shard_map/ppermute | solution.py:19
  24.2 1.4 copy-start.10
  26.5 1.3 copy-start.7
  27.8 1.3 copy-start.8
  29.1 0.7 copy-start.21
  42.2 1.4 copy-start.12
  43.8 23.1 %collective-permute-start.1 = (bf16[2056,128]{1,0:T(8,128)(2,1)S(1)}, bf16[2056,128]{1,0:T(8,128)(2,1)S(1)}, u32[]{:S(2)}, u32[]{:S(2)}) collective-permute-start(bf16[2056,128]{1,0:T(8,128)(2,1)S(1)} %concatenate.32), channel_id=1, source_target_pairs={{0,4},{4,8},{8,12},{1,5},{5,9},{9,13},{2,6},{6,10},{10,14},{3,7},{... | collective-permute-start | bytes 1579016 | tf_op jit(solution)/shard_map/ppermute | solution.py:15
  66.9 0.8 copy-start.14
  70.7 0.9 copy-start.19
  77.3 7.3 %copy-start.4 = (bf16[320,8,128]{2,1,0:T(8,128)(2,1)S(1)}, bf16[320,8,128]{2,1,0:T(8,128)(2,1)}, u32[]{:S(2)}) copy-start(bf16[320,8,128]{2,1,0:T(8,128)(2,1)} %get-tuple-element.43) | copy-start | bytes 1966084
  77.3 7.3 %copy-start.6 = (f32[1024,128]{1,0:T(8,128)S(1)}, f32[1024,128]{1,0:T(8,128)}, u32[]{:S(2)}) copy-start(f32[1024,128]{1,0:T(8,128)} %get-tuple-element.12) | copy-start | bytes 1572868
  79.2 7.2 %copy-start.5 = (bf16[320,8,128]{2,1,0:T(8,128)(2,1)S(1)}, bf16[320,8,128]{2,1,0:T(8,128)(2,1)}, u32[]{:S(2)}) copy-start(bf16[320,8,128]{2,1,0:T(8,128)(2,1)} %get-tuple-element.43) | copy-start | bytes 1966084
  79.2 7.2 %copy-start.13 = (bf16[320,8,128]{2,1,0:T(8,128)(2,1)S(1)}, bf16[320,8,128]{2,1,0:T(8,128)(2,1)}, u32[]{:S(2)}) copy-start(bf16[320,8,128]{2,1,0:T(8,128)(2,1)} %get-tuple-element.8) | copy-start | bytes 1966084
  79.2 35.1 %collective-permute-start.7 = (bf16[320,8,128]{2,0,1:T(8,128)(2,1)S(1)}, bf16[320,8,128]{2,0,1:T(8,128)(2,1)}, u32[]{:S(2)}, u32[]{:S(2)}) collective-permute-start(bf16[320,8,128]{2,0,1:T(8,128)(2,1)S(1)} %fusion.70), channel_id=1, source_target_pairs={{0,4},{4,8},{8,12},{1,5},{5,9},{9,13},{2,6},{6,10},{10,14},{3,7},{... | collective-permute-start | bytes 1966088 | tf_op jit(solution)/shard_map/ppermute | solution.py:15
  91.9 5.2 %copy-start.18 = (bf16[320]{0:T(512)(128)(2,1)S(1)}, bf16[320]{0:T(512)(128)(2,1)}, u32[]{:S(2)}) copy-start(bf16[320]{0:T(512)(128)(2,1)} %copy-done.17) | copy-start | bytes 1924
  92.0 6.3 %copy-start.20 = (pred[640]{0:T(1024)(128)(4,1)S(1)}, pred[640]{0:T(1024)(128)(4,1)}, u32[]{:S(2)}) copy-start(pred[640]{0:T(1024)(128)(4,1)} %concatenate.38) | copy-start | bytes 1924
  92.0 28.4 %collective-permute-start.4 = (bf16[320,8,128]{2,0,1:T(8,128)(2,1)S(1)}, bf16[320,8,128]{2,0,1:T(8,128)(2,1)S(1)}, u32[]{:S(2)}, u32[]{:S(2)}) collective-permute-start(bf16[320,8,128]{2,0,1:T(8,128)(2,1)S(1)} %fusion.69), channel_id=1, source_target_pairs={{0,4},{4,8},{8,12},{1,5},{5,9},{9,13},{2,6},{6,10},{10,14},{3,7},{... | collective-permute-start | bytes 1966088 | tf_op jit(solution)/shard_map/ppermute | solution.py:15
  98.4 1.8 %copy-start.9 = (bf16[320,16,128]{2,0,1:T(8,128)(2,1)S(1)}, bf16[320,16,128]{2,0,1:T(8,128)(2,1)}, u32[]{:S(2)}) copy-start(bf16[320,16,128]{2,0,1:T(8,128)(2,1)} %copy_bitcast_fusion.3) | copy-start | bytes 3932164
  109.5 13.7 %collective-permute-start.6 = (f32[2,8,320]{2,1,0:T(8,128)S(1)}, f32[2,8,320]{2,1,0:T(8,128)S(1)}, u32[]{:S(2)}, u32[]{:S(2)}) collective-permute-start(f32[2,8,320]{2,1,0:T(8,128)S(1)} %pad_maximum_fusion.2), channel_id=1, source_target_pairs={{0,4},{4,8},{8,12},{1,5},{5,9},{9,13},{2,6},{6,10},{10,14},{3,7},{... | collective-permute-start | bytes 61448 | tf_op jit(solution)/shard_map/ppermute | solution.py:15
  116.2 17.7 %collective-permute-start.8 = (bf16[320,8,128]{2,0,1:T(8,128)(2,1)S(1)}, bf16[320,8,128]{2,0,1:T(8,128)(2,1)S(1)}, u32[]{:S(2)}, u32[]{:S(2)}) collective-permute-start(bf16[320,8,128]{2,0,1:T(8,128)(2,1)S(1)} %fusion.75), channel_id=1, source_target_pairs={{0,4},{4,8},{8,12},{1,5},{5,9},{9,13},{2,6},{6,10},{10,14},{3,7},{... | collective-permute-start | bytes 1966088 | tf_op jit(solution)/shard_map/ppermute | solution.py:15
  118.2 15.6 %copy-start.15 = (f32[16,320]{1,0:T(8,128)S(1)}, f32[16,320]{1,0:T(8,128)}, u32[]{:S(2)}) copy-start(f32[16,320]{1,0:T(8,128)} %get-tuple-element.4) | copy-start | bytes 61444
  118.2 15.7 %copy-start.3 = (bf16[16,320,320]{1,2,0:T(8,128)(2,1)S(1)}, bf16[16,320,320]{1,2,0:T(8,128)(2,1)}, u32[]{:S(2)}) copy-start(bf16[16,320,320]{1,2,0:T(8,128)(2,1)} %get-tuple-element.5) | copy-start | bytes 9830404
  118.2 15.6 %collective-permute-start.9 = (f32[2,8,320]{2,1,0:T(8,128)S(1)}, f32[2,8,320]{2,1,0:T(8,128)S(1)}, u32[]{:S(2)}, u32[]{:S(2)}) collective-permute-start(f32[2,8,320]{2,1,0:T(8,128)S(1)} %pad_maximum_fusion.3), channel_id=1, source_target_pairs={{0,4},{4,8},{8,12},{1,5},{5,9},{9,13},{2,6},{6,10},{10,14},{3,7},{... | collective-permute-start | bytes 61448 | tf_op jit(solution)/shard_map/ppermute | solution.py:15
  121.2 24.1 %collective-permute-start.5 = (bf16[320,8,128]{2,0,1:T(8,128)(2,1)S(1)}, bf16[320,8,128]{2,0,1:T(8,128)(2,1)S(1)}, u32[]{:S(2)}, u32[]{:S(2)}) collective-permute-start(bf16[320,8,128]{2,0,1:T(8,128)(2,1)S(1)} %fusion.72), channel_id=1, source_target_pairs={{0,4},{4,8},{8,12},{1,5},{5,9},{9,13},{2,6},{6,10},{10,14},{3,7},{... | collective-permute-start | bytes 1966088 | tf_op jit(solution)/shard_map/ppermute | solution.py:15
  145.3 3.1 %copy-start.1 = (bf16[320,2048]{1,0:T(8,128)(2,1)S(1)}, bf16[320,2048]{1,0:T(8,128)(2,1)}, u32[]{:S(2)}) copy-start(bf16[320,2048]{1,0:T(8,128)(2,1)} %param.10) | copy-start | bytes 3932164

commit v15 on v12

--- a/solution.py
+++ b/solution.py
@@ -68,11 +68,18 @@
     next_msg = shift_down(jnp.concatenate([soft_query, doc_cols], axis=1), 1, n_seq)
     next_queries = next_msg[:, :width].reshape(row_count, head_count, HD)
     next_docs = next_msg[:, width].astype(jnp.int32)
-    key_msgs = [jnp.concatenate([soft_key, doc_cols], axis=1)]
+    half = head_count // 2
+    late_keys, _ = lax.optimization_barrier((soft_key[:, half * HD :], carried))
+    key_msgs = [jnp.concatenate([soft_key[:, : half * HD], doc_cols], axis=1)]
+    late_msgs = [late_keys]
     for d in dists[:-1]:
         key_msgs.append(shift_up(key_msgs[-1], 1, n_seq))
-    key_blocks = [m[:, :width].reshape(row_count, head_count, HD) for m in key_msgs]
-    key_docs = [m[:, width].astype(jnp.int32) for m in key_msgs]
+        late_msgs.append(shift_up(late_msgs[-1], 1, n_seq))
+    key_halves = [
+        [m[:, : half * HD].reshape(row_count, half, HD) for m in key_msgs],
+        [m.reshape(row_count, head_count - half, HD) for m in late_msgs],
+    ]
+    key_docs = [m[:, half * HD].astype(jnp.int32) for m in key_msgs]
 
     positions = jnp.arange(row_count, dtype=jnp.int32)
     causal = positions[:, None] >= positions[None, :]
@@ -89,14 +96,16 @@
         probs = jnp.where(keep[None], jnp.exp(logits - row_max[..., None]), 0.0)
         return probs.astype(jnp.bfloat16), row_max, jnp.sum(probs, axis=-1)
 
-    key_all = key_blocks[0]
+    key_all = soft_key.reshape(row_count, head_count, HD)
     diag = weights_of(soft_query.reshape(row_count, head_count, HD), keep_local)
-    key_all = jnp.concatenate(key_blocks, axis=0)
     valid = jnp.concatenate(
-        [jnp.full((row_count,), my_index >= d, jnp.bool_) for d in range(len(key_blocks))]
+        [jnp.full((row_count,), my_index >= d, jnp.bool_) for d in range(len(key_docs))]
     )
     keep_next = (next_docs[:, None] == jnp.concatenate(key_docs)[None, :]) & valid[None, :]
-    ahead = weights_of(next_queries, keep_next)
+    aheads = []
+    for (lo, hi), blocks in zip(((0, half), (half, head_count)), key_halves):
+        key_all = jnp.concatenate(blocks, axis=0)
+        aheads.append(weights_of(next_queries[:, lo:hi], keep_next))
 
     scores = jnp.einsum("qhd,khd->hqk", queries, key_rows, preferred_element_type=jnp.float32)
     rounded = jnp.where(keep_local[None], scores, jnp.zeros_like(scores)).astype(jnp.bfloat16)
@@ -115,12 +124,10 @@
     lin_out = normed.astype(jnp.bfloat16).reshape(row_count, width)
 
     value_own = lin_out.reshape(row_count, head_count, HD)
-    probs, ahead_max, ahead_sum = ahead
     diag_probs, diag_max, diag_sum = diag
     has_source = my_index >= 1
-    half = head_count // 2
     pieces = []
-    for lo, hi in ((0, half), (half, head_count)):
+    for (lo, hi), (probs, ahead_max, ahead_sum) in zip(((0, half), (half, head_count)), aheads):
         value_blocks = [value_own[:, lo:hi]]
         for d in dists[:-1]:
             value_blocks.append(shift_up(value_blocks[-1], 1, n_seq))
@@ -128,12 +135,12 @@
         for d, value_block in enumerate(value_blocks):
             ahead_out = ahead_out + jnp.einsum(
                 "hqk,khd->qhd",
-                probs[lo:hi, :, d * row_count : (d + 1) * row_count],
+                probs[:, :, d * row_count : (d + 1) * row_count],
                 value_block,
                 preferred_element_type=jnp.float32,
             )
         out_in = shift_up(ahead_out.astype(jnp.bfloat16), 1, n_seq)
-        stats_in = shift_up(jnp.stack([ahead_max[lo:hi], ahead_sum[lo:hi]]), 1, n_seq)
+        stats_in = shift_up(jnp.stack([ahead_max, ahead_sum]), 1, n_seq)
         max_in = jnp.where(has_source, stats_in[0], -1e30)
         sum_in = jnp.where(has_source, stats_in[1], 0.0)
         out_in = jnp.where(has_source, out_in.astype(jnp.float32), 0.0)

time: 137 us -> 135 us (0.985)
  starting transfers between devices: 35.5 us -> 41.1 us
  waiting for transfers between devices: 37.1 us -> 33.7 us
  other arithmetic: 19.6 us -> 16.4 us
  matrix products: 29.7 us -> 26.7 us
  local copies, waits for them, and re-layouts: 8.93 us -> 10.6 us
    ppermute x9 -> x10, starting transfers between devices: 34.2 us -> 39.8 us  [shift_up(): return lax.ppermute(x, 'seq', [(s, s + dist) for s in range(n_seq - dist)])]
    ppermute x9 -> x10, waiting for transfers between devices: 37.1 us -> 33.7 us  [shift_up(): return lax.ppermute(x, 'seq', [(s, s + dist) for s in range(n_seq - dist)])]
    dot_general x2 -> x3, matrix products: 10.1 us -> 7.2 us  [weights_of(): jnp.einsum('qhd,khd->hqk', query_rows, key_all, preferred_element_type=jn...]
    convert_element_type x1, other arithmetic: 5.17 us -> 2.53 us  [weights_of(): return (probs.astype(jnp.bfloat16), row_max, jnp.sum(probs, axis=-1))]
    reduce_sum x1, other arithmetic: 5.75 us -> 3.6 us  [weights_of(): return (probs.astype(jnp.bfloat16), row_max, jnp.sum(probs, axis=-1))]
    unnamed x20 -> x23, local copies, waits for them, and re-layouts: 0.05 us -> 2.18 us
    reshape x2 -> x4, local copies, waits for them, and re-layouts: 3.15 us -> 1.31 us  [the longest x2 1.08 us: per_device(): m[:, :half * HD].reshape(row_count, half, HD)]
    concatenate x2, local copies, waits for them, and re-layouts: 0.07 us -> 1.62 us  [per_device(): msg_in = shift_up(jnp.concatenate([state_rows, tag_rows], axis=0), 1, n_seq)]
  transfers between devices with their start and end apart: 10 -> 11, of which waited for: 4 -> 5; matrix products, arithmetic and copies ran while one was open for 35% -> 32% of each run, Pallas kernels for 0% -> 0%
where the time goes in v15:
time: 135 us; the launch traced here: 134 us
  starting transfers between devices  41.1 us (30%)
  waiting for transfers between devices  33.7 us (25%)
  matrix products  26.7 us (20%)
  other arithmetic  16.4 us (12%)
  local copies, waits for them, and re-layouts  10.6 us (8%)
  between operations  5.46 us (4%)
    ppermute x10, starting transfers between devices, shift_up(): return lax.ppermute(x, 'seq', [(s, s + dist) for s in range(n_seq - dist)])  39.8 us
    ppermute x10, waiting for transfers between devices, shift_up(): return lax.ppermute(x, 'seq', [(s, s + dist) for s in range(n_seq - dist)])  33.7 us
    dot_general x3, matrix products, weights_of(): jnp.einsum('qhd,khd->hqk', query_rows, key_all, preferred_element_type=jn...  7.2 us
    dot_general x1, matrix products, per_device(): jnp.einsum('hqk,khd->qhd', rounded, value_rows, preferred_element_type=jn...  5.46 us
    dot_general x1, matrix products, per_device(): jnp.einsum('qhd,hde->qhe', queries.astype(jnp.float32), carried, precisio...  3.97 us
    dot_general x1, matrix products, per_device(): jnp.einsum('thd,the->hde', tail_keys, value_rows, preferred_element_type=...  3.67 us
    reduce_sum x1, other arithmetic, weights_of(): return (probs.astype(jnp.bfloat16), row_max, jnp.sum(probs, axis=-1))  3.6 us
    dot_general x2, matrix products, per_device(): jnp.einsum('hqk,khd->qhd', diag_probs[lo:hi], value_blocks[0], preferred_...  3.41 us
  transfers between devices with their start and end apart: 11, of which 5 were waited for; matrix products, arithmetic and copies ran while one was open for 32% of the time, Pallas kernels for 0%

profile of v15, /device:TPU:0, one launch (start us, length us, event | category | flops | bytes accessed | tf_op | source)
XLA Modules:
  0.0 133.9 jit_solution(4501633116213687328)
XLA Ops:
  0.6 1.4 %fusion.117 = (s32[1]{0:T(128)}, s32[1]{0:T(128)}) fusion(s32[320]{0:T(512)} %param.15), kind=kLoop, calls=%fused_computation.142 | loop fusion | bytes 16 | tf_op jit(solution)/shard_map/slice | solution.py:45
  2.7 1.9 %broadcast_compare_fusion.1 = (pred[320]{0:T(512)(128)(4,1)S(1)}, pred[320]{0:T(512)(128)(4,1)S(1)}) fusion(s32[320]{0:T(512)} %param.15, s32[]{:T(128)} %bitcast.1, s32[]{:T(128)} %bitcast.2), kind=kLoop, calls=%fused_computation.132 | loop fusion | flops 640 | bytes 1928 | tf_op jit(solution)/shard_map/eq | solution.py:117
  4.7 3.7 %fusion.118 = (bf16[16,128,128]{2,1,0:T(8,128)(2,1)S(1)}, f32[16,128,128]{2,1,0:T(8,128)}) fusion(pred[320]{0:T(512)(128)(4,1)S(1)} %get-tuple-element.25, bf16[320,2048]{1,0:T(8,128)(2,1)} %param.10, bf16[320,2048]{1,0:T(8,128)(2,1)} %param.9), kind=kOutput, calls=%fused_computation.143 | convolution fusion | flops 168689664 | bytes 4194624 | tf_op jit(solution)/shard_map/thd,the->hde/dot_general | solution.py:51
  9.2 5.7 %collective-permute-start = (bf16[2056,128]{1,0:T(8,128)(2,1)}, bf16[2056,128]{1,0:T(8,128)(2,1)}, u32[]{:S(2)}, u32[]{:S(2)}) collective-permute-start(bf16[2056,128]{1,0:T(8,128)(2,1)} %concatenate.31), channel_id=1, source_target_pairs={{0,4},{4,8},{8,12},{1,5},{5,9},{9,13},{2,6},{6,10},{10,14},{3,7},{... | collective-permute-start | bytes 1579016 | tf_op jit(solution)/shard_map/ppermute | solution.py:15
  16.2 2.7 %collective-permute-start.3 = (bf16[320,1152]{1,0:T(8,128)(2,1)}, bf16[320,1152]{1,0:T(8,128)(2,1)S(1)}, u32[]{:S(2)}, u32[]{:S(2)}) collective-permute-start(bf16[320,1152]{1,0:T(8,128)(2,1)} %pad_maximum_fusion.1), channel_id=1, source_target_pairs={{0,4},{4,8},{8,12},{1,5},{5,9},{9,13},{2,6},{6,10},{10,14},{3,7},{... | collective-permute-start | bytes 2211848 | tf_op jit(solution)/shard_map/ppermute | solution.py:15
  18.9 1.2 pad_maximum_fusion
  20.2 1.3 collective-permute-start.2
  21.6 1.6 %fusion = (f32[16,320]{1,0:T(8,128)S(1)}, f32[16,320,320]{1,2,0:T(8,128)S(1)}) fusion(pred[320,320]{0,1:T(8,128)(4,1)S(1)} %fusion.90, bf16[320,2048]{1,0:T(8,128)(2,1)S(1)} %copy-done.3, bf16[320,2048]{1,0:T(8,128)(2,1)S(1)} %copy-done.5), kind=kOutput, calls=%fused_computation.3 | convolution fusion | flops 424340480 | bytes 9297920 | tf_op jit(solution)/shard_map/qhd,khd->hqk/dot_general | solution.py:91
  23.2 3.6 %fusion.3 = (f32[16,320]{1,0:T(8,128)S(1)}, bf16[16,320,320]{1,2,0:T(8,128)(2,1)}) fusion(f32[16,320,320]{1,2,0:T(8,128)S(1)} %get-tuple-element.33, f32[16,320]{1,0:T(8,128)S(1)} %get-tuple-element.32, pred[320,320]{0,1:T(8,128)(4,1)S(1)} %fusion.90), kind=kLoop, calls=%fused_computation.10 | loop fusion | flops 9825280 | bytes 9973760 | tf_op jit(solution)/shard_map/reduce_sum | solution.py:97
  28.1 5.5 %fusion.9 = f32[16,320,128]{2,1,0:T(8,128)} fusion(pred[320,320]{0,1:T(8,128)(4,1)S(1)} %fusion.90, bf16[320,2048]{1,0:T(8,128)(2,1)} %param.10, bf16[320,2048]{1,0:T(8,128)(2,1)} %param.9, bf16[320,2048]{1,0:T(8,128)(2,1)S(1)} %copy-done), kind=kOutput, calls=%fused_computation.16 | convolution fusion | flops 842137600 | bytes 6656000 | tf_op jit(solution)/shard_map/hqk,khd->qhd/dot_general | solution.py:112
  36.0 1.2 convert_select_fusion.1
  38.3 5.3 %collective-permute-start.1 = (bf16[2056,128]{1,0:T(8,128)(2,1)}, bf16[2056,128]{1,0:T(8,128)(2,1)}, u32[]{:S(2)}, u32[]{:S(2)}) collective-permute-start(bf16[2056,128]{1,0:T(8,128)(2,1)} %concatenate.32), channel_id=1, source_target_pairs={{0,4},{4,8},{8,12},{1,5},{5,9},{9,13},{2,6},{6,10},{10,14},{3,7},{... | collective-permute-start | bytes 1579016 | tf_op jit(solution)/shard_map/ppermute | solution.py:15
  45.0 8.6 %collective-permute-done.1 = bf16[2056,128]{1,0:T(8,128)(2,1)} collective-permute-done((bf16[2056,128]{1,0:T(8,128)(2,1)}, bf16[2056,128]{1,0:T(8,128)(2,1)}, u32[]{:S(2)}, u32[]{:S(2)}) %collective-permute-start.1) | collective-permute-done | bytes 526368 | tf_op jit(solution)/shard_map/ppermute | solution.py:15
  57.1 4.4 %collective-permute-start.7 = (bf16[320,1024]{1,0:T(8,128)(2,1)S(1)}, bf16[320,1024]{1,0:T(8,128)(2,1)S(1)}, u32[]{:S(2)}, u32[]{:S(2)}) collective-permute-start(bf16[320,1024]{1,0:T(8,128)(2,1)S(1)} %get-tuple-element.3), channel_id=1, source_target_pairs={{0,4},{4,8},{8,12},{1,5},{5,9},{9,13},{2,6},{6,10},{10,14},{3,7},{... | collective-permute-start | bytes 1966088 | tf_op jit(solution)/shard_map/ppermute | solution.py:15
  61.6 4.0 %multiply_reduce_fusion = (f32[320,16]{0,1:T(8,128)S(1)}, f32[320,16,128]{2,0,1:T(8,128)S(1)}) fusion(f32[16,128,128]{2,1,0:T(8,128)S(1)} %bitcast.195, pred[320]{0:T(512)(128)(4,1)S(1)} %get-tuple-element.24, f32[16,320,128]{2,1,0:T(8,128)} %fusion.9, bf16[320,2048]{1,0:T(8,128)(2,1)S(1)} %copy-done), kind=kOutput, calls=%fused_computation.24 | convolution fusion | flops 1009249280 | bytes 7622976 | tf_op jit(solution)/shard_map/qhd,hde->qhe/dot_general | solution.py:113
  66.6 3.4 %collective-permute-start.4 = (bf16[320,8,128]{2,0,1:T(8,128)(2,1)S(1)}, bf16[320,8,128]{2,0,1:T(8,128)(2,1)S(1)}, u32[]{:S(2)}, u32[]{:S(2)}) collective-permute-start(bf16[320,8,128]{2,0,1:T(8,128)(2,1)S(1)} %get-tuple-element.11), channel_id=1, source_target_pairs={{0,4},{4,8},{8,12},{1,5},{5,9},{9,13},{2,6},{6,10},{10,14},{3,7},{... | collective-permute-start | bytes 1966088 | tf_op jit(solution)/shard_map/ppermute | solution.py:15
  70.1 3.5 %collective-permute-start.8 = (bf16[320,8,128]{2,0,1:T(8,128)(2,1)S(1)}, bf16[320,8,128]{2,0,1:T(8,128)(2,1)S(1)}, u32[]{:S(2)}, u32[]{:S(2)}) collective-permute-start(bf16[320,8,128]{2,0,1:T(8,128)(2,1)S(1)} %get-tuple-element.12), channel_id=1, source_target_pairs={{0,4},{4,8},{8,12},{1,5},{5,9},{9,13},{2,6},{6,10},{10,14},{3,7},{... | collective-permute-start | bytes 1966088 | tf_op jit(solution)/shard_map/ppermute | solution.py:15
  73.7 1.3 copy_bitcast_fusion.1
  75.0 1.4 %slice_bitcast_fusion = bf16[40,8,16,128]{3,1,2,0:T(8,128)(2,1)S(1)} fusion(bf16[320,2176]{1,0:T(8,128)(2,1)} %collective-permute-done.2), kind=kLoop, calls=%fused_computation.60 | loop fusion | bytes 2621440
  78.2 1.5 %fusion.1 = (f32[8,320]{1,0:T(8,128)S(1)}, f32[8,320,640]{2,1,0:T(8,128)S(1)}) fusion(pred[320,640]{1,0:T(8,128)(4,1)S(1)} %compare_and_fusion, bf16[320,8,128]{2,0,1:T(8,128)(2,1)S(1)} %copy_bitcast_fusion.4, bf16[320,8,128]{2,0,1:T(8,128)(2,1)S(1)} %bitcast.198, bf16[320,8,128]{2,1,0:T(8,128)(2,1)S(1)} %get-tuple-element.13), kind=kOutput, calls=%fused_computation.8 | convolution fusion | flops 426964480 | bytes 8734720 | tf_op jit(solution)/shard_map/qhd,khd->hqk/dot_general | solution.py:91
  79.9 4.0 %fusion.5 = (f32[8,320]{1,0:T(8,128)S(1)}, f32[8,320]{1,0:T(8,128)S(1)}, bf16[8,320,640]{2,1,0:T(8,128)(2,1)S(1)}, f32[8,320,640]{2,1,0:T(8,128)S(1)}) fusion(f32[8,320,640]{2,1,0:T(8,128)S(1)} %get-tuple-element.35, f32[8,320]{1,0:T(8,128)S(1)} %get-tuple-element.34, pred[320,640]{1,0:T(8,128)(4,1)S(1)} %compare_and_fusion, ...), kind=kOutput, calls=%fused_computation.12 | convolution fusion | flops 436792320 | bytes 18585600 | tf_op jit(solution)/shard_map/qhd,khd->hqk/dot_general | solution.py:91
  84.5 6.2 %collective-permute-done.4 = bf16[320,8,128]{2,0,1:T(8,128)(2,1)S(1)} collective-permute-done((bf16[320,8,128]{2,0,1:T(8,128)(2,1)S(1)}, bf16[320,8,128]{2,0,1:T(8,128)(2,1)S(1)}, u32[]{:S(2)}, u32[]{:S(2)}) %collective-permute-start.4) | collective-permute-done | bytes 655392 | tf_op jit(solution)/shard_map/ppermute | solution.py:15
  91.6 4.4 %collective-permute-start.5 = (bf16[320,8,128]{2,0,1:T(8,128)(2,1)S(1)}, bf16[320,8,128]{2,0,1:T(8,128)(2,1)S(1)}, u32[]{:S(2)}, u32[]{:S(2)}) collective-permute-start(bf16[320,8,128]{2,0,1:T(8,128)(2,1)S(1)} %fusion.73), channel_id=1, source_target_pairs={{0,4},{4,8},{8,12},{1,5},{5,9},{9,13},{2,6},{6,10},{10,14},{3,7},{... | collective-permute-start | bytes 1966088 | tf_op jit(solution)/shard_map/ppermute | solution.py:15
  96.0 2.5 %fusion.8 = (bf16[8,320,640]{2,1,0:T(8,128)(2,1)S(1)}, f32[8,320]{1,0:T(8,128)S(1)}) fusion(f32[8,320,640]{2,1,0:T(8,128)S(1)} %get-tuple-element.36, f32[8,320]{1,0:T(8,128)S(1)} %get-tuple-element.5, pred[320,640]{1,0:T(8,128)(4,1)S(1)} %compare_and_fusion), kind=kLoop, calls=%fused_computation.15 | loop fusion | flops 9827840 | bytes 10055680 | tf_op jit(solution)/shard_map/convert_element_type | solution.py:97
  98.5 3.4 %collective-permute-start.10 = (f32[2,8,320]{2,1,0:T(8,128)S(1)}, f32[2,8,320]{2,1,0:T(8,128)S(1)}, u32[]{:S(2)}, u32[]{:S(2)}) collective-permute-start(f32[2,8,320]{2,1,0:T(8,128)S(1)} %pad_maximum_fusion.3), channel_id=1, source_target_pairs={{0,4},{4,8},{8,12},{1,5},{5,9},{9,13},{2,6},{6,10},{10,14},{3,7},{... | collective-permute-start | bytes 61448 | tf_op jit(solution)/shard_map/ppermute | solution.py:15
  102.0 3.4 %collective-permute-start.6 = (f32[2,8,320]{2,1,0:T(8,128)S(1)}, f32[2,8,320]{2,1,0:T(8,128)S(1)}, u32[]{:S(2)}, u32[]{:S(2)}) collective-permute-start(f32[2,8,320]{2,1,0:T(8,128)S(1)} %pad_maximum_fusion.2), channel_id=1, source_target_pairs={{0,4},{4,8},{8,12},{1,5},{5,9},{9,13},{2,6},{6,10},{10,14},{3,7},{... | collective-permute-start | bytes 61448 | tf_op jit(solution)/shard_map/ppermute | solution.py:15
  106.8 3.4 %collective-permute-start.9 = (bf16[320,8,128]{2,0,1:T(8,128)(2,1)S(1)}, bf16[320,8,128]{2,0,1:T(8,128)(2,1)S(1)}, u32[]{:S(2)}, u32[]{:S(2)}) collective-permute-start(bf16[320,8,128]{2,0,1:T(8,128)(2,1)S(1)} %fusion.76), channel_id=1, source_target_pairs={{0,4},{4,8},{8,12},{1,5},{5,9},{9,13},{2,6},{6,10},{10,14},{3,7},{... | collective-permute-start | bytes 1966088 | tf_op jit(solution)/shard_map/ppermute | solution.py:15
  110.3 9.1 %collective-permute-done.10 = f32[2,8,320]{2,1,0:T(8,128)S(1)} collective-permute-done((f32[2,8,320]{2,1,0:T(8,128)S(1)}, f32[2,8,320]{2,1,0:T(8,128)S(1)}, u32[]{:S(2)}, u32[]{:S(2)}) %collective-permute-start.10) | collective-permute-done | bytes 20512 | tf_op jit(solution)/shard_map/ppermute | solution.py:15
  119.9 1.7 %divide_convert_fusion.1 = bf16[320,8,128]{2,0,1:T(8,128)(2,1)S(1)} fusion(bf16[320,8,128]{2,0,1:T(8,128)(2,1)S(1)} %collective-permute-done.5, f32[320,8]{0,1:T(8,128)S(1)} %get-tuple-element.19, f32[320,8]{0,1:T(8,128)S(1)} %get-tuple-element.18, pred[]{:T(512)S(6)} %ge.29, f32[320,8]{0,1:T(8,128)S(1)} %get-tuple-element.23, ...), kind=kOutput, calls=%fused_computation.71 | convolution fusion | flops 212008960 | bytes 4624385 | tf_op jit(solution)/shard_map/hqk,khd->qhd/dot_general | solution.py:147
  121.6 9.3 %collective-permute-done.9 = bf16[320,8,128]{2,0,1:T(8,128)(2,1)S(1)} collective-permute-done((bf16[320,8,128]{2,0,1:T(8,128)(2,1)S(1)}, bf16[320,8,128]{2,0,1:T(8,128)(2,1)S(1)}, u32[]{:S(2)}, u32[]{:S(2)}) %collective-permute-start.9) | collective-permute-done | bytes 655392 | tf_op jit(solution)/shard_map/ppermute | solution.py:15
  131.0 1.7 %divide_convert_fusion = bf16[320,8,128]{2,0,1:T(8,128)(2,1)S(1)} fusion(bf16[320,8,128]{2,0,1:T(8,128)(2,1)S(1)} %collective-permute-done.9, f32[320,8]{0,1:T(8,128)S(1)} %get-tuple-element.20, f32[320,8]{0,1:T(8,128)S(1)} %get-tuple-element.22, pred[]{:T(512)S(6)} %ge.29, f32[320,8]{0,1:T(8,128)S(1)} %get-tuple-element.21, ...), kind=kOutput, calls=%fused_computation.70 | convolution fusion | flops 212008960 | bytes 4624385 | tf_op jit(solution)/shard_map/hqk,khd->qhd/dot_general | solution.py:147
  132.7 1.3 copy_bitcast_fusion
  (61 shorter events, 14.6 us)
Async XLA Ops:
  0.6 27.5 %copy-start = (bf16[320,2048]{1,0:T(8,128)(2,1)S(1)}, bf16[320,2048]{1,0:T(8,128)(2,1)}, u32[]{:S(2)}) copy-start(bf16[320,2048]{1,0:T(8,128)(2,1)} %param.8) | copy-start | bytes 3932164
  4.7 10.2 %copy-start.8 = (s32[320]{0:T(512)S(1)}, s32[320]{0:T(512)}, u32[]{:S(2)}) copy-start(s32[320]{0:T(512)} %param.15) | copy-start | bytes 3844
  4.7 10.2 %copy-start.3 = (bf16[320,2048]{1,0:T(8,128)(2,1)S(1)}, bf16[320,2048]{1,0:T(8,128)(2,1)}, u32[]{:S(2)}) copy-start(bf16[320,2048]{1,0:T(8,128)(2,1)} %param.14) | copy-start | bytes 3932164
  9.2 24.4 %collective-permute-start = (bf16[2056,128]{1,0:T(8,128)(2,1)}, bf16[2056,128]{1,0:T(8,128)(2,1)}, u32[]{:S(2)}, u32[]{:S(2)}) collective-permute-start(bf16[2056,128]{1,0:T(8,128)(2,1)} %concatenate.31), channel_id=1, source_target_pairs={{0,4},{4,8},{8,12},{1,5},{5,9},{9,13},{2,6},{6,10},{10,14},{3,7},{... | collective-permute-start | bytes 1579016 | tf_op jit(solution)/shard_map/ppermute | solution.py:15
  15.1 3.8 %copy-start.5 = (bf16[320,2048]{1,0:T(8,128)(2,1)S(1)}, bf16[320,2048]{1,0:T(8,128)(2,1)}, u32[]{:S(2)}) copy-start(bf16[320,2048]{1,0:T(8,128)(2,1)} %param.13) | copy-start | bytes 3932164
  16.2 28.5 %collective-permute-start.3 = (bf16[320,1152]{1,0:T(8,128)(2,1)}, bf16[320,1152]{1,0:T(8,128)(2,1)S(1)}, u32[]{:S(2)}, u32[]{:S(2)}) collective-permute-start(bf16[320,1152]{1,0:T(8,128)(2,1)} %pad_maximum_fusion.1), channel_id=1, source_target_pairs={{0,4},{4,8},{8,12},{1,5},{5,9},{9,13},{2,6},{6,10},{10,14},{3,7},{... | collective-permute-start | bytes 2211848 | tf_op jit(solution)/shard_map/ppermute | solution.py:15
  20.2 54.8 %collective-permute-start.2 = (bf16[320,2176]{1,0:T(8,128)(2,1)}, bf16[320,2176]{1,0:T(8,128)(2,1)}, u32[]{:S(2)}, u32[]{:S(2)}) collective-permute-start(bf16[320,2176]{1,0:T(8,128)(2,1)} %pad_maximum_fusion), channel_id=1, source_target_pairs={{4,0},{8,4},{12,8},{5,1},{9,5},{13,9},{6,2},{10,6},{14,10},{7,3},{... | collective-permute-start | bytes 4177928 | tf_op jit(solution)/shard_map/ppermute | solution.py:19
  36.0 1.4 %copy-start.6 = (f32[16,128,128]{2,1,0:T(8,128)S(1)}, f32[16,128,128]{2,1,0:T(8,128)}, u32[]{:S(2)}) copy-start(f32[16,128,128]{2,1,0:T(8,128)} %get-tuple-element.29) | copy-start | bytes 3145732
  37.4 6.3 %copy-start.9 = (bf16[2048]{0:T(1024)(128)(2,1)S(1)}, bf16[2048]{0:T(1024)(128)(2,1)}, u32[]{:S(2)}) copy-start(bf16[2048]{0:T(1024)(128)(2,1)} %param.11) | copy-start | bytes 12292
  38.3 15.2 %collective-permute-start.1 = (bf16[2056,128]{1,0:T(8,128)(2,1)}, bf16[2056,128]{1,0:T(8,128)(2,1)}, u32[]{:S(2)}, u32[]{:S(2)}) collective-permute-start(bf16[2056,128]{1,0:T(8,128)(2,1)} %concatenate.32), channel_id=1, source_target_pairs={{0,4},{4,8},{8,12},{1,5},{5,9},{9,13},{2,6},{6,10},{10,14},{3,7},{... | collective-permute-start | bytes 1579016 | tf_op jit(solution)/shard_map/ppermute | solution.py:15
  57.1 22.6 %collective-permute-start.7 = (bf16[320,1024]{1,0:T(8,128)(2,1)S(1)}, bf16[320,1024]{1,0:T(8,128)(2,1)S(1)}, u32[]{:S(2)}, u32[]{:S(2)}) collective-permute-start(bf16[320,1024]{1,0:T(8,128)(2,1)S(1)} %get-tuple-element.3), channel_id=1, source_target_pairs={{0,4},{4,8},{8,12},{1,5},{5,9},{9,13},{2,6},{6,10},{10,14},{3,7},{... | collective-permute-start | bytes 1966088 | tf_op jit(solution)/shard_map/ppermute | solution.py:15
  61.6 4.0 %copy-start.4 = (bf16[320,2048]{1,0:T(8,128)(2,1)S(1)}, bf16[320,2048]{1,0:T(8,128)(2,1)}, u32[]{:S(2)}) copy-start(bf16[320,2048]{1,0:T(8,128)(2,1)} %param.12) | copy-start | bytes 3932164
  66.6 24.1 %collective-permute-start.4 = (bf16[320,8,128]{2,0,1:T(8,128)(2,1)S(1)}, bf16[320,8,128]{2,0,1:T(8,128)(2,1)S(1)}, u32[]{:S(2)}, u32[]{:S(2)}) collective-permute-start(bf16[320,8,128]{2,0,1:T(8,128)(2,1)S(1)} %get-tuple-element.11), channel_id=1, source_target_pairs={{0,4},{4,8},{8,12},{1,5},{5,9},{9,13},{2,6},{6,10},{10,14},{3,7},{... | collective-permute-start | bytes 1966088 | tf_op jit(solution)/shard_map/ppermute | solution.py:15
  70.1 35.9 %collective-permute-start.8 = (bf16[320,8,128]{2,0,1:T(8,128)(2,1)S(1)}, bf16[320,8,128]{2,0,1:T(8,128)(2,1)S(1)}, u32[]{:S(2)}, u32[]{:S(2)}) collective-permute-start(bf16[320,8,128]{2,0,1:T(8,128)(2,1)S(1)} %get-tuple-element.12), channel_id=1, source_target_pairs={{0,4},{4,8},{8,12},{1,5},{5,9},{9,13},{2,6},{6,10},{10,14},{3,7},{... | collective-permute-start | bytes 1966088 | tf_op jit(solution)/shard_map/ppermute | solution.py:15
  76.8 1.4 %copy-start.7 = (bf16[40,8,8,128]{3,2,0,1:T(8,128)(2,1)S(1)}, bf16[40,8,8,128]{3,2,0,1:T(8,128)(2,1)}, u32[]{:S(2)}) copy-start(bf16[40,8,8,128]{3,2,0,1:T(8,128)(2,1)} %copy.114) | copy-start | bytes 1966084
  91.6 28.4 %collective-permute-start.5 = (bf16[320,8,128]{2,0,1:T(8,128)(2,1)S(1)}, bf16[320,8,128]{2,0,1:T(8,128)(2,1)S(1)}, u32[]{:S(2)}, u32[]{:S(2)}) collective-permute-start(bf16[320,8,128]{2,0,1:T(8,128)(2,1)S(1)} %fusion.73), channel_id=1, source_target_pairs={{0,4},{4,8},{8,12},{1,5},{5,9},{9,13},{2,6},{6,10},{10,14},{3,7},{... | collective-permute-start | bytes 1966088 | tf_op jit(solution)/shard_map/ppermute | solution.py:15
  98.5 20.8 %collective-permute-start.10 = (f32[2,8,320]{2,1,0:T(8,128)S(1)}, f32[2,8,320]{2,1,0:T(8,128)S(1)}, u32[]{:S(2)}, u32[]{:S(2)}) collective-permute-start(f32[2,8,320]{2,1,0:T(8,128)S(1)} %pad_maximum_fusion.3), channel_id=1, source_target_pairs={{0,4},{4,8},{8,12},{1,5},{5,9},{9,13},{2,6},{6,10},{10,14},{3,7},{... | collective-permute-start | bytes 61448 | tf_op jit(solution)/shard_map/ppermute | solution.py:15
  102.0 17.9 %collective-permute-start.6 = (f32[2,8,320]{2,1,0:T(8,128)S(1)}, f32[2,8,320]{2,1,0:T(8,128)S(1)}, u32[]{:S(2)}, u32[]{:S(2)}) collective-permute-start(f32[2,8,320]{2,1,0:T(8,128)S(1)} %pad_maximum_fusion.2), channel_id=1, source_target_pairs={{0,4},{4,8},{8,12},{1,5},{5,9},{9,13},{2,6},{6,10},{10,14},{3,7},{... | collective-permute-start | bytes 61448 | tf_op jit(solution)/shard_map/ppermute | solution.py:15
  106.0 13.9 %copy-start.2 = (bf16[16,320,320]{1,2,0:T(8,128)(2,1)S(1)}, bf16[16,320,320]{1,2,0:T(8,128)(2,1)}, u32[]{:S(2)}) copy-start(bf16[16,320,320]{1,2,0:T(8,128)(2,1)} %get-tuple-element.7) | copy-start | bytes 9830404
  106.8 24.1 %collective-permute-start.9 = (bf16[320,8,128]{2,0,1:T(8,128)(2,1)S(1)}, bf16[320,8,128]{2,0,1:T(8,128)(2,1)S(1)}, u32[]{:S(2)}, u32[]{:S(2)}) collective-permute-start(bf16[320,8,128]{2,0,1:T(8,128)(2,1)S(1)} %fusion.76), channel_id=1, source_target_pairs={{0,4},{4,8},{8,12},{1,5},{5,9},{9,13},{2,6},{6,10},{10,14},{3,7},{... | collective-permute-start | bytes 1966088 | tf_op jit(solution)/shard_map/ppermute | solution.py:15
  131.0 3.0 %copy-start.1 = (bf16[320,2048]{1,0:T(8,128)(2,1)S(1)}, bf16[320,2048]{1,0:T(8,128)(2,1)}, u32[]{:S(2)}) copy-start(bf16[320,2048]{1,0:T(8,128)(2,1)} %param.8) | copy-start | bytes 3932164

commit v16 on v15

--- a/solution.py
+++ b/solution.py
@@ -69,17 +69,19 @@
     next_queries = next_msg[:, :width].reshape(row_count, head_count, HD)
     next_docs = next_msg[:, width].astype(jnp.int32)
     half = head_count // 2
-    late_keys, _ = lax.optimization_barrier((soft_key[:, half * HD :], carried))
-    key_msgs = [jnp.concatenate([soft_key[:, : half * HD], doc_cols], axis=1)]
+    late_keys, _ = lax.optimization_barrier(
+        (jnp.concatenate([soft_key[:, half * HD :], doc_cols], axis=1), carried)
+    )
+    key_msgs = [soft_key[:, : half * HD]]
     late_msgs = [late_keys]
     for d in dists[:-1]:
         key_msgs.append(shift_up(key_msgs[-1], 1, n_seq))
         late_msgs.append(shift_up(late_msgs[-1], 1, n_seq))
     key_halves = [
-        [m[:, : half * HD].reshape(row_count, half, HD) for m in key_msgs],
-        [m.reshape(row_count, head_count - half, HD) for m in late_msgs],
+        [m.reshape(row_count, half, HD) for m in key_msgs],
+        [m[:, : width - half * HD].reshape(row_count, head_count - half, HD) for m in late_msgs],
     ]
-    key_docs = [m[:, half * HD].astype(jnp.int32) for m in key_msgs]
+    key_docs = [m[:, width - half * HD].astype(jnp.int32) for m in late_msgs]
 
     positions = jnp.arange(row_count, dtype=jnp.int32)
     causal = positions[:, None] >= positions[None, :]

time: 135 us -> 136 us (level)
  waiting for transfers between devices: 33.7 us -> 37.1 us
  matrix products: 26.7 us -> 24.9 us
    ppermute x10, waiting for transfers between devices: 33.7 us -> 37.1 us  [shift_up(): return lax.ppermute(x, 'seq', [(s, s + dist) for s in range(n_seq - dist)])]
    dot_general x1, matrix products: 3.97 us -> 2.23 us  [per_device(): jnp.einsum('qhd,hde->qhe', queries.astype(jnp.float32), carried, precisio...]
  transfers between devices with their start and end apart: 11 -> 11, of which waited for: 5 -> 6; matrix products, arithmetic and copies ran while one was open for 32% -> 30% of each run, Pallas kernels for 0% -> 0%
where the time goes in v16:
time: 136 us; the launch traced here: 135 us
  starting transfers between devices  41.1 us (30%)
  waiting for transfers between devices  37.1 us (27%)
  matrix products  24.9 us (18%)
  other arithmetic  15.6 us (11%)
  local copies, waits for them, and re-layouts  10.9 us (8%)
  between operations  5.67 us (4%)
    ppermute x10, starting transfers between devices, shift_up(): return lax.ppermute(x, 'seq', [(s, s + dist) for s in range(n_seq - dist)])  39.8 us
    ppermute x10, waiting for transfers between devices, shift_up(): return lax.ppermute(x, 'seq', [(s, s + dist) for s in range(n_seq - dist)])  37.1 us
    dot_general x3, matrix products, weights_of(): jnp.einsum('qhd,khd->hqk', query_rows, key_all, preferred_element_type=jn...  7.21 us
    dot_general x1, matrix products, per_device(): jnp.einsum('hqk,khd->qhd', rounded, value_rows, preferred_element_type=jn...  5.48 us
    dot_general x1, matrix products, per_device(): jnp.einsum('thd,the->hde', tail_keys, value_rows, preferred_element_type=...  3.67 us
    reduce_sum x1, other arithmetic, weights_of(): return (probs.astype(jnp.bfloat16), row_max, jnp.sum(probs, axis=-1))  3.59 us
    dot_general x2, matrix products, per_device(): jnp.einsum('hqk,khd->qhd', diag_probs[lo:hi], value_blocks[0], preferred_...  3.41 us
    unnamed x23, local copies, waits for them, and re-layouts  3.02 us
  transfers between devices with their start and end apart: 11, of which 6 were waited for; matrix products, arithmetic and copies ran while one was open for 30% of the time, Pallas kernels for 0%

profile of v16, /device:TPU:0, one launch (start us, length us, event | category | flops | bytes accessed | tf_op | source)
XLA Modules:
  0.0 135.4 jit_solution(9576707398732110453)
XLA Ops:
  0.6 1.4 %fusion.117 = (s32[1]{0:T(128)}, s32[1]{0:T(128)}) fusion(s32[320]{0:T(512)} %param.15), kind=kLoop, calls=%fused_computation.144 | loop fusion | bytes 16 | tf_op jit(solution)/shard_map/slice | solution.py:45
  2.7 2.0 %broadcast_compare_fusion.1 = (pred[320]{0:T(512)(128)(4,1)S(1)}, pred[320]{0:T(512)(128)(4,1)S(1)}) fusion(s32[320]{0:T(512)} %param.15, s32[]{:T(128)} %bitcast.1, s32[]{:T(128)} %bitcast.2), kind=kLoop, calls=%fused_computation.134 | loop fusion | flops 640 | bytes 1928 | tf_op jit(solution)/shard_map/eq | solution.py:119
  4.7 3.7 %fusion.118 = (bf16[16,128,128]{2,1,0:T(8,128)(2,1)S(1)}, f32[16,128,128]{2,1,0:T(8,128)}) fusion(pred[320]{0:T(512)(128)(4,1)S(1)} %get-tuple-element.25, bf16[320,2048]{1,0:T(8,128)(2,1)} %param.10, bf16[320,2048]{1,0:T(8,128)(2,1)} %param.9), kind=kOutput, calls=%fused_computation.145 | convolution fusion | flops 168689664 | bytes 4194624 | tf_op jit(solution)/shard_map/thd,the->hde/dot_general | solution.py:51
  8.4 5.7 %collective-permute-start = (bf16[2056,128]{1,0:T(8,128)(2,1)S(1)}, bf16[2056,128]{1,0:T(8,128)(2,1)}, u32[]{:S(2)}, u32[]{:S(2)}) collective-permute-start(bf16[2056,128]{1,0:T(8,128)(2,1)S(1)} %concatenate.31), channel_id=1, source_target_pairs={{0,4},{4,8},{8,12},{1,5},{5,9},{9,13},{2,6},{6,10},{10,14},{3,7},{... | collective-permute-start | bytes 1579016 | tf_op jit(solution)/shard_map/ppermute | solution.py:15
  15.5 1.3 collective-permute-start.2
  17.8 5.4 %collective-permute-start.4 = (bf16[320,1024]{1,0:T(8,128)(2,1)}, bf16[320,1024]{1,0:T(8,128)(2,1)}, u32[]{:S(2)}, u32[]{:S(2)}) collective-permute-start(bf16[320,1024]{1,0:T(8,128)(2,1)} %get-tuple-element.17), channel_id=1, source_target_pairs={{0,4},{4,8},{8,12},{1,5},{5,9},{9,13},{2,6},{6,10},{10,14},{3,7},{... | collective-permute-start | bytes 1966088 | tf_op jit(solution)/shard_map/ppermute | solution.py:15
  23.4 1.6 %fusion = (f32[16,320]{1,0:T(8,128)S(1)}, f32[16,320,320]{1,2,0:T(8,128)S(1)}) fusion(pred[320,320]{0,1:T(8,128)(4,1)S(1)} %fusion.90, bf16[320,2048]{1,0:T(8,128)(2,1)S(1)} %copy-done.4, bf16[320,2048]{1,0:T(8,128)(2,1)S(1)} %copy-done.6), kind=kOutput, calls=%fused_computation.3 | convolution fusion | flops 424340480 | bytes 9297920 | tf_op jit(solution)/shard_map/qhd,khd->hqk/dot_general | solution.py:93
  25.0 3.6 %fusion.3 = (f32[16,320]{1,0:T(8,128)S(1)}, bf16[16,320,320]{1,2,0:T(8,128)(2,1)}) fusion(f32[16,320,320]{1,2,0:T(8,128)S(1)} %get-tuple-element.33, f32[16,320]{1,0:T(8,128)S(1)} %get-tuple-element.32, pred[320,320]{0,1:T(8,128)(4,1)S(1)} %fusion.90), kind=kLoop, calls=%fused_computation.10 | loop fusion | flops 9825280 | bytes 9973760 | tf_op jit(solution)/shard_map/reduce_sum | solution.py:99
  29.9 5.5 %fusion.9 = f32[16,320,128]{2,1,0:T(8,128)} fusion(pred[320,320]{0,1:T(8,128)(4,1)S(1)} %fusion.90, bf16[320,2048]{1,0:T(8,128)(2,1)} %param.10, bf16[320,2048]{1,0:T(8,128)(2,1)} %param.9, bf16[320,2048]{1,0:T(8,128)(2,1)S(1)} %copy-done), kind=kOutput, calls=%fused_computation.16 | convolution fusion | flops 842137600 | bytes 6656000 | tf_op jit(solution)/shard_map/hqk,khd->qhd/dot_general | solution.py:114
  40.2 2.7 %collective-permute-start.1 = (bf16[2056,128]{1,0:T(8,128)(2,1)}, bf16[2056,128]{1,0:T(8,128)(2,1)}, u32[]{:S(2)}, u32[]{:S(2)}) collective-permute-start(bf16[2056,128]{1,0:T(8,128)(2,1)} %concatenate.32), channel_id=1, source_target_pairs={{0,4},{4,8},{8,12},{1,5},{5,9},{9,13},{2,6},{6,10},{10,14},{3,7},{... | collective-permute-start | bytes 1579016 | tf_op jit(solution)/shard_map/ppermute | solution.py:15
  44.3 8.5 %collective-permute-done.1 = bf16[2056,128]{1,0:T(8,128)(2,1)} collective-permute-done((bf16[2056,128]{1,0:T(8,128)(2,1)}, bf16[2056,128]{1,0:T(8,128)(2,1)}, u32[]{:S(2)}, u32[]{:S(2)}) %collective-permute-start.1) | collective-permute-done | bytes 526368 | tf_op jit(solution)/shard_map/ppermute | solution.py:15
  55.3 1.3 convert_select_fusion
  56.5 4.7 %collective-permute-start.3 = (bf16[320,1152]{1,0:T(8,128)(2,1)S(1)}, bf16[320,1152]{1,0:T(8,128)(2,1)S(1)}, u32[]{:S(2)}, u32[]{:S(2)}) collective-permute-start(bf16[320,1152]{1,0:T(8,128)(2,1)S(1)} %pad_maximum_fusion.1), channel_id=1, source_target_pairs={{0,4},{4,8},{8,12},{1,5},{5,9},{9,13},{2,6},{6,10},{10,14},{3,7},{... | collective-permute-start | bytes 2211848 | tf_op jit(solution)/shard_map/ppermute | solution.py:15
  61.4 2.2 %multiply_reduce_fusion = (f32[320,16]{0,1:T(8,128)S(1)}, f32[320,16,128]{2,0,1:T(8,128)S(1)}) fusion(f32[16,128,128]{2,1,0:T(8,128)S(1)} %bitcast.195, pred[320]{0:T(512)(128)(4,1)S(1)} %get-tuple-element.24, f32[16,320,128]{2,1,0:T(8,128)S(1)} %copy-done.3, bf16[320,2048]{1,0:T(8,128)(2,1)S(1)} %copy-done), kind=kOutput, calls=%fused_computation.24 | convolution fusion | flops 1009249280 | bytes 7622976 | tf_op jit(solution)/shard_map/qhd,hde->qhe/dot_general | solution.py:115
  64.7 1.3 copy_bitcast_fusion.1
  66.1 4.4 %collective-permute-start.5 = (bf16[320,8,128]{2,0,1:T(8,128)(2,1)S(1)}, bf16[320,8,128]{2,0,1:T(8,128)(2,1)S(1)}, u32[]{:S(2)}, u32[]{:S(2)}) collective-permute-start(bf16[320,8,128]{2,0,1:T(8,128)(2,1)S(1)} %get-tuple-element.11), channel_id=1, source_target_pairs={{0,4},{4,8},{8,12},{1,5},{5,9},{9,13},{2,6},{6,10},{10,14},{3,7},{... | collective-permute-start | bytes 1966088 | tf_op jit(solution)/shard_map/ppermute | solution.py:15
  70.5 2.4 %collective-permute-start.8 = (bf16[320,8,128]{2,0,1:T(8,128)(2,1)S(1)}, bf16[320,8,128]{2,0,1:T(8,128)(2,1)S(1)}, u32[]{:S(2)}, u32[]{:S(2)}) collective-permute-start(bf16[320,8,128]{2,0,1:T(8,128)(2,1)S(1)} %get-tuple-element.12), channel_id=1, source_target_pairs={{0,4},{4,8},{8,12},{1,5},{5,9},{9,13},{2,6},{6,10},{10,14},{3,7},{... | collective-permute-start | bytes 1966088 | tf_op jit(solution)/shard_map/ppermute | solution.py:15
  72.8 1.4 %slice_bitcast_fusion = bf16[40,8,16,128]{3,1,2,0:T(8,128)(2,1)S(1)} fusion(bf16[320,2176]{1,0:T(8,128)(2,1)} %collective-permute-done.2), kind=kLoop, calls=%fused_computation.60 | loop fusion | bytes 2621440
  75.7 2.4 %collective-permute-done.3 = bf16[320,1152]{1,0:T(8,128)(2,1)S(1)} collective-permute-done((bf16[320,1152]{1,0:T(8,128)(2,1)S(1)}, bf16[320,1152]{1,0:T(8,128)(2,1)S(1)}, u32[]{:S(2)}, u32[]{:S(2)}) %collective-permute-start.3) | collective-permute-done | bytes 737312 | tf_op jit(solution)/shard_map/ppermute | solution.py:15
  78.5 1.5 %fusion.1 = (f32[8,320]{1,0:T(8,128)S(1)}, f32[8,320,640]{2,1,0:T(8,128)S(1)}) fusion(pred[320,640]{1,0:T(8,128)(4,1)S(1)} %compare_and_fusion, bf16[320,8,128]{2,0,1:T(8,128)(2,1)S(1)} %copy_bitcast_fusion.4, bf16[320,8,128]{2,0,1:T(8,128)(2,1)S(1)} %bitcast.198, bf16[320,8,128]{2,1,0:T(8,128)(2,1)S(1)} %get-tuple-element.13), kind=kOutput, calls=%fused_computation.8 | convolution fusion | flops 426964480 | bytes 8734720 | tf_op jit(solution)/shard_map/qhd,khd->hqk/dot_general | solution.py:93
  80.2 4.0 %fusion.5 = (f32[8,320]{1,0:T(8,128)S(1)}, f32[8,320]{1,0:T(8,128)S(1)}, bf16[8,320,640]{2,1,0:T(8,128)(2,1)S(1)}, f32[8,320,640]{2,1,0:T(8,128)S(1)}) fusion(f32[8,320,640]{2,1,0:T(8,128)S(1)} %get-tuple-element.35, f32[8,320]{1,0:T(8,128)S(1)} %get-tuple-element.34, pred[320,640]{1,0:T(8,128)(4,1)S(1)} %compare_and_fusion, ...), kind=kOutput, calls=%fused_computation.12 | convolution fusion | flops 436792320 | bytes 18585600 | tf_op jit(solution)/shard_map/qhd,khd->hqk/dot_general | solution.py:93
  84.9 7.3 %collective-permute-done.5 = bf16[320,8,128]{2,0,1:T(8,128)(2,1)S(1)} collective-permute-done((bf16[320,8,128]{2,0,1:T(8,128)(2,1)S(1)}, bf16[320,8,128]{2,0,1:T(8,128)(2,1)S(1)}, u32[]{:S(2)}, u32[]{:S(2)}) %collective-permute-start.5) | collective-permute-done | bytes 655392 | tf_op jit(solution)/shard_map/ppermute | solution.py:15
  93.0 4.4 %collective-permute-start.6 = (bf16[320,8,128]{2,0,1:T(8,128)(2,1)S(1)}, bf16[320,8,128]{2,0,1:T(8,128)(2,1)S(1)}, u32[]{:S(2)}, u32[]{:S(2)}) collective-permute-start(bf16[320,8,128]{2,0,1:T(8,128)(2,1)S(1)} %fusion.73), channel_id=1, source_target_pairs={{0,4},{4,8},{8,12},{1,5},{5,9},{9,13},{2,6},{6,10},{10,14},{3,7},{... | collective-permute-start | bytes 1966088 | tf_op jit(solution)/shard_map/ppermute | solution.py:15
  97.4 2.5 %fusion.8 = (bf16[8,320,640]{2,1,0:T(8,128)(2,1)S(1)}, f32[8,320]{1,0:T(8,128)S(1)}) fusion(f32[8,320,640]{2,1,0:T(8,128)S(1)} %get-tuple-element.36, f32[8,320]{1,0:T(8,128)S(1)} %get-tuple-element.5, pred[320,640]{1,0:T(8,128)(4,1)S(1)} %compare_and_fusion), kind=kLoop, calls=%fused_computation.15 | loop fusion | flops 9827840 | bytes 10055680 | tf_op jit(solution)/shard_map/convert_element_type | solution.py:99
  100.0 4.3 %collective-permute-start.10 = (f32[2,8,320]{2,1,0:T(8,128)S(1)}, f32[2,8,320]{2,1,0:T(8,128)S(1)}, u32[]{:S(2)}, u32[]{:S(2)}) collective-permute-start(f32[2,8,320]{2,1,0:T(8,128)S(1)} %pad_maximum_fusion.3), channel_id=1, source_target_pairs={{0,4},{4,8},{8,12},{1,5},{5,9},{9,13},{2,6},{6,10},{10,14},{3,7},{... | collective-permute-start | bytes 61448 | tf_op jit(solution)/shard_map/ppermute | solution.py:15
  104.4 2.2 %collective-permute-start.7 = (f32[2,8,320]{2,1,0:T(8,128)S(1)}, f32[2,8,320]{2,1,0:T(8,128)S(1)}, u32[]{:S(2)}, u32[]{:S(2)}) collective-permute-start(f32[2,8,320]{2,1,0:T(8,128)S(1)} %pad_maximum_fusion.2), channel_id=1, source_target_pairs={{0,4},{4,8},{8,12},{1,5},{5,9},{9,13},{2,6},{6,10},{10,14},{3,7},{... | collective-permute-start | bytes 61448 | tf_op jit(solution)/shard_map/ppermute | solution.py:15
  108.1 3.6 %collective-permute-start.9 = (bf16[320,8,128]{2,0,1:T(8,128)(2,1)S(1)}, bf16[320,8,128]{2,0,1:T(8,128)(2,1)S(1)}, u32[]{:S(2)}, u32[]{:S(2)}) collective-permute-start(bf16[320,8,128]{2,0,1:T(8,128)(2,1)S(1)} %fusion.76), channel_id=1, source_target_pairs={{0,4},{4,8},{8,12},{1,5},{5,9},{9,13},{2,6},{6,10},{10,14},{3,7},{... | collective-permute-start | bytes 1966088 | tf_op jit(solution)/shard_map/ppermute | solution.py:15
  111.7 9.1 %collective-permute-done.10 = f32[2,8,320]{2,1,0:T(8,128)S(1)} collective-permute-done((f32[2,8,320]{2,1,0:T(8,128)S(1)}, f32[2,8,320]{2,1,0:T(8,128)S(1)}, u32[]{:S(2)}, u32[]{:S(2)}) %collective-permute-start.10) | collective-permute-done | bytes 20512 | tf_op jit(solution)/shard_map/ppermute | solution.py:15
  121.4 1.7 %divide_convert_fusion.1 = bf16[320,8,128]{2,0,1:T(8,128)(2,1)S(1)} fusion(bf16[320,8,128]{2,0,1:T(8,128)(2,1)S(1)} %collective-permute-done.6, f32[320,8]{0,1:T(8,128)S(1)} %get-tuple-element.19, f32[320,8]{0,1:T(8,128)S(1)} %get-tuple-element.18, pred[]{:T(512)S(6)} %ge.29, f32[320,8]{0,1:T(8,128)S(1)} %get-tuple-element.23, ...), kind=kOutput, calls=%fused_computation.71 | convolution fusion | flops 212008960 | bytes 4624385 | tf_op jit(solution)/shard_map/hqk,khd->qhd/dot_general | solution.py:149
  123.1 9.3 %collective-permute-done.9 = bf16[320,8,128]{2,0,1:T(8,128)(2,1)S(1)} collective-permute-done((bf16[320,8,128]{2,0,1:T(8,128)(2,1)S(1)}, bf16[320,8,128]{2,0,1:T(8,128)(2,1)S(1)}, u32[]{:S(2)}, u32[]{:S(2)}) %collective-permute-start.9) | collective-permute-done | bytes 655392 | tf_op jit(solution)/shard_map/ppermute | solution.py:15
  132.4 1.7 %divide_convert_fusion = bf16[320,8,128]{2,0,1:T(8,128)(2,1)S(1)} fusion(bf16[320,8,128]{2,0,1:T(8,128)(2,1)S(1)} %collective-permute-done.9, f32[320,8]{0,1:T(8,128)S(1)} %get-tuple-element.20, f32[320,8]{0,1:T(8,128)S(1)} %get-tuple-element.22, pred[]{:T(512)S(6)} %ge.29, f32[320,8]{0,1:T(8,128)S(1)} %get-tuple-element.21, ...), kind=kOutput, calls=%fused_computation.70 | convolution fusion | flops 212008960 | bytes 4624385 | tf_op jit(solution)/shard_map/hqk,khd->qhd/dot_general | solution.py:149
  134.1 1.3 copy_bitcast_fusion
  (62 shorter events, 15.3 us)
Async XLA Ops:
  0.6 29.3 %copy-start = (bf16[320,2048]{1,0:T(8,128)(2,1)S(1)}, bf16[320,2048]{1,0:T(8,128)(2,1)}, u32[]{:S(2)}) copy-start(bf16[320,2048]{1,0:T(8,128)(2,1)} %param.8) | copy-start | bytes 3932164
  4.7 9.4 %copy-start.8 = (s32[320]{0:T(512)S(1)}, s32[320]{0:T(512)}, u32[]{:S(2)}) copy-start(s32[320]{0:T(512)} %param.15) | copy-start | bytes 3844
  4.7 9.6 %copy-start.6 = (bf16[320,2048]{1,0:T(8,128)(2,1)S(1)}, bf16[320,2048]{1,0:T(8,128)(2,1)}, u32[]{:S(2)}) copy-start(bf16[320,2048]{1,0:T(8,128)(2,1)} %param.13) | copy-start | bytes 3932164
  8.4 27.0 %collective-permute-start = (bf16[2056,128]{1,0:T(8,128)(2,1)S(1)}, bf16[2056,128]{1,0:T(8,128)(2,1)}, u32[]{:S(2)}, u32[]{:S(2)}) collective-permute-start(bf16[2056,128]{1,0:T(8,128)(2,1)S(1)} %concatenate.31), channel_id=1, source_target_pairs={{0,4},{4,8},{8,12},{1,5},{5,9},{9,13},{2,6},{6,10},{10,14},{3,7},{... | collective-permute-start | bytes 1579016 | tf_op jit(solution)/shard_map/ppermute | solution.py:15
  14.3 2.5 %copy-start.4 = (bf16[320,2048]{1,0:T(8,128)(2,1)S(1)}, bf16[320,2048]{1,0:T(8,128)(2,1)}, u32[]{:S(2)}) copy-start(bf16[320,2048]{1,0:T(8,128)(2,1)} %param.14) | copy-start | bytes 3932164
  15.5 57.3 %collective-permute-start.2 = (bf16[320,2176]{1,0:T(8,128)(2,1)}, bf16[320,2176]{1,0:T(8,128)(2,1)}, u32[]{:S(2)}, u32[]{:S(2)}) collective-permute-start(bf16[320,2176]{1,0:T(8,128)(2,1)} %pad_maximum_fusion), channel_id=1, source_target_pairs={{4,0},{8,4},{12,8},{5,1},{9,5},{13,9},{6,2},{10,6},{14,10},{7,3},{... | collective-permute-start | bytes 4177928 | tf_op jit(solution)/shard_map/ppermute | solution.py:19
  17.8 25.3 %collective-permute-start.4 = (bf16[320,1024]{1,0:T(8,128)(2,1)}, bf16[320,1024]{1,0:T(8,128)(2,1)}, u32[]{:S(2)}, u32[]{:S(2)}) collective-permute-start(bf16[320,1024]{1,0:T(8,128)(2,1)} %get-tuple-element.17), channel_id=1, source_target_pairs={{0,4},{4,8},{8,12},{1,5},{5,9},{9,13},{2,6},{6,10},{10,14},{3,7},{... | collective-permute-start | bytes 1966088 | tf_op jit(solution)/shard_map/ppermute | solution.py:15
  37.9 1.4 %copy-start.7 = (f32[16,128,128]{2,1,0:T(8,128)S(1)}, f32[16,128,128]{2,1,0:T(8,128)}, u32[]{:S(2)}) copy-start(f32[16,128,128]{2,1,0:T(8,128)} %get-tuple-element.29) | copy-start | bytes 3145732
  39.3 3.6 %copy-start.9 = (bf16[2048]{0:T(1024)(128)(2,1)S(1)}, bf16[2048]{0:T(1024)(128)(2,1)}, u32[]{:S(2)}) copy-start(bf16[2048]{0:T(1024)(128)(2,1)} %param.11) | copy-start | bytes 12292
  40.2 12.6 %collective-permute-start.1 = (bf16[2056,128]{1,0:T(8,128)(2,1)}, bf16[2056,128]{1,0:T(8,128)(2,1)}, u32[]{:S(2)}, u32[]{:S(2)}) collective-permute-start(bf16[2056,128]{1,0:T(8,128)(2,1)} %concatenate.32), channel_id=1, source_target_pairs={{0,4},{4,8},{8,12},{1,5},{5,9},{9,13},{2,6},{6,10},{10,14},{3,7},{... | collective-permute-start | bytes 1579016 | tf_op jit(solution)/shard_map/ppermute | solution.py:15
  55.3 6.1 %copy-start.3 = (f32[16,320,128]{2,1,0:T(8,128)S(1)}, f32[16,320,128]{2,1,0:T(8,128)}, u32[]{:S(2)}) copy-start(f32[16,320,128]{2,1,0:T(8,128)} %fusion.9) | copy-start | bytes 7864324
  56.5 21.6 %collective-permute-start.3 = (bf16[320,1152]{1,0:T(8,128)(2,1)S(1)}, bf16[320,1152]{1,0:T(8,128)(2,1)S(1)}, u32[]{:S(2)}, u32[]{:S(2)}) collective-permute-start(bf16[320,1152]{1,0:T(8,128)(2,1)S(1)} %pad_maximum_fusion.1), channel_id=1, source_target_pairs={{0,4},{4,8},{8,12},{1,5},{5,9},{9,13},{2,6},{6,10},{10,14},{3,7},{... | collective-permute-start | bytes 2211848 | tf_op jit(solution)/shard_map/ppermute | solution.py:15
  61.4 2.3 %copy-start.5 = (bf16[320,2048]{1,0:T(8,128)(2,1)S(1)}, bf16[320,2048]{1,0:T(8,128)(2,1)}, u32[]{:S(2)}) copy-start(bf16[320,2048]{1,0:T(8,128)(2,1)} %param.12) | copy-start | bytes 3932164
  66.1 26.1 %collective-permute-start.5 = (bf16[320,8,128]{2,0,1:T(8,128)(2,1)S(1)}, bf16[320,8,128]{2,0,1:T(8,128)(2,1)S(1)}, u32[]{:S(2)}, u32[]{:S(2)}) collective-permute-start(bf16[320,8,128]{2,0,1:T(8,128)(2,1)S(1)} %get-tuple-element.11), channel_id=1, source_target_pairs={{0,4},{4,8},{8,12},{1,5},{5,9},{9,13},{2,6},{6,10},{10,14},{3,7},{... | collective-permute-start | bytes 1966088 | tf_op jit(solution)/shard_map/ppermute | solution.py:15
  70.5 36.8 %collective-permute-start.8 = (bf16[320,8,128]{2,0,1:T(8,128)(2,1)S(1)}, bf16[320,8,128]{2,0,1:T(8,128)(2,1)S(1)}, u32[]{:S(2)}, u32[]{:S(2)}) collective-permute-start(bf16[320,8,128]{2,0,1:T(8,128)(2,1)S(1)} %get-tuple-element.12), channel_id=1, source_target_pairs={{0,4},{4,8},{8,12},{1,5},{5,9},{9,13},{2,6},{6,10},{10,14},{3,7},{... | collective-permute-start | bytes 1966088 | tf_op jit(solution)/shard_map/ppermute | solution.py:15
  93.0 28.3 %collective-permute-start.6 = (bf16[320,8,128]{2,0,1:T(8,128)(2,1)S(1)}, bf16[320,8,128]{2,0,1:T(8,128)(2,1)S(1)}, u32[]{:S(2)}, u32[]{:S(2)}) collective-permute-start(bf16[320,8,128]{2,0,1:T(8,128)(2,1)S(1)} %fusion.73), channel_id=1, source_target_pairs={{0,4},{4,8},{8,12},{1,5},{5,9},{9,13},{2,6},{6,10},{10,14},{3,7},{... | collective-permute-start | bytes 1966088 | tf_op jit(solution)/shard_map/ppermute | solution.py:15
  100.0 20.8 %collective-permute-start.10 = (f32[2,8,320]{2,1,0:T(8,128)S(1)}, f32[2,8,320]{2,1,0:T(8,128)S(1)}, u32[]{:S(2)}, u32[]{:S(2)}) collective-permute-start(f32[2,8,320]{2,1,0:T(8,128)S(1)} %pad_maximum_fusion.3), channel_id=1, source_target_pairs={{0,4},{4,8},{8,12},{1,5},{5,9},{9,13},{2,6},{6,10},{10,14},{3,7},{... | collective-permute-start | bytes 61448 | tf_op jit(solution)/shard_map/ppermute | solution.py:15
  104.4 16.9 %collective-permute-start.7 = (f32[2,8,320]{2,1,0:T(8,128)S(1)}, f32[2,8,320]{2,1,0:T(8,128)S(1)}, u32[]{:S(2)}, u32[]{:S(2)}) collective-permute-start(f32[2,8,320]{2,1,0:T(8,128)S(1)} %pad_maximum_fusion.2), channel_id=1, source_target_pairs={{0,4},{4,8},{8,12},{1,5},{5,9},{9,13},{2,6},{6,10},{10,14},{3,7},{... | collective-permute-start | bytes 61448 | tf_op jit(solution)/shard_map/ppermute | solution.py:15
  107.2 14.1 %copy-start.2 = (bf16[16,320,320]{1,2,0:T(8,128)(2,1)S(1)}, bf16[16,320,320]{1,2,0:T(8,128)(2,1)}, u32[]{:S(2)}) copy-start(bf16[16,320,320]{1,2,0:T(8,128)(2,1)} %get-tuple-element.7) | copy-start | bytes 9830404
  108.1 24.3 %collective-permute-start.9 = (bf16[320,8,128]{2,0,1:T(8,128)(2,1)S(1)}, bf16[320,8,128]{2,0,1:T(8,128)(2,1)S(1)}, u32[]{:S(2)}, u32[]{:S(2)}) collective-permute-start(bf16[320,8,128]{2,0,1:T(8,128)(2,1)S(1)} %fusion.76), channel_id=1, source_target_pairs={{0,4},{4,8},{8,12},{1,5},{5,9},{9,13},{2,6},{6,10},{10,14},{3,7},{... | collective-permute-start | bytes 1966088 | tf_op jit(solution)/shard_map/ppermute | solution.py:15
  132.4 3.0 %copy-start.1 = (bf16[320,2048]{1,0:T(8,128)(2,1)S(1)}, bf16[320,2048]{1,0:T(8,128)(2,1)}, u32[]{:S(2)}) copy-start(bf16[320,2048]{1,0:T(8,128)(2,1)} %param.8) | copy-start | bytes 3932164
